TPU v7x, 32 devices: a whole 2x2x4 slice. The times are simulated.
32 devices in a mesh: ctx: 8 (over y, x, core), tp: 4 (over z).
Axes of the slice: x: 2, y: 2, z: 4, core: 2. Of those that a mesh axis runs over, the one named last changes fastest.
Arguments:
- stream: bfloat16 [1024, 4096], P('ctx', 'tp'), may hold values from -52 to 52
- shutter: bfloat16 [1024, 4096], P('ctx', 'tp'), may hold values from -6 to 6
- feeder: bfloat16 [1024, 4096], P('ctx', 'tp'), may hold values from -6 to 6
- stencil: float32 [7, 4096], P(None, 'tp'), may hold values from -2 to 2
- valves: bfloat16 [1024, 4096], P('ctx', 'tp'), may hold values from -6 to 6
- intake: bfloat16 [1024, 4096], P('ctx', 'tp'), may hold values from -6 to 6
- kernel: float32 [128, 4096], P(None, 'tp'), may hold values from -0.5 to 0.5
- scaling: float32 [4096], P('tp'), may hold values from 0.1 to 1.9
- queries: bfloat16 [1024, 4096], P('ctx', 'tp'), may hold values from -87 to 87
- matchers: bfloat16 [1024, 4096], P('ctx', 'tp'), may hold values from -6 to 6
- segments: int32 [1024], replicated, may hold values from 0 to 3, never falling along the last dimension, each value on 1 to 768 neighbouring positions
- cotangent: bfloat16 [1024, 4096], P('ctx', 'tp'), may hold values from -6 to 6
Outputs:
- result: bfloat16 [1024, 4096], P('ctx', 'tp')
- stream_grad: bfloat16 [1024, 4096], P('ctx', 'tp')
- shutter_grad: bfloat16 [1024, 4096], P('ctx', 'tp')
- feeder_grad: bfloat16 [1024, 4096], P('ctx', 'tp')
- stencil_grad: float32 [7, 4096], P(None, 'tp')
- valves_grad: bfloat16 [1024, 4096], P('ctx', 'tp')
- intake_grad: bfloat16 [1024, 4096], P('ctx', 'tp')
- kernel_grad: float32 [128, 4096], P(None, 'tp')
- scaling_grad: float32 [4096], P('tp')
- queries_grad: bfloat16 [1024, 4096], P('ctx', 'tp')
- matchers_grad: bfloat16 [1024, 4096], P('ctx', 'tp')
Inputs may be any that keep to these rules, and one draw needn't show every extreme that they name: `segments`: document numbers never fall along the context; each of the 4 documents covers 1 to 768 positions, and one covers exactly 768.
All inputs are finite; a program needn't handle non-finite values.
Results may differ from a plain program's by a relative error of at most 0.03.
Values may be sent and summed in bfloat16 or wider, within the bound.
No kernel may reach another device: no remote copies, remote signals or barrier semaphores. Data moves between devices by JAX's collectives and lax.ppermute only.
A program may use at most 192 MiB of HBM per device.

v0:
```python
import math

import jax
import jax.numpy as jnp
from jax import lax
from jax.sharding import PartitionSpec as P

HD = 128
D = 4096
KS = 7
KM = 128


epsilon = 1e-06


def as_sent(shard):

    def short(part):
        return part.astype(jnp.bfloat16) if part.dtype == jnp.float32 else part

    return jax.tree.map(short, shard)


def passed_along(value, axis, steps):
    count = lax.axis_size(axis)
    leading, last = (max(0, -steps), min(count, count - steps))
    return lax.ppermute(value, axis, [(source, source + steps) for source in range(leading, last)])


def depthwise(padded, tap_rows):
    return lax.conv_general_dilated(
        padded[None],
        tap_rows[:, None, :],
        (1,),
        "VALID",
        dimension_numbers=("NWC", "WIO", "NWC"),
        feature_group_count=padded.shape[1],
        precision=lax.Precision.HIGHEST,
    )[0]


def neighbor_rows(edge_rows, offset):
    return passed_along(as_sent(edge_rows), "ctx", offset).astype(edge_rows.dtype)


def channel_total(partial_value):
    return lax.psum(partial_value, "tp")


def shards(
    stream,
    shutter,
    feeder,
    stencil,
    valves,
    intake,
    kernel,
    scaling,
    queries,
    matchers,
    segments,
    cotangent,
):
    local_rows = stream.shape[0]
    width_local = stream.shape[1]
    head_count = width_local // HD
    total_rows = local_rows * lax.axis_size("ctx")
    position = lax.axis_index("ctx") * local_rows
    scale_factor = 1.0 / math.sqrt(HD)
    widened = stream.astype(jnp.float32)
    inner_one = feeder.astype(jnp.float32) * widened
    rim_one = neighbor_rows(inner_one[local_rows - (KS - 1) :], 1)
    padded_one = jnp.concatenate([rim_one, inner_one], axis=0)
    conv_one = depthwise(padded_one, stencil[::-1])
    first_out = (widened + shutter.astype(jnp.float32) * conv_one).astype(jnp.bfloat16)
    first_wide = first_out.astype(jnp.float32)
    inner_two = intake.astype(jnp.float32) * first_wide
    rim_two = neighbor_rows(inner_two[local_rows - (KM - 1) :], 1)
    padded_two = jnp.concatenate([rim_two, inner_two], axis=0)
    conv_two = depthwise(padded_two, kernel[::-1])
    second_out = (first_wide + valves.astype(jnp.float32) * conv_two).astype(jnp.bfloat16)
    second_wide = second_out.astype(jnp.float32)
    squares = channel_total(jnp.sum(second_wide * second_wide, axis=1))
    inverse_rms = lax.rsqrt(squares / D + epsilon)
    normed = (second_wide * inverse_rms[:, None] * scaling).astype(jnp.bfloat16)
    keys_whole, values_whole = (
        lax.all_gather(matchers, "ctx", axis=0, tiled=True),
        lax.all_gather(normed, "ctx", axis=0, tiled=True),
    )
    query_pos = position + jnp.arange(local_rows, dtype=jnp.int32)
    key_pos = jnp.arange(total_rows, dtype=jnp.int32)
    query_seg = lax.dynamic_slice_in_dim(segments, position, local_rows, 0)
    visible = (key_pos[None, :] <= query_pos[:, None]) & (segments[None, :] == query_seg[:, None])
    contract = (((1,), (1,)), ((), ()))
    weight_list = []
    dscore_list = []
    attended_list = []
    query_grad_list = []
    logsum_list = []
    delta_list = []
    for head_index in range(head_count):
        columns = slice(head_index * HD, (head_index + 1) * HD)
        query_head = queries[:, columns]
        key_head = keys_whole[:, columns]
        value_head = values_whole[:, columns]
        cotangent_head = cotangent[:, columns]
        scores = (
            lax.dot_general(query_head, key_head, contract, preferred_element_type=jnp.float32)
            * scale_factor
        )
        scores = jnp.where(visible, scores, -jnp.inf)
        row_max = jnp.max(scores, axis=1)
        logsum = row_max + jnp.log(jnp.sum(jnp.exp(scores - row_max[:, None]), axis=1))
        weights = jnp.exp(scores - logsum[:, None]).astype(jnp.bfloat16)
        attended = jnp.dot(weights, value_head, preferred_element_type=jnp.float32)
        weight_grad = lax.dot_general(
            cotangent_head, value_head, contract, preferred_element_type=jnp.float32
        )
        row_delta = jnp.sum(cotangent_head.astype(jnp.float32) * attended, axis=1)
        dscore = (
            scale_factor * weights.astype(jnp.float32) * (weight_grad - row_delta[:, None])
        ).astype(jnp.bfloat16)
        query_grad = jnp.dot(dscore, key_head, preferred_element_type=jnp.float32)
        weight_list.append(weights)
        dscore_list.append(dscore)
        attended_list.append(attended)
        query_grad_list.append(query_grad)
        logsum_list.append(logsum)
        delta_list.append(row_delta)
    attended_all = jnp.concatenate(attended_list, axis=1)
    result = (second_wide + attended_all).astype(jnp.bfloat16)
    queries_grad = jnp.concatenate(query_grad_list, axis=1).astype(jnp.bfloat16)
    query_heads = queries.reshape(local_rows, head_count, HD)
    cotangent_heads = cotangent.reshape(local_rows, head_count, HD)
    weights_all = jnp.stack(weight_list)
    dscore_all = jnp.stack(dscore_list)
    dscore_part = lax.slice_in_dim(dscore_all, 0, local_rows * lax.axis_size("ctx"), axis=2)
    key_part = jnp.einsum(
        "hts,the->she", dscore_part, query_heads, preferred_element_type=jnp.float32
    )
    value_part = jnp.einsum(
        "hts,the->she", weights_all, cotangent_heads, preferred_element_type=jnp.float32
    )
    summed = lax.psum_scatter(
        jnp.concatenate(
            [
                key_part.reshape(local_rows * lax.axis_size("ctx"), width_local),
                value_part.reshape(local_rows * lax.axis_size("ctx"), width_local),
            ],
            axis=1,
        ).astype(jnp.bfloat16),
        "ctx",
        scatter_dimension=0,
        tiled=True,
    ).astype(jnp.float32)
    matchers_grad = summed[:, :width_local].astype(jnp.bfloat16)
    value_grad = summed[:, width_local:]
    gain_part = value_grad * scaling
    projected = channel_total(jnp.sum(gain_part * second_wide, axis=1))
    scaling_part = jnp.sum(value_grad * second_wide * inverse_rms[:, None], axis=0)
    second_grad = (
        cotangent.astype(jnp.float32)
        + inverse_rms[:, None] * gain_part
        - second_wide * (inverse_rms**3 * projected / D)[:, None]
    )
    valves_grad = (second_grad * conv_two).astype(jnp.bfloat16)
    dconv_two = second_grad * valves.astype(jnp.float32)
    back_two = neighbor_rows(dconv_two[: KM - 1], -1)
    dinner_two = depthwise(jnp.concatenate([dconv_two, back_two], axis=0), kernel)
    intake_grad = (dinner_two * first_wide).astype(jnp.bfloat16)
    kernel_part = depthwise(padded_two, dconv_two)[::-1]
    first_grad = second_grad + dinner_two * intake.astype(jnp.float32)
    shutter_grad = (first_grad * conv_one).astype(jnp.bfloat16)
    dconv_one = first_grad * shutter.astype(jnp.float32)
    back_one = neighbor_rows(dconv_one[: KS - 1], -1)
    dinner_one = depthwise(jnp.concatenate([dconv_one, back_one], axis=0), stencil)
    feeder_grad = (dinner_one * widened).astype(jnp.bfloat16)
    stencil_part = depthwise(padded_one, dconv_one)[::-1]
    stream_grad = (first_grad + dinner_one * feeder.astype(jnp.float32)).astype(jnp.bfloat16)
    stencil_sum, kernel_sum, scaling_sum = (
        lax.psum(stencil_part.astype(jnp.bfloat16), "ctx").astype(jnp.float32),
        lax.psum(kernel_part.astype(jnp.bfloat16), "ctx").astype(jnp.float32),
        lax.psum(scaling_part.astype(jnp.bfloat16), "ctx").astype(jnp.float32),
    )
    normalizer = math.sqrt(total_rows)
    return (
        result,
        stream_grad,
        shutter_grad,
        feeder_grad,
        stencil_sum / normalizer,
        valves_grad,
        intake_grad,
        kernel_sum / normalizer,
        scaling_sum / normalizer,
        queries_grad,
        matchers_grad,
    )


def solution(mesh):
    placed = (
        P("ctx", "tp"),
        P("ctx", "tp"),
        P("ctx", "tp"),
        P(None, "tp"),
        P("ctx", "tp"),
        P("ctx", "tp"),
        P(None, "tp"),
        P("tp"),
        P("ctx", "tp"),
        P("ctx", "tp"),
        P(),
        P("ctx", "tp"),
    )
    return jax.shard_map(
        shards,
        mesh=mesh,
        in_specs=placed,
        out_specs=(
            P("ctx", "tp"),
            P("ctx", "tp"),
            P("ctx", "tp"),
            P("ctx", "tp"),
            P(None, "tp"),
            P("ctx", "tp"),
            P("ctx", "tp"),
            P(None, "tp"),
            P("tp"),
            P("ctx", "tp"),
            P("ctx", "tp"),
        ),
        check_vma=False,
    )
```

profile of v0, /device:TPU:0, one launch (start us, length us, event | category | flops | bytes accessed | tf_op | source)
XLA Modules:
  0.0 272.9 jit_solution(10646670163490515569)
XLA Ops:
  9.1 2.4 collective-permute-start
  11.4 2.8 %rev.12 = f32[7,1024]{1,0:T(8,128)S(1)} reverse(f32[7,1024]{1,0:T(8,128)} %param.15), dimensions={0} | reverse | bytes 57344 | tf_op jit(solution)/shard_map/rev | solution.py:75
  18.3 4.5 %collective-permute-start.1 = (bf16[127,1024]{1,0:T(8,128)(2,1)}, bf16[127,1024]{1,0:T(8,128)(2,1)S(1)}, u32[]{:S(2)}, u32[]{:S(2)}) collective-permute-start(bf16[127,1024]{1,0:T(8,128)(2,1)} %slice.349), channel_id=1, source_target_pairs={{0,4},{4,8},{8,12},{12,16},{16,20},{20,24},{24,28},{1,5},{5,9},{9,... | collective-permute-start | bytes 780296 | tf_op jit(solution)/shard_map/ppermute | solution.py:28
  25.1 5.6 %fusion.74 = f32[1,128,1024]{2,0,1:T(1,128)S(1)} fusion(f32[1,255,1024]{2,0,1:T(1,128)S(1)} %broadcast_in_dim.33, f32[128,1,1024]{2,0,1:T(8,128)S(1)} %bitcast.165), kind=kOutput, calls=%fused_computation.133 | convolution fusion | flops 201326592 | bytes 2093056 | tf_op jit(solution)/shard_map/conv_general_dilated | solution.py:32
  31.6 11.9 %psum.35 = f32[128]{0:T(128)S(1)} all-reduce(f32[128]{0:T(128)S(1)} %get-tuple-element.63), channel_id=1, replica_groups=mesh['ctx'=8,'tp'=4] {'tp'}, use_global_device_ids=true, to_apply=%region_3.4 | all-reduce | flops 128 | bytes 1024 | tf_op jit(solution)/shard_map/psum | solution.py:48
  64.7 2.6 copy.116
  67.3 7.6 %all-gather.5.cloned.1.call-done = bf16[1024,1024]{1,0:T(8,128)(2,1)} async-done(((bf16[128,1024]{1,0:T(8,128)(2,1)}), bf16[1024,1024]{1,0:T(8,128)(2,1)}) %all-gather.5.cloned.1.call-update) | async-done | bytes 2097168 | tf_op jit(solution)/shard_map/all_gather | solution.py:89
  91.7 2.6 copy.114
  94.3 4.7 %pad_maximum_fusion = bf16[1024,2048]{1,0:T(8,128)(2,1)} fusion(bf16[1024,1024]{1,0:T(8,128)(2,1)} %copy.116, bf16[1024,1024]{1,0:T(8,128)(2,1)} %copy.114), kind=kLoop, calls=%fused_computation | loop fusion | flops 8388608 | bytes 8388608 | tf_op jit(solution)/shard_map/concatenate | solution.py:146
  111.6 1.9 fusion.39
  113.5 1.9 fusion.38
  115.4 1.8 fusion.37
  117.2 1.8 fusion.36
  119.1 1.9 fusion.35
  120.9 1.9 fusion.34
  124.7 25.8 %reduce-scatter.2.cloned.1.call-done = bf16[128,2048]{1,0:T(8,128)(2,1)} async-done(((bf16[1024,2048]{1,0:T(8,128)(2,1)}), bf16[128,2048]{1,0:T(8,128)(2,1)}) %reduce-scatter.2.cloned.1.call-update) | async-done | bytes 524304 | tf_op jit(solution)/shard_map/reduce_scatter | solution.py:145
  151.7 11.7 %psum.36 = f32[128]{0:T(128)S(1)} all-reduce(f32[128]{0:T(128)S(1)} %get-tuple-element.34), channel_id=1, replica_groups=mesh['ctx'=8,'tp'=4] {'tp'}, use_global_device_ids=true, to_apply=%region_28.29 | all-reduce | flops 128 | bytes 1024 | tf_op jit(solution)/shard_map/psum | solution.py:48
  164.6 6.8 %fusion.70 = bf16[1,128,1024]{2,0,1:T(2,128)(2,1)S(1)} fusion(f32[1,255,1024]{2,0,1:T(1,128)} %copy-done.30, f32[128,1,1024]{2,0,1:T(8,128)S(1)} %bitcast.159), kind=kOutput, calls=%fused_computation.129 | convolution fusion | flops 201326592 | bytes 1830912 | tf_op jit(solution)/shard_map/conv_general_dilated | solution.py:32
  171.5 2.6 rev.15
  179.4 45.7 %all-reduce.3.cloned.1.call-done = bf16[128,1024]{1,0:T(8,128)(2,1)} async-done(((bf16[128,1024]{1,0:T(8,128)(2,1)}), bf16[128,1024]{1,0:T(8,128)(2,1)}) %all-reduce.3.cloned.1.call-update) | async-done | bytes 262160 | tf_op jit(solution)/shard_map/psum | solution.py:183
  225.1 1.8 convert_multiply_fusion.16
  227.1 5.8 %fusion.40 = f32[1,128,1024]{2,0,1:T(1,128)S(1)} fusion(f32[1,255,1024]{2,1,0:T(8,128)S(1)} %maximum_bitcast_fusion, f32[128,1,1024]{2,0,1:T(8,128)S(1)} %bitcast.164), kind=kOutput, calls=%fused_computation.77 | convolution fusion | flops 201326592 | bytes 2093056 | tf_op jit(solution)/shard_map/conv_general_dilated | solution.py:32
  232.9 2.7 %multiply_convert_fusion = (bf16[128,1024]{1,0:T(8,128)(2,1)}, f32[128,1024]{1,0:T(8,128)S(1)}, bf16[128,1024]{1,0:T(8,128)(2,1)}, bf16[128,1024]{1,0:T(8,128)(2,1)}, bf16[128,1024]{1,0:T(8,128)(2,1)}) fusion(f32[1,136,1024]{2,1,0:T(8,128)S(1)} %reshape.119, bf16[128,1024]{1,0:T(8,128)(2,1)S(1)} %copy-done.26, f32[1,128,1024]{2,0,1:T(1,128)S(1)} %fusion.40, ...), kind=kLoop, calls=%fused_computation.136 | loop fusion | flops 2621440 | bytes 4985856 | tf_op jit(solution)/shard_map/convert_element_type | solution.py:174
  237.1 22.4 %all-reduce = (bf16[7,1024]{1,0:T(8,128)(2,1)S(1)}, bf16[1024]{0:T(1024)(128)(2,1)S(1)}) all-reduce(bf16[7,1024]{1,0:T(8,128)(2,1)S(1)} %rev.14, bf16[1024]{0:T(1024)(128)(2,1)S(1)} %get-tuple-element.33), channel_id=1, replica_groups=mesh['ctx'=8,'tp'=4] {'ctx'}, use_global_device_ids=true, to_apply=%region_29.30 | all-reduce | flops 8192 | bytes 32768 | tf_op jit(solution)/shard_map/psum | solution.py:182
  (215 shorter events, 77.0 us)
Async XLA Ops:
  7.2 37.5 %all-gather.3.cloned.1.call-start = ((), (), s32[]{:S(2)}) async-start(), calls=%async_computation.1 | async-start | bytes 2359296 | tf_op jit(solution)/shard_map/all_gather | solution.py:88
  7.9 67.0 %all-gather.5.cloned.1.call-start = ((), (), s32[]{:S(2)}) async-start(), calls=%async_computation.2 | async-start | bytes 2359296 | tf_op jit(solution)/shard_map/all_gather | solution.py:89
  9.1 5.2 %collective-permute-start = (bf16[6,1024]{1,0:T(8,128)(2,1)S(1)}, bf16[6,1024]{1,0:T(8,128)(2,1)S(1)}, u32[]{:S(2)}, u32[]{:S(2)}) collective-permute-start(bf16[6,1024]{1,0:T(8,128)(2,1)S(1)} %slice.351), channel_id=1, source_target_pairs={{0,4},{4,8},{8,12},{12,16},{16,20},{20,24},{24,28},{1,5},{5,9},{9,... | collective-permute-start | bytes 36872 | tf_op jit(solution)/shard_map/ppermute | solution.py:28
  16.6 6.2 %copy-start.33 = (f32[128,1024]{1,0:T(8,128)S(1)}, f32[128,1024]{1,0:T(8,128)}, u32[]{:S(2)}) copy-start(f32[128,1024]{1,0:T(8,128)} %param.18) | copy-start | bytes 1572868
  17.4 5.9 %copy-start.36 = (bf16[128,1024]{1,0:T(8,128)(2,1)S(1)}, bf16[128,1024]{1,0:T(8,128)(2,1)}, u32[]{:S(2)}) copy-start(bf16[128,1024]{1,0:T(8,128)(2,1)} %param.20) | copy-start | bytes 786436
  17.4 6.8 %copy-start.39 = (s32[1024]{0:T(1024)S(1)}, s32[1024]{0:T(1024)}, u32[]{:S(2)}) copy-start(s32[1024]{0:T(1024)} %param.22) | copy-start | bytes 12292
  17.5 13.3 %copy-start.2 = (bf16[128,1024]{1,0:T(8,128)(2,1)}, bf16[128,1024]{1,0:T(8,128)(2,1)S(1)}, u32[]{:S(2)}) copy-start(bf16[128,1024]{1,0:T(8,128)(2,1)S(1)} %get-tuple-element.66) | copy-start | bytes 786436
  18.3 5.9 %collective-permute-start.1 = (bf16[127,1024]{1,0:T(8,128)(2,1)}, bf16[127,1024]{1,0:T(8,128)(2,1)S(1)}, u32[]{:S(2)}, u32[]{:S(2)}) collective-permute-start(bf16[127,1024]{1,0:T(8,128)(2,1)} %slice.349), channel_id=1, source_target_pairs={{0,4},{4,8},{8,12},{12,16},{16,20},{20,24},{24,28},{1,5},{5,9},{9,... | collective-permute-start | bytes 780296 | tf_op jit(solution)/shard_map/ppermute | solution.py:28
  25.1 18.4 %copy-start.37 = (f32[1024]{0:T(1024)S(1)}, f32[1024]{0:T(1024)}, u32[]{:S(2)}) copy-start(f32[1024]{0:T(1024)} %param.19) | copy-start | bytes 12292
  44.4 106.1 %reduce-scatter.2.cloned.1.call-start = ((), (), s32[]{:S(2)}) async-start(), calls=%async_computation.3 | async-start | bytes 4718592 | tf_op jit(solution)/shard_map/reduce_scatter | solution.py:145
  67.3 14.2 %copy-start.4 = (bf16[128,1024]{1,0:T(8,128)(2,1)S(1)}, bf16[128,1024]{1,0:T(8,128)(2,1)}, u32[]{:S(2)}) copy-start(bf16[128,1024]{1,0:T(8,128)(2,1)} %get-tuple-element.60) | copy-start | bytes 786436
  74.9 6.9 %copy-start.24 = (bf16[128,1024]{1,0:T(8,128)(2,1)S(1)}, bf16[128,1024]{1,0:T(8,128)(2,1)}, u32[]{:S(2)}) copy-start(bf16[128,1024]{1,0:T(8,128)(2,1)} %get-tuple-element.62) | copy-start | bytes 786436
  74.9 7.3 %copy-start.10 = (bf16[128,1024]{1,0:T(8,128)(2,1)S(1)}, bf16[128,1024]{1,0:T(8,128)(2,1)}, u32[]{:S(2)}) copy-start(bf16[128,1024]{1,0:T(8,128)(2,1)} %get-tuple-element.48) | copy-start | bytes 786436
  99.0 12.6 %copy-start.17 = (bf16[1024,1024]{1,0:T(8,128)(2,1)S(1)}, bf16[1024,1024]{1,0:T(8,128)(2,1)}, u32[]{:S(2)}) copy-start(bf16[1024,1024]{1,0:T(8,128)(2,1)} %all-gather.3.cloned.1.call-done) | copy-start | bytes 6291460
  99.0 126.1 %all-reduce.3.cloned.1.call-start = ((), (), s32[]{:S(2)}) async-start(), calls=%async_computation.4 | async-start | bytes 524288 | tf_op jit(solution)/shard_map/psum | solution.py:183
  104.3 18.6 %copy-start.22 = (bf16[128,1024]{1,0:T(8,128)(2,1)S(1)}, bf16[128,1024]{1,0:T(8,128)(2,1)}, u32[]{:S(2)}) copy-start(bf16[128,1024]{1,0:T(8,128)(2,1)} %get-tuple-element.102) | copy-start | bytes 786436
  110.3 13.4 %copy-start.23 = (bf16[128,1024]{1,0:T(8,128)(2,1)S(1)}, bf16[128,1024]{1,0:T(8,128)(2,1)}, u32[]{:S(2)}) copy-start(bf16[128,1024]{1,0:T(8,128)(2,1)} %get-tuple-element.104) | copy-start | bytes 786436
  113.5 49.9 %copy-start.21 = (bf16[128,1024]{1,0:T(8,128)(2,1)S(1)}, bf16[128,1024]{1,0:T(8,128)(2,1)}, u32[]{:S(2)}) copy-start(bf16[128,1024]{1,0:T(8,128)(2,1)} %param.16) | copy-start | bytes 786436
  164.6 10.2 %copy-start.35 = (f32[128,128]{0,1:T(8,128)S(1)}, f32[128,128]{0,1:T(8,128)}, u32[]{:S(2)}) copy-start(f32[128,128]{0,1:T(8,128)} %get-tuple-element.88) | copy-start | bytes 196612
  171.4 7.2 %copy-start.18 = (bf16[128,2048]{1,0:T(8,128)(2,1)S(1)}, bf16[128,2048]{1,0:T(8,128)(2,1)}, u32[]{:S(2)}) copy-start(bf16[128,2048]{1,0:T(8,128)(2,1)} %reduce-scatter.2.cloned.1.call-done) | copy-start | bytes 1572868
  174.9 51.9 %collective-permute-start.2 = (bf16[127,1024]{1,0:T(8,128)(2,1)S(1)}, bf16[127,1024]{1,0:T(8,128)(2,1)S(1)}, u32[]{:S(2)}, u32[]{:S(2)}) collective-permute-start(bf16[127,1024]{1,0:T(8,128)(2,1)S(1)} %slice.348), channel_id=1, source_target_pairs={{4,0},{8,4},{12,8},{16,12},{20,16},{24,20},{28,24},{5,1},{9,5},{13... | collective-permute-start | bytes 780296 | tf_op jit(solution)/shard_map/ppermute | solution.py:28
  178.7 48.4 %copy-start.34 = (f32[128,1024]{1,0:T(8,128)S(1)}, f32[128,1024]{1,0:T(8,128)}, u32[]{:S(2)}) copy-start(f32[128,1024]{1,0:T(8,128)} %param.18) | copy-start | bytes 1572868
  227.0 5.8 %copy-start.3 = (bf16[128,1024]{1,0:T(8,128)(2,1)S(1)}, bf16[128,1024]{1,0:T(8,128)(2,1)}, u32[]{:S(2)}) copy-start(bf16[128,1024]{1,0:T(8,128)(2,1)} %copy-done.2) | copy-start | bytes 786436
  260.1 3.1 %collective-permute-start.3 = (bf16[6,1024]{1,0:T(8,128)(2,1)S(1)}, bf16[6,1024]{1,0:T(8,128)(2,1)S(1)}, u32[]{:S(2)}, u32[]{:S(2)}) collective-permute-start(bf16[6,1024]{1,0:T(8,128)(2,1)S(1)} %slice.350), channel_id=1, source_target_pairs={{4,0},{8,4},{12,8},{16,12},{20,16},{24,20},{28,24},{5,1},{9,5},{13... | collective-permute-start | bytes 36872 | tf_op jit(solution)/shard_map/ppermute | solution.py:28
  (25 other events, 73.2 us)
Sparse Core Ops, SparseCore 0:
  9.9 30.5 all-gather.2
  44.5 30.3 all-gather.4
  99.1 51.3 reduce-scatter.1
  174.3 50.7 all-reduce.2
where the time goes:
time: 274 us; the launch traced here: 273 us
  waiting for transfers between devices  81 us (30%)
  matrix products  60.8 us (22%)
  blocking collectives  46 us (17%)
  local copies, waits for them, and re-layouts  35.2 us (13%)
  other arithmetic  25.2 us (9%)
  between operations  14.6 us (5%)
  starting transfers between devices  10 us (4%)
    psum x1, waiting for transfers between devices, shards(): lax.psum(kernel_part.astype(jnp.bfloat16), 'ctx').astype(jnp.float32)  45.7 us
    reduce_scatter x1, waiting for transfers between devices, shards(): lax.psum_scatter(jnp.concatenate([key_part.reshape(local_rows * lax.axis_...  25.8 us
    psum x2, blocking collectives, channel_total(): return lax.psum(partial_value, 'tp')  23.6 us
    psum x1, blocking collectives, shards(): lax.psum(stencil_part.astype(jnp.bfloat16), 'ctx').astype(jnp.float32)  22.4 us
    conv_general_dilated x6, matrix products, depthwise(): lax.conv_general_dilated(padded[None], tap_rows[:, None, :], (1,), 'VALID...  19.9 us
    dot_general x8, matrix products, shards(): query_grad = jnp.dot(dscore, key_head, preferred_element_type=jnp.float32)  13 us
    unnamed x93, local copies, waits for them, and re-layouts  12.7 us
    dot_general x8, matrix products, shards(): lax.dot_general(query_head, key_head, contract, preferred_element_type=jn...  10.6 us
  transfers between devices with their start and end apart: 8, of which 4 were waited for; matrix products, arithmetic and copies ran while one was open for 25% of the time, Pallas kernels for 0%

commit v1 on v0

--- a/solution.py
+++ b/solution.py
@@ -44,8 +44,26 @@
     return passed_along(as_sent(edge_rows), "ctx", offset).astype(edge_rows.dtype)
 
 
+def butterfly_total(value, axis, sent_type=None):
+    count = lax.axis_size(axis)
+    if count & (count - 1):
+        if sent_type is None:
+            return lax.psum(value, axis)
+        return lax.psum(value.astype(sent_type), axis).astype(value.dtype)
+    step = 1
+    while step < count:
+        pairs = [(source, source ^ step) for source in range(count)]
+        if sent_type is None:
+            value = value + lax.ppermute(value, axis, pairs)
+        else:
+            rounded = value.astype(sent_type)
+            value = rounded.astype(value.dtype) + lax.ppermute(rounded, axis, pairs).astype(value.dtype)
+        step *= 2
+    return value
+
+
 def channel_total(partial_value):
-    return lax.psum(partial_value, "tp")
+    return butterfly_total(partial_value, "tp")
 
 
 def shards(
@@ -178,11 +196,12 @@
     feeder_grad = (dinner_one * widened).astype(jnp.bfloat16)
     stencil_part = depthwise(padded_one, dconv_one)[::-1]
     stream_grad = (first_grad + dinner_one * feeder.astype(jnp.float32)).astype(jnp.bfloat16)
-    stencil_sum, kernel_sum, scaling_sum = (
-        lax.psum(stencil_part.astype(jnp.bfloat16), "ctx").astype(jnp.float32),
-        lax.psum(kernel_part.astype(jnp.bfloat16), "ctx").astype(jnp.float32),
-        lax.psum(scaling_part.astype(jnp.bfloat16), "ctx").astype(jnp.float32),
-    )
+    filter_sum = butterfly_total(
+        jnp.concatenate([kernel_part, scaling_part[None]], axis=0), "ctx", jnp.bfloat16
+    )
+    kernel_sum = filter_sum[:KM]
+    scaling_sum = filter_sum[KM]
+    stencil_sum = butterfly_total(stencil_part, "ctx", jnp.bfloat16)
     normalizer = math.sqrt(total_rows)
     return (
         result,

time: 274 us -> 212 us (0.77)
  blocking collectives: 46 us -> 0 us
  waiting for transfers between devices: 81 us -> 48 us
  starting transfers between devices: 10 us -> 25.2 us
  local copies, waits for them, and re-layouts: 35.2 us -> 41.4 us
  matrix products: 60.8 us -> 56.3 us
    psum x3 -> x0, blocking collectives: 46 us -> none  [the longest x2 23.6 us: channel_total(): return lax.psum(partial_value, 'tp')]
    psum x1 -> x0, waiting for transfers between devices: 45.7 us -> none  [shards(): lax.psum(kernel_part.astype(jnp.bfloat16), 'ctx').astype(jnp.float32)]
    ppermute x0 -> x10, starting transfers between devices: none -> 15.4 us  [the longest x4 8.12 us: butterfly_total(): value = value + lax.ppermute(value, axis, pairs)]
    ppermute x0 -> x10, waiting for transfers between devices: none -> 12.8 us  [the longest x6 9.67 us: butterfly_total(): lax.ppermute(rounded, axis, pairs).astype(value.dtype)]
    dot_general x8, local copies, waits for them, and re-layouts: 5.06 us -> 10.3 us  [shards(): attended = jnp.dot(weights, value_head, preferred_element_type=jnp.float32)]
    dot_general x8, matrix products: 13 us -> 9.23 us  [shards(): query_grad = jnp.dot(dscore, key_head, preferred_element_type=jnp.float32)]
    reduce_scatter x1, waiting for transfers between devices: 25.8 us -> 23 us  [shards(): lax.psum_scatter(jnp.concatenate([key_part.reshape(local_rows * lax.axis_...]
    unnamed x93 -> x107, local copies, waits for them, and re-layouts: 12.7 us -> 14.7 us
  transfers between devices with their start and end apart: 8 -> 17, of which waited for: 4 -> 10; matrix products, arithmetic and copies ran while one was open for 25% -> 44% of each run, Pallas kernels for 0% -> 0%
where the time goes in v1:
time: 212 us; the launch traced here: 211 us
  matrix products  56.3 us (27%)
  waiting for transfers between devices  48 us (23%)
  local copies, waits for them, and re-layouts  41.4 us (20%)
  other arithmetic  25.3 us (12%)
  starting transfers between devices  25.2 us (12%)
  between operations  14.8 us (7%)
    reduce_scatter x1, waiting for transfers between devices, shards(): lax.psum_scatter(jnp.concatenate([key_part.reshape(local_rows * lax.axis_...  23 us
    conv_general_dilated x6, matrix products, depthwise(): lax.conv_general_dilated(padded[None], tap_rows[:, None, :], (1,), 'VALID...  19.9 us
    unnamed x107, local copies, waits for them, and re-layouts  14.7 us
    dot_general x8, matrix products, shards(): lax.dot_general(query_head, key_head, contract, preferred_element_type=jn...  10.5 us
    dot_general x8, local copies, waits for them, and re-layouts, shards(): attended = jnp.dot(weights, value_head, preferred_element_type=jnp.float32)  10.3 us
    ppermute x4, starting transfers between devices, passed_along(): lax.ppermute(value, axis, [(source, source + steps) for source in range(l...  9.7 us
    ppermute x6, waiting for transfers between devices, butterfly_total(): lax.ppermute(rounded, axis, pairs).astype(value.dtype)  9.67 us
    all_gather x1, waiting for transfers between devices, shards(): lax.all_gather(normed, 'ctx', axis=0, tiled=True)  9.44 us
  transfers between devices with their start and end apart: 17, of which 10 were waited for; matrix products, arithmetic and copies ran while one was open for 44% of the time, Pallas kernels for 0%

profile of v1, /device:TPU:0, one launch (start us, length us, event | category | flops | bytes accessed | tf_op | source)
XLA Modules:
  0.0 211.0 jit_solution(7569038224400578180)
XLA Ops:
  9.1 2.4 %collective-permute-start = (bf16[6,1024]{1,0:T(8,128)(2,1)S(1)}, bf16[6,1024]{1,0:T(8,128)(2,1)S(1)}, u32[]{:S(2)}, u32[]{:S(2)}) collective-permute-start(bf16[6,1024]{1,0:T(8,128)(2,1)S(1)} %slice.363), channel_id=1, source_target_pairs={{0,4},{4,8},{8,12},{12,16},{16,20},{20,24},{24,28},{1,5},{5,9},{9,... | collective-permute-start | bytes 36872 | tf_op jit(solution)/shard_map/ppermute | solution.py:28
  11.4 2.8 %rev.12 = f32[7,1024]{1,0:T(8,128)S(1)} reverse(f32[7,1024]{1,0:T(8,128)} %param.15), dimensions={0} | reverse | bytes 57344 | tf_op jit(solution)/shard_map/rev | solution.py:93
  17.6 4.6 %collective-permute-start.1 = (bf16[127,1024]{1,0:T(8,128)(2,1)S(1)}, bf16[127,1024]{1,0:T(8,128)(2,1)S(1)}, u32[]{:S(2)}, u32[]{:S(2)}) collective-permute-start(bf16[127,1024]{1,0:T(8,128)(2,1)S(1)} %slice.361), channel_id=1, source_target_pairs={{0,4},{4,8},{8,12},{12,16},{16,20},{20,24},{24,28},{1,5},{5,9},{9,... | collective-permute-start | bytes 780296 | tf_op jit(solution)/shard_map/ppermute | solution.py:28
  24.2 5.6 %fusion.74 = f32[1,128,1024]{2,0,1:T(1,128)S(1)} fusion(f32[1,255,1024]{2,0,1:T(1,128)S(1)} %broadcast_in_dim.36, f32[128,1,1024]{2,0,1:T(8,128)S(1)} %bitcast.166), kind=kOutput, calls=%fused_computation.137 | convolution fusion | flops 201326592 | bytes 2093056 | tf_op jit(solution)/shard_map/conv_general_dilated | solution.py:32
  32.2 2.0 collective-permute-done.2
  34.2 2.6 %collective-permute-start.3 = (f32[128]{0:T(128)S(1)}, f32[128]{0:T(128)S(1)}, u32[]{:S(2)}, u32[]{:S(2)}) collective-permute-start(f32[128]{0:T(128)S(1)} %add.131), channel_id=1, source_target_pairs={{0,2},{1,3},{2,0},{3,1},{4,6},{5,7},{6,4},{7,5},{8,10},{9,11},{10,... | collective-permute-start | bytes 1544 | tf_op jit(solution)/shard_map/ppermute | solution.py:57
  60.8 2.8 %copy.116 = bf16[1024,1024]{1,0:T(8,128)(2,1)} copy(bf16[1024,1024]{0,1:T(8,128)(2,1)S(1)} %bitcast.159) | data formatting | bytes 4194304 | tf_op jit(solution)/shard_map/reshape | solution.py:167
  63.6 9.4 %all-gather.5.cloned.1.call-done = bf16[1024,1024]{1,0:T(8,128)(2,1)} async-done(((bf16[128,1024]{1,0:T(8,128)(2,1)}), bf16[1024,1024]{1,0:T(8,128)(2,1)}) %all-gather.5.cloned.1.call-update) | async-done | bytes 2097168 | tf_op jit(solution)/shard_map/all_gather | solution.py:107
  89.3 2.7 %copy.114 = bf16[1024,1024]{1,0:T(8,128)(2,1)} copy(bf16[1024,1024]{0,1:T(8,128)(2,1)S(1)} %bitcast.158) | data formatting | bytes 4194304 | tf_op jit(solution)/shard_map/reshape | solution.py:166
  92.0 4.7 %pad_maximum_fusion = bf16[1024,2048]{1,0:T(8,128)(2,1)} fusion(bf16[1024,1024]{1,0:T(8,128)(2,1)} %copy.116, bf16[1024,1024]{1,0:T(8,128)(2,1)} %copy.114), kind=kLoop, calls=%fused_computation | loop fusion | flops 8388608 | bytes 8388608 | tf_op jit(solution)/shard_map/concatenate | solution.py:164
  96.7 1.7 copy.68
  107.0 1.6 constant_dynamic-update-slice_fusion.7
  116.0 1.9 fusion.39
  118.7 2.0 fusion.37
  125.2 23.0 %reduce-scatter.2.cloned.1.call-done = bf16[128,2048]{1,0:T(8,128)(2,1)} async-done(((bf16[1024,2048]{1,0:T(8,128)(2,1)}), bf16[128,2048]{1,0:T(8,128)(2,1)}) %reduce-scatter.2.cloned.1.call-update) | async-done | bytes 524304 | tf_op jit(solution)/shard_map/reduce_scatter | solution.py:163
  153.0 2.4 %collective-permute-start.5 = (f32[128]{0:T(128)S(1)}, f32[128]{0:T(128)S(1)}, u32[]{:S(2)}, u32[]{:S(2)}) collective-permute-start(f32[128]{0:T(128)S(1)} %add.144), channel_id=1, source_target_pairs={{0,2},{1,3},{2,0},{3,1},{4,6},{5,7},{6,4},{7,5},{8,10},{9,11},{10,... | collective-permute-start | bytes 1544 | tf_op jit(solution)/shard_map/ppermute | solution.py:57
  156.1 1.8 copy.104
  157.9 1.7 slice.208
  161.9 6.8 %fusion.70 = bf16[1,128,1024]{2,0,1:T(2,128)(2,1)S(1)} fusion(f32[1,255,1024]{2,0,1:T(1,128)} %copy-done.33, f32[128,1,1024]{2,0,1:T(8,128)S(1)} %bitcast.160), kind=kOutput, calls=%fused_computation.133 | convolution fusion | flops 201326592 | bytes 1830912 | tf_op jit(solution)/shard_map/conv_general_dilated | solution.py:32
  172.2 5.8 %fusion.40 = f32[1,128,1024]{2,0,1:T(1,128)S(1)} fusion(f32[1,255,1024]{2,1,0:T(8,128)S(1)} %maximum_bitcast_fusion, f32[128,1,1024]{2,0,1:T(8,128)S(1)} %bitcast.165), kind=kOutput, calls=%fused_computation.77 | convolution fusion | flops 201326592 | bytes 2093056 | tf_op jit(solution)/shard_map/conv_general_dilated | solution.py:32
  178.0 2.7 %multiply_convert_fusion = (bf16[128,1024]{1,0:T(8,128)(2,1)}, f32[128,1024]{1,0:T(8,128)S(1)}, bf16[128,1024]{1,0:T(8,128)(2,1)}, bf16[128,1024]{1,0:T(8,128)(2,1)}, bf16[128,1024]{1,0:T(8,128)(2,1)}) fusion(f32[1,136,1024]{2,1,0:T(8,128)S(1)} %reshape.121, bf16[128,1024]{1,0:T(8,128)(2,1)S(1)} %copy-done.29, f32[1,128,1024]{2,0,1:T(1,128)S(1)} %fusion.40, ...), kind=kLoop, calls=%fused_computation.139 | loop fusion | flops 2621440 | bytes 4985856 | tf_op jit(solution)/shard_map/convert_element_type | solution.py:192
  183.9 2.8 %collective-permute-start.12 = (bf16[129,1024]{1,0:T(8,128)(2,1)S(1)}, bf16[129,1024]{1,0:T(8,128)(2,1)S(1)}, u32[]{:S(2)}, u32[]{:S(2)}) collective-permute-start(bf16[129,1024]{1,0:T(8,128)(2,1)S(1)} %add_convert_fusion.1), channel_id=1, source_target_pairs={{0,8},{4,12},{8,0},{12,4},{16,24},{20,28},{24,16},{28,20},{1,9},{5... | collective-permute-start | bytes 792584 | tf_op jit(solution)/shard_map/ppermute | solution.py:60
  189.5 4.7 %collective-permute-done.9 = bf16[7,1024]{1,0:T(8,128)(2,1)S(1)} collective-permute-done((bf16[7,1024]{1,0:T(8,128)(2,1)S(1)}, bf16[7,1024]{1,0:T(8,128)(2,1)S(1)}, u32[]{:S(2)}, u32[]{:S(2)}) %collective-permute-start.9) | collective-permute-done | bytes 14368 | tf_op jit(solution)/shard_map/ppermute | solution.py:60
  198.8 4.2 %collective-permute-done.13 = bf16[129,1024]{1,0:T(8,128)(2,1)S(1)} collective-permute-done((bf16[129,1024]{1,0:T(8,128)(2,1)S(1)}, bf16[129,1024]{1,0:T(8,128)(2,1)S(1)}, u32[]{:S(2)}, u32[]{:S(2)}) %collective-permute-start.13) | collective-permute-done | bytes 264224 | tf_op jit(solution)/shard_map/ppermute | solution.py:60
  (252 shorter events, 93.8 us)
Async XLA Ops:
  7.2 33.6 %all-gather.3.cloned.1.call-start = ((), (), s32[]{:S(2)}) async-start(), calls=%async_computation.1 | async-start | bytes 2359296 | tf_op jit(solution)/shard_map/all_gather | solution.py:106
  7.9 65.2 %all-gather.5.cloned.1.call-start = ((), (), s32[]{:S(2)}) async-start(), calls=%async_computation.2 | async-start | bytes 2359296 | tf_op jit(solution)/shard_map/all_gather | solution.py:107
  9.1 5.2 %collective-permute-start = (bf16[6,1024]{1,0:T(8,128)(2,1)S(1)}, bf16[6,1024]{1,0:T(8,128)(2,1)S(1)}, u32[]{:S(2)}, u32[]{:S(2)}) collective-permute-start(bf16[6,1024]{1,0:T(8,128)(2,1)S(1)} %slice.363), channel_id=1, source_target_pairs={{0,4},{4,8},{8,12},{12,16},{16,20},{20,24},{24,28},{1,5},{5,9},{9,... | collective-permute-start | bytes 36872 | tf_op jit(solution)/shard_map/ppermute | solution.py:28
  17.6 5.7 %collective-permute-start.1 = (bf16[127,1024]{1,0:T(8,128)(2,1)S(1)}, bf16[127,1024]{1,0:T(8,128)(2,1)S(1)}, u32[]{:S(2)}, u32[]{:S(2)}) collective-permute-start(bf16[127,1024]{1,0:T(8,128)(2,1)S(1)} %slice.361), channel_id=1, source_target_pairs={{0,4},{4,8},{8,12},{12,16},{16,20},{20,24},{24,28},{1,5},{5,9},{9,... | collective-permute-start | bytes 780296 | tf_op jit(solution)/shard_map/ppermute | solution.py:28
  30.6 3.5 %collective-permute-start.2 = (f32[128]{0:T(128)S(1)}, f32[128]{0:T(128)S(1)}, u32[]{:S(2)}, u32[]{:S(2)}) collective-permute-start(f32[128]{0:T(128)S(1)} %get-tuple-element.61), channel_id=1, source_target_pairs={{0,1},{1,0},{2,3},{3,2},{4,5},{5,4},{6,7},{7,6},{8,9},{9,8},{10,11... | collective-permute-start | bytes 1544 | tf_op jit(solution)/shard_map/ppermute | solution.py:57
  34.2 4.4 %collective-permute-start.3 = (f32[128]{0:T(128)S(1)}, f32[128]{0:T(128)S(1)}, u32[]{:S(2)}, u32[]{:S(2)}) collective-permute-start(f32[128]{0:T(128)S(1)} %add.131), channel_id=1, source_target_pairs={{0,2},{1,3},{2,0},{3,1},{4,6},{5,7},{6,4},{7,5},{8,10},{9,11},{10,... | collective-permute-start | bytes 1544 | tf_op jit(solution)/shard_map/ppermute | solution.py:57
  39.5 108.7 %reduce-scatter.2.cloned.1.call-start = ((), (), s32[]{:S(2)}) async-start(), calls=%async_computation.3 | async-start | bytes 4718592 | tf_op jit(solution)/shard_map/reduce_scatter | solution.py:163
  63.6 16.2 %copy-start.4 = (bf16[128,1024]{1,0:T(8,128)(2,1)S(1)}, bf16[128,1024]{1,0:T(8,128)(2,1)}, u32[]{:S(2)}) copy-start(bf16[128,1024]{1,0:T(8,128)(2,1)} %get-tuple-element.58) | copy-start | bytes 786436
  96.7 19.3 %copy-start.17 = (bf16[1024,1024]{1,0:T(8,128)(2,1)S(1)}, bf16[1024,1024]{1,0:T(8,128)(2,1)}, u32[]{:S(2)}) copy-start(bf16[1024,1024]{1,0:T(8,128)(2,1)} %all-gather.3.cloned.1.call-done) | copy-start | bytes 6291460
  107.0 14.6 %copy-start.23 = (bf16[128,1024]{1,0:T(8,128)(2,1)S(1)}, bf16[128,1024]{1,0:T(8,128)(2,1)}, u32[]{:S(2)}) copy-start(bf16[128,1024]{1,0:T(8,128)(2,1)} %get-tuple-element.96) | copy-start | bytes 786436
  107.0 15.5 %copy-start.24 = (bf16[128,1024]{1,0:T(8,128)(2,1)S(1)}, bf16[128,1024]{1,0:T(8,128)(2,1)}, u32[]{:S(2)}) copy-start(bf16[128,1024]{1,0:T(8,128)(2,1)} %get-tuple-element.98) | copy-start | bytes 786436
  107.0 16.4 %copy-start.25 = (bf16[128,1024]{1,0:T(8,128)(2,1)S(1)}, bf16[128,1024]{1,0:T(8,128)(2,1)}, u32[]{:S(2)}) copy-start(bf16[128,1024]{1,0:T(8,128)(2,1)} %get-tuple-element.100) | copy-start | bytes 786436
  118.7 33.7 %copy-start.42 = (f32[128,128]{0,1:T(8,128)S(1)}, f32[128,128]{0,1:T(8,128)}, u32[]{:S(2)}) copy-start(f32[128,128]{0,1:T(8,128)} %get-tuple-element.86) | copy-start | bytes 196612
  121.6 38.0 %copy-start.21 = (bf16[128,1024]{1,0:T(8,128)(2,1)S(1)}, bf16[128,1024]{1,0:T(8,128)(2,1)}, u32[]{:S(2)}) copy-start(bf16[128,1024]{1,0:T(8,128)(2,1)} %param.16) | copy-start | bytes 786436
  149.4 3.6 %collective-permute-start.4 = (f32[128]{0:T(128)S(1)}, f32[128]{0:T(128)S(1)}, u32[]{:S(2)}, u32[]{:S(2)}) collective-permute-start(f32[128]{0:T(128)S(1)} %get-tuple-element.34), channel_id=1, source_target_pairs={{0,1},{1,0},{2,3},{3,2},{4,5},{5,4},{6,7},{7,6},{8,9},{9,8},{10,11... | collective-permute-start | bytes 1544 | tf_op jit(solution)/shard_map/ppermute | solution.py:57
  153.0 6.5 %collective-permute-start.5 = (f32[128]{0:T(128)S(1)}, f32[128]{0:T(128)S(1)}, u32[]{:S(2)}, u32[]{:S(2)}) collective-permute-start(f32[128]{0:T(128)S(1)} %add.144), channel_id=1, source_target_pairs={{0,2},{1,3},{2,0},{3,1},{4,6},{5,7},{6,4},{7,5},{8,10},{9,11},{10,... | collective-permute-start | bytes 1544 | tf_op jit(solution)/shard_map/ppermute | solution.py:57
  160.6 10.4 %collective-permute-start.6 = (bf16[127,1024]{1,0:T(8,128)(2,1)}, bf16[127,1024]{1,0:T(8,128)(2,1)}, u32[]{:S(2)}, u32[]{:S(2)}) collective-permute-start(bf16[127,1024]{1,0:T(8,128)(2,1)} %slice.360), channel_id=1, source_target_pairs={{4,0},{8,4},{12,8},{16,12},{20,16},{24,20},{28,24},{5,1},{9,5},{13... | collective-permute-start | bytes 780296 | tf_op jit(solution)/shard_map/ppermute | solution.py:28
  169.9 13.9 %collective-permute-start.11 = (bf16[129,1024]{1,0:T(8,128)(2,1)}, bf16[129,1024]{1,0:T(8,128)(2,1)S(1)}, u32[]{:S(2)}, u32[]{:S(2)}) collective-permute-start(bf16[129,1024]{1,0:T(8,128)(2,1)} %pad_maximum_fusion.2), channel_id=1, source_target_pairs={{0,4},{4,0},{8,12},{12,8},{16,20},{20,16},{24,28},{28,24},{1,5},{5... | collective-permute-start | bytes 792584 | tf_op jit(solution)/shard_map/ppermute | solution.py:60
  182.2 5.4 %collective-permute-start.8 = (bf16[7,1024]{1,0:T(8,128)(2,1)S(1)}, bf16[7,1024]{1,0:T(8,128)(2,1)S(1)}, u32[]{:S(2)}, u32[]{:S(2)}) collective-permute-start(bf16[7,1024]{1,0:T(8,128)(2,1)S(1)} %rev.14), channel_id=1, source_target_pairs={{0,4},{4,0},{8,12},{12,8},{16,20},{20,16},{24,28},{28,24},{1,5},{5... | collective-permute-start | bytes 43016 | tf_op jit(solution)/shard_map/ppermute | solution.py:60
  182.3 4.4 %collective-permute-start.7 = (bf16[6,1024]{1,0:T(8,128)(2,1)S(1)}, bf16[6,1024]{1,0:T(8,128)(2,1)S(1)}, u32[]{:S(2)}, u32[]{:S(2)}) collective-permute-start(bf16[6,1024]{1,0:T(8,128)(2,1)S(1)} %slice.362), channel_id=1, source_target_pairs={{4,0},{8,4},{12,8},{16,12},{20,16},{24,20},{28,24},{5,1},{9,5},{13... | collective-permute-start | bytes 36872 | tf_op jit(solution)/shard_map/ppermute | solution.py:28
  183.9 11.7 %collective-permute-start.12 = (bf16[129,1024]{1,0:T(8,128)(2,1)S(1)}, bf16[129,1024]{1,0:T(8,128)(2,1)S(1)}, u32[]{:S(2)}, u32[]{:S(2)}) collective-permute-start(bf16[129,1024]{1,0:T(8,128)(2,1)S(1)} %add_convert_fusion.1), channel_id=1, source_target_pairs={{0,8},{4,12},{8,0},{12,4},{16,24},{20,28},{24,16},{28,20},{1,9},{5... | collective-permute-start | bytes 792584 | tf_op jit(solution)/shard_map/ppermute | solution.py:60
  187.7 6.5 %collective-permute-start.9 = (bf16[7,1024]{1,0:T(8,128)(2,1)S(1)}, bf16[7,1024]{1,0:T(8,128)(2,1)S(1)}, u32[]{:S(2)}, u32[]{:S(2)}) collective-permute-start(bf16[7,1024]{1,0:T(8,128)(2,1)S(1)} %add_convert_fusion.3), channel_id=1, source_target_pairs={{0,8},{4,12},{8,0},{12,4},{16,24},{20,28},{24,16},{28,20},{1,9},{5... | collective-permute-start | bytes 43016 | tf_op jit(solution)/shard_map/ppermute | solution.py:60
  194.2 4.0 %collective-permute-start.10 = (bf16[7,1024]{1,0:T(8,128)(2,1)S(1)}, bf16[7,1024]{1,0:T(8,128)(2,1)S(1)}, u32[]{:S(2)}, u32[]{:S(2)}) collective-permute-start(bf16[7,1024]{1,0:T(8,128)(2,1)S(1)} %add_convert_fusion.2), channel_id=1, source_target_pairs={{0,16},{4,20},{8,24},{12,28},{16,0},{20,4},{24,8},{28,12},{1,17},{... | collective-permute-start | bytes 43016 | tf_op jit(solution)/shard_map/ppermute | solution.py:60
  195.7 7.2 %collective-permute-start.13 = (bf16[129,1024]{1,0:T(8,128)(2,1)S(1)}, bf16[129,1024]{1,0:T(8,128)(2,1)S(1)}, u32[]{:S(2)}, u32[]{:S(2)}) collective-permute-start(bf16[129,1024]{1,0:T(8,128)(2,1)S(1)} %add_convert_fusion), channel_id=1, source_target_pairs={{0,16},{4,20},{8,24},{12,28},{16,0},{20,4},{24,8},{28,12},{1,17},{... | collective-permute-start | bytes 792584 | tf_op jit(solution)/shard_map/ppermute | solution.py:60
  (41 other events, 215.6 us)
Sparse Core Ops, SparseCore 0:
  9.9 30.8 all-gather.2
  42.6 30.3 all-gather.4
  96.8 51.3 reduce-scatter.1

commit v2 on v1

--- a/solution.py
+++ b/solution.py
@@ -160,20 +160,20 @@
     value_part = jnp.einsum(
         "hts,the->she", weights_all, cotangent_heads, preferred_element_type=jnp.float32
     )
-    summed = lax.psum_scatter(
-        jnp.concatenate(
-            [
-                key_part.reshape(local_rows * lax.axis_size("ctx"), width_local),
-                value_part.reshape(local_rows * lax.axis_size("ctx"), width_local),
-            ],
-            axis=1,
-        ).astype(jnp.bfloat16),
+    ctx_rows = local_rows * lax.axis_size("ctx")
+    value_grad = lax.psum_scatter(
+        value_part.reshape(ctx_rows, width_local).astype(jnp.bfloat16),
         "ctx",
         scatter_dimension=0,
         tiled=True,
     ).astype(jnp.float32)
-    matchers_grad = summed[:, :width_local].astype(jnp.bfloat16)
-    value_grad = summed[:, width_local:]
+    key_part, value_grad = lax.optimization_barrier((key_part, value_grad))
+    matchers_grad = lax.psum_scatter(
+        key_part.reshape(ctx_rows, width_local).astype(jnp.bfloat16),
+        "ctx",
+        scatter_dimension=0,
+        tiled=True,
+    )
     gain_part = value_grad * scaling
     projected = channel_total(jnp.sum(gain_part * second_wide, axis=1))
     scaling_part = jnp.sum(value_grad * second_wide * inverse_rms[:, None], axis=0)

time: 212 us -> 197 us (0.929)
  waiting for transfers between devices: 48 us -> 29.8 us
  matrix products: 56.3 us -> 63.8 us
  other arithmetic: 25.3 us -> 18.6 us
    reduce_scatter x1, waiting for transfers between devices: 23 us -> 0.02 us  [shards(): lax.psum_scatter(value_part.reshape(ctx_rows, width_local).astype(jnp.bfl...]
    reshape x3 -> x0, local copies, waits for them, and re-layouts: 6.35 us -> none  [the longest x1 2.83 us: shards(): value_part.reshape(local_rows * lax.axis_size('ctx'), width_local)]
    convert_element_type x0 -> x2, local copies, waits for them, and re-layouts: none -> 5.13 us  [the longest x1 2.58 us: shards(): key_part.reshape(ctx_rows, width_local).astype(jnp.bfloat16)]
    unnamed x107 -> x90, local copies, waits for them, and re-layouts: 14.7 us -> 19.6 us
    concatenate x1 -> x0, other arithmetic: 4.71 us -> none  [shards(): jnp.concatenate([key_part.reshape(local_rows * lax.axis_size('ctx'), widt...]
    dot_general x8, matrix products: 8.14 us -> 12.8 us  [shards(): attended = jnp.dot(weights, value_head, preferred_element_type=jnp.float32)]
    ppermute x6, waiting for transfers between devices: 9.67 us -> 13.3 us  [butterfly_total(): lax.ppermute(rounded, axis, pairs).astype(value.dtype)]
    convert_element_type x0 -> x2, other arithmetic: none -> 3.27 us  [the longest x1 2.28 us: shards(): valves_grad = (second_grad * conv_two).astype(jnp.bfloat16)]
  transfers between devices with their start and end apart: 17 -> 18, of which waited for: 10 -> 8; matrix products, arithmetic and copies ran while one was open for 44% -> 61% of each run, Pallas kernels for 0% -> 0%
where the time goes in v2:
time: 197 us; the launch traced here: 196 us
  matrix products  63.8 us (32%)
  local copies, waits for them, and re-layouts  43.2 us (22%)
  waiting for transfers between devices  29.8 us (15%)
  starting transfers between devices  25.6 us (13%)
  other arithmetic  18.6 us (9%)
  between operations  14.7 us (7%)
    unnamed x90, local copies, waits for them, and re-layouts  19.6 us
    conv_general_dilated x6, matrix products, depthwise(): lax.conv_general_dilated(padded[None], tap_rows[:, None, :], (1,), 'VALID...  18.7 us
    ppermute x6, waiting for transfers between devices, butterfly_total(): lax.ppermute(rounded, axis, pairs).astype(value.dtype)  13.3 us
    dot_general x8, matrix products, shards(): attended = jnp.dot(weights, value_head, preferred_element_type=jnp.float32)  12.8 us
    dot_general x8, matrix products, shards(): query_grad = jnp.dot(dscore, key_head, preferred_element_type=jnp.float32)  11.2 us
    dot_general x8, matrix products, shards(): lax.dot_general(query_head, key_head, contract, preferred_element_type=jn...  10.6 us
    all_gather x1, waiting for transfers between devices, shards(): lax.all_gather(normed, 'ctx', axis=0, tiled=True)  10.1 us
    ppermute x4, starting transfers between devices, passed_along(): lax.ppermute(value, axis, [(source, source + steps) for source in range(l...  9.7 us
  transfers between devices with their start and end apart: 18, of which 8 were waited for; matrix products, arithmetic and copies ran while one was open for 61% of the time, Pallas kernels for 0%

profile of v2, /device:TPU:0, one launch (start us, length us, event | category | flops | bytes accessed | tf_op | source)
XLA Modules:
  0.0 195.6 jit_solution(15684918051641627792)
XLA Ops:
  9.1 2.4 %collective-permute-start = (bf16[6,1024]{1,0:T(8,128)(2,1)S(1)}, bf16[6,1024]{1,0:T(8,128)(2,1)S(1)}, u32[]{:S(2)}, u32[]{:S(2)}) collective-permute-start(bf16[6,1024]{1,0:T(8,128)(2,1)S(1)} %slice.317), channel_id=1, source_target_pairs={{0,4},{4,8},{8,12},{12,16},{16,20},{20,24},{24,28},{1,5},{5,9},{9,... | collective-permute-start | bytes 36872 | tf_op jit(solution)/shard_map/ppermute | solution.py:28
  11.4 2.8 %rev.12 = f32[7,1024]{1,0:T(8,128)S(1)} reverse(f32[7,1024]{1,0:T(8,128)} %param.15), dimensions={0} | reverse | bytes 57344 | tf_op jit(solution)/shard_map/rev | solution.py:93
  17.6 4.6 %collective-permute-start.1 = (bf16[127,1024]{1,0:T(8,128)(2,1)S(1)}, bf16[127,1024]{1,0:T(8,128)(2,1)S(1)}, u32[]{:S(2)}, u32[]{:S(2)}) collective-permute-start(bf16[127,1024]{1,0:T(8,128)(2,1)S(1)} %slice.315), channel_id=1, source_target_pairs={{0,4},{4,8},{8,12},{12,16},{16,20},{20,24},{24,28},{1,5},{5,9},{9,... | collective-permute-start | bytes 780296 | tf_op jit(solution)/shard_map/ppermute | solution.py:28
  24.2 5.6 %fusion.72 = f32[1,128,1024]{2,0,1:T(1,128)S(1)} fusion(f32[1,255,1024]{2,0,1:T(1,128)S(1)} %broadcast_in_dim.36, f32[128,1,1024]{2,0,1:T(8,128)S(1)} %bitcast.171), kind=kOutput, calls=%fused_computation.133 | convolution fusion | flops 201326592 | bytes 2093056 | tf_op jit(solution)/shard_map/conv_general_dilated | solution.py:32
  32.2 2.0 %collective-permute-done.2 = f32[128]{0:T(128)S(1)} collective-permute-done((f32[128]{0:T(128)S(1)}, f32[128]{0:T(128)S(1)}, u32[]{:S(2)}, u32[]{:S(2)}) %collective-permute-start.2) | collective-permute-done | bytes 544 | tf_op jit(solution)/shard_map/ppermute | solution.py:57
  34.2 2.6 %collective-permute-start.3 = (f32[128]{0:T(128)S(1)}, f32[128]{0:T(128)S(1)}, u32[]{:S(2)}, u32[]{:S(2)}) collective-permute-start(f32[128]{0:T(128)S(1)} %add.133), channel_id=1, source_target_pairs={{0,2},{1,3},{2,0},{3,1},{4,6},{5,7},{6,4},{7,5},{8,10},{9,11},{10,... | collective-permute-start | bytes 1544 | tf_op jit(solution)/shard_map/ppermute | solution.py:57
  60.2 2.6 %copy.162 = bf16[1024,1024]{1,0:T(8,128)(2,1)} copy(bf16[1024,1024]{0,1:T(8,128)(2,1)S(1)} %bitcast.164) | data formatting | bytes 4194304 | tf_op jit(solution)/shard_map/convert_element_type | solution.py:165
  63.0 10.1 %all-gather.5.cloned.1.call-done = bf16[1024,1024]{1,0:T(8,128)(2,1)} async-done(((bf16[128,1024]{1,0:T(8,128)(2,1)}), bf16[1024,1024]{1,0:T(8,128)(2,1)}) %all-gather.5.cloned.1.call-update) | async-done | bytes 2097168 | tf_op jit(solution)/shard_map/all_gather | solution.py:107
  75.3 1.9 fusion.97
  78.8 1.9 fusion.102
  85.7 1.9 fusion.112
  96.6 2.3 %multiply_reduce_fusion = (f32[128]{0:T(128)S(1)}, f32[128]{0:T(128)S(1)}, f32[128]{0:T(128)S(1)}, f32[128]{0:T(128)S(1)}, f32[128]{0:T(128)S(1)}, /*index=5*/f3...) fusion(bf16[128,1024]{0,1:T(8,128)(2,1)S(1)} %copy.120, f32[128,128]{0,1:T(8,128)} %copy-done.29, ...), kind=kOutput, calls=%fused_computation.225 | convolution fusion | flops 33946624 | bytes 1314816 | tf_op jit(solution)/shard_map/dot_general | solution.py:134
  108.5 2.1 %fusion.37 = bf16[128,1024]{0,1:T(8,128)(2,1)} fusion(bf16[128,1024]{0,1:T(8,128)(2,1)} %fusion.38, bf16[128,1024]{1,0:T(8,128)(2,1)} %get-tuple-element.108, bf16[1024,1024]{1,0:T(8,128)(2,1)} %all-gather.3.cloned.1.call-done), kind=kOutput, calls=%fused_computation.69 | convolution fusion | flops 33570816 | bytes 557056 | tf_op jit(solution)/shard_map/dot_general | solution.py:142
  110.5 1.9 bitcast_dynamic-update-slice_fusion.12
  121.9 2.4 %convolution_bitcast_fusion = bf16[1024,8,128]{2,0,1:T(8,128)(2,1)S(1)} fusion(bf16[8,128,1024]{2,1,0:T(8,128)(2,1)} %get-tuple-element.117, bf16[128,1024]{1,0:T(8,128)(2,1)S(1)} %copy-done.32), kind=kOutput, calls=%fused_computation | convolution fusion | flops 268435456 | bytes 4456448 | tf_op jit(solution)/shard_map/hts,the->she/dot_general | solution.py:157
  129.1 2.4 %collective-permute-start.5 = (f32[128]{0:T(128)S(1)}, f32[128]{0:T(128)S(1)}, u32[]{:S(2)}, u32[]{:S(2)}) collective-permute-start(f32[128]{0:T(128)S(1)} %add.146), channel_id=1, source_target_pairs={{0,2},{1,3},{2,0},{3,1},{4,6},{5,7},{6,4},{7,5},{8,10},{9,11},{10,... | collective-permute-start | bytes 1544 | tf_op jit(solution)/shard_map/ppermute | solution.py:57
  134.8 2.6 %copy.149 = bf16[1024,8,128]{0,2,1:T(8,128)(2,1)} copy(bf16[1024,8,128]{2,0,1:T(8,128)(2,1)S(1)} %convolution_bitcast_fusion) | data formatting | bytes 4194304 | tf_op jit(solution)/shard_map/convert_element_type | solution.py:172
  137.3 3.9 %copy.163 = bf16[1024,1024]{1,0:T(8,128)(2,1)} copy(bf16[1024,1024]{0,1:T(8,128)(2,1)} %bitcast.165) | data formatting | bytes 4194304
  142.4 2.3 %fusion.67 = (bf16[128,1024]{1,0:T(8,128)(2,1)}, f32[128,1024]{1,0:T(8,128)S(1)}, bf16[128,1024]{1,0:T(8,128)(2,1)}) fusion(f32[1,128,1024]{2,0,1:T(1,128)S(1)} %copy-done.15, f32[128]{0:T(128)S(1)} %fusion.140, bf16[128,1024]{1,0:T(8,128)(2,1)S(1)} %get-tuple-element.79, f32[128,1024]{1,0:T(8,128)S(1)} %convert_element_type.287, f32[1024]{0:T(1024)S(1)} %copy-done.35, ...), kind=kLoop, calls=%fused_computation.128 | loop fusion | flops 1441792 | bytes 3150848 | tf_op jit(solution)/shard_map/convert_element_type | solution.py:185
  146.8 5.6 %fusion.68 = bf16[1,128,1024]{2,0,1:T(2,128)(2,1)S(1)} fusion(f32[1,255,1024]{2,0,1:T(1,128)S(1)} %copy-done.27, f32[128,1,1024]{2,0,1:T(8,128)S(1)} %bitcast.166), kind=kOutput, calls=%fused_computation.129 | convolution fusion | flops 201326592 | bytes 1830912 | tf_op jit(solution)/shard_map/conv_general_dilated | solution.py:32
  154.3 5.8 %fusion.40 = f32[1,128,1024]{2,0,1:T(1,128)S(1)} fusion(f32[1,255,1024]{2,1,0:T(8,128)S(1)} %maximum_bitcast_fusion, f32[128,1,1024]{2,0,1:T(8,128)S(1)} %bitcast.170), kind=kOutput, calls=%fused_computation.76 | convolution fusion | flops 201326592 | bytes 2093056 | tf_op jit(solution)/shard_map/conv_general_dilated | solution.py:32
  170.1 5.0 %collective-permute-done.9 = bf16[7,1024]{1,0:T(8,128)(2,1)S(1)} collective-permute-done((bf16[7,1024]{1,0:T(8,128)(2,1)S(1)}, bf16[7,1024]{1,0:T(8,128)(2,1)S(1)}, u32[]{:S(2)}, u32[]{:S(2)}) %collective-permute-start.9) | collective-permute-done | bytes 14368 | tf_op jit(solution)/shard_map/ppermute | solution.py:60
  175.0 2.5 %collective-permute-start.10 = (bf16[7,1024]{1,0:T(8,128)(2,1)S(1)}, bf16[7,1024]{1,0:T(8,128)(2,1)S(1)}, u32[]{:S(2)}, u32[]{:S(2)}) collective-permute-start(bf16[7,1024]{1,0:T(8,128)(2,1)S(1)} %add_convert_fusion.2), channel_id=1, source_target_pairs={{0,16},{4,20},{8,24},{12,28},{16,0},{20,4},{24,8},{28,12},{1,17},{... | collective-permute-start | bytes 43016 | tf_op jit(solution)/shard_map/ppermute | solution.py:60
  180.0 7.6 %collective-permute-done.13 = bf16[129,1024]{1,0:T(8,128)(2,1)S(1)} collective-permute-done((bf16[129,1024]{1,0:T(8,128)(2,1)S(1)}, bf16[129,1024]{1,0:T(8,128)(2,1)S(1)}, u32[]{:S(2)}, u32[]{:S(2)}) %collective-permute-start.13) | collective-permute-done | bytes 264224 | tf_op jit(solution)/shard_map/ppermute | solution.py:60
  (237 shorter events, 96.4 us)
Async XLA Ops:
  7.2 33.6 %all-gather.3.cloned.1.call-start = ((), (), s32[]{:S(2)}) async-start(), calls=%async_computation.2 | async-start | bytes 2359296 | tf_op jit(solution)/shard_map/all_gather | solution.py:106
  7.9 65.2 %all-gather.5.cloned.1.call-start = ((), (), s32[]{:S(2)}) async-start(), calls=%async_computation.3 | async-start | bytes 2359296 | tf_op jit(solution)/shard_map/all_gather | solution.py:107
  9.1 5.2 %collective-permute-start = (bf16[6,1024]{1,0:T(8,128)(2,1)S(1)}, bf16[6,1024]{1,0:T(8,128)(2,1)S(1)}, u32[]{:S(2)}, u32[]{:S(2)}) collective-permute-start(bf16[6,1024]{1,0:T(8,128)(2,1)S(1)} %slice.317), channel_id=1, source_target_pairs={{0,4},{4,8},{8,12},{12,16},{16,20},{20,24},{24,28},{1,5},{5,9},{9,... | collective-permute-start | bytes 36872 | tf_op jit(solution)/shard_map/ppermute | solution.py:28
  17.5 12.3 %copy-start.1 = (bf16[128,1024]{1,0:T(8,128)(2,1)}, bf16[128,1024]{1,0:T(8,128)(2,1)S(1)}, u32[]{:S(2)}) copy-start(bf16[128,1024]{1,0:T(8,128)(2,1)S(1)} %get-tuple-element.81) | copy-start | bytes 786436
  17.6 5.7 %collective-permute-start.1 = (bf16[127,1024]{1,0:T(8,128)(2,1)S(1)}, bf16[127,1024]{1,0:T(8,128)(2,1)S(1)}, u32[]{:S(2)}, u32[]{:S(2)}) collective-permute-start(bf16[127,1024]{1,0:T(8,128)(2,1)S(1)} %slice.315), channel_id=1, source_target_pairs={{0,4},{4,8},{8,12},{12,16},{16,20},{20,24},{24,28},{1,5},{5,9},{9,... | collective-permute-start | bytes 780296 | tf_op jit(solution)/shard_map/ppermute | solution.py:28
  24.2 12.6 %copy-start.18 = (bf16[128,1024]{1,0:T(8,128)(2,1)S(1)}, bf16[128,1024]{1,0:T(8,128)(2,1)}, u32[]{:S(2)}) copy-start(bf16[128,1024]{1,0:T(8,128)(2,1)} %param.23) | copy-start | bytes 786436
  24.2 12.8 %copy-start.37 = (s32[1024]{0:T(1024)S(1)}, s32[1024]{0:T(1024)}, u32[]{:S(2)}) copy-start(s32[1024]{0:T(1024)} %param.22) | copy-start | bytes 12292
  24.2 14.5 %copy-start.35 = (f32[1024]{0:T(1024)S(1)}, f32[1024]{0:T(1024)}, u32[]{:S(2)}) copy-start(f32[1024]{0:T(1024)} %param.19) | copy-start | bytes 12292
  30.7 3.5 %collective-permute-start.2 = (f32[128]{0:T(128)S(1)}, f32[128]{0:T(128)S(1)}, u32[]{:S(2)}, u32[]{:S(2)}) collective-permute-start(f32[128]{0:T(128)S(1)} %get-tuple-element.78), channel_id=1, source_target_pairs={{0,1},{1,0},{2,3},{3,2},{4,5},{5,4},{6,7},{7,6},{8,9},{9,8},{10,11... | collective-permute-start | bytes 1544 | tf_op jit(solution)/shard_map/ppermute | solution.py:57
  34.2 4.4 %collective-permute-start.3 = (f32[128]{0:T(128)S(1)}, f32[128]{0:T(128)S(1)}, u32[]{:S(2)}, u32[]{:S(2)}) collective-permute-start(f32[128]{0:T(128)S(1)} %add.133), channel_id=1, source_target_pairs={{0,2},{1,3},{2,0},{3,1},{4,6},{5,7},{6,4},{7,5},{8,10},{9,11},{10,... | collective-permute-start | bytes 1544 | tf_op jit(solution)/shard_map/ppermute | solution.py:57
  39.5 84.8 %reduce-scatter.5.cloned.1.call-start = ((), (), s32[]{:S(2)}) async-start(), calls=%async_computation.4 | async-start | bytes 2359296 | tf_op jit(solution)/shard_map/reduce_scatter | solution.py:164
  62.7 126.3 %reduce-scatter.7.cloned.1.call-start = ((), (), s32[]{:S(2)}) async-start(), calls=%async_computation.5 | async-start | bytes 2359296
  74.6 20.6 %copy-start.29 = (f32[128,128]{0,1:T(8,128)}, f32[128,128]{0,1:T(8,128)S(1)}, u32[]{:S(2)}) copy-start(f32[128,128]{0,1:T(8,128)S(1)} %fusion.117) | copy-start | bytes 196612
  89.1 9.8 %copy-start.20 = (bf16[128,1024]{1,0:T(8,128)(2,1)S(1)}, bf16[128,1024]{1,0:T(8,128)(2,1)}, u32[]{:S(2)}) copy-start(bf16[128,1024]{1,0:T(8,128)(2,1)} %get-tuple-element.77) | copy-start | bytes 786436
  125.5 3.6 %collective-permute-start.4 = (f32[128]{0:T(128)S(1)}, f32[128]{0:T(128)S(1)}, u32[]{:S(2)}, u32[]{:S(2)}) collective-permute-start(f32[128]{0:T(128)S(1)} %get-tuple-element.49), channel_id=1, source_target_pairs={{0,1},{1,0},{2,3},{3,2},{4,5},{5,4},{6,7},{7,6},{8,9},{9,8},{10,11... | collective-permute-start | bytes 1544 | tf_op jit(solution)/shard_map/ppermute | solution.py:57
  129.1 12.2 %collective-permute-start.5 = (f32[128]{0:T(128)S(1)}, f32[128]{0:T(128)S(1)}, u32[]{:S(2)}, u32[]{:S(2)}) collective-permute-start(f32[128]{0:T(128)S(1)} %add.146), channel_id=1, source_target_pairs={{0,2},{1,3},{2,0},{3,1},{4,6},{5,7},{6,4},{7,5},{8,10},{9,11},{10,... | collective-permute-start | bytes 1544 | tf_op jit(solution)/shard_map/ppermute | solution.py:57
  145.5 8.6 %collective-permute-start.6 = (bf16[127,1024]{1,0:T(8,128)(2,1)}, bf16[127,1024]{1,0:T(8,128)(2,1)S(1)}, u32[]{:S(2)}, u32[]{:S(2)}) collective-permute-start(bf16[127,1024]{1,0:T(8,128)(2,1)} %slice.314), channel_id=1, source_target_pairs={{4,0},{8,4},{12,8},{16,12},{20,16},{24,20},{28,24},{5,1},{9,5},{13... | collective-permute-start | bytes 780296 | tf_op jit(solution)/shard_map/ppermute | solution.py:28
  152.9 12.8 %collective-permute-start.11 = (bf16[129,1024]{1,0:T(8,128)(2,1)S(1)}, bf16[129,1024]{1,0:T(8,128)(2,1)S(1)}, u32[]{:S(2)}, u32[]{:S(2)}) collective-permute-start(bf16[129,1024]{1,0:T(8,128)(2,1)S(1)} %pad_maximum_fusion.1), channel_id=1, source_target_pairs={{0,4},{4,0},{8,12},{12,8},{16,20},{20,16},{24,28},{28,24},{1,5},{5... | collective-permute-start | bytes 792584 | tf_op jit(solution)/shard_map/ppermute | solution.py:60
  163.0 4.4 %collective-permute-start.7 = (bf16[6,1024]{1,0:T(8,128)(2,1)S(1)}, bf16[6,1024]{1,0:T(8,128)(2,1)S(1)}, u32[]{:S(2)}, u32[]{:S(2)}) collective-permute-start(bf16[6,1024]{1,0:T(8,128)(2,1)S(1)} %slice.316), channel_id=1, source_target_pairs={{4,0},{8,4},{12,8},{16,12},{20,16},{24,20},{28,24},{5,1},{9,5},{13... | collective-permute-start | bytes 36872 | tf_op jit(solution)/shard_map/ppermute | solution.py:28
  164.5 3.8 %collective-permute-start.8 = (bf16[7,1024]{1,0:T(8,128)(2,1)S(1)}, bf16[7,1024]{1,0:T(8,128)(2,1)S(1)}, u32[]{:S(2)}, u32[]{:S(2)}) collective-permute-start(bf16[7,1024]{1,0:T(8,128)(2,1)S(1)} %rev.14), channel_id=1, source_target_pairs={{0,4},{4,0},{8,12},{12,8},{16,20},{20,16},{24,28},{28,24},{1,5},{5... | collective-permute-start | bytes 43016 | tf_op jit(solution)/shard_map/ppermute | solution.py:60
  165.7 11.8 %collective-permute-start.12 = (bf16[129,1024]{1,0:T(8,128)(2,1)S(1)}, bf16[129,1024]{1,0:T(8,128)(2,1)S(1)}, u32[]{:S(2)}, u32[]{:S(2)}) collective-permute-start(bf16[129,1024]{1,0:T(8,128)(2,1)S(1)} %add_convert_fusion.1), channel_id=1, source_target_pairs={{0,8},{4,12},{8,0},{12,4},{16,24},{20,28},{24,16},{28,20},{1,9},{5... | collective-permute-start | bytes 792584 | tf_op jit(solution)/shard_map/ppermute | solution.py:60
  168.3 6.7 %collective-permute-start.9 = (bf16[7,1024]{1,0:T(8,128)(2,1)S(1)}, bf16[7,1024]{1,0:T(8,128)(2,1)S(1)}, u32[]{:S(2)}, u32[]{:S(2)}) collective-permute-start(bf16[7,1024]{1,0:T(8,128)(2,1)S(1)} %add_convert_fusion.3), channel_id=1, source_target_pairs={{0,8},{4,12},{8,0},{12,4},{16,24},{20,28},{24,16},{28,20},{1,9},{5... | collective-permute-start | bytes 43016 | tf_op jit(solution)/shard_map/ppermute | solution.py:60
  175.0 4.3 %collective-permute-start.10 = (bf16[7,1024]{1,0:T(8,128)(2,1)S(1)}, bf16[7,1024]{1,0:T(8,128)(2,1)S(1)}, u32[]{:S(2)}, u32[]{:S(2)}) collective-permute-start(bf16[7,1024]{1,0:T(8,128)(2,1)S(1)} %add_convert_fusion.2), channel_id=1, source_target_pairs={{0,16},{4,20},{8,24},{12,28},{16,0},{20,4},{24,8},{28,12},{1,17},{... | collective-permute-start | bytes 43016 | tf_op jit(solution)/shard_map/ppermute | solution.py:60
  177.6 10.0 %collective-permute-start.13 = (bf16[129,1024]{1,0:T(8,128)(2,1)S(1)}, bf16[129,1024]{1,0:T(8,128)(2,1)S(1)}, u32[]{:S(2)}, u32[]{:S(2)}) collective-permute-start(bf16[129,1024]{1,0:T(8,128)(2,1)S(1)} %add_convert_fusion), channel_id=1, source_target_pairs={{0,16},{4,20},{8,24},{12,28},{16,0},{20,4},{24,8},{28,12},{1,17},{... | collective-permute-start | bytes 792584 | tf_op jit(solution)/shard_map/ppermute | solution.py:60
  (33 other events, 136.2 us)
Sparse Core Ops, SparseCore 0:
  9.9 30.8 all-gather.2
  43.2 29.8 all-gather.4
  76.4 41.2 reduce-scatter.4
  141.4 43.0 reduce-scatter.6

commit v3 on v2

--- a/solution.py
+++ b/solution.py
@@ -1,8 +1,10 @@
+import functools
 import math
 
 import jax
 import jax.numpy as jnp
 from jax import lax
+from jax.experimental import pallas as pl
 from jax.sharding import PartitionSpec as P
 
 HD = 128
@@ -64,6 +66,59 @@
 
 def channel_total(partial_value):
     return butterfly_total(partial_value, "tp")
+
+
+def attention_block(scale_factor, q_ref, k_ref, v_ref, cot_ref, vis_ref, dk_ref, dv_ref, att_ref, dq_ref):
+    contract_last = (((1,), (1,)), ((), ()))
+    contract_first = (((0,), (0,)), ((), ()))
+    query_head = q_ref[...]
+    key_head = k_ref[...]
+    value_head = v_ref[...]
+    cotangent_head = cot_ref[...]
+    scores = (
+        lax.dot_general(query_head, key_head, contract_last, preferred_element_type=jnp.float32)
+        * scale_factor
+    )
+    scores = jnp.where(vis_ref[...] > 0.5, scores, -jnp.inf)
+    row_max = jnp.max(scores, axis=1, keepdims=True)
+    logsum = row_max + jnp.log(jnp.sum(jnp.exp(scores - row_max), axis=1, keepdims=True))
+    weights = jnp.exp(scores - logsum).astype(jnp.bfloat16)
+    attended = jnp.dot(weights, value_head, preferred_element_type=jnp.float32)
+    weight_grad = lax.dot_general(
+        cotangent_head, value_head, contract_last, preferred_element_type=jnp.float32
+    )
+    row_delta = jnp.sum(cotangent_head.astype(jnp.float32) * attended, axis=1, keepdims=True)
+    dscore = (scale_factor * weights.astype(jnp.float32) * (weight_grad - row_delta)).astype(
+        jnp.bfloat16
+    )
+    att_ref[...] = attended
+    dq_ref[...] = jnp.dot(dscore, key_head, preferred_element_type=jnp.float32).astype(jnp.bfloat16)
+    dk_ref[...] = lax.dot_general(
+        dscore, query_head, contract_first, preferred_element_type=jnp.float32
+    ).astype(jnp.bfloat16)
+    dv_ref[...] = lax.dot_general(
+        weights, cotangent_head, contract_first, preferred_element_type=jnp.float32
+    ).astype(jnp.bfloat16)
+
+
+def head_attention(queries, keys_whole, values_whole, cotangent, visible, scale_factor):
+    local_rows, width_local = queries.shape
+    total_rows = keys_whole.shape[0]
+    local_spec = pl.BlockSpec((local_rows, HD), lambda h: (0, h))
+    whole_spec = pl.BlockSpec((total_rows, HD), lambda h: (0, h))
+    mask_spec = pl.BlockSpec((local_rows, total_rows), lambda h: (0, 0))
+    return pl.pallas_call(
+        functools.partial(attention_block, scale_factor),
+        grid=(width_local // HD,),
+        in_specs=[local_spec, whole_spec, whole_spec, local_spec, mask_spec],
+        out_specs=[whole_spec, whole_spec, local_spec, local_spec],
+        out_shape=[
+            jax.ShapeDtypeStruct((total_rows, width_local), jnp.bfloat16),
+            jax.ShapeDtypeStruct((total_rows, width_local), jnp.bfloat16),
+            jax.ShapeDtypeStruct((local_rows, width_local), jnp.float32),
+            jax.ShapeDtypeStruct((local_rows, width_local), jnp.bfloat16),
+        ],
+    )(queries, keys_whole, values_whole, cotangent, visible)
 
 
 def shards(
@@ -110,66 +165,19 @@
     key_pos = jnp.arange(total_rows, dtype=jnp.int32)
     query_seg = lax.dynamic_slice_in_dim(segments, position, local_rows, 0)
     visible = (key_pos[None, :] <= query_pos[:, None]) & (segments[None, :] == query_seg[:, None])
-    contract = (((1,), (1,)), ((), ()))
-    weight_list = []
-    dscore_list = []
-    attended_list = []
-    query_grad_list = []
-    logsum_list = []
-    delta_list = []
-    for head_index in range(head_count):
-        columns = slice(head_index * HD, (head_index + 1) * HD)
-        query_head = queries[:, columns]
-        key_head = keys_whole[:, columns]
-        value_head = values_whole[:, columns]
-        cotangent_head = cotangent[:, columns]
-        scores = (
-            lax.dot_general(query_head, key_head, contract, preferred_element_type=jnp.float32)
-            * scale_factor
-        )
-        scores = jnp.where(visible, scores, -jnp.inf)
-        row_max = jnp.max(scores, axis=1)
-        logsum = row_max + jnp.log(jnp.sum(jnp.exp(scores - row_max[:, None]), axis=1))
-        weights = jnp.exp(scores - logsum[:, None]).astype(jnp.bfloat16)
-        attended = jnp.dot(weights, value_head, preferred_element_type=jnp.float32)
-        weight_grad = lax.dot_general(
-            cotangent_head, value_head, contract, preferred_element_type=jnp.float32
-        )
-        row_delta = jnp.sum(cotangent_head.astype(jnp.float32) * attended, axis=1)
-        dscore = (
-            scale_factor * weights.astype(jnp.float32) * (weight_grad - row_delta[:, None])
-        ).astype(jnp.bfloat16)
-        query_grad = jnp.dot(dscore, key_head, preferred_element_type=jnp.float32)
-        weight_list.append(weights)
-        dscore_list.append(dscore)
-        attended_list.append(attended)
-        query_grad_list.append(query_grad)
-        logsum_list.append(logsum)
-        delta_list.append(row_delta)
-    attended_all = jnp.concatenate(attended_list, axis=1)
+    key_part, value_part, attended_all, queries_grad = head_attention(
+        queries, keys_whole, values_whole, cotangent, visible.astype(jnp.float32), scale_factor
+    )
     result = (second_wide + attended_all).astype(jnp.bfloat16)
-    queries_grad = jnp.concatenate(query_grad_list, axis=1).astype(jnp.bfloat16)
-    query_heads = queries.reshape(local_rows, head_count, HD)
-    cotangent_heads = cotangent.reshape(local_rows, head_count, HD)
-    weights_all = jnp.stack(weight_list)
-    dscore_all = jnp.stack(dscore_list)
-    dscore_part = lax.slice_in_dim(dscore_all, 0, local_rows * lax.axis_size("ctx"), axis=2)
-    key_part = jnp.einsum(
-        "hts,the->she", dscore_part, query_heads, preferred_element_type=jnp.float32
-    )
-    value_part = jnp.einsum(
-        "hts,the->she", weights_all, cotangent_heads, preferred_element_type=jnp.float32
-    )
-    ctx_rows = local_rows * lax.axis_size("ctx")
     value_grad = lax.psum_scatter(
-        value_part.reshape(ctx_rows, width_local).astype(jnp.bfloat16),
+        value_part,
         "ctx",
         scatter_dimension=0,
         tiled=True,
     ).astype(jnp.float32)
     key_part, value_grad = lax.optimization_barrier((key_part, value_grad))
     matchers_grad = lax.psum_scatter(
-        key_part.reshape(ctx_rows, width_local).astype(jnp.bfloat16),
+        key_part,
         "ctx",
         scatter_dimension=0,
         tiled=True,

time: 197 us -> 188 us (0.954)
  waiting for transfers between devices: 29.8 us -> 94.1 us
  matrix products: 63.8 us -> 19.7 us
  local copies, waits for them, and re-layouts: 43.2 us -> 8.76 us
  Pallas kernels: 0 us -> 11.4 us
  other arithmetic: 18.6 us -> 14.3 us
    dot_general x34 -> x0, matrix products: 45.1 us -> none  [the longest x8 12.8 us: shards(): attended = jnp.dot(weights, value_head, preferred_element_type=jnp.float32)]
    reduce_scatter x1 -> x2, waiting for transfers between devices: 0.02 us -> 41.3 us  [the longest x1 41.3 us: shards(): lax.psum_scatter(value_part, 'ctx', scatter_dimension=0, tiled=True)]
    all_gather x1, waiting for transfers between devices: 10.1 us -> 30.4 us  [shards(): lax.all_gather(normed, 'ctx', axis=0, tiled=True)]
    unnamed x90 -> x40, local copies, waits for them, and re-layouts: 19.6 us -> 1.34 us
    pallas_call x0 -> x1, Pallas kernels: none -> 11.4 us  [head_attention(): pl.pallas_call(functools.partial(attention_block, scale_factor), grid=(wi...]
    dot_general x8 -> x0, local copies, waits for them, and re-layouts: 9.34 us -> none  [shards(): attended = jnp.dot(weights, value_head, preferred_element_type=jnp.float32)]
    unnamed x7 -> x0, other arithmetic: 5.22 us -> none
    convert_element_type x2 -> x0, local copies, waits for them, and re-layouts: 5.13 us -> none  [the longest x1 2.58 us: shards(): key_part.reshape(ctx_rows, width_local).astype(jnp.bfloat16)]
  transfers between devices with their start and end apart: 18 -> 18, of which waited for: 8 -> 10; matrix products, arithmetic and copies ran while one was open for 61% -> 21% of each run, Pallas kernels for 0% -> 0%
where the time goes in v3:
time: 188 us
  waiting for transfers between devices  94.1 us (50%)
  starting transfers between devices  25.2 us (13%)
  matrix products  19.7 us (10%)
  other arithmetic  14.3 us (8%)
  between operations  14.3 us (8%)
  Pallas kernels  11.4 us (6%)
  local copies, waits for them, and re-layouts  8.76 us (5%)
    reduce_scatter x1, waiting for transfers between devices, shards(): lax.psum_scatter(value_part, 'ctx', scatter_dimension=0, tiled=True)  41.3 us
    all_gather x1, waiting for transfers between devices, shards(): lax.all_gather(normed, 'ctx', axis=0, tiled=True)  30.4 us
    conv_general_dilated x6, matrix products, depthwise(): lax.conv_general_dilated(padded[None], tap_rows[:, None, :], (1,), 'VALID...  19.7 us
    ppermute x6, waiting for transfers between devices, butterfly_total(): lax.ppermute(rounded, axis, pairs).astype(value.dtype)  12.2 us
    pallas_call x1, Pallas kernels, head_attention(): pl.pallas_call(functools.partial(attention_block, scale_factor), grid=(wi...  11.4 us
    ppermute x4, starting transfers between devices, passed_along(): lax.ppermute(value, axis, [(source, source + steps) for source in range(l...  9.47 us
    ppermute x4, starting transfers between devices, butterfly_total(): value = value + lax.ppermute(value, axis, pairs)  8.17 us
    ppermute x4, waiting for transfers between devices, butterfly_total(): value = value + lax.ppermute(value, axis, pairs)  7.86 us
  transfers between devices with their start and end apart: 18, of which 10 were waited for; matrix products, arithmetic and copies ran while one was open for 21% of the time, Pallas kernels for 0%

profile of v3, /device:TPU:0, one launch (start us, length us, event | category | flops | bytes accessed | tf_op | source)
XLA Modules:
  0.0 187.7 jit_solution(5565998470878798919)
XLA Ops:
  9.1 2.4 %collective-permute-start = (bf16[6,1024]{1,0:T(8,128)(2,1)S(1)}, bf16[6,1024]{1,0:T(8,128)(2,1)S(1)}, u32[]{:S(2)}, u32[]{:S(2)}) collective-permute-start(bf16[6,1024]{1,0:T(8,128)(2,1)S(1)} %slice.52), channel_id=1, source_target_pairs={{0,4},{4,8},{8,12},{12,16},{16,20},{20,24},{24,28},{1,5},{5,9},{9,... | collective-permute-start | bytes 36872 | tf_op jit(solution)/shard_map/ppermute | solution.py:30
  11.4 2.8 %rev.12 = f32[7,1024]{1,0:T(8,128)S(1)} reverse(f32[7,1024]{1,0:T(8,128)} %param.15), dimensions={0} | reverse | bytes 57344 | tf_op jit(solution)/shard_map/rev | solution.py:148
  15.9 4.5 %collective-permute-start.1 = (bf16[127,1024]{1,0:T(8,128)(2,1)S(1)}, bf16[127,1024]{1,0:T(8,128)(2,1)S(1)}, u32[]{:S(2)}, u32[]{:S(2)}) collective-permute-start(bf16[127,1024]{1,0:T(8,128)(2,1)S(1)} %slice.50), channel_id=1, source_target_pairs={{0,4},{4,8},{8,12},{12,16},{16,20},{20,24},{24,28},{1,5},{5,9},{9,... | collective-permute-start | bytes 780296 | tf_op jit(solution)/shard_map/ppermute | solution.py:30
  20.5 2.6 %rev.13 = f32[128,1024]{1,0:T(8,128)} reverse(f32[128,1024]{1,0:T(8,128)S(1)} %copy-done.12), dimensions={0} | reverse | bytes 1048576 | tf_op jit(solution)/shard_map/rev | solution.py:154
  24.1 5.8 %fusion.8 = f32[1,128,1024]{2,0,1:T(1,128)S(1)} fusion(f32[1,255,1024]{2,1,0:T(8,128)S(1)} %maximum_bitcast_fusion, f32[128,1,1024]{2,0,1:T(8,128)S(1)} %bitcast.50), kind=kOutput, calls=%fused_computation.35 | convolution fusion | flops 201326592 | bytes 2093056 | tf_op jit(solution)/shard_map/conv_general_dilated | solution.py:34
  30.1 1.6 collective-permute-start.2
  31.8 2.0 %collective-permute-done.2 = f32[128]{0:T(128)S(1)} collective-permute-done((f32[128]{0:T(128)S(1)}, f32[128]{0:T(128)S(1)}, u32[]{:S(2)}, u32[]{:S(2)}) %collective-permute-start.2) | collective-permute-done | bytes 544 | tf_op jit(solution)/shard_map/ppermute | solution.py:59
  33.7 2.6 %collective-permute-start.3 = (f32[128]{0:T(128)S(1)}, f32[128]{0:T(128)S(1)}, u32[]{:S(2)}, u32[]{:S(2)}) collective-permute-start(f32[128]{0:T(128)S(1)} %add.73), channel_id=1, source_target_pairs={{0,2},{1,3},{2,0},{3,1},{4,6},{5,7},{6,4},{7,5},{8,10},{9,11},{10,... | collective-permute-start | bytes 1544 | tf_op jit(solution)/shard_map/ppermute | solution.py:59
  36.3 1.9 collective-permute-done.3
  40.2 1.6 all-gather.3.cloned.1.call-done.k_ref
  41.8 30.4 %all-gather.5.cloned.1.call-done.v_ref = bf16[1024,1024]{1,0:T(8,128)(2,1)} async-done(((bf16[128,1024]{1,0:T(8,128)(2,1)}), bf16[1024,1024]{1,0:T(8,128)(2,1)}) %all-gather.5.cloned.1.call-update) | async-done | bytes 2097168 | tf_op jit(solution)/shard_map/all_gather | solution.py:162
  72.2 11.4 %shard_map.203 = (bf16[1024,1024]{1,0:T(8,128)(2,1)}, bf16[1024,1024]{1,0:T(8,128)(2,1)}, f32[128,1024]{1,0:T(8,128)}, bf16[128,1024]{1,0:T(8,128)(2,1)}) custom-call(bf16[128,1024]{1,0:T(8,128)(2,1)} %q_ref.1, bf16[1024,1024]{1,0:T(8,128)(2,1)} %all-gather.3.cloned.1.call-done.k_ref, bf16[1024,1024]{1,0:T(8,128)(2,1)} %all-gather.5.cloned.1.call-done.v_ref, ...), custom_call_target="tpu_custom_call" | custom-call | tf_op jit(solution)/shard_map/pallas_call | solution.py:110
  83.7 41.3 %reduce-scatter.3.cloned.1.call-done = bf16[128,1024]{1,0:T(8,128)(2,1)} async-done(((bf16[1024,1024]{1,0:T(8,128)(2,1)}), bf16[128,1024]{1,0:T(8,128)(2,1)}) %reduce-scatter.3.cloned.1.call-update) | async-done | bytes 262160 | tf_op jit(solution)/shard_map/reduce_scatter | solution.py:172
  126.2 1.5 collective-permute-start.4
  127.7 2.1 %collective-permute-done.4 = f32[128]{0:T(128)S(1)} collective-permute-done((f32[128]{0:T(128)S(1)}, f32[128]{0:T(128)S(1)}, u32[]{:S(2)}, u32[]{:S(2)}) %collective-permute-start.4) | collective-permute-done | bytes 544 | tf_op jit(solution)/shard_map/ppermute | solution.py:59
  129.8 2.4 %collective-permute-start.5 = (f32[128]{0:T(128)S(1)}, f32[128]{0:T(128)S(1)}, u32[]{:S(2)}, u32[]{:S(2)}) collective-permute-start(f32[128]{0:T(128)S(1)} %add.82), channel_id=1, source_target_pairs={{0,2},{1,3},{2,0},{3,1},{4,6},{5,7},{6,4},{7,5},{8,10},{9,11},{10,... | collective-permute-start | bytes 1544 | tf_op jit(solution)/shard_map/ppermute | solution.py:59
  132.2 2.0 %collective-permute-done.5 = f32[128]{0:T(128)S(1)} collective-permute-done((f32[128]{0:T(128)S(1)}, f32[128]{0:T(128)S(1)}, u32[]{:S(2)}, u32[]{:S(2)}) %collective-permute-start.5) | collective-permute-done | bytes 544 | tf_op jit(solution)/shard_map/ppermute | solution.py:59
  134.2 2.3 %fusion.25 = (bf16[128,1024]{1,0:T(8,128)(2,1)}, f32[128,1024]{1,0:T(8,128)S(1)}, bf16[128,1024]{1,0:T(8,128)(2,1)}) fusion(f32[1,128,1024]{2,0,1:T(1,128)S(1)} %fusion.8, f32[128]{0:T(128)S(1)} %fusion.42, bf16[128,1024]{1,0:T(8,128)(2,1)S(1)} %get-tuple-element.30, f32[128,1024]{1,0:T(8,128)S(1)} %convert_element_type.144, f32[1024]{0:T(1024)S(1)} %copy-done.15, ...), kind=kLoop, calls=%fused_computation.58 | loop fusion | flops 1441792 | bytes 3150848 | tf_op jit(solution)/shard_map/convert_element_type | solution.py:193
  137.9 5.8 %fusion.6 = bf16[1,128,1024]{2,0,1:T(2,128)(2,1)S(1)} fusion(f32[1,255,1024]{2,1,0:T(8,128)S(1)} %copy-done.4, f32[128,1,1024]{2,0,1:T(8,128)S(1)} %bitcast.46), kind=kOutput, calls=%fused_computation.33 | convolution fusion | flops 201326592 | bytes 1830912 | tf_op jit(solution)/shard_map/conv_general_dilated | solution.py:34
  147.2 5.8 %fusion = f32[1,128,1024]{2,0,1:T(1,128)S(1)} fusion(f32[1,255,1024]{2,1,0:T(8,128)S(1)} %maximum_bitcast_fusion.1, f32[128,1,1024]{2,0,1:T(8,128)S(1)} %bitcast.49), kind=kOutput, calls=%fused_computation.9 | convolution fusion | flops 201326592 | bytes 2093056 | tf_op jit(solution)/shard_map/conv_general_dilated | solution.py:34
  159.1 1.5 collective-permute-start.12
  163.0 6.3 %collective-permute-done.9 = bf16[7,1024]{1,0:T(8,128)(2,1)S(1)} collective-permute-done((bf16[7,1024]{1,0:T(8,128)(2,1)S(1)}, bf16[7,1024]{1,0:T(8,128)(2,1)S(1)}, u32[]{:S(2)}, u32[]{:S(2)}) %collective-permute-start.9) | collective-permute-done | bytes 14368 | tf_op jit(solution)/shard_map/ppermute | solution.py:62
  169.3 2.8 %collective-permute-start.10 = (bf16[7,1024]{1,0:T(8,128)(2,1)S(1)}, bf16[7,1024]{1,0:T(8,128)(2,1)S(1)}, u32[]{:S(2)}, u32[]{:S(2)}) collective-permute-start(bf16[7,1024]{1,0:T(8,128)(2,1)S(1)} %add_convert_fusion.2), channel_id=1, source_target_pairs={{0,16},{4,20},{8,24},{12,28},{16,0},{20,4},{24,8},{28,12},{1,17},{... | collective-permute-start | bytes 43016 | tf_op jit(solution)/shard_map/ppermute | solution.py:62
  174.6 5.1 %collective-permute-done.13 = bf16[129,1024]{1,0:T(8,128)(2,1)S(1)} collective-permute-done((bf16[129,1024]{1,0:T(8,128)(2,1)S(1)}, bf16[129,1024]{1,0:T(8,128)(2,1)S(1)}, u32[]{:S(2)}, u32[]{:S(2)}) %collective-permute-start.13) | collective-permute-done | bytes 264224 | tf_op jit(solution)/shard_map/ppermute | solution.py:62
  (113 shorter events, 25.1 us)
Async XLA Ops:
  7.2 34.6 %all-gather.3.cloned.1.call-start = ((), (), s32[]{:S(2)}) async-start(), calls=%async_computation.2 | async-start | bytes 2359296 | tf_op jit(solution)/shard_map/all_gather | solution.py:161
  7.9 64.3 %all-gather.5.cloned.1.call-start = ((), (), s32[]{:S(2)}) async-start(), calls=%async_computation.3 | async-start | bytes 2359296 | tf_op jit(solution)/shard_map/all_gather | solution.py:162
  9.1 5.2 %collective-permute-start = (bf16[6,1024]{1,0:T(8,128)(2,1)S(1)}, bf16[6,1024]{1,0:T(8,128)(2,1)S(1)}, u32[]{:S(2)}, u32[]{:S(2)}) collective-permute-start(bf16[6,1024]{1,0:T(8,128)(2,1)S(1)} %slice.52), channel_id=1, source_target_pairs={{0,4},{4,8},{8,12},{12,16},{16,20},{20,24},{24,28},{1,5},{5,9},{9,... | collective-permute-start | bytes 36872 | tf_op jit(solution)/shard_map/ppermute | solution.py:30
  15.9 7.2 %collective-permute-start.1 = (bf16[127,1024]{1,0:T(8,128)(2,1)S(1)}, bf16[127,1024]{1,0:T(8,128)(2,1)S(1)}, u32[]{:S(2)}, u32[]{:S(2)}) collective-permute-start(bf16[127,1024]{1,0:T(8,128)(2,1)S(1)} %slice.50), channel_id=1, source_target_pairs={{0,4},{4,8},{8,12},{12,16},{16,20},{20,24},{24,28},{1,5},{5,9},{9,... | collective-permute-start | bytes 780296 | tf_op jit(solution)/shard_map/ppermute | solution.py:30
  23.3 6.6 %copy-start.3 = (f32[1,255,1024]{2,1,0:T(8,128)}, f32[1,255,1024]{2,1,0:T(8,128)S(1)}, u32[]{:S(2)}) copy-start(f32[1,255,1024]{2,1,0:T(8,128)S(1)} %maximum_bitcast_fusion) | copy-start | bytes 3133444
  24.1 14.1 %copy-start.15 = (f32[1024]{0:T(1024)S(1)}, f32[1024]{0:T(1024)}, u32[]{:S(2)}) copy-start(f32[1024]{0:T(1024)} %param.19) | copy-start | bytes 12292
  29.9 9.2 %copy-start.17 = (s32[1024]{0:T(1024)S(1)}, s32[1024]{0:T(1024)}, u32[]{:S(2)}) copy-start(s32[1024]{0:T(1024)} %param.22) | copy-start | bytes 12292
  30.1 3.6 %collective-permute-start.2 = (f32[128]{0:T(128)S(1)}, f32[128]{0:T(128)S(1)}, u32[]{:S(2)}, u32[]{:S(2)}) collective-permute-start(f32[128]{0:T(128)S(1)} %get-tuple-element.29), channel_id=1, source_target_pairs={{0,1},{1,0},{2,3},{3,2},{4,5},{5,4},{6,7},{7,6},{8,9},{9,8},{10,11... | collective-permute-start | bytes 1544 | tf_op jit(solution)/shard_map/ppermute | solution.py:59
  33.7 4.4 %collective-permute-start.3 = (f32[128]{0:T(128)S(1)}, f32[128]{0:T(128)S(1)}, u32[]{:S(2)}, u32[]{:S(2)}) collective-permute-start(f32[128]{0:T(128)S(1)} %add.73), channel_id=1, source_target_pairs={{0,2},{1,3},{2,0},{3,1},{4,6},{5,7},{6,4},{7,5},{8,10},{9,11},{10,... | collective-permute-start | bytes 1544 | tf_op jit(solution)/shard_map/ppermute | solution.py:59
  39.1 86.0 %reduce-scatter.3.cloned.1.call-start = ((), (), s32[]{:S(2)}) async-start(), calls=%async_computation.4 | async-start | bytes 2359296 | tf_op jit(solution)/shard_map/reduce_scatter | solution.py:172
  83.6 50.6 %copy-start.1 = (bf16[128,1024]{1,0:T(8,128)(2,1)S(1)}, bf16[128,1024]{1,0:T(8,128)(2,1)}, u32[]{:S(2)}) copy-start(bf16[128,1024]{1,0:T(8,128)(2,1)} %cot_ref.1) | copy-start | bytes 786436
  83.6 97.5 %reduce-scatter.5.cloned.1.call-start = ((), (), s32[]{:S(2)}) async-start(), calls=%async_computation.5 | async-start | bytes 2359296 | tf_op jit(solution)/shard_map/reduce_scatter | solution.py:179
  126.2 3.6 %collective-permute-start.4 = (f32[128]{0:T(128)S(1)}, f32[128]{0:T(128)S(1)}, u32[]{:S(2)}, u32[]{:S(2)}) collective-permute-start(f32[128]{0:T(128)S(1)} %get-tuple-element.24), channel_id=1, source_target_pairs={{0,1},{1,0},{2,3},{3,2},{4,5},{5,4},{6,7},{7,6},{8,9},{9,8},{10,11... | collective-permute-start | bytes 1544 | tf_op jit(solution)/shard_map/ppermute | solution.py:59
  129.8 4.4 %collective-permute-start.5 = (f32[128]{0:T(128)S(1)}, f32[128]{0:T(128)S(1)}, u32[]{:S(2)}, u32[]{:S(2)}) collective-permute-start(f32[128]{0:T(128)S(1)} %add.82), channel_id=1, source_target_pairs={{0,2},{1,3},{2,0},{3,1},{4,6},{5,7},{6,4},{7,5},{8,10},{9,11},{10,... | collective-permute-start | bytes 1544 | tf_op jit(solution)/shard_map/ppermute | solution.py:59
  136.6 9.4 %collective-permute-start.6 = (bf16[127,1024]{1,0:T(8,128)(2,1)S(1)}, bf16[127,1024]{1,0:T(8,128)(2,1)}, u32[]{:S(2)}, u32[]{:S(2)}) collective-permute-start(bf16[127,1024]{1,0:T(8,128)(2,1)S(1)} %slice.49), channel_id=1, source_target_pairs={{4,0},{8,4},{12,8},{16,12},{20,16},{24,20},{28,24},{5,1},{9,5},{13... | collective-permute-start | bytes 780296 | tf_op jit(solution)/shard_map/ppermute | solution.py:30
  144.9 13.2 %collective-permute-start.11 = (bf16[129,1024]{1,0:T(8,128)(2,1)}, bf16[129,1024]{1,0:T(8,128)(2,1)}, u32[]{:S(2)}, u32[]{:S(2)}) collective-permute-start(bf16[129,1024]{1,0:T(8,128)(2,1)} %pad_maximum_fusion), channel_id=1, source_target_pairs={{0,4},{4,0},{8,12},{12,8},{16,20},{20,16},{24,28},{28,24},{1,5},{5... | collective-permute-start | bytes 792584 | tf_op jit(solution)/shard_map/ppermute | solution.py:62
  147.2 5.8 %copy-start.6 = (bf16[128,1024]{1,0:T(8,128)(2,1)S(1)}, bf16[128,1024]{1,0:T(8,128)(2,1)}, u32[]{:S(2)}) copy-start(bf16[128,1024]{1,0:T(8,128)(2,1)} %param.17) | copy-start | bytes 786436
  155.6 5.0 %collective-permute-start.7 = (bf16[6,1024]{1,0:T(8,128)(2,1)S(1)}, bf16[6,1024]{1,0:T(8,128)(2,1)S(1)}, u32[]{:S(2)}, u32[]{:S(2)}) collective-permute-start(bf16[6,1024]{1,0:T(8,128)(2,1)S(1)} %slice.51), channel_id=1, source_target_pairs={{4,0},{8,4},{12,8},{16,12},{20,16},{24,20},{28,24},{5,1},{9,5},{13... | collective-permute-start | bytes 36872 | tf_op jit(solution)/shard_map/ppermute | solution.py:30
  156.9 4.6 %collective-permute-start.8 = (bf16[7,1024]{1,0:T(8,128)(2,1)S(1)}, bf16[7,1024]{1,0:T(8,128)(2,1)S(1)}, u32[]{:S(2)}, u32[]{:S(2)}) collective-permute-start(bf16[7,1024]{1,0:T(8,128)(2,1)S(1)} %rev.14), channel_id=1, source_target_pairs={{0,4},{4,0},{8,12},{12,8},{16,20},{20,16},{24,28},{28,24},{1,5},{5... | collective-permute-start | bytes 43016 | tf_op jit(solution)/shard_map/ppermute | solution.py:62
  159.1 13.0 %collective-permute-start.12 = (bf16[129,1024]{1,0:T(8,128)(2,1)S(1)}, bf16[129,1024]{1,0:T(8,128)(2,1)S(1)}, u32[]{:S(2)}, u32[]{:S(2)}) collective-permute-start(bf16[129,1024]{1,0:T(8,128)(2,1)S(1)} %add_convert_fusion.1), channel_id=1, source_target_pairs={{0,8},{4,12},{8,0},{12,4},{16,24},{20,28},{24,16},{28,20},{1,9},{5... | collective-permute-start | bytes 792584 | tf_op jit(solution)/shard_map/ppermute | solution.py:62
  161.6 7.7 %collective-permute-start.9 = (bf16[7,1024]{1,0:T(8,128)(2,1)S(1)}, bf16[7,1024]{1,0:T(8,128)(2,1)S(1)}, u32[]{:S(2)}, u32[]{:S(2)}) collective-permute-start(bf16[7,1024]{1,0:T(8,128)(2,1)S(1)} %add_convert_fusion.3), channel_id=1, source_target_pairs={{0,8},{4,12},{8,0},{12,4},{16,24},{20,28},{24,16},{28,20},{1,9},{5... | collective-permute-start | bytes 43016 | tf_op jit(solution)/shard_map/ppermute | solution.py:62
  162.5 9.7 %copy-start.9 = (bf16[128,1024]{1,0:T(8,128)(2,1)S(1)}, bf16[128,1024]{1,0:T(8,128)(2,1)}, u32[]{:S(2)}) copy-start(bf16[128,1024]{1,0:T(8,128)(2,1)} %param.14) | copy-start | bytes 786436
  169.3 4.7 %collective-permute-start.10 = (bf16[7,1024]{1,0:T(8,128)(2,1)S(1)}, bf16[7,1024]{1,0:T(8,128)(2,1)S(1)}, u32[]{:S(2)}, u32[]{:S(2)}) collective-permute-start(bf16[7,1024]{1,0:T(8,128)(2,1)S(1)} %add_convert_fusion.2), channel_id=1, source_target_pairs={{0,16},{4,20},{8,24},{12,28},{16,0},{20,4},{24,8},{28,12},{1,17},{... | collective-permute-start | bytes 43016 | tf_op jit(solution)/shard_map/ppermute | solution.py:62
  172.2 7.5 %collective-permute-start.13 = (bf16[129,1024]{1,0:T(8,128)(2,1)S(1)}, bf16[129,1024]{1,0:T(8,128)(2,1)S(1)}, u32[]{:S(2)}, u32[]{:S(2)}) collective-permute-start(bf16[129,1024]{1,0:T(8,128)(2,1)S(1)} %add_convert_fusion), channel_id=1, source_target_pairs={{0,16},{4,20},{8,24},{12,28},{16,0},{20,4},{24,8},{28,12},{1,17},{... | collective-permute-start | bytes 792584 | tf_op jit(solution)/shard_map/ppermute | solution.py:62
  (13 other events, 28.9 us)
Sparse Core Ops, SparseCore 0:
  9.9 31.8 all-gather.2
  44.2 27.8 all-gather.4
  83.7 41.2 reduce-scatter.2
  132.3 39.6 reduce-scatter.4

commit v4 on v3

--- a/solution.py
+++ b/solution.py
@@ -157,10 +157,17 @@
     squares = channel_total(jnp.sum(second_wide * second_wide, axis=1))
     inverse_rms = lax.rsqrt(squares / D + epsilon)
     normed = (second_wide * inverse_rms[:, None] * scaling).astype(jnp.bfloat16)
-    keys_whole, values_whole = (
-        lax.all_gather(matchers, "ctx", axis=0, tiled=True),
-        lax.all_gather(normed, "ctx", axis=0, tiled=True),
-    )
+    ctx_count = lax.axis_size("ctx")
+    ctx_index = lax.axis_index("ctx")
+    keys_whole = lax.all_gather(matchers, "ctx", axis=0, tiled=True)
+    reach = min(ctx_count - 1, (3 * total_rows // 4 - 1 + local_rows - 1) // local_rows)
+    values_whole = lax.dynamic_update_slice_in_dim(
+        jnp.zeros((total_rows, width_local), jnp.bfloat16), normed, position, 0
+    )
+    for distance in range(1, reach + 1):
+        arrived = passed_along(normed, "ctx", distance)
+        block_start = ((ctx_index - distance) % ctx_count) * local_rows
+        values_whole = lax.dynamic_update_slice_in_dim(values_whole, arrived, block_start, 0)
     query_pos = position + jnp.arange(local_rows, dtype=jnp.int32)
     key_pos = jnp.arange(total_rows, dtype=jnp.int32)
     query_seg = lax.dynamic_slice_in_dim(segments, position, local_rows, 0)
@@ -169,12 +176,11 @@
         queries, keys_whole, values_whole, cotangent, visible.astype(jnp.float32), scale_factor
     )
     result = (second_wide + attended_all).astype(jnp.bfloat16)
-    value_grad = lax.psum_scatter(
-        value_part,
-        "ctx",
-        scatter_dimension=0,
-        tiled=True,
-    ).astype(jnp.float32)
+    value_grad = lax.dynamic_slice_in_dim(value_part, position, local_rows, 0).astype(jnp.float32)
+    for distance in range(1, reach + 1):
+        block_start = ((ctx_index - distance) % ctx_count) * local_rows
+        leaving = lax.dynamic_slice_in_dim(value_part, block_start, local_rows, 0)
+        value_grad = value_grad + passed_along(leaving, "ctx", -distance).astype(jnp.float32)
     key_part, value_grad = lax.optimization_barrier((key_part, value_grad))
     matchers_grad = lax.psum_scatter(
         key_part,

time: 188 us -> 177 us (0.941)
  waiting for transfers between devices: 94.1 us -> 50.2 us
  starting transfers between devices: 25.2 us -> 56.8 us
  local copies, waits for them, and re-layouts: 8.76 us -> 12.3 us
  other arithmetic: 14.3 us -> 10.8 us
    reduce_scatter x1 -> x0, waiting for transfers between devices: 41.3 us -> none  [shards(): lax.psum_scatter(value_part, 'ctx', scatter_dimension=0, tiled=True)]
    all_gather x2 -> x1, waiting for transfers between devices: 32 us -> 0.02 us  [shards(): keys_whole = lax.all_gather(matchers, 'ctx', axis=0, tiled=True)]
    ppermute x4 -> x16, starting transfers between devices: 9.47 us -> 39 us  [passed_along(): lax.ppermute(value, axis, [(source, source + steps) for source in range(l...]
    ppermute x4 -> x16, waiting for transfers between devices: 0.01 us -> 26 us  [passed_along(): lax.ppermute(value, axis, [(source, source + steps) for source in range(l...]
    ppermute x6, waiting for transfers between devices: 12.2 us -> 16.5 us  [butterfly_total(): lax.ppermute(rounded, axis, pairs).astype(value.dtype)]
    dynamic_update_slice x0 -> x6, local copies, waits for them, and re-layouts: none -> 2.99 us  [shards(): lax.dynamic_update_slice_in_dim(values_whole, arrived, block_start, 0)]
    rev x1, local copies, waits for them, and re-layouts: 2.62 us -> 0.24 us  [shards(): conv_two = depthwise(padded_two, kernel[::-1])]
    ppermute x6, starting transfers between devices: 7.36 us -> 9.3 us  [butterfly_total(): lax.ppermute(rounded, axis, pairs).astype(value.dtype)]
  transfers between devices with their start and end apart: 18 -> 28, of which waited for: 10 -> 13; matrix products, arithmetic and copies ran while one was open for 21% -> 21% of each run, Pallas kernels for 0% -> 0%
where the time goes in v4:
time: 177 us; the launch traced here: 176 us
  starting transfers between devices  56.8 us (32%)
  waiting for transfers between devices  50.2 us (28%)
  matrix products  19.7 us (11%)
  between operations  14.8 us (8%)
  local copies, waits for them, and re-layouts  12.3 us (7%)
  Pallas kernels  11.4 us (6%)
  other arithmetic  10.8 us (6%)
    ppermute x16, starting transfers between devices, passed_along(): lax.ppermute(value, axis, [(source, source + steps) for source in range(l...  39 us
    ppermute x16, waiting for transfers between devices, passed_along(): lax.ppermute(value, axis, [(source, source + steps) for source in range(l...  26 us
    conv_general_dilated x6, matrix products, depthwise(): lax.conv_general_dilated(padded[None], tap_rows[:, None, :], (1,), 'VALID...  19.7 us
    ppermute x6, waiting for transfers between devices, butterfly_total(): lax.ppermute(rounded, axis, pairs).astype(value.dtype)  16.5 us
    pallas_call x1, Pallas kernels, head_attention(): pl.pallas_call(functools.partial(attention_block, scale_factor), grid=(wi...  11.4 us
    ppermute x6, starting transfers between devices, butterfly_total(): lax.ppermute(rounded, axis, pairs).astype(value.dtype)  9.3 us
    ppermute x4, starting transfers between devices, butterfly_total(): value = value + lax.ppermute(value, axis, pairs)  8.39 us
    ppermute x4, waiting for transfers between devices, butterfly_total(): value = value + lax.ppermute(value, axis, pairs)  7.63 us
  transfers between devices with their start and end apart: 28, of which 13 were waited for; matrix products, arithmetic and copies ran while one was open for 21% of the time, Pallas kernels for 0%

profile of v4, /device:TPU:0, one launch (start us, length us, event | category | flops | bytes accessed | tf_op | source)
XLA Modules:
  0.0 175.9 jit_solution(12290161833625434806)
XLA Ops:
  8.3 2.4 %collective-permute-start = (bf16[6,1024]{1,0:T(8,128)(2,1)S(1)}, bf16[6,1024]{1,0:T(8,128)(2,1)S(1)}, u32[]{:S(2)}, u32[]{:S(2)}) collective-permute-start(bf16[6,1024]{1,0:T(8,128)(2,1)S(1)} %slice.52), channel_id=1, source_target_pairs={{0,4},{4,8},{8,12},{12,16},{16,20},{20,24},{24,28},{1,5},{5,9},{9,... | collective-permute-start | bytes 36872 | tf_op jit(solution)/shard_map/ppermute | solution.py:30
  10.8 2.8 %rev.12 = f32[7,1024]{1,0:T(8,128)S(1)} reverse(f32[7,1024]{1,0:T(8,128)} %param.15), dimensions={0} | reverse | bytes 57344 | tf_op jit(solution)/shard_map/rev | solution.py:148
  15.3 4.7 %collective-permute-start.1 = (bf16[127,1024]{1,0:T(8,128)(2,1)S(1)}, bf16[127,1024]{1,0:T(8,128)(2,1)S(1)}, u32[]{:S(2)}, u32[]{:S(2)}) collective-permute-start(bf16[127,1024]{1,0:T(8,128)(2,1)S(1)} %slice.50), channel_id=1, source_target_pairs={{0,4},{4,8},{8,12},{12,16},{16,20},{20,24},{24,28},{1,5},{5,9},{9,... | collective-permute-start | bytes 780296 | tf_op jit(solution)/shard_map/ppermute | solution.py:30
  21.2 5.8 %fusion.8 = f32[1,128,1024]{2,0,1:T(1,128)S(1)} fusion(f32[1,255,1024]{2,1,0:T(8,128)S(1)} %maximum_bitcast_fusion, f32[128,1,1024]{2,0,1:T(8,128)S(1)} %bitcast.50), kind=kOutput, calls=%fused_computation.35 | convolution fusion | flops 201326592 | bytes 2093056 | tf_op jit(solution)/shard_map/conv_general_dilated | solution.py:34
  28.9 2.0 %collective-permute-done.2 = f32[128]{0:T(128)S(1)} collective-permute-done((f32[128]{0:T(128)S(1)}, f32[128]{0:T(128)S(1)}, u32[]{:S(2)}, u32[]{:S(2)}) %collective-permute-start.2) | collective-permute-done | bytes 544 | tf_op jit(solution)/shard_map/ppermute | solution.py:59
  30.9 2.6 %collective-permute-start.3 = (f32[128]{0:T(128)S(1)}, f32[128]{0:T(128)S(1)}, u32[]{:S(2)}, u32[]{:S(2)}) collective-permute-start(f32[128]{0:T(128)S(1)} %add.146), channel_id=1, source_target_pairs={{0,2},{1,3},{2,0},{3,1},{4,6},{5,7},{6,4},{7,5},{8,10},{9,11},{10,... | collective-permute-start | bytes 1544 | tf_op jit(solution)/shard_map/ppermute | solution.py:59
  33.5 1.9 %collective-permute-done.3 = f32[128]{0:T(128)S(1)} collective-permute-done((f32[128]{0:T(128)S(1)}, f32[128]{0:T(128)S(1)}, u32[]{:S(2)}, u32[]{:S(2)}) %collective-permute-start.3) | collective-permute-done | bytes 544 | tf_op jit(solution)/shard_map/ppermute | solution.py:59
  36.4 5.6 %collective-permute-start.4 = (bf16[128,1024]{1,0:T(8,128)(2,1)}, bf16[128,1024]{1,0:T(8,128)(2,1)}, u32[]{:S(2)}, u32[]{:S(2)}) collective-permute-start(bf16[128,1024]{1,0:T(8,128)(2,1)} %get-tuple-element.30), channel_id=1, source_target_pairs={{0,4},{4,8},{8,12},{12,16},{16,20},{20,24},{24,28},{1,5},{5,9},{9,... | collective-permute-start | bytes 786440 | tf_op jit(solution)/shard_map/ppermute | solution.py:30
  42.1 9.5 %collective-permute-start.6 = (bf16[128,1024]{1,0:T(8,128)(2,1)}, bf16[128,1024]{1,0:T(8,128)(2,1)}, u32[]{:S(2)}, u32[]{:S(2)}) collective-permute-start(bf16[128,1024]{1,0:T(8,128)(2,1)} %get-tuple-element.30), channel_id=1, source_target_pairs={{0,12},{4,16},{8,20},{12,24},{16,28},{1,13},{5,17},{9,21},{13,25},... | collective-permute-start | bytes 786440 | tf_op jit(solution)/shard_map/ppermute | solution.py:30
  51.7 2.3 %collective-permute-start.5 = (bf16[128,1024]{1,0:T(8,128)(2,1)}, bf16[128,1024]{1,0:T(8,128)(2,1)}, u32[]{:S(2)}, u32[]{:S(2)}) collective-permute-start(bf16[128,1024]{1,0:T(8,128)(2,1)} %get-tuple-element.30), channel_id=1, source_target_pairs={{0,8},{4,12},{8,16},{12,20},{16,24},{20,28},{1,9},{5,13},{9,17},{1... | collective-permute-start | bytes 786440 | tf_op jit(solution)/shard_map/ppermute | solution.py:30
  59.8 2.3 %collective-permute-done.5 = bf16[128,1024]{1,0:T(8,128)(2,1)} collective-permute-done((bf16[128,1024]{1,0:T(8,128)(2,1)}, bf16[128,1024]{1,0:T(8,128)(2,1)}, u32[]{:S(2)}, u32[]{:S(2)}) %collective-permute-start.5) | collective-permute-done | bytes 262176 | tf_op jit(solution)/shard_map/ppermute | solution.py:30
  64.1 7.8 %collective-permute-done.7 = bf16[128,1024]{1,0:T(8,128)(2,1)S(1)} collective-permute-done((bf16[128,1024]{1,0:T(8,128)(2,1)}, bf16[128,1024]{1,0:T(8,128)(2,1)S(1)}, u32[]{:S(2)}, u32[]{:S(2)}) %collective-permute-start.7) | collective-permute-done | bytes 262176 | tf_op jit(solution)/shard_map/ppermute | solution.py:30
  73.4 11.4 %shard_map.203 = (bf16[1024,1024]{1,0:T(8,128)(2,1)}, bf16[1024,1024]{1,0:T(8,128)(2,1)}, f32[128,1024]{1,0:T(8,128)}, bf16[128,1024]{1,0:T(8,128)(2,1)}) custom-call(bf16[128,1024]{1,0:T(8,128)(2,1)} %q_ref.1, bf16[1024,1024]{1,0:T(8,128)(2,1)} %all-gather.2.cloned.1.call-done.k_ref, bf16[1024,1024]{1,0:T(8,128)(2,1)} %copy-done, ...), custom_call_target="tpu_custom_call" | custom-call | tf_op jit(solution)/shard_map/pallas_call | solution.py:110
  94.3 9.2 %collective-permute-done.15 = bf16[128,1024]{1,0:T(8,128)(2,1)S(1)} collective-permute-done((bf16[128,1024]{1,0:T(8,128)(2,1)S(1)}, bf16[128,1024]{1,0:T(8,128)(2,1)S(1)}, u32[]{:S(2)}, u32[]{:S(2)}) %collective-permute-start.15) | collective-permute-done | bytes 262176 | tf_op jit(solution)/shard_map/ppermute | solution.py:30
  104.4 4.8 %collective-permute-done.13 = bf16[128,1024]{1,0:T(8,128)(2,1)S(1)} collective-permute-done((bf16[128,1024]{1,0:T(8,128)(2,1)S(1)}, bf16[128,1024]{1,0:T(8,128)(2,1)S(1)}, u32[]{:S(2)}, u32[]{:S(2)}) %collective-permute-start.13) | collective-permute-done | bytes 262176 | tf_op jit(solution)/shard_map/ppermute | solution.py:30
  112.3 2.0 %collective-permute-done.16 = f32[128]{0:T(128)S(1)} collective-permute-done((f32[128]{0:T(128)S(1)}, f32[128]{0:T(128)S(1)}, u32[]{:S(2)}, u32[]{:S(2)}) %collective-permute-start.16) | collective-permute-done | bytes 544 | tf_op jit(solution)/shard_map/ppermute | solution.py:59
  114.2 2.5 %collective-permute-start.17 = (f32[128]{0:T(128)S(1)}, f32[128]{0:T(128)S(1)}, u32[]{:S(2)}, u32[]{:S(2)}) collective-permute-start(f32[128]{0:T(128)S(1)} %add.173), channel_id=1, source_target_pairs={{0,2},{1,3},{2,0},{3,1},{4,6},{5,7},{6,4},{7,5},{8,10},{9,11},{10,... | collective-permute-start | bytes 1544 | tf_op jit(solution)/shard_map/ppermute | solution.py:59
  116.8 1.9 %collective-permute-done.17 = f32[128]{0:T(128)S(1)} collective-permute-done((f32[128]{0:T(128)S(1)}, f32[128]{0:T(128)S(1)}, u32[]{:S(2)}, u32[]{:S(2)}) %collective-permute-start.17) | collective-permute-done | bytes 544 | tf_op jit(solution)/shard_map/ppermute | solution.py:59
  122.0 5.8 %fusion.6 = bf16[1,128,1024]{2,0,1:T(2,128)(2,1)S(1)} fusion(f32[1,255,1024]{2,1,0:T(8,128)S(1)} %copy-done.8, f32[128,1,1024]{2,0,1:T(8,128)S(1)} %bitcast.46), kind=kOutput, calls=%fused_computation.33 | convolution fusion | flops 201326592 | bytes 1830912 | tf_op jit(solution)/shard_map/conv_general_dilated | solution.py:34
  128.2 2.6 %collective-permute-start.23 = (bf16[129,1024]{1,0:T(8,128)(2,1)S(1)}, bf16[129,1024]{1,0:T(8,128)(2,1)S(1)}, u32[]{:S(2)}, u32[]{:S(2)}) collective-permute-start(bf16[129,1024]{1,0:T(8,128)(2,1)S(1)} %pad_maximum_fusion), channel_id=1, source_target_pairs={{0,4},{4,0},{8,12},{12,8},{16,20},{20,16},{24,28},{28,24},{1,5},{5... | collective-permute-start | bytes 792584 | tf_op jit(solution)/shard_map/ppermute | solution.py:62
  131.0 5.8 %fusion = f32[1,128,1024]{2,0,1:T(1,128)S(1)} fusion(f32[1,255,1024]{2,1,0:T(8,128)S(1)} %maximum_bitcast_fusion.1, f32[128,1,1024]{2,0,1:T(8,128)S(1)} %bitcast.49), kind=kOutput, calls=%fused_computation.9 | convolution fusion | flops 201326592 | bytes 2093056 | tf_op jit(solution)/shard_map/conv_general_dilated | solution.py:34
  142.2 2.6 %collective-permute-start.24 = (bf16[129,1024]{1,0:T(8,128)(2,1)S(1)}, bf16[129,1024]{1,0:T(8,128)(2,1)S(1)}, u32[]{:S(2)}, u32[]{:S(2)}) collective-permute-start(bf16[129,1024]{1,0:T(8,128)(2,1)S(1)} %add_convert_fusion.1), channel_id=1, source_target_pairs={{0,8},{4,12},{8,0},{12,4},{16,24},{20,28},{24,16},{28,20},{1,9},{5... | collective-permute-start | bytes 792584 | tf_op jit(solution)/shard_map/ppermute | solution.py:62
  147.3 7.7 %collective-permute-done.21 = bf16[7,1024]{1,0:T(8,128)(2,1)S(1)} collective-permute-done((bf16[7,1024]{1,0:T(8,128)(2,1)S(1)}, bf16[7,1024]{1,0:T(8,128)(2,1)S(1)}, u32[]{:S(2)}, u32[]{:S(2)}) %collective-permute-start.21) | collective-permute-done | bytes 14368 | tf_op jit(solution)/shard_map/ppermute | solution.py:62
  159.4 8.2 %collective-permute-done.25 = bf16[129,1024]{1,0:T(8,128)(2,1)S(1)} collective-permute-done((bf16[129,1024]{1,0:T(8,128)(2,1)S(1)}, bf16[129,1024]{1,0:T(8,128)(2,1)S(1)}, u32[]{:S(2)}, u32[]{:S(2)}) %collective-permute-start.25) | collective-permute-done | bytes 264224 | tf_op jit(solution)/shard_map/ppermute | solution.py:62
  (147 shorter events, 47.1 us)
Async XLA Ops:
  7.2 64.9 %all-gather.2.cloned.1.call-start = ((), (), s32[]{:S(2)}) async-start(), calls=%async_computation.1 | async-start | bytes 2359296 | tf_op jit(solution)/shard_map/all_gather | solution.py:162
  8.3 5.2 %collective-permute-start = (bf16[6,1024]{1,0:T(8,128)(2,1)S(1)}, bf16[6,1024]{1,0:T(8,128)(2,1)S(1)}, u32[]{:S(2)}, u32[]{:S(2)}) collective-permute-start(bf16[6,1024]{1,0:T(8,128)(2,1)S(1)} %slice.52), channel_id=1, source_target_pairs={{0,4},{4,8},{8,12},{12,16},{16,20},{20,24},{24,28},{1,5},{5,9},{9,... | collective-permute-start | bytes 36872 | tf_op jit(solution)/shard_map/ppermute | solution.py:30
  10.7 158.4 %reduce-scatter.2.cloned.1.call-start = ((), (), s32[]{:S(2)}) async-start(), calls=%async_computation.2 | async-start | bytes 2359296 | tf_op jit(solution)/shard_map/reduce_scatter | solution.py:185
  15.3 5.8 %collective-permute-start.1 = (bf16[127,1024]{1,0:T(8,128)(2,1)S(1)}, bf16[127,1024]{1,0:T(8,128)(2,1)S(1)}, u32[]{:S(2)}, u32[]{:S(2)}) collective-permute-start(bf16[127,1024]{1,0:T(8,128)(2,1)S(1)} %slice.50), channel_id=1, source_target_pairs={{0,4},{4,8},{8,12},{12,16},{16,20},{20,24},{24,28},{1,5},{5,9},{9,... | collective-permute-start | bytes 780296 | tf_op jit(solution)/shard_map/ppermute | solution.py:30
  30.9 4.4 %collective-permute-start.3 = (f32[128]{0:T(128)S(1)}, f32[128]{0:T(128)S(1)}, u32[]{:S(2)}, u32[]{:S(2)}) collective-permute-start(f32[128]{0:T(128)S(1)} %add.146), channel_id=1, source_target_pairs={{0,2},{1,3},{2,0},{3,1},{4,6},{5,7},{6,4},{7,5},{8,10},{9,11},{10,... | collective-permute-start | bytes 1544 | tf_op jit(solution)/shard_map/ppermute | solution.py:59
  36.4 21.1 %collective-permute-start.4 = (bf16[128,1024]{1,0:T(8,128)(2,1)}, bf16[128,1024]{1,0:T(8,128)(2,1)}, u32[]{:S(2)}, u32[]{:S(2)}) collective-permute-start(bf16[128,1024]{1,0:T(8,128)(2,1)} %get-tuple-element.30), channel_id=1, source_target_pairs={{0,4},{4,8},{8,12},{12,16},{16,20},{20,24},{24,28},{1,5},{5,9},{9,... | collective-permute-start | bytes 786440 | tf_op jit(solution)/shard_map/ppermute | solution.py:30
  42.1 21.0 %collective-permute-start.6 = (bf16[128,1024]{1,0:T(8,128)(2,1)}, bf16[128,1024]{1,0:T(8,128)(2,1)}, u32[]{:S(2)}, u32[]{:S(2)}) collective-permute-start(bf16[128,1024]{1,0:T(8,128)(2,1)} %get-tuple-element.30), channel_id=1, source_target_pairs={{0,12},{4,16},{8,20},{12,24},{16,28},{1,13},{5,17},{9,21},{13,25},... | collective-permute-start | bytes 786440 | tf_op jit(solution)/shard_map/ppermute | solution.py:30
  51.7 10.5 %collective-permute-start.5 = (bf16[128,1024]{1,0:T(8,128)(2,1)}, bf16[128,1024]{1,0:T(8,128)(2,1)}, u32[]{:S(2)}, u32[]{:S(2)}) collective-permute-start(bf16[128,1024]{1,0:T(8,128)(2,1)} %get-tuple-element.30), channel_id=1, source_target_pairs={{0,8},{4,12},{8,16},{12,20},{16,24},{20,28},{1,9},{5,13},{9,17},{1... | collective-permute-start | bytes 786440 | tf_op jit(solution)/shard_map/ppermute | solution.py:30
  54.9 17.1 %collective-permute-start.8 = (bf16[128,1024]{1,0:T(8,128)(2,1)}, bf16[128,1024]{1,0:T(8,128)(2,1)S(1)}, u32[]{:S(2)}, u32[]{:S(2)}) collective-permute-start(bf16[128,1024]{1,0:T(8,128)(2,1)} %get-tuple-element.30), channel_id=1, source_target_pairs={{0,20},{4,24},{8,28},{1,21},{5,25},{9,29},{2,22},{6,26},{10,30},{3... | collective-permute-start | bytes 786440 | tf_op jit(solution)/shard_map/ppermute | solution.py:30
  56.2 15.7 %collective-permute-start.7 = (bf16[128,1024]{1,0:T(8,128)(2,1)}, bf16[128,1024]{1,0:T(8,128)(2,1)S(1)}, u32[]{:S(2)}, u32[]{:S(2)}) collective-permute-start(bf16[128,1024]{1,0:T(8,128)(2,1)} %get-tuple-element.30), channel_id=1, source_target_pairs={{0,16},{4,20},{8,24},{12,28},{1,17},{5,21},{9,25},{13,29},{2,18},{... | collective-permute-start | bytes 786440 | tf_op jit(solution)/shard_map/ppermute | solution.py:30
  57.5 14.5 %collective-permute-start.9 = (bf16[128,1024]{1,0:T(8,128)(2,1)}, bf16[128,1024]{1,0:T(8,128)(2,1)S(1)}, u32[]{:S(2)}, u32[]{:S(2)}) collective-permute-start(bf16[128,1024]{1,0:T(8,128)(2,1)} %get-tuple-element.30), channel_id=1, source_target_pairs={{0,24},{4,28},{1,25},{5,29},{2,26},{6,30},{3,27},{7,31}} | collective-permute-start | bytes 786440 | tf_op jit(solution)/shard_map/ppermute | solution.py:30
  86.3 6.5 %collective-permute-start.10 = (bf16[128,1024]{1,0:T(8,128)(2,1)S(1)}, bf16[128,1024]{1,0:T(8,128)(2,1)S(1)}, u32[]{:S(2)}, u32[]{:S(2)}) collective-permute-start(bf16[128,1024]{1,0:T(8,128)(2,1)S(1)} %get-tuple-element.35), channel_id=1, source_target_pairs={{4,0},{8,4},{12,8},{16,12},{20,16},{24,20},{28,24},{5,1},{9,5},{13... | collective-permute-start | bytes 786440 | tf_op jit(solution)/shard_map/ppermute | solution.py:30
  87.6 15.9 %collective-permute-start.15 = (bf16[128,1024]{1,0:T(8,128)(2,1)S(1)}, bf16[128,1024]{1,0:T(8,128)(2,1)S(1)}, u32[]{:S(2)}, u32[]{:S(2)}) collective-permute-start(bf16[128,1024]{1,0:T(8,128)(2,1)S(1)} %get-tuple-element.36), channel_id=1, source_target_pairs={{24,0},{28,4},{25,1},{29,5},{26,2},{30,6},{27,3},{31,7}} | collective-permute-start | bytes 786440 | tf_op jit(solution)/shard_map/ppermute | solution.py:30
  88.9 15.4 %collective-permute-start.14 = (bf16[128,1024]{1,0:T(8,128)(2,1)S(1)}, bf16[128,1024]{1,0:T(8,128)(2,1)S(1)}, u32[]{:S(2)}, u32[]{:S(2)}) collective-permute-start(bf16[128,1024]{1,0:T(8,128)(2,1)S(1)} %get-tuple-element.37), channel_id=1, source_target_pairs={{20,0},{24,4},{28,8},{21,1},{25,5},{29,9},{22,2},{26,6},{30,10},{2... | collective-permute-start | bytes 786440 | tf_op jit(solution)/shard_map/ppermute | solution.py:30
  90.2 19.0 %collective-permute-start.13 = (bf16[128,1024]{1,0:T(8,128)(2,1)S(1)}, bf16[128,1024]{1,0:T(8,128)(2,1)S(1)}, u32[]{:S(2)}, u32[]{:S(2)}) collective-permute-start(bf16[128,1024]{1,0:T(8,128)(2,1)S(1)} %get-tuple-element.38), channel_id=1, source_target_pairs={{16,0},{20,4},{24,8},{28,12},{17,1},{21,5},{25,9},{29,13},{18,2},{... | collective-permute-start | bytes 786440 | tf_op jit(solution)/shard_map/ppermute | solution.py:30
  91.5 17.7 %collective-permute-start.12 = (bf16[128,1024]{1,0:T(8,128)(2,1)S(1)}, bf16[128,1024]{1,0:T(8,128)(2,1)S(1)}, u32[]{:S(2)}, u32[]{:S(2)}) collective-permute-start(bf16[128,1024]{1,0:T(8,128)(2,1)S(1)} %get-tuple-element.39), channel_id=1, source_target_pairs={{12,0},{16,4},{20,8},{24,12},{28,16},{13,1},{17,5},{21,9},{25,13},... | collective-permute-start | bytes 786440 | tf_op jit(solution)/shard_map/ppermute | solution.py:30
  92.8 16.4 %collective-permute-start.11 = (bf16[128,1024]{1,0:T(8,128)(2,1)S(1)}, bf16[128,1024]{1,0:T(8,128)(2,1)S(1)}, u32[]{:S(2)}, u32[]{:S(2)}) collective-permute-start(bf16[128,1024]{1,0:T(8,128)(2,1)S(1)} %get-tuple-element.40), channel_id=1, source_target_pairs={{8,0},{12,4},{16,8},{20,12},{24,16},{28,20},{9,1},{13,5},{17,9},{2... | collective-permute-start | bytes 786440 | tf_op jit(solution)/shard_map/ppermute | solution.py:30
  120.7 10.2 %collective-permute-start.18 = (bf16[127,1024]{1,0:T(8,128)(2,1)}, bf16[127,1024]{1,0:T(8,128)(2,1)S(1)}, u32[]{:S(2)}, u32[]{:S(2)}) collective-permute-start(bf16[127,1024]{1,0:T(8,128)(2,1)} %slice.49), channel_id=1, source_target_pairs={{4,0},{8,4},{12,8},{16,12},{20,16},{24,20},{28,24},{5,1},{9,5},{13... | collective-permute-start | bytes 780296 | tf_op jit(solution)/shard_map/ppermute | solution.py:30
  128.2 13.9 %collective-permute-start.23 = (bf16[129,1024]{1,0:T(8,128)(2,1)S(1)}, bf16[129,1024]{1,0:T(8,128)(2,1)S(1)}, u32[]{:S(2)}, u32[]{:S(2)}) collective-permute-start(bf16[129,1024]{1,0:T(8,128)(2,1)S(1)} %pad_maximum_fusion), channel_id=1, source_target_pairs={{0,4},{4,0},{8,12},{12,8},{16,20},{20,16},{24,28},{28,24},{1,5},{5... | collective-permute-start | bytes 792584 | tf_op jit(solution)/shard_map/ppermute | solution.py:62
  139.5 5.3 %collective-permute-start.19 = (bf16[6,1024]{1,0:T(8,128)(2,1)S(1)}, bf16[6,1024]{1,0:T(8,128)(2,1)S(1)}, u32[]{:S(2)}, u32[]{:S(2)}) collective-permute-start(bf16[6,1024]{1,0:T(8,128)(2,1)S(1)} %slice.51), channel_id=1, source_target_pairs={{4,0},{8,4},{12,8},{16,12},{20,16},{24,20},{28,24},{5,1},{9,5},{13... | collective-permute-start | bytes 36872 | tf_op jit(solution)/shard_map/ppermute | solution.py:30
  140.9 4.8 %collective-permute-start.20 = (bf16[7,1024]{1,0:T(8,128)(2,1)S(1)}, bf16[7,1024]{1,0:T(8,128)(2,1)S(1)}, u32[]{:S(2)}, u32[]{:S(2)}) collective-permute-start(bf16[7,1024]{1,0:T(8,128)(2,1)S(1)} %rev.14), channel_id=1, source_target_pairs={{0,4},{4,0},{8,12},{12,8},{16,20},{20,16},{24,28},{28,24},{1,5},{5... | collective-permute-start | bytes 43016 | tf_op jit(solution)/shard_map/ppermute | solution.py:62
  142.2 14.3 %collective-permute-start.24 = (bf16[129,1024]{1,0:T(8,128)(2,1)S(1)}, bf16[129,1024]{1,0:T(8,128)(2,1)S(1)}, u32[]{:S(2)}, u32[]{:S(2)}) collective-permute-start(bf16[129,1024]{1,0:T(8,128)(2,1)S(1)} %add_convert_fusion.1), channel_id=1, source_target_pairs={{0,8},{4,12},{8,0},{12,4},{16,24},{20,28},{24,16},{28,20},{1,9},{5... | collective-permute-start | bytes 792584 | tf_op jit(solution)/shard_map/ppermute | solution.py:62
  145.8 9.2 %collective-permute-start.21 = (bf16[7,1024]{1,0:T(8,128)(2,1)S(1)}, bf16[7,1024]{1,0:T(8,128)(2,1)S(1)}, u32[]{:S(2)}, u32[]{:S(2)}) collective-permute-start(bf16[7,1024]{1,0:T(8,128)(2,1)S(1)} %add_convert_fusion.3), channel_id=1, source_target_pairs={{0,8},{4,12},{8,0},{12,4},{16,24},{20,28},{24,16},{28,20},{1,9},{5... | collective-permute-start | bytes 43016 | tf_op jit(solution)/shard_map/ppermute | solution.py:62
  156.6 11.0 %collective-permute-start.25 = (bf16[129,1024]{1,0:T(8,128)(2,1)S(1)}, bf16[129,1024]{1,0:T(8,128)(2,1)S(1)}, u32[]{:S(2)}, u32[]{:S(2)}) collective-permute-start(bf16[129,1024]{1,0:T(8,128)(2,1)S(1)} %add_convert_fusion), channel_id=1, source_target_pairs={{0,16},{4,20},{8,24},{12,28},{16,0},{20,4},{24,8},{28,12},{1,17},{... | collective-permute-start | bytes 792584 | tf_op jit(solution)/shard_map/ppermute | solution.py:62
  (27 other events, 155.8 us)
Sparse Core Ops, SparseCore 0:
  10.8 31.9 all-gather.1
  116.9 48.5 reduce-scatter.1

commit v5 on v4

--- a/solution.py
+++ b/solution.py
@@ -68,21 +68,34 @@
     return butterfly_total(partial_value, "tp")
 
 
-def attention_block(scale_factor, q_ref, k_ref, v_ref, cot_ref, vis_ref, dk_ref, dv_ref, att_ref, dq_ref):
+def head_weights(scale_factor, query_head, key_head, visible):
+    contract_last = (((1,), (1,)), ((), ()))
+    scores = (
+        lax.dot_general(query_head, key_head, contract_last, preferred_element_type=jnp.float32)
+        * scale_factor
+    )
+    scores = jnp.where(visible > 0.5, scores, -jnp.inf)
+    row_max = jnp.max(scores, axis=1, keepdims=True)
+    logsum = row_max + jnp.log(jnp.sum(jnp.exp(scores - row_max), axis=1, keepdims=True))
+    return jnp.exp(scores - logsum).astype(jnp.bfloat16)
+
+
+def value_block(scale_factor, q_ref, k_ref, cot_ref, vis_ref, dv_ref):
+    contract_first = (((0,), (0,)), ((), ()))
+    weights = head_weights(scale_factor, q_ref[...], k_ref[...], vis_ref[...])
+    dv_ref[...] = lax.dot_general(
+        weights, cot_ref[...], contract_first, preferred_element_type=jnp.float32
+    ).astype(jnp.bfloat16)
+
+
+def attention_block(scale_factor, q_ref, k_ref, v_ref, cot_ref, vis_ref, dk_ref, att_ref, dq_ref):
     contract_last = (((1,), (1,)), ((), ()))
     contract_first = (((0,), (0,)), ((), ()))
     query_head = q_ref[...]
     key_head = k_ref[...]
     value_head = v_ref[...]
     cotangent_head = cot_ref[...]
-    scores = (
-        lax.dot_general(query_head, key_head, contract_last, preferred_element_type=jnp.float32)
-        * scale_factor
-    )
-    scores = jnp.where(vis_ref[...] > 0.5, scores, -jnp.inf)
-    row_max = jnp.max(scores, axis=1, keepdims=True)
-    logsum = row_max + jnp.log(jnp.sum(jnp.exp(scores - row_max), axis=1, keepdims=True))
-    weights = jnp.exp(scores - logsum).astype(jnp.bfloat16)
+    weights = head_weights(scale_factor, query_head, key_head, vis_ref[...])
     attended = jnp.dot(weights, value_head, preferred_element_type=jnp.float32)
     weight_grad = lax.dot_general(
         cotangent_head, value_head, contract_last, preferred_element_type=jnp.float32
@@ -96,24 +109,38 @@
     dk_ref[...] = lax.dot_general(
         dscore, query_head, contract_first, preferred_element_type=jnp.float32
     ).astype(jnp.bfloat16)
-    dv_ref[...] = lax.dot_general(
-        weights, cotangent_head, contract_first, preferred_element_type=jnp.float32
-    ).astype(jnp.bfloat16)
+
+
+def head_specs(local_rows, total_rows):
+    local_spec = pl.BlockSpec((local_rows, HD), lambda h: (0, h))
+    whole_spec = pl.BlockSpec((total_rows, HD), lambda h: (0, h))
+    mask_spec = pl.BlockSpec((local_rows, total_rows), lambda h: (0, 0))
+    return local_spec, whole_spec, mask_spec
+
+
+def head_values_grad(queries, keys_whole, cotangent, visible, scale_factor):
+    local_rows, width_local = queries.shape
+    total_rows = keys_whole.shape[0]
+    local_spec, whole_spec, mask_spec = head_specs(local_rows, total_rows)
+    return pl.pallas_call(
+        functools.partial(value_block, scale_factor),
+        grid=(width_local // HD,),
+        in_specs=[local_spec, whole_spec, local_spec, mask_spec],
+        out_specs=whole_spec,
+        out_shape=jax.ShapeDtypeStruct((total_rows, width_local), jnp.bfloat16),
+    )(queries, keys_whole, cotangent, visible)
 
 
 def head_attention(queries, keys_whole, values_whole, cotangent, visible, scale_factor):
     local_rows, width_local = queries.shape
     total_rows = keys_whole.shape[0]
-    local_spec = pl.BlockSpec((local_rows, HD), lambda h: (0, h))
-    whole_spec = pl.BlockSpec((total_rows, HD), lambda h: (0, h))
-    mask_spec = pl.BlockSpec((local_rows, total_rows), lambda h: (0, 0))
+    local_spec, whole_spec, mask_spec = head_specs(local_rows, total_rows)
     return pl.pallas_call(
         functools.partial(attention_block, scale_factor),
         grid=(width_local // HD,),
         in_specs=[local_spec, whole_spec, whole_spec, local_spec, mask_spec],
-        out_specs=[whole_spec, whole_spec, local_spec, local_spec],
+        out_specs=[whole_spec, local_spec, local_spec],
         out_shape=[
-            jax.ShapeDtypeStruct((total_rows, width_local), jnp.bfloat16),
             jax.ShapeDtypeStruct((total_rows, width_local), jnp.bfloat16),
             jax.ShapeDtypeStruct((local_rows, width_local), jnp.float32),
             jax.ShapeDtypeStruct((local_rows, width_local), jnp.bfloat16),
@@ -172,8 +199,10 @@
     key_pos = jnp.arange(total_rows, dtype=jnp.int32)
     query_seg = lax.dynamic_slice_in_dim(segments, position, local_rows, 0)
     visible = (key_pos[None, :] <= query_pos[:, None]) & (segments[None, :] == query_seg[:, None])
-    key_part, value_part, attended_all, queries_grad = head_attention(
-        queries, keys_whole, values_whole, cotangent, visible.astype(jnp.float32), scale_factor
+    mask = visible.astype(jnp.float32)
+    value_part = head_values_grad(queries, keys_whole, cotangent, mask, scale_factor)
+    key_part, attended_all, queries_grad = head_attention(
+        queries, keys_whole, values_whole, cotangent, mask, scale_factor
     )
     result = (second_wide + attended_all).astype(jnp.bfloat16)
     value_grad = lax.dynamic_slice_in_dim(value_part, position, local_rows, 0).astype(jnp.float32)

time: 177 us -> 164 us (0.927)
  waiting for transfers between devices: 50.2 us -> 24.7 us
  Pallas kernels: 11.4 us -> 19.3 us
  local copies, waits for them, and re-layouts: 12.3 us -> 18.4 us
  starting transfers between devices: 56.8 us -> 53 us
  other arithmetic: 10.8 us -> 13 us
    ppermute x16, waiting for transfers between devices: 26 us -> 1.59 us  [passed_along(): lax.ppermute(value, axis, [(source, source + steps) for source in range(l...]
    pallas_call x0 -> x1, Pallas kernels: none -> 8.76 us  [head_values_grad(): pl.pallas_call(functools.partial(value_block, scale_factor), grid=(width_...]
    ppermute x16, starting transfers between devices: 39 us -> 36.4 us  [passed_along(): lax.ppermute(value, axis, [(source, source + steps) for source in range(l...]
    rev x1, local copies, waits for them, and re-layouts: 0.24 us -> 2.62 us  [shards(): conv_two = depthwise(padded_two, kernel[::-1])]
    dynamic_update_slice x6, local copies, waits for them, and re-layouts: 2.99 us -> 4.9 us  [shards(): lax.dynamic_update_slice_in_dim(values_whole, arrived, block_start, 0)]
    ppermute x6, waiting for transfers between devices: 16.5 us -> 14.7 us  [butterfly_total(): lax.ppermute(rounded, axis, pairs).astype(value.dtype)]
  transfers between devices with their start and end apart: 28 -> 28, of which waited for: 13 -> 8; matrix products, arithmetic and copies ran while one was open for 21% -> 29% of each run, Pallas kernels for 0% -> 12%
where the time goes in v5:
time: 164 us; the launch traced here: 163 us
  starting transfers between devices  53 us (32%)
  waiting for transfers between devices  24.7 us (15%)
  matrix products  19.7 us (12%)
  Pallas kernels  19.3 us (12%)
  local copies, waits for them, and re-layouts  18.4 us (11%)
  between operations  14.8 us (9%)
  other arithmetic  13 us (8%)
    ppermute x16, starting transfers between devices, passed_along(): lax.ppermute(value, axis, [(source, source + steps) for source in range(l...  36.4 us
    conv_general_dilated x6, matrix products, depthwise(): lax.conv_general_dilated(padded[None], tap_rows[:, None, :], (1,), 'VALID...  19.7 us
    ppermute x6, waiting for transfers between devices, butterfly_total(): lax.ppermute(rounded, axis, pairs).astype(value.dtype)  14.7 us
    pallas_call x1, Pallas kernels, head_attention(): pl.pallas_call(functools.partial(attention_block, scale_factor), grid=(wi...  10.5 us
    pallas_call x1, Pallas kernels, head_values_grad(): pl.pallas_call(functools.partial(value_block, scale_factor), grid=(width_...  8.76 us
    ppermute x6, starting transfers between devices, butterfly_total(): lax.ppermute(rounded, axis, pairs).astype(value.dtype)  8.38 us
    ppermute x4, starting transfers between devices, butterfly_total(): value = value + lax.ppermute(value, axis, pairs)  8.17 us
    ppermute x4, waiting for transfers between devices, butterfly_total(): value = value + lax.ppermute(value, axis, pairs)  7.78 us
  transfers between devices with their start and end apart: 28, of which 8 were waited for; matrix products, arithmetic and copies ran while one was open for 29% of the time, Pallas kernels for 12%

profile of v5, /device:TPU:0, one launch (start us, length us, event | category | flops | bytes accessed | tf_op | source)
XLA Modules:
  0.0 162.9 jit_solution(6254592169880419154)
XLA Ops:
  9.1 2.4 %collective-permute-start = (bf16[6,1024]{1,0:T(8,128)(2,1)S(1)}, bf16[6,1024]{1,0:T(8,128)(2,1)S(1)}, u32[]{:S(2)}, u32[]{:S(2)}) collective-permute-start(bf16[6,1024]{1,0:T(8,128)(2,1)S(1)} %slice.52), channel_id=1, source_target_pairs={{0,4},{4,8},{8,12},{12,16},{16,20},{20,24},{24,28},{1,5},{5,9},{9,... | collective-permute-start | bytes 36872 | tf_op jit(solution)/shard_map/ppermute | solution.py:30
  11.4 2.8 %rev.12 = f32[7,1024]{1,0:T(8,128)S(1)} reverse(f32[7,1024]{1,0:T(8,128)} %param.15), dimensions={0} | reverse | bytes 57344 | tf_op jit(solution)/shard_map/rev | solution.py:175
  15.9 4.7 %collective-permute-start.1 = (bf16[127,1024]{1,0:T(8,128)(2,1)S(1)}, bf16[127,1024]{1,0:T(8,128)(2,1)S(1)}, u32[]{:S(2)}, u32[]{:S(2)}) collective-permute-start(bf16[127,1024]{1,0:T(8,128)(2,1)S(1)} %slice.50), channel_id=1, source_target_pairs={{0,4},{4,8},{8,12},{12,16},{16,20},{20,24},{24,28},{1,5},{5,9},{9,... | collective-permute-start | bytes 780296 | tf_op jit(solution)/shard_map/ppermute | solution.py:30
  20.6 2.6 %rev.13 = f32[128,1024]{1,0:T(8,128)} reverse(f32[128,1024]{1,0:T(8,128)S(1)} %copy-done.16), dimensions={0} | reverse | bytes 1048576 | tf_op jit(solution)/shard_map/rev | solution.py:181
  24.3 5.8 %fusion.8 = f32[1,128,1024]{2,0,1:T(1,128)S(1)} fusion(f32[1,255,1024]{2,1,0:T(8,128)S(1)} %maximum_bitcast_fusion, f32[128,1,1024]{2,0,1:T(8,128)S(1)} %bitcast.50), kind=kOutput, calls=%fused_computation.35 | convolution fusion | flops 201326592 | bytes 2093056 | tf_op jit(solution)/shard_map/conv_general_dilated | solution.py:34
  31.9 2.0 %collective-permute-done.2 = f32[128]{0:T(128)S(1)} collective-permute-done((f32[128]{0:T(128)S(1)}, f32[128]{0:T(128)S(1)}, u32[]{:S(2)}, u32[]{:S(2)}) %collective-permute-start.2) | collective-permute-done | bytes 544 | tf_op jit(solution)/shard_map/ppermute | solution.py:59
  33.9 2.6 %collective-permute-start.3 = (f32[128]{0:T(128)S(1)}, f32[128]{0:T(128)S(1)}, u32[]{:S(2)}, u32[]{:S(2)}) collective-permute-start(f32[128]{0:T(128)S(1)} %add.146), channel_id=1, source_target_pairs={{0,2},{1,3},{2,0},{3,1},{4,6},{5,7},{6,4},{7,5},{8,10},{9,11},{10,... | collective-permute-start | bytes 1544 | tf_op jit(solution)/shard_map/ppermute | solution.py:59
  39.4 3.0 %collective-permute-start.4 = (bf16[128,1024]{1,0:T(8,128)(2,1)}, bf16[128,1024]{1,0:T(8,128)(2,1)}, u32[]{:S(2)}, u32[]{:S(2)}) collective-permute-start(bf16[128,1024]{1,0:T(8,128)(2,1)} %get-tuple-element.28), channel_id=1, source_target_pairs={{0,4},{4,8},{8,12},{12,16},{16,20},{20,24},{24,28},{1,5},{5,9},{9,... | collective-permute-start | bytes 786440 | tf_op jit(solution)/shard_map/ppermute | solution.py:30
  42.4 6.1 %collective-permute-start.5 = (bf16[128,1024]{1,0:T(8,128)(2,1)}, bf16[128,1024]{1,0:T(8,128)(2,1)}, u32[]{:S(2)}, u32[]{:S(2)}) collective-permute-start(bf16[128,1024]{1,0:T(8,128)(2,1)} %get-tuple-element.28), channel_id=1, source_target_pairs={{0,8},{4,12},{8,16},{12,20},{16,24},{20,28},{1,9},{5,13},{9,17},{1... | collective-permute-start | bytes 786440 | tf_op jit(solution)/shard_map/ppermute | solution.py:30
  49.5 4.5 %collective-permute-start.6 = (bf16[128,1024]{1,0:T(8,128)(2,1)}, bf16[128,1024]{1,0:T(8,128)(2,1)}, u32[]{:S(2)}, u32[]{:S(2)}) collective-permute-start(bf16[128,1024]{1,0:T(8,128)(2,1)} %get-tuple-element.28), channel_id=1, source_target_pairs={{0,12},{4,16},{8,20},{12,24},{16,28},{1,13},{5,17},{9,21},{13,25},... | collective-permute-start | bytes 786440 | tf_op jit(solution)/shard_map/ppermute | solution.py:30
  54.0 2.0 %collective-permute-start.7 = (bf16[128,1024]{1,0:T(8,128)(2,1)}, bf16[128,1024]{1,0:T(8,128)(2,1)}, u32[]{:S(2)}, u32[]{:S(2)}) collective-permute-start(bf16[128,1024]{1,0:T(8,128)(2,1)} %get-tuple-element.28), channel_id=1, source_target_pairs={{0,16},{4,20},{8,24},{12,28},{1,17},{5,21},{9,25},{13,29},{2,18},{... | collective-permute-start | bytes 786440 | tf_op jit(solution)/shard_map/ppermute | solution.py:30
  56.0 2.0 %collective-permute-start.8 = (bf16[128,1024]{1,0:T(8,128)(2,1)}, bf16[128,1024]{1,0:T(8,128)(2,1)}, u32[]{:S(2)}, u32[]{:S(2)}) collective-permute-start(bf16[128,1024]{1,0:T(8,128)(2,1)} %get-tuple-element.28), channel_id=1, source_target_pairs={{0,20},{4,24},{8,28},{1,21},{5,25},{9,29},{2,22},{6,26},{10,30},{3... | collective-permute-start | bytes 786440 | tf_op jit(solution)/shard_map/ppermute | solution.py:30
  58.0 8.8 %shard_map.204 = bf16[1024,1024]{1,0:T(8,128)(2,1)} custom-call(bf16[128,1024]{1,0:T(8,128)(2,1)} %q_ref.3, bf16[1024,1024]{1,0:T(8,128)(2,1)} %all-gather.2.cloned.1.call-done.k_ref, bf16[128,1024]{1,0:T(8,128)(2,1)} %cot_ref.3, f32[128,1024]{1,0:T(8,128)} %fusion.33.vis_ref), custom_call_target="tpu_custom_call" | custom-call | tf_op jit(solution)/shard_map/pallas_call | solution.py:125
  66.8 2.4 %constant_dynamic-slice_fusion.5 = (bf16[128,1024]{1,0:T(8,128)(2,1)}, bf16[128,1024]{1,0:T(8,128)(2,1)S(1)}, bf16[128,1024]{1,0:T(8,128)(2,1)}, bf16[128,1024]{...) fusion(bf16[1024,1024]{1,0:T(8,128)(2,1)} %shard_map.204, s32[]{:T(128)S(6)} %select_n.70, ...), kind=kLoop, calls=%fused_computation.90 | loop fusion | bytes 3145752 | tf_op jit(solution)/shard_map/dynamic_slice | solution.py:211
  86.2 10.5 %shard_map.203 = (bf16[1024,1024]{1,0:T(8,128)(2,1)}, f32[128,1024]{1,0:T(8,128)}, bf16[128,1024]{1,0:T(8,128)(2,1)}) custom-call(bf16[128,1024]{1,0:T(8,128)(2,1)} %q_ref.3, bf16[1024,1024]{1,0:T(8,128)(2,1)} %all-gather.2.cloned.1.call-done.k_ref, bf16[1024,1024]{1,0:T(8,128)(2,1)} %copy-done, bf16[128,1024]{1,0:T(8,128)(2,1)} %cot_ref.3, ...), custom_call_target="tpu_custom_call" | custom-call | tf_op jit(solution)/shard_map/pallas_call | solution.py:138
  96.8 1.8 %convert_add_fusion.4 = f32[128,1024]{1,0:T(8,128)S(1)} fusion(bf16[128,1024]{1,0:T(8,128)(2,1)} %copy-done.20, bf16[128,1024]{1,0:T(8,128)(2,1)} %collective-permute-done.14, bf16[128,1024]{1,0:T(8,128)(2,1)} %collective-permute-done.13, bf16[128,1024]{1,0:T(8,128)(2,1)} %collective-permute-done.12, bf16[128,1024]{1,0:T(8,128)(2,1)} %collective-permute-done.11, ...), kind=kLoop, calls=%fused_computation.66 | loop fusion | flops 1703936 | bytes 2359300 | tf_op jit(solution)/shard_map/add | solution.py:212
  100.3 2.1 %collective-permute-done.16 = f32[128]{0:T(128)S(1)} collective-permute-done((f32[128]{0:T(128)S(1)}, f32[128]{0:T(128)S(1)}, u32[]{:S(2)}, u32[]{:S(2)}) %collective-permute-start.16) | collective-permute-done | bytes 544 | tf_op jit(solution)/shard_map/ppermute | solution.py:59
  102.4 2.4 %collective-permute-start.17 = (f32[128]{0:T(128)S(1)}, f32[128]{0:T(128)S(1)}, u32[]{:S(2)}, u32[]{:S(2)}) collective-permute-start(f32[128]{0:T(128)S(1)} %add.173), channel_id=1, source_target_pairs={{0,2},{1,3},{2,0},{3,1},{4,6},{5,7},{6,4},{7,5},{8,10},{9,11},{10,... | collective-permute-start | bytes 1544 | tf_op jit(solution)/shard_map/ppermute | solution.py:59
  104.8 2.0 %collective-permute-done.17 = f32[128]{0:T(128)S(1)} collective-permute-done((f32[128]{0:T(128)S(1)}, f32[128]{0:T(128)S(1)}, u32[]{:S(2)}, u32[]{:S(2)}) %collective-permute-start.17) | collective-permute-done | bytes 544 | tf_op jit(solution)/shard_map/ppermute | solution.py:59
  110.1 5.8 %fusion.6 = bf16[1,128,1024]{2,0,1:T(2,128)(2,1)S(1)} fusion(f32[1,255,1024]{2,1,0:T(8,128)S(1)} %copy-done.8, f32[128,1,1024]{2,0,1:T(8,128)S(1)} %bitcast.46), kind=kOutput, calls=%fused_computation.33 | convolution fusion | flops 201326592 | bytes 1830912 | tf_op jit(solution)/shard_map/conv_general_dilated | solution.py:34
  118.4 5.8 %fusion = f32[1,128,1024]{2,0,1:T(1,128)S(1)} fusion(f32[1,255,1024]{2,1,0:T(8,128)S(1)} %maximum_bitcast_fusion.1, f32[128,1,1024]{2,0,1:T(8,128)S(1)} %bitcast.49), kind=kOutput, calls=%fused_computation.9 | convolution fusion | flops 201326592 | bytes 2093056 | tf_op jit(solution)/shard_map/conv_general_dilated | solution.py:34
  130.6 3.7 %collective-permute-start.24 = (bf16[129,1024]{1,0:T(8,128)(2,1)S(1)}, bf16[129,1024]{1,0:T(8,128)(2,1)S(1)}, u32[]{:S(2)}, u32[]{:S(2)}) collective-permute-start(bf16[129,1024]{1,0:T(8,128)(2,1)S(1)} %add_convert_fusion.1), channel_id=1, source_target_pairs={{0,8},{4,12},{8,0},{12,4},{16,24},{20,28},{24,16},{28,20},{1,9},{5... | collective-permute-start | bytes 792584 | tf_op jit(solution)/shard_map/ppermute | solution.py:62
  136.1 6.8 %collective-permute-done.21 = bf16[7,1024]{1,0:T(8,128)(2,1)S(1)} collective-permute-done((bf16[7,1024]{1,0:T(8,128)(2,1)S(1)}, bf16[7,1024]{1,0:T(8,128)(2,1)S(1)}, u32[]{:S(2)}, u32[]{:S(2)}) %collective-permute-start.21) | collective-permute-done | bytes 14368 | tf_op jit(solution)/shard_map/ppermute | solution.py:62
  147.5 7.1 %collective-permute-done.25 = bf16[129,1024]{1,0:T(8,128)(2,1)S(1)} collective-permute-done((bf16[129,1024]{1,0:T(8,128)(2,1)S(1)}, bf16[129,1024]{1,0:T(8,128)(2,1)S(1)}, u32[]{:S(2)}, u32[]{:S(2)}) %collective-permute-start.25) | collective-permute-done | bytes 264224 | tf_op jit(solution)/shard_map/ppermute | solution.py:62
  (152 shorter events, 48.8 us)
Async XLA Ops:
  7.2 50.8 %all-gather.2.cloned.1.call-start = ((), (), s32[]{:S(2)}) async-start(), calls=%async_computation.1 | async-start | bytes 2359296 | tf_op jit(solution)/shard_map/all_gather | solution.py:189
  7.9 148.2 %reduce-scatter.2.cloned.1.call-start = ((), (), s32[]{:S(2)}) async-start(), calls=%async_computation.2 | async-start | bytes 2359296 | tf_op jit(solution)/shard_map/reduce_scatter | solution.py:214
  9.1 5.2 %collective-permute-start = (bf16[6,1024]{1,0:T(8,128)(2,1)S(1)}, bf16[6,1024]{1,0:T(8,128)(2,1)S(1)}, u32[]{:S(2)}, u32[]{:S(2)}) collective-permute-start(bf16[6,1024]{1,0:T(8,128)(2,1)S(1)} %slice.52), channel_id=1, source_target_pairs={{0,4},{4,8},{8,12},{12,16},{16,20},{20,24},{24,28},{1,5},{5,9},{9,... | collective-permute-start | bytes 36872 | tf_op jit(solution)/shard_map/ppermute | solution.py:30
  15.9 7.3 %collective-permute-start.1 = (bf16[127,1024]{1,0:T(8,128)(2,1)S(1)}, bf16[127,1024]{1,0:T(8,128)(2,1)S(1)}, u32[]{:S(2)}, u32[]{:S(2)}) collective-permute-start(bf16[127,1024]{1,0:T(8,128)(2,1)S(1)} %slice.50), channel_id=1, source_target_pairs={{0,4},{4,8},{8,12},{12,16},{16,20},{20,24},{24,28},{1,5},{5,9},{9,... | collective-permute-start | bytes 780296 | tf_op jit(solution)/shard_map/ppermute | solution.py:30
  39.4 29.7 %collective-permute-start.4 = (bf16[128,1024]{1,0:T(8,128)(2,1)}, bf16[128,1024]{1,0:T(8,128)(2,1)}, u32[]{:S(2)}, u32[]{:S(2)}) collective-permute-start(bf16[128,1024]{1,0:T(8,128)(2,1)} %get-tuple-element.28), channel_id=1, source_target_pairs={{0,4},{4,8},{8,12},{12,16},{16,20},{20,24},{24,28},{1,5},{5,9},{9,... | collective-permute-start | bytes 786440 | tf_op jit(solution)/shard_map/ppermute | solution.py:30
  42.4 28.0 %collective-permute-start.5 = (bf16[128,1024]{1,0:T(8,128)(2,1)}, bf16[128,1024]{1,0:T(8,128)(2,1)}, u32[]{:S(2)}, u32[]{:S(2)}) collective-permute-start(bf16[128,1024]{1,0:T(8,128)(2,1)} %get-tuple-element.28), channel_id=1, source_target_pairs={{0,8},{4,12},{8,16},{12,20},{16,24},{20,28},{1,9},{5,13},{9,17},{1... | collective-permute-start | bytes 786440 | tf_op jit(solution)/shard_map/ppermute | solution.py:30
  49.5 24.2 %collective-permute-start.6 = (bf16[128,1024]{1,0:T(8,128)(2,1)}, bf16[128,1024]{1,0:T(8,128)(2,1)}, u32[]{:S(2)}, u32[]{:S(2)}) collective-permute-start(bf16[128,1024]{1,0:T(8,128)(2,1)} %get-tuple-element.28), channel_id=1, source_target_pairs={{0,12},{4,16},{8,20},{12,24},{16,28},{1,13},{5,17},{9,21},{13,25},... | collective-permute-start | bytes 786440 | tf_op jit(solution)/shard_map/ppermute | solution.py:30
  54.0 22.0 %collective-permute-start.7 = (bf16[128,1024]{1,0:T(8,128)(2,1)}, bf16[128,1024]{1,0:T(8,128)(2,1)}, u32[]{:S(2)}, u32[]{:S(2)}) collective-permute-start(bf16[128,1024]{1,0:T(8,128)(2,1)} %get-tuple-element.28), channel_id=1, source_target_pairs={{0,16},{4,20},{8,24},{12,28},{1,17},{5,21},{9,25},{13,29},{2,18},{... | collective-permute-start | bytes 786440 | tf_op jit(solution)/shard_map/ppermute | solution.py:30
  56.0 21.3 %collective-permute-start.8 = (bf16[128,1024]{1,0:T(8,128)(2,1)}, bf16[128,1024]{1,0:T(8,128)(2,1)}, u32[]{:S(2)}, u32[]{:S(2)}) collective-permute-start(bf16[128,1024]{1,0:T(8,128)(2,1)} %get-tuple-element.28), channel_id=1, source_target_pairs={{0,20},{4,24},{8,28},{1,21},{5,25},{9,29},{2,22},{6,26},{10,30},{3... | collective-permute-start | bytes 786440 | tf_op jit(solution)/shard_map/ppermute | solution.py:30
  69.2 9.5 %collective-permute-start.9 = (bf16[128,1024]{1,0:T(8,128)(2,1)}, bf16[128,1024]{1,0:T(8,128)(2,1)S(1)}, u32[]{:S(2)}, u32[]{:S(2)}) collective-permute-start(bf16[128,1024]{1,0:T(8,128)(2,1)} %get-tuple-element.28), channel_id=1, source_target_pairs={{0,24},{4,28},{1,25},{5,29},{2,26},{6,30},{3,27},{7,31}} | collective-permute-start | bytes 786440 | tf_op jit(solution)/shard_map/ppermute | solution.py:30
  70.5 11.0 %collective-permute-start.15 = (bf16[128,1024]{1,0:T(8,128)(2,1)S(1)}, bf16[128,1024]{1,0:T(8,128)(2,1)S(1)}, u32[]{:S(2)}, u32[]{:S(2)}) collective-permute-start(bf16[128,1024]{1,0:T(8,128)(2,1)S(1)} %get-tuple-element.34), channel_id=1, source_target_pairs={{24,0},{28,4},{25,1},{29,5},{26,2},{30,6},{27,3},{31,7}} | collective-permute-start | bytes 786440 | tf_op jit(solution)/shard_map/ppermute | solution.py:30
  74.7 22.0 %collective-permute-start.14 = (bf16[128,1024]{1,0:T(8,128)(2,1)}, bf16[128,1024]{1,0:T(8,128)(2,1)}, u32[]{:S(2)}, u32[]{:S(2)}) collective-permute-start(bf16[128,1024]{1,0:T(8,128)(2,1)} %get-tuple-element.35), channel_id=1, source_target_pairs={{20,0},{24,4},{28,8},{21,1},{25,5},{29,9},{22,2},{26,6},{30,10},{2... | collective-permute-start | bytes 786440 | tf_op jit(solution)/shard_map/ppermute | solution.py:30
  76.0 20.7 %collective-permute-start.13 = (bf16[128,1024]{1,0:T(8,128)(2,1)}, bf16[128,1024]{1,0:T(8,128)(2,1)}, u32[]{:S(2)}, u32[]{:S(2)}) collective-permute-start(bf16[128,1024]{1,0:T(8,128)(2,1)} %get-tuple-element.36), channel_id=1, source_target_pairs={{16,0},{20,4},{24,8},{28,12},{17,1},{21,5},{25,9},{29,13},{18,2},{... | collective-permute-start | bytes 786440 | tf_op jit(solution)/shard_map/ppermute | solution.py:30
  77.3 19.4 %collective-permute-start.12 = (bf16[128,1024]{1,0:T(8,128)(2,1)}, bf16[128,1024]{1,0:T(8,128)(2,1)}, u32[]{:S(2)}, u32[]{:S(2)}) collective-permute-start(bf16[128,1024]{1,0:T(8,128)(2,1)} %get-tuple-element.37), channel_id=1, source_target_pairs={{12,0},{16,4},{20,8},{24,12},{28,16},{13,1},{17,5},{21,9},{25,13},... | collective-permute-start | bytes 786440 | tf_op jit(solution)/shard_map/ppermute | solution.py:30
  78.7 18.1 %collective-permute-start.11 = (bf16[128,1024]{1,0:T(8,128)(2,1)}, bf16[128,1024]{1,0:T(8,128)(2,1)}, u32[]{:S(2)}, u32[]{:S(2)}) collective-permute-start(bf16[128,1024]{1,0:T(8,128)(2,1)} %get-tuple-element.38), channel_id=1, source_target_pairs={{8,0},{12,4},{16,8},{20,12},{24,16},{28,20},{9,1},{13,5},{17,9},{2... | collective-permute-start | bytes 786440 | tf_op jit(solution)/shard_map/ppermute | solution.py:30
  81.5 15.3 %collective-permute-start.10 = (bf16[128,1024]{1,0:T(8,128)(2,1)}, bf16[128,1024]{1,0:T(8,128)(2,1)}, u32[]{:S(2)}, u32[]{:S(2)}) collective-permute-start(bf16[128,1024]{1,0:T(8,128)(2,1)} %get-tuple-element.33), channel_id=1, source_target_pairs={{4,0},{8,4},{12,8},{16,12},{20,16},{24,20},{28,24},{5,1},{9,5},{13... | collective-permute-start | bytes 786440 | tf_op jit(solution)/shard_map/ppermute | solution.py:30
  102.4 4.4 %collective-permute-start.17 = (f32[128]{0:T(128)S(1)}, f32[128]{0:T(128)S(1)}, u32[]{:S(2)}, u32[]{:S(2)}) collective-permute-start(f32[128]{0:T(128)S(1)} %add.173), channel_id=1, source_target_pairs={{0,2},{1,3},{2,0},{3,1},{4,6},{5,7},{6,4},{7,5},{8,10},{9,11},{10,... | collective-permute-start | bytes 1544 | tf_op jit(solution)/shard_map/ppermute | solution.py:59
  108.8 9.4 %collective-permute-start.18 = (bf16[127,1024]{1,0:T(8,128)(2,1)}, bf16[127,1024]{1,0:T(8,128)(2,1)S(1)}, u32[]{:S(2)}, u32[]{:S(2)}) collective-permute-start(bf16[127,1024]{1,0:T(8,128)(2,1)} %slice.49), channel_id=1, source_target_pairs={{4,0},{8,4},{12,8},{16,12},{20,16},{24,20},{28,24},{5,1},{9,5},{13... | collective-permute-start | bytes 780296 | tf_op jit(solution)/shard_map/ppermute | solution.py:30
  117.1 12.6 %collective-permute-start.23 = (bf16[129,1024]{1,0:T(8,128)(2,1)}, bf16[129,1024]{1,0:T(8,128)(2,1)}, u32[]{:S(2)}, u32[]{:S(2)}) collective-permute-start(bf16[129,1024]{1,0:T(8,128)(2,1)} %pad_maximum_fusion), channel_id=1, source_target_pairs={{0,4},{4,0},{8,12},{12,8},{16,20},{20,16},{24,28},{28,24},{1,5},{5... | collective-permute-start | bytes 792584 | tf_op jit(solution)/shard_map/ppermute | solution.py:62
  125.4 8.9 %collective-permute-start.19 = (bf16[6,1024]{1,0:T(8,128)(2,1)S(1)}, bf16[6,1024]{1,0:T(8,128)(2,1)S(1)}, u32[]{:S(2)}, u32[]{:S(2)}) collective-permute-start(bf16[6,1024]{1,0:T(8,128)(2,1)S(1)} %slice.51), channel_id=1, source_target_pairs={{4,0},{8,4},{12,8},{16,12},{20,16},{24,20},{28,24},{5,1},{9,5},{13... | collective-permute-start | bytes 36872 | tf_op jit(solution)/shard_map/ppermute | solution.py:30
  128.3 7.0 %collective-permute-start.20 = (bf16[7,1024]{1,0:T(8,128)(2,1)S(1)}, bf16[7,1024]{1,0:T(8,128)(2,1)S(1)}, u32[]{:S(2)}, u32[]{:S(2)}) collective-permute-start(bf16[7,1024]{1,0:T(8,128)(2,1)S(1)} %rev.14), channel_id=1, source_target_pairs={{0,4},{4,0},{8,12},{12,8},{16,20},{20,16},{24,28},{28,24},{1,5},{5... | collective-permute-start | bytes 43016 | tf_op jit(solution)/shard_map/ppermute | solution.py:62
  130.6 14.0 %collective-permute-start.24 = (bf16[129,1024]{1,0:T(8,128)(2,1)S(1)}, bf16[129,1024]{1,0:T(8,128)(2,1)S(1)}, u32[]{:S(2)}, u32[]{:S(2)}) collective-permute-start(bf16[129,1024]{1,0:T(8,128)(2,1)S(1)} %add_convert_fusion.1), channel_id=1, source_target_pairs={{0,8},{4,12},{8,0},{12,4},{16,24},{20,28},{24,16},{28,20},{1,9},{5... | collective-permute-start | bytes 792584 | tf_op jit(solution)/shard_map/ppermute | solution.py:62
  135.3 7.6 %collective-permute-start.21 = (bf16[7,1024]{1,0:T(8,128)(2,1)S(1)}, bf16[7,1024]{1,0:T(8,128)(2,1)S(1)}, u32[]{:S(2)}, u32[]{:S(2)}) collective-permute-start(bf16[7,1024]{1,0:T(8,128)(2,1)S(1)} %add_convert_fusion.3), channel_id=1, source_target_pairs={{0,8},{4,12},{8,0},{12,4},{16,24},{20,28},{24,16},{28,20},{1,9},{5... | collective-permute-start | bytes 43016 | tf_op jit(solution)/shard_map/ppermute | solution.py:62
  144.7 9.9 %collective-permute-start.25 = (bf16[129,1024]{1,0:T(8,128)(2,1)S(1)}, bf16[129,1024]{1,0:T(8,128)(2,1)S(1)}, u32[]{:S(2)}, u32[]{:S(2)}) collective-permute-start(bf16[129,1024]{1,0:T(8,128)(2,1)S(1)} %add_convert_fusion), channel_id=1, source_target_pairs={{0,16},{4,20},{8,24},{12,28},{16,0},{20,4},{24,8},{28,12},{1,17},{... | collective-permute-start | bytes 792584 | tf_op jit(solution)/shard_map/ppermute | solution.py:62
  (29 other events, 127.7 us)
Sparse Core Ops, SparseCore 0:
  9.9 31.7 all-gather.1
  104.9 46.4 reduce-scatter.1

commit v6 on v5

--- a/solution.py
+++ b/solution.py
@@ -188,28 +188,22 @@
     ctx_index = lax.axis_index("ctx")
     keys_whole = lax.all_gather(matchers, "ctx", axis=0, tiled=True)
     reach = min(ctx_count - 1, (3 * total_rows // 4 - 1 + local_rows - 1) // local_rows)
-    values_whole = lax.dynamic_update_slice_in_dim(
-        jnp.zeros((total_rows, width_local), jnp.bfloat16), normed, position, 0
-    )
-    for distance in range(1, reach + 1):
-        arrived = passed_along(normed, "ctx", distance)
-        block_start = ((ctx_index - distance) % ctx_count) * local_rows
-        values_whole = lax.dynamic_update_slice_in_dim(values_whole, arrived, block_start, 0)
     query_pos = position + jnp.arange(local_rows, dtype=jnp.int32)
     key_pos = jnp.arange(total_rows, dtype=jnp.int32)
     query_seg = lax.dynamic_slice_in_dim(segments, position, local_rows, 0)
     visible = (key_pos[None, :] <= query_pos[:, None]) & (segments[None, :] == query_seg[:, None])
     mask = visible.astype(jnp.float32)
     value_part = head_values_grad(queries, keys_whole, cotangent, mask, scale_factor)
-    key_part, attended_all, queries_grad = head_attention(
-        queries, keys_whole, values_whole, cotangent, mask, scale_factor
-    )
-    result = (second_wide + attended_all).astype(jnp.bfloat16)
     value_grad = lax.dynamic_slice_in_dim(value_part, position, local_rows, 0).astype(jnp.float32)
     for distance in range(1, reach + 1):
         block_start = ((ctx_index - distance) % ctx_count) * local_rows
         leaving = lax.dynamic_slice_in_dim(value_part, block_start, local_rows, 0)
         value_grad = value_grad + passed_along(leaving, "ctx", -distance).astype(jnp.float32)
+    values_whole = lax.all_gather(normed, "ctx", axis=0, tiled=True)
+    key_part, attended_all, queries_grad = head_attention(
+        queries, keys_whole, values_whole, cotangent, mask, scale_factor
+    )
+    result = (second_wide + attended_all).astype(jnp.bfloat16)
     key_part, value_grad = lax.optimization_barrier((key_part, value_grad))
     matchers_grad = lax.psum_scatter(
         key_part,

time: 164 us -> 163 us (level)
  waiting for transfers between devices: 24.7 us -> 45.4 us
  starting transfers between devices: 53 us -> 39.5 us
  local copies, waits for them, and re-layouts: 18.4 us -> 7.74 us
    ppermute x16 -> x10, starting transfers between devices: 36.4 us -> 17.4 us  [passed_along(): lax.ppermute(value, axis, [(source, source + steps) for source in range(l...]
    ppermute x16 -> x10, waiting for transfers between devices: 1.59 us -> 17.9 us  [passed_along(): lax.ppermute(value, axis, [(source, source + steps) for source in range(l...]
    ppermute x6, starting transfers between devices: 8.38 us -> 13.8 us  [butterfly_total(): lax.ppermute(rounded, axis, pairs).astype(value.dtype)]
    dynamic_update_slice x6 -> x0, local copies, waits for them, and re-layouts: 4.9 us -> none  [shards(): lax.dynamic_update_slice_in_dim(values_whole, arrived, block_start, 0)]
    all_gather x1, waiting for transfers between devices: 0.01 us -> 3.87 us  [shards(): keys_whole = lax.all_gather(matchers, 'ctx', axis=0, tiled=True)]
    rev x1, local copies, waits for them, and re-layouts: 2.62 us -> 0.24 us  [shards(): conv_two = depthwise(padded_two, kernel[::-1])]
    unnamed x52 -> x36, local copies, waits for them, and re-layouts: 2.76 us -> 0.47 us
    all_gather x0 -> x1, waiting for transfers between devices: none -> 2.14 us  [shards(): values_whole = lax.all_gather(normed, 'ctx', axis=0, tiled=True)]
  transfers between devices with their start and end apart: 28 -> 23, of which waited for: 8 -> 12; matrix products, arithmetic and copies ran while one was open for 29% -> 26% of each run, Pallas kernels for 12% -> 5%
where the time goes in v6:
time: 163 us; the launch traced here: 162 us
  waiting for transfers between devices  45.4 us (28%)
  starting transfers between devices  39.5 us (24%)
  matrix products  20.8 us (13%)
  Pallas kernels  19.4 us (12%)
  other arithmetic  14.5 us (9%)
  between operations  14.4 us (9%)
  local copies, waits for them, and re-layouts  7.74 us (5%)
    conv_general_dilated x6, matrix products, depthwise(): lax.conv_general_dilated(padded[None], tap_rows[:, None, :], (1,), 'VALID...  20.8 us
    ppermute x10, waiting for transfers between devices, passed_along(): lax.ppermute(value, axis, [(source, source + steps) for source in range(l...  17.9 us
    ppermute x10, starting transfers between devices, passed_along(): lax.ppermute(value, axis, [(source, source + steps) for source in range(l...  17.4 us
    ppermute x6, starting transfers between devices, butterfly_total(): lax.ppermute(rounded, axis, pairs).astype(value.dtype)  13.8 us
    ppermute x6, waiting for transfers between devices, butterfly_total(): lax.ppermute(rounded, axis, pairs).astype(value.dtype)  12.9 us
    pallas_call x1, Pallas kernels, head_attention(): pl.pallas_call(functools.partial(attention_block, scale_factor), grid=(wi...  10.6 us
    pallas_call x1, Pallas kernels, head_values_grad(): pl.pallas_call(functools.partial(value_block, scale_factor), grid=(width_...  8.8 us
    ppermute x4, starting transfers between devices, butterfly_total(): value = value + lax.ppermute(value, axis, pairs)  8.17 us
  transfers between devices with their start and end apart: 23, of which 12 were waited for; matrix products, arithmetic and copies ran while one was open for 26% of the time, Pallas kernels for 5%

profile of v6, /device:TPU:0, one launch (start us, length us, event | category | flops | bytes accessed | tf_op | source)
XLA Modules:
  0.0 161.8 jit_solution(16064894119438025054)
XLA Ops:
  9.1 2.4 %collective-permute-start = (bf16[6,1024]{1,0:T(8,128)(2,1)S(1)}, bf16[6,1024]{1,0:T(8,128)(2,1)S(1)}, u32[]{:S(2)}, u32[]{:S(2)}) collective-permute-start(bf16[6,1024]{1,0:T(8,128)(2,1)S(1)} %slice.52), channel_id=1, source_target_pairs={{0,4},{4,8},{8,12},{12,16},{16,20},{20,24},{24,28},{1,5},{5,9},{9,... | collective-permute-start | bytes 36872 | tf_op jit(solution)/shard_map/ppermute | solution.py:30
  11.4 2.8 %rev.12 = f32[7,1024]{1,0:T(8,128)S(1)} reverse(f32[7,1024]{1,0:T(8,128)} %param.15), dimensions={0} | reverse | bytes 57344 | tf_op jit(solution)/shard_map/rev | solution.py:175
  15.9 4.5 %collective-permute-start.1 = (bf16[127,1024]{1,0:T(8,128)(2,1)S(1)}, bf16[127,1024]{1,0:T(8,128)(2,1)S(1)}, u32[]{:S(2)}, u32[]{:S(2)}) collective-permute-start(bf16[127,1024]{1,0:T(8,128)(2,1)S(1)} %slice.50), channel_id=1, source_target_pairs={{0,4},{4,8},{8,12},{12,16},{16,20},{20,24},{24,28},{1,5},{5,9},{9,... | collective-permute-start | bytes 780296 | tf_op jit(solution)/shard_map/ppermute | solution.py:30
  21.8 5.8 %fusion.8 = f32[1,128,1024]{2,0,1:T(1,128)S(1)} fusion(f32[1,255,1024]{2,1,0:T(8,128)S(1)} %maximum_bitcast_fusion, f32[128,1,1024]{2,0,1:T(8,128)S(1)} %bitcast.50), kind=kOutput, calls=%fused_computation.35 | convolution fusion | flops 201326592 | bytes 2093056 | tf_op jit(solution)/shard_map/conv_general_dilated | solution.py:34
  29.4 2.0 %collective-permute-done.2 = f32[128]{0:T(128)S(1)} collective-permute-done((f32[128]{0:T(128)S(1)}, f32[128]{0:T(128)S(1)}, u32[]{:S(2)}, u32[]{:S(2)}) %collective-permute-start.2) | collective-permute-done | bytes 544 | tf_op jit(solution)/shard_map/ppermute | solution.py:59
  31.4 2.6 %collective-permute-start.3 = (f32[128]{0:T(128)S(1)}, f32[128]{0:T(128)S(1)}, u32[]{:S(2)}, u32[]{:S(2)}) collective-permute-start(f32[128]{0:T(128)S(1)} %add.133), channel_id=1, source_target_pairs={{0,2},{1,3},{2,0},{3,1},{4,6},{5,7},{6,4},{7,5},{8,10},{9,11},{10,... | collective-permute-start | bytes 1544 | tf_op jit(solution)/shard_map/ppermute | solution.py:59
  37.9 3.9 %all-gather.3.cloned.1.call-done.k_ref = bf16[1024,1024]{1,0:T(8,128)(2,1)} async-done(((bf16[128,1024]{1,0:T(8,128)(2,1)}), bf16[1024,1024]{1,0:T(8,128)(2,1)}) %all-gather.3.cloned.1.call-update) | async-done | bytes 2097168 | tf_op jit(solution)/shard_map/all_gather | solution.py:189
  41.8 8.8 %shard_map.204 = bf16[1024,1024]{1,0:T(8,128)(2,1)} custom-call(bf16[128,1024]{1,0:T(8,128)(2,1)} %q_ref.3, bf16[1024,1024]{1,0:T(8,128)(2,1)} %all-gather.3.cloned.1.call-done.k_ref, bf16[128,1024]{1,0:T(8,128)(2,1)} %cot_ref.3, f32[128,1024]{1,0:T(8,128)} %fusion.33.vis_ref), custom_call_target="tpu_custom_call" | custom-call | tf_op jit(solution)/shard_map/pallas_call | solution.py:125
  58.6 5.4 %collective-permute-done.9 = bf16[128,1024]{1,0:T(8,128)(2,1)S(1)} collective-permute-done((bf16[128,1024]{1,0:T(8,128)(2,1)S(1)}, bf16[128,1024]{1,0:T(8,128)(2,1)S(1)}, u32[]{:S(2)}, u32[]{:S(2)}) %collective-permute-start.9) | collective-permute-done | bytes 262176 | tf_op jit(solution)/shard_map/ppermute | solution.py:30
  65.3 11.2 %collective-permute-done.8 = bf16[128,1024]{1,0:T(8,128)(2,1)S(1)} collective-permute-done((bf16[128,1024]{1,0:T(8,128)(2,1)S(1)}, bf16[128,1024]{1,0:T(8,128)(2,1)S(1)}, u32[]{:S(2)}, u32[]{:S(2)}) %collective-permute-start.8) | collective-permute-done | bytes 262176 | tf_op jit(solution)/shard_map/ppermute | solution.py:30
  78.2 2.1 %all-gather.5.cloned.1.call-done.v_ref = bf16[1024,1024]{1,0:T(8,128)(2,1)} async-done(((bf16[128,1024]{1,0:T(8,128)(2,1)}), bf16[1024,1024]{1,0:T(8,128)(2,1)}) %all-gather.5.cloned.1.call-update) | async-done | bytes 2097168 | tf_op jit(solution)/shard_map/all_gather | solution.py:202
  80.3 10.6 %shard_map.203 = (bf16[1024,1024]{1,0:T(8,128)(2,1)}, f32[128,1024]{1,0:T(8,128)}, bf16[128,1024]{1,0:T(8,128)(2,1)}) custom-call(bf16[128,1024]{1,0:T(8,128)(2,1)} %q_ref.3, bf16[1024,1024]{1,0:T(8,128)(2,1)} %all-gather.3.cloned.1.call-done.k_ref, bf16[1024,1024]{1,0:T(8,128)(2,1)} %all-gather.5.cloned.1.call-done.v_ref, bf16[128,1024]{1,0:T(8,128)(2,1)} %cot_ref.3, ...), custom_call_target="tpu_custom_call" | custom-call | tf_op jit(solution)/shard_map/pallas_call | solution.py:138
  92.6 2.1 %collective-permute-done.10 = f32[128]{0:T(128)S(1)} collective-permute-done((f32[128]{0:T(128)S(1)}, f32[128]{0:T(128)S(1)}, u32[]{:S(2)}, u32[]{:S(2)}) %collective-permute-start.10) | collective-permute-done | bytes 544 | tf_op jit(solution)/shard_map/ppermute | solution.py:59
  94.7 2.4 %collective-permute-start.11 = (f32[128]{0:T(128)S(1)}, f32[128]{0:T(128)S(1)}, u32[]{:S(2)}, u32[]{:S(2)}) collective-permute-start(f32[128]{0:T(128)S(1)} %add.160), channel_id=1, source_target_pairs={{0,2},{1,3},{2,0},{3,1},{4,6},{5,7},{6,4},{7,5},{8,10},{9,11},{10,... | collective-permute-start | bytes 1544 | tf_op jit(solution)/shard_map/ppermute | solution.py:59
  97.1 2.0 %collective-permute-done.11 = f32[128]{0:T(128)S(1)} collective-permute-done((f32[128]{0:T(128)S(1)}, f32[128]{0:T(128)S(1)}, u32[]{:S(2)}, u32[]{:S(2)}) %collective-permute-start.11) | collective-permute-done | bytes 544 | tf_op jit(solution)/shard_map/ppermute | solution.py:59
  99.1 2.3 %fusion.25 = (bf16[128,1024]{1,0:T(8,128)(2,1)}, f32[128,1024]{1,0:T(8,128)S(1)}, bf16[128,1024]{1,0:T(8,128)(2,1)}) fusion(f32[1,128,1024]{2,0,1:T(1,128)S(1)} %fusion.8, f32[128]{0:T(128)S(1)} %fusion.42, bf16[128,1024]{1,0:T(8,128)(2,1)S(1)} %get-tuple-element.28, f32[128,1024]{1,0:T(8,128)S(1)} %convert_add_fusion.4, f32[1024]{0:T(1024)S(1)} %copy-done.13, ...), kind=kLoop, calls=%fused_computation.58 | loop fusion | flops 1441792 | bytes 3150848 | tf_op jit(solution)/shard_map/convert_element_type | solution.py:222
  103.5 5.8 %fusion.6 = bf16[1,128,1024]{2,0,1:T(2,128)(2,1)S(1)} fusion(f32[1,255,1024]{2,1,0:T(8,128)S(1)} %copy-done.4, f32[128,1,1024]{2,0,1:T(8,128)S(1)} %bitcast.46), kind=kOutput, calls=%fused_computation.33 | convolution fusion | flops 201326592 | bytes 1830912 | tf_op jit(solution)/shard_map/conv_general_dilated | solution.py:34
  110.5 2.5 %collective-permute-start.17 = (bf16[129,1024]{1,0:T(8,128)(2,1)}, bf16[129,1024]{1,0:T(8,128)(2,1)}, u32[]{:S(2)}, u32[]{:S(2)}) collective-permute-start(bf16[129,1024]{1,0:T(8,128)(2,1)} %pad_maximum_fusion), channel_id=1, source_target_pairs={{0,4},{4,0},{8,12},{12,8},{16,20},{20,16},{24,28},{28,24},{1,5},{5... | collective-permute-start | bytes 792584 | tf_op jit(solution)/shard_map/ppermute | solution.py:62
  113.1 6.9 %fusion = f32[1,128,1024]{2,0,1:T(1,128)S(1)} fusion(f32[1,255,1024]{2,1,0:T(8,128)S(1)} %maximum_bitcast_fusion.1, f32[128,1,1024]{2,0,1:T(8,128)} %bitcast.49), kind=kOutput, calls=%fused_computation.9 | convolution fusion | flops 201326592 | bytes 2093056 | tf_op jit(solution)/shard_map/conv_general_dilated | solution.py:34
  124.2 4.5 %collective-permute-start.14 = (bf16[7,1024]{1,0:T(8,128)(2,1)S(1)}, bf16[7,1024]{1,0:T(8,128)(2,1)S(1)}, u32[]{:S(2)}, u32[]{:S(2)}) collective-permute-start(bf16[7,1024]{1,0:T(8,128)(2,1)S(1)} %rev.14), channel_id=1, source_target_pairs={{0,4},{4,0},{8,12},{12,8},{16,20},{20,16},{24,28},{28,24},{1,5},{5... | collective-permute-start | bytes 43016 | tf_op jit(solution)/shard_map/ppermute | solution.py:62
  129.7 3.7 %collective-permute-start.18 = (bf16[129,1024]{1,0:T(8,128)(2,1)S(1)}, bf16[129,1024]{1,0:T(8,128)(2,1)}, u32[]{:S(2)}, u32[]{:S(2)}) collective-permute-start(bf16[129,1024]{1,0:T(8,128)(2,1)S(1)} %add_convert_fusion.1), channel_id=1, source_target_pairs={{0,8},{4,12},{8,0},{12,4},{16,24},{20,28},{24,16},{28,20},{1,9},{5... | collective-permute-start | bytes 792584 | tf_op jit(solution)/shard_map/ppermute | solution.py:62
  135.2 7.2 %collective-permute-done.15 = bf16[7,1024]{1,0:T(8,128)(2,1)S(1)} collective-permute-done((bf16[7,1024]{1,0:T(8,128)(2,1)S(1)}, bf16[7,1024]{1,0:T(8,128)(2,1)S(1)}, u32[]{:S(2)}, u32[]{:S(2)}) %collective-permute-start.15) | collective-permute-done | bytes 14368 | tf_op jit(solution)/shard_map/ppermute | solution.py:62
  142.4 3.0 %collective-permute-start.16 = (bf16[7,1024]{1,0:T(8,128)(2,1)S(1)}, bf16[7,1024]{1,0:T(8,128)(2,1)S(1)}, u32[]{:S(2)}, u32[]{:S(2)}) collective-permute-start(bf16[7,1024]{1,0:T(8,128)(2,1)S(1)} %add_convert_fusion.2), channel_id=1, source_target_pairs={{0,16},{4,20},{8,24},{12,28},{16,0},{20,4},{24,8},{28,12},{1,17},{... | collective-permute-start | bytes 43016 | tf_op jit(solution)/shard_map/ppermute | solution.py:62
  148.0 5.7 %collective-permute-done.19 = bf16[129,1024]{1,0:T(8,128)(2,1)S(1)} collective-permute-done((bf16[129,1024]{1,0:T(8,128)(2,1)S(1)}, bf16[129,1024]{1,0:T(8,128)(2,1)S(1)}, u32[]{:S(2)}, u32[]{:S(2)}) %collective-permute-start.19) | collective-permute-done | bytes 264224 | tf_op jit(solution)/shard_map/ppermute | solution.py:62
  (120 shorter events, 37.4 us)
Async XLA Ops:
  7.2 34.6 %all-gather.3.cloned.1.call-start = ((), (), s32[]{:S(2)}) async-start(), calls=%async_computation.1 | async-start | bytes 2359296 | tf_op jit(solution)/shard_map/all_gather | solution.py:189
  7.9 72.4 %all-gather.5.cloned.1.call-start = ((), (), s32[]{:S(2)}) async-start(), calls=%async_computation.2 | async-start | bytes 2359296 | tf_op jit(solution)/shard_map/all_gather | solution.py:202
  9.1 5.2 %collective-permute-start = (bf16[6,1024]{1,0:T(8,128)(2,1)S(1)}, bf16[6,1024]{1,0:T(8,128)(2,1)S(1)}, u32[]{:S(2)}, u32[]{:S(2)}) collective-permute-start(bf16[6,1024]{1,0:T(8,128)(2,1)S(1)} %slice.52), channel_id=1, source_target_pairs={{0,4},{4,8},{8,12},{12,16},{16,20},{20,24},{24,28},{1,5},{5,9},{9,... | collective-permute-start | bytes 36872 | tf_op jit(solution)/shard_map/ppermute | solution.py:30
  15.9 5.7 %collective-permute-start.1 = (bf16[127,1024]{1,0:T(8,128)(2,1)S(1)}, bf16[127,1024]{1,0:T(8,128)(2,1)S(1)}, u32[]{:S(2)}, u32[]{:S(2)}) collective-permute-start(bf16[127,1024]{1,0:T(8,128)(2,1)S(1)} %slice.50), channel_id=1, source_target_pairs={{0,4},{4,8},{8,12},{12,16},{16,20},{20,24},{24,28},{1,5},{5,9},{9,... | collective-permute-start | bytes 780296 | tf_op jit(solution)/shard_map/ppermute | solution.py:30
  21.7 14.1 %copy-start.13 = (f32[1024]{0:T(1024)S(1)}, f32[1024]{0:T(1024)}, u32[]{:S(2)}) copy-start(f32[1024]{0:T(1024)} %param.19) | copy-start | bytes 12292
  27.8 3.6 %collective-permute-start.2 = (f32[128]{0:T(128)S(1)}, f32[128]{0:T(128)S(1)}, u32[]{:S(2)}, u32[]{:S(2)}) collective-permute-start(f32[128]{0:T(128)S(1)} %get-tuple-element.27), channel_id=1, source_target_pairs={{0,1},{1,0},{2,3},{3,2},{4,5},{5,4},{6,7},{7,6},{8,9},{9,8},{10,11... | collective-permute-start | bytes 1544 | tf_op jit(solution)/shard_map/ppermute | solution.py:59
  31.4 4.4 %collective-permute-start.3 = (f32[128]{0:T(128)S(1)}, f32[128]{0:T(128)S(1)}, u32[]{:S(2)}, u32[]{:S(2)}) collective-permute-start(f32[128]{0:T(128)S(1)} %add.133), channel_id=1, source_target_pairs={{0,2},{1,3},{2,0},{3,1},{4,6},{5,7},{6,4},{7,5},{8,10},{9,11},{10,... | collective-permute-start | bytes 1544 | tf_op jit(solution)/shard_map/ppermute | solution.py:59
  36.7 118.5 %reduce-scatter.2.cloned.1.call-start = ((), (), s32[]{:S(2)}) async-start(), calls=%async_computation.3 | async-start | bytes 2359296 | tf_op jit(solution)/shard_map/reduce_scatter | solution.py:208
  52.1 11.9 %collective-permute-start.9 = (bf16[128,1024]{1,0:T(8,128)(2,1)S(1)}, bf16[128,1024]{1,0:T(8,128)(2,1)S(1)}, u32[]{:S(2)}, u32[]{:S(2)}) collective-permute-start(bf16[128,1024]{1,0:T(8,128)(2,1)S(1)} %get-tuple-element.32), channel_id=1, source_target_pairs={{24,0},{28,4},{25,1},{29,5},{26,2},{30,6},{27,3},{31,7}} | collective-permute-start | bytes 786440 | tf_op jit(solution)/shard_map/ppermute | solution.py:30
  53.4 23.1 %collective-permute-start.8 = (bf16[128,1024]{1,0:T(8,128)(2,1)S(1)}, bf16[128,1024]{1,0:T(8,128)(2,1)S(1)}, u32[]{:S(2)}, u32[]{:S(2)}) collective-permute-start(bf16[128,1024]{1,0:T(8,128)(2,1)S(1)} %get-tuple-element.33), channel_id=1, source_target_pairs={{20,0},{24,4},{28,8},{21,1},{25,5},{29,9},{22,2},{26,6},{30,10},{2... | collective-permute-start | bytes 786440 | tf_op jit(solution)/shard_map/ppermute | solution.py:30
  54.7 22.2 %collective-permute-start.7 = (bf16[128,1024]{1,0:T(8,128)(2,1)S(1)}, bf16[128,1024]{1,0:T(8,128)(2,1)S(1)}, u32[]{:S(2)}, u32[]{:S(2)}) collective-permute-start(bf16[128,1024]{1,0:T(8,128)(2,1)S(1)} %get-tuple-element.34), channel_id=1, source_target_pairs={{16,0},{20,4},{24,8},{28,12},{17,1},{21,5},{25,9},{29,13},{18,2},{... | collective-permute-start | bytes 786440 | tf_op jit(solution)/shard_map/ppermute | solution.py:30
  56.0 20.9 %collective-permute-start.6 = (bf16[128,1024]{1,0:T(8,128)(2,1)S(1)}, bf16[128,1024]{1,0:T(8,128)(2,1)S(1)}, u32[]{:S(2)}, u32[]{:S(2)}) collective-permute-start(bf16[128,1024]{1,0:T(8,128)(2,1)S(1)} %get-tuple-element.35), channel_id=1, source_target_pairs={{12,0},{16,4},{20,8},{24,12},{28,16},{13,1},{17,5},{21,9},{25,13},... | collective-permute-start | bytes 786440 | tf_op jit(solution)/shard_map/ppermute | solution.py:30
  57.3 19.6 %collective-permute-start.5 = (bf16[128,1024]{1,0:T(8,128)(2,1)S(1)}, bf16[128,1024]{1,0:T(8,128)(2,1)S(1)}, u32[]{:S(2)}, u32[]{:S(2)}) collective-permute-start(bf16[128,1024]{1,0:T(8,128)(2,1)S(1)} %get-tuple-element.36), channel_id=1, source_target_pairs={{8,0},{12,4},{16,8},{20,12},{24,16},{28,20},{9,1},{13,5},{17,9},{2... | collective-permute-start | bytes 786440 | tf_op jit(solution)/shard_map/ppermute | solution.py:30
  64.0 12.9 %collective-permute-start.4 = (bf16[128,1024]{1,0:T(8,128)(2,1)S(1)}, bf16[128,1024]{1,0:T(8,128)(2,1)S(1)}, u32[]{:S(2)}, u32[]{:S(2)}) collective-permute-start(bf16[128,1024]{1,0:T(8,128)(2,1)S(1)} %get-tuple-element.31), channel_id=1, source_target_pairs={{4,0},{8,4},{12,8},{16,12},{20,16},{24,20},{28,24},{5,1},{9,5},{13... | collective-permute-start | bytes 786440 | tf_op jit(solution)/shard_map/ppermute | solution.py:30
  91.1 3.6 %collective-permute-start.10 = (f32[128]{0:T(128)S(1)}, f32[128]{0:T(128)S(1)}, u32[]{:S(2)}, u32[]{:S(2)}) collective-permute-start(f32[128]{0:T(128)S(1)} %get-tuple-element.22), channel_id=1, source_target_pairs={{0,1},{1,0},{2,3},{3,2},{4,5},{5,4},{6,7},{7,6},{8,9},{9,8},{10,11... | collective-permute-start | bytes 1544 | tf_op jit(solution)/shard_map/ppermute | solution.py:59
  94.7 4.4 %collective-permute-start.11 = (f32[128]{0:T(128)S(1)}, f32[128]{0:T(128)S(1)}, u32[]{:S(2)}, u32[]{:S(2)}) collective-permute-start(f32[128]{0:T(128)S(1)} %add.160), channel_id=1, source_target_pairs={{0,2},{1,3},{2,0},{3,1},{4,6},{5,7},{6,4},{7,5},{8,10},{9,11},{10,... | collective-permute-start | bytes 1544 | tf_op jit(solution)/shard_map/ppermute | solution.py:59
  102.2 10.7 %collective-permute-start.12 = (bf16[127,1024]{1,0:T(8,128)(2,1)}, bf16[127,1024]{1,0:T(8,128)(2,1)S(1)}, u32[]{:S(2)}, u32[]{:S(2)}) collective-permute-start(bf16[127,1024]{1,0:T(8,128)(2,1)} %slice.49), channel_id=1, source_target_pairs={{4,0},{8,4},{12,8},{16,12},{20,16},{24,20},{28,24},{5,1},{9,5},{13... | collective-permute-start | bytes 780296 | tf_op jit(solution)/shard_map/ppermute | solution.py:30
  110.5 18.2 %collective-permute-start.17 = (bf16[129,1024]{1,0:T(8,128)(2,1)}, bf16[129,1024]{1,0:T(8,128)(2,1)}, u32[]{:S(2)}, u32[]{:S(2)}) collective-permute-start(bf16[129,1024]{1,0:T(8,128)(2,1)} %pad_maximum_fusion), channel_id=1, source_target_pairs={{0,4},{4,0},{8,12},{12,8},{16,20},{20,16},{24,28},{28,24},{1,5},{5... | collective-permute-start | bytes 792584 | tf_op jit(solution)/shard_map/ppermute | solution.py:62
  121.3 12.2 %collective-permute-start.13 = (bf16[6,1024]{1,0:T(8,128)(2,1)S(1)}, bf16[6,1024]{1,0:T(8,128)(2,1)S(1)}, u32[]{:S(2)}, u32[]{:S(2)}) collective-permute-start(bf16[6,1024]{1,0:T(8,128)(2,1)S(1)} %slice.51), channel_id=1, source_target_pairs={{4,0},{8,4},{12,8},{16,12},{20,16},{24,20},{28,24},{5,1},{9,5},{13... | collective-permute-start | bytes 36872 | tf_op jit(solution)/shard_map/ppermute | solution.py:30
  124.2 10.2 %collective-permute-start.14 = (bf16[7,1024]{1,0:T(8,128)(2,1)S(1)}, bf16[7,1024]{1,0:T(8,128)(2,1)S(1)}, u32[]{:S(2)}, u32[]{:S(2)}) collective-permute-start(bf16[7,1024]{1,0:T(8,128)(2,1)S(1)} %rev.14), channel_id=1, source_target_pairs={{0,4},{4,0},{8,12},{12,8},{16,20},{20,16},{24,28},{28,24},{1,5},{5... | collective-permute-start | bytes 43016 | tf_op jit(solution)/shard_map/ppermute | solution.py:62
  129.7 15.6 %collective-permute-start.18 = (bf16[129,1024]{1,0:T(8,128)(2,1)S(1)}, bf16[129,1024]{1,0:T(8,128)(2,1)}, u32[]{:S(2)}, u32[]{:S(2)}) collective-permute-start(bf16[129,1024]{1,0:T(8,128)(2,1)S(1)} %add_convert_fusion.1), channel_id=1, source_target_pairs={{0,8},{4,12},{8,0},{12,4},{16,24},{20,28},{24,16},{28,20},{1,9},{5... | collective-permute-start | bytes 792584 | tf_op jit(solution)/shard_map/ppermute | solution.py:62
  134.4 8.0 %collective-permute-start.15 = (bf16[7,1024]{1,0:T(8,128)(2,1)S(1)}, bf16[7,1024]{1,0:T(8,128)(2,1)S(1)}, u32[]{:S(2)}, u32[]{:S(2)}) collective-permute-start(bf16[7,1024]{1,0:T(8,128)(2,1)S(1)} %add_convert_fusion.3), channel_id=1, source_target_pairs={{0,8},{4,12},{8,0},{12,4},{16,24},{20,28},{24,16},{28,20},{1,9},{5... | collective-permute-start | bytes 43016 | tf_op jit(solution)/shard_map/ppermute | solution.py:62
  142.4 5.0 %collective-permute-start.16 = (bf16[7,1024]{1,0:T(8,128)(2,1)S(1)}, bf16[7,1024]{1,0:T(8,128)(2,1)S(1)}, u32[]{:S(2)}, u32[]{:S(2)}) collective-permute-start(bf16[7,1024]{1,0:T(8,128)(2,1)S(1)} %add_convert_fusion.2), channel_id=1, source_target_pairs={{0,16},{4,20},{8,24},{12,28},{16,0},{20,4},{24,8},{28,12},{1,17},{... | collective-permute-start | bytes 43016 | tf_op jit(solution)/shard_map/ppermute | solution.py:62
  146.4 7.3 %collective-permute-start.19 = (bf16[129,1024]{1,0:T(8,128)(2,1)S(1)}, bf16[129,1024]{1,0:T(8,128)(2,1)S(1)}, u32[]{:S(2)}, u32[]{:S(2)}) collective-permute-start(bf16[129,1024]{1,0:T(8,128)(2,1)S(1)} %add_convert_fusion), channel_id=1, source_target_pairs={{0,16},{4,20},{8,24},{12,28},{16,0},{20,4},{24,8},{28,12},{1,17},{... | collective-permute-start | bytes 792584 | tf_op jit(solution)/shard_map/ppermute | solution.py:62
  (16 other events, 67.6 us)
Sparse Core Ops, SparseCore 0:
  9.9 31.8 all-gather.2
  44.2 36.0 all-gather.4
  97.2 47.1 reduce-scatter.1

commit v7 on v6

--- a/solution.py
+++ b/solution.py
@@ -64,7 +64,21 @@
     return value
 
 
+def exchange_total(value, axis):
+    count = lax.axis_size(axis)
+    index = lax.axis_index(axis)
+    stacked = jnp.zeros((count,) + value.shape, value.dtype)
+    stacked = lax.dynamic_update_index_in_dim(stacked, value, index, 0)
+    for shift in range(1, count):
+        pairs = [(source, (source + shift) % count) for source in range(count)]
+        arrived = lax.ppermute(value, axis, pairs)
+        stacked = lax.dynamic_update_index_in_dim(stacked, arrived, (index - shift) % count, 0)
+    return jnp.sum(stacked, axis=0)
+
+
 def channel_total(partial_value):
+    if lax.axis_size("tp") <= 4:
+        return exchange_total(partial_value, "tp")
     return butterfly_total(partial_value, "tp")
 
 
@@ -234,11 +248,11 @@
     stencil_part = depthwise(padded_one, dconv_one)[::-1]
     stream_grad = (first_grad + dinner_one * feeder.astype(jnp.float32)).astype(jnp.bfloat16)
     filter_sum = butterfly_total(
-        jnp.concatenate([kernel_part, scaling_part[None]], axis=0), "ctx", jnp.bfloat16
+        jnp.concatenate([kernel_part, scaling_part[None], stencil_part], axis=0), "ctx", jnp.bfloat16
     )
     kernel_sum = filter_sum[:KM]
     scaling_sum = filter_sum[KM]
-    stencil_sum = butterfly_total(stencil_part, "ctx", jnp.bfloat16)
+    stencil_sum = filter_sum[KM + 1 :]
     normalizer = math.sqrt(total_rows)
     return (
         result,

time: 163 us -> 158 us (0.969)
  waiting for transfers between devices: 45.4 us -> 41.1 us
    ppermute x4 -> x6, waiting for transfers between devices: 7.87 us -> 4.14 us  [exchange_total(): arrived = lax.ppermute(value, axis, pairs)]
    ppermute x6 -> x3, waiting for transfers between devices: 12.9 us -> 10.1 us  [butterfly_total(): lax.ppermute(rounded, axis, pairs).astype(value.dtype)]
    ppermute x4 -> x6, starting transfers between devices: 8.17 us -> 10.8 us  [exchange_total(): arrived = lax.ppermute(value, axis, pairs)]
    ppermute x6 -> x3, starting transfers between devices: 13.8 us -> 11.3 us  [butterfly_total(): lax.ppermute(rounded, axis, pairs).astype(value.dtype)]
    convert_element_type x4 -> x2, other arithmetic: 2.08 us -> 0.15 us  [butterfly_total(): rounded = value.astype(sent_type)]
  transfers between devices with their start and end apart: 23 -> 22, of which waited for: 12 -> 15; matrix products, arithmetic and copies ran while one was open for 26% -> 26% of each run, Pallas kernels for 5% -> 6%
where the time goes in v7:
time: 158 us; the launch traced here: 156 us
  waiting for transfers between devices  41.1 us (26%)
  starting transfers between devices  39.4 us (25%)
  matrix products  20.9 us (13%)
  Pallas kernels  19.3 us (12%)
  between operations  14.5 us (9%)
  other arithmetic  12.9 us (8%)
  local copies, waits for them, and re-layouts  8.53 us (5%)
    conv_general_dilated x6, matrix products, depthwise(): lax.conv_general_dilated(padded[None], tap_rows[:, None, :], (1,), 'VALID...  20.9 us
    ppermute x10, waiting for transfers between devices, passed_along(): lax.ppermute(value, axis, [(source, source + steps) for source in range(l...  19.4 us
    ppermute x10, starting transfers between devices, passed_along(): lax.ppermute(value, axis, [(source, source + steps) for source in range(l...  17.2 us
    ppermute x3, starting transfers between devices, butterfly_total(): lax.ppermute(rounded, axis, pairs).astype(value.dtype)  11.3 us
    ppermute x6, starting transfers between devices, exchange_total(): arrived = lax.ppermute(value, axis, pairs)  10.8 us
    pallas_call x1, Pallas kernels, head_attention(): pl.pallas_call(functools.partial(attention_block, scale_factor), grid=(wi...  10.5 us
    ppermute x3, waiting for transfers between devices, butterfly_total(): lax.ppermute(rounded, axis, pairs).astype(value.dtype)  10.1 us
    pallas_call x1, Pallas kernels, head_values_grad(): pl.pallas_call(functools.partial(value_block, scale_factor), grid=(width_...  8.75 us
  transfers between devices with their start and end apart: 22, of which 15 were waited for; matrix products, arithmetic and copies ran while one was open for 26% of the time, Pallas kernels for 6%

profile of v7, /device:TPU:0, one launch (start us, length us, event | category | flops | bytes accessed | tf_op | source)
XLA Modules:
  0.0 156.5 jit_solution(6382414360277726330)
XLA Ops:
  9.1 2.4 %collective-permute-start = (bf16[6,1024]{1,0:T(8,128)(2,1)S(1)}, bf16[6,1024]{1,0:T(8,128)(2,1)S(1)}, u32[]{:S(2)}, u32[]{:S(2)}) collective-permute-start(bf16[6,1024]{1,0:T(8,128)(2,1)S(1)} %slice.58), channel_id=1, source_target_pairs={{0,4},{4,8},{8,12},{12,16},{16,20},{20,24},{24,28},{1,5},{5,9},{9,... | collective-permute-start | bytes 36872 | tf_op jit(solution)/shard_map/ppermute | solution.py:30
  11.4 2.8 %rev.12 = f32[7,1024]{1,0:T(8,128)S(1)} reverse(f32[7,1024]{1,0:T(8,128)} %param.15), dimensions={0} | reverse | bytes 57344 | tf_op jit(solution)/shard_map/rev | solution.py:189
  15.9 4.5 %collective-permute-start.1 = (bf16[127,1024]{1,0:T(8,128)(2,1)S(1)}, bf16[127,1024]{1,0:T(8,128)(2,1)S(1)}, u32[]{:S(2)}, u32[]{:S(2)}) collective-permute-start(bf16[127,1024]{1,0:T(8,128)(2,1)S(1)} %slice.56), channel_id=1, source_target_pairs={{0,4},{4,8},{8,12},{12,16},{16,20},{20,24},{24,28},{1,5},{5,9},{9,... | collective-permute-start | bytes 780296 | tf_op jit(solution)/shard_map/ppermute | solution.py:30
  21.8 5.8 %fusion.8 = f32[1,128,1024]{2,0,1:T(1,128)S(1)} fusion(f32[1,255,1024]{2,1,0:T(8,128)S(1)} %maximum_bitcast_fusion, f32[128,1,1024]{2,0,1:T(8,128)S(1)} %bitcast.58), kind=kOutput, calls=%fused_computation.35 | convolution fusion | flops 201326592 | bytes 2093056 | tf_op jit(solution)/shard_map/conv_general_dilated | solution.py:34
  27.8 1.6 %collective-permute-start.2 = (f32[128]{0:T(128)S(1)}, f32[128]{0:T(128)S(1)}, u32[]{:S(2)}, u32[]{:S(2)}) collective-permute-start(f32[128]{0:T(128)S(1)} %get-tuple-element.27), channel_id=1, source_target_pairs={{0,1},{1,2},{2,3},{3,0},{4,5},{5,6},{6,7},{7,4},{8,9},{9,10},{10,1... | collective-permute-start | bytes 1544 | tf_op jit(solution)/shard_map/ppermute | solution.py:74
  29.4 2.6 %collective-permute-start.3 = (f32[128]{0:T(128)S(1)}, f32[128]{0:T(128)S(1)}, u32[]{:S(2)}, u32[]{:S(2)}) collective-permute-start(f32[128]{0:T(128)S(1)} %get-tuple-element.27), channel_id=1, source_target_pairs={{0,2},{1,3},{2,0},{3,1},{4,6},{5,7},{6,4},{7,5},{8,10},{9,11},{10,... | collective-permute-start | bytes 1544 | tf_op jit(solution)/shard_map/ppermute | solution.py:74
  33.9 1.7 %collective-permute-done.4 = f32[128]{0:T(128)S(1)} collective-permute-done((f32[128]{0:T(128)S(1)}, f32[128]{0:T(128)S(1)}, u32[]{:S(2)}, u32[]{:S(2)}) %collective-permute-start.4) | collective-permute-done | bytes 544 | tf_op jit(solution)/shard_map/ppermute | solution.py:74
  37.7 4.1 %all-gather.3.cloned.1.call-done.k_ref = bf16[1024,1024]{1,0:T(8,128)(2,1)} async-done(((bf16[128,1024]{1,0:T(8,128)(2,1)}), bf16[1024,1024]{1,0:T(8,128)(2,1)}) %all-gather.3.cloned.1.call-update) | async-done | bytes 2097168 | tf_op jit(solution)/shard_map/all_gather | solution.py:203
  41.8 8.8 %shard_map.204 = bf16[1024,1024]{1,0:T(8,128)(2,1)} custom-call(bf16[128,1024]{1,0:T(8,128)(2,1)} %q_ref.3, bf16[1024,1024]{1,0:T(8,128)(2,1)} %all-gather.3.cloned.1.call-done.k_ref, bf16[128,1024]{1,0:T(8,128)(2,1)} %cot_ref.3, f32[128,1024]{1,0:T(8,128)} %fusion.33.vis_ref), custom_call_target="tpu_custom_call" | custom-call | tf_op jit(solution)/shard_map/pallas_call | solution.py:139
  58.6 5.8 %collective-permute-done.10 = bf16[128,1024]{1,0:T(8,128)(2,1)S(1)} collective-permute-done((bf16[128,1024]{1,0:T(8,128)(2,1)S(1)}, bf16[128,1024]{1,0:T(8,128)(2,1)S(1)}, u32[]{:S(2)}, u32[]{:S(2)}) %collective-permute-start.10) | collective-permute-done | bytes 262176 | tf_op jit(solution)/shard_map/ppermute | solution.py:30
  65.7 10.4 %collective-permute-done.9 = bf16[128,1024]{1,0:T(8,128)(2,1)S(1)} collective-permute-done((bf16[128,1024]{1,0:T(8,128)(2,1)S(1)}, bf16[128,1024]{1,0:T(8,128)(2,1)S(1)}, u32[]{:S(2)}, u32[]{:S(2)}) %collective-permute-start.9) | collective-permute-done | bytes 262176 | tf_op jit(solution)/shard_map/ppermute | solution.py:30
  78.0 2.6 %all-gather.5.cloned.1.call-done.v_ref = bf16[1024,1024]{1,0:T(8,128)(2,1)} async-done(((bf16[128,1024]{1,0:T(8,128)(2,1)}), bf16[1024,1024]{1,0:T(8,128)(2,1)}) %all-gather.5.cloned.1.call-update) | async-done | bytes 2097168 | tf_op jit(solution)/shard_map/all_gather | solution.py:216
  80.5 10.5 %shard_map.203 = (bf16[1024,1024]{1,0:T(8,128)(2,1)}, f32[128,1024]{1,0:T(8,128)}, bf16[128,1024]{1,0:T(8,128)(2,1)}) custom-call(bf16[128,1024]{1,0:T(8,128)(2,1)} %q_ref.3, bf16[1024,1024]{1,0:T(8,128)(2,1)} %all-gather.3.cloned.1.call-done.k_ref, bf16[1024,1024]{1,0:T(8,128)(2,1)} %all-gather.5.cloned.1.call-done.v_ref, bf16[128,1024]{1,0:T(8,128)(2,1)} %cot_ref.3, ...), custom_call_target="tpu_custom_call" | custom-call | tf_op jit(solution)/shard_map/pallas_call | solution.py:152
  92.6 2.5 %collective-permute-start.12 = (f32[128]{0:T(128)S(1)}, f32[128]{0:T(128)S(1)}, u32[]{:S(2)}, u32[]{:S(2)}) collective-permute-start(f32[128]{0:T(128)S(1)} %get-tuple-element.22), channel_id=1, source_target_pairs={{0,2},{1,3},{2,0},{3,1},{4,6},{5,7},{6,4},{7,5},{8,10},{9,11},{10,... | collective-permute-start | bytes 1544 | tf_op jit(solution)/shard_map/ppermute | solution.py:74
  97.1 1.6 %collective-permute-done.13 = f32[128]{0:T(128)S(1)} collective-permute-done((f32[128]{0:T(128)S(1)}, f32[128]{0:T(128)S(1)}, u32[]{:S(2)}, u32[]{:S(2)}) %collective-permute-start.13) | collective-permute-done | bytes 544 | tf_op jit(solution)/shard_map/ppermute | solution.py:74
  98.7 2.3 %fusion.25 = (bf16[128,1024]{1,0:T(8,128)(2,1)}, f32[128,1024]{1,0:T(8,128)S(1)}, bf16[128,1024]{1,0:T(8,128)(2,1)}) fusion(f32[1,128,1024]{2,0,1:T(1,128)S(1)} %fusion.8, f32[128]{0:T(128)S(1)} %fusion.42, bf16[128,1024]{1,0:T(8,128)(2,1)S(1)} %get-tuple-element.28, f32[128,1024]{1,0:T(8,128)S(1)} %convert_add_fusion.4, f32[1024]{0:T(1024)S(1)} %copy-done.13, ...), kind=kLoop, calls=%fused_computation.58 | loop fusion | flops 1441792 | bytes 3150848 | tf_op jit(solution)/shard_map/convert_element_type | solution.py:236
  103.1 5.8 %fusion.6 = bf16[1,128,1024]{2,0,1:T(2,128)(2,1)S(1)} fusion(f32[1,255,1024]{2,1,0:T(8,128)S(1)} %copy-done.4, f32[128,1,1024]{2,0,1:T(8,128)S(1)} %bitcast.54), kind=kOutput, calls=%fused_computation.33 | convolution fusion | flops 201326592 | bytes 1830912 | tf_op jit(solution)/shard_map/conv_general_dilated | solution.py:34
  109.5 6.9 %fusion = f32[1,128,1024]{2,0,1:T(1,128)S(1)} fusion(f32[1,255,1024]{2,1,0:T(8,128)S(1)} %maximum_bitcast_fusion.1, f32[128,1,1024]{2,0,1:T(8,128)} %bitcast.57), kind=kOutput, calls=%fused_computation.9 | convolution fusion | flops 201326592 | bytes 2093056 | tf_op jit(solution)/shard_map/conv_general_dilated | solution.py:34
  119.1 6.6 %collective-permute-start.16 = (bf16[136,1024]{1,0:T(8,128)(2,1)S(1)}, bf16[136,1024]{1,0:T(8,128)(2,1)S(1)}, u32[]{:S(2)}, u32[]{:S(2)}) collective-permute-start(bf16[136,1024]{1,0:T(8,128)(2,1)S(1)} %pad_maximum_fusion), channel_id=1, source_target_pairs={{0,4},{4,0},{8,12},{12,8},{16,20},{20,16},{24,28},{28,24},{1,5},{5... | collective-permute-start | bytes 835592 | tf_op jit(solution)/shard_map/ppermute | solution.py:62
  127.0 2.5 %collective-permute-start.17 = (bf16[136,1024]{1,0:T(8,128)(2,1)S(1)}, bf16[136,1024]{1,0:T(8,128)(2,1)S(1)}, u32[]{:S(2)}, u32[]{:S(2)}) collective-permute-start(bf16[136,1024]{1,0:T(8,128)(2,1)S(1)} %add_convert_fusion.1), channel_id=1, source_target_pairs={{0,8},{4,12},{8,0},{12,4},{16,24},{20,28},{24,16},{28,20},{1,9},{5... | collective-permute-start | bytes 835592 | tf_op jit(solution)/shard_map/ppermute | solution.py:62
  130.8 1.8 %collective-permute-done.15 = bf16[6,1024]{1,0:T(8,128)(2,1)S(1)} collective-permute-done((bf16[6,1024]{1,0:T(8,128)(2,1)S(1)}, bf16[6,1024]{1,0:T(8,128)(2,1)S(1)}, u32[]{:S(2)}, u32[]{:S(2)}) %collective-permute-start.15) | collective-permute-done | bytes 12320 | tf_op jit(solution)/shard_map/ppermute | solution.py:30
  133.5 3.2 %collective-permute-done.17 = bf16[136,1024]{1,0:T(8,128)(2,1)S(1)} collective-permute-done((bf16[136,1024]{1,0:T(8,128)(2,1)S(1)}, bf16[136,1024]{1,0:T(8,128)(2,1)S(1)}, u32[]{:S(2)}, u32[]{:S(2)}) %collective-permute-start.17) | collective-permute-done | bytes 278560 | tf_op jit(solution)/shard_map/ppermute | solution.py:62
  136.7 2.2 %collective-permute-start.18 = (bf16[136,1024]{1,0:T(8,128)(2,1)S(1)}, bf16[136,1024]{1,0:T(8,128)(2,1)}, u32[]{:S(2)}, u32[]{:S(2)}) collective-permute-start(bf16[136,1024]{1,0:T(8,128)(2,1)S(1)} %add_convert_fusion), channel_id=1, source_target_pairs={{0,16},{4,20},{8,24},{12,28},{16,0},{20,4},{24,8},{28,12},{1,17},{... | collective-permute-start | bytes 835592 | tf_op jit(solution)/shard_map/ppermute | solution.py:62
  141.1 5.7 %collective-permute-done.18 = bf16[136,1024]{1,0:T(8,128)(2,1)} collective-permute-done((bf16[136,1024]{1,0:T(8,128)(2,1)S(1)}, bf16[136,1024]{1,0:T(8,128)(2,1)}, u32[]{:S(2)}, u32[]{:S(2)}) %collective-permute-start.18) | collective-permute-done | bytes 278560 | tf_op jit(solution)/shard_map/ppermute | solution.py:62
  (126 shorter events, 37.3 us)
Async XLA Ops:
  7.2 34.6 %all-gather.3.cloned.1.call-start = ((), (), s32[]{:S(2)}) async-start(), calls=%async_computation.1 | async-start | bytes 2359296 | tf_op jit(solution)/shard_map/all_gather | solution.py:203
  7.9 72.6 %all-gather.5.cloned.1.call-start = ((), (), s32[]{:S(2)}) async-start(), calls=%async_computation.2 | async-start | bytes 2359296 | tf_op jit(solution)/shard_map/all_gather | solution.py:216
  9.1 5.2 %collective-permute-start = (bf16[6,1024]{1,0:T(8,128)(2,1)S(1)}, bf16[6,1024]{1,0:T(8,128)(2,1)S(1)}, u32[]{:S(2)}, u32[]{:S(2)}) collective-permute-start(bf16[6,1024]{1,0:T(8,128)(2,1)S(1)} %slice.58), channel_id=1, source_target_pairs={{0,4},{4,8},{8,12},{12,16},{16,20},{20,24},{24,28},{1,5},{5,9},{9,... | collective-permute-start | bytes 36872 | tf_op jit(solution)/shard_map/ppermute | solution.py:30
  15.9 5.7 %collective-permute-start.1 = (bf16[127,1024]{1,0:T(8,128)(2,1)S(1)}, bf16[127,1024]{1,0:T(8,128)(2,1)S(1)}, u32[]{:S(2)}, u32[]{:S(2)}) collective-permute-start(bf16[127,1024]{1,0:T(8,128)(2,1)S(1)} %slice.56), channel_id=1, source_target_pairs={{0,4},{4,8},{8,12},{12,16},{16,20},{20,24},{24,28},{1,5},{5,9},{9,... | collective-permute-start | bytes 780296 | tf_op jit(solution)/shard_map/ppermute | solution.py:30
  21.7 13.9 %copy-start.13 = (f32[1024]{0:T(1024)S(1)}, f32[1024]{0:T(1024)}, u32[]{:S(2)}) copy-start(f32[1024]{0:T(1024)} %param.19) | copy-start | bytes 12292
  27.5 9.1 %copy-start.15 = (s32[1024]{0:T(1024)S(1)}, s32[1024]{0:T(1024)}, u32[]{:S(2)}) copy-start(s32[1024]{0:T(1024)} %param.22) | copy-start | bytes 12292
  27.8 5.6 %collective-permute-start.2 = (f32[128]{0:T(128)S(1)}, f32[128]{0:T(128)S(1)}, u32[]{:S(2)}, u32[]{:S(2)}) collective-permute-start(f32[128]{0:T(128)S(1)} %get-tuple-element.27), channel_id=1, source_target_pairs={{0,1},{1,2},{2,3},{3,0},{4,5},{5,6},{6,7},{7,4},{8,9},{9,10},{10,1... | collective-permute-start | bytes 1544 | tf_op jit(solution)/shard_map/ppermute | solution.py:74
  29.4 4.4 %collective-permute-start.3 = (f32[128]{0:T(128)S(1)}, f32[128]{0:T(128)S(1)}, u32[]{:S(2)}, u32[]{:S(2)}) collective-permute-start(f32[128]{0:T(128)S(1)} %get-tuple-element.27), channel_id=1, source_target_pairs={{0,2},{1,3},{2,0},{3,1},{4,6},{5,7},{6,4},{7,5},{8,10},{9,11},{10,... | collective-permute-start | bytes 1544 | tf_op jit(solution)/shard_map/ppermute | solution.py:74
  32.0 3.5 %collective-permute-start.4 = (f32[128]{0:T(128)S(1)}, f32[128]{0:T(128)S(1)}, u32[]{:S(2)}, u32[]{:S(2)}) collective-permute-start(f32[128]{0:T(128)S(1)} %get-tuple-element.27), channel_id=1, source_target_pairs={{0,3},{1,0},{2,1},{3,2},{4,7},{5,4},{6,5},{7,6},{8,11},{9,8},{10,9... | collective-permute-start | bytes 1544 | tf_op jit(solution)/shard_map/ppermute | solution.py:74
  36.5 113.5 %reduce-scatter.2.cloned.1.call-start = ((), (), s32[]{:S(2)}) async-start(), calls=%async_computation.3 | async-start | bytes 2359296 | tf_op jit(solution)/shard_map/reduce_scatter | solution.py:222
  52.1 12.3 %collective-permute-start.10 = (bf16[128,1024]{1,0:T(8,128)(2,1)S(1)}, bf16[128,1024]{1,0:T(8,128)(2,1)S(1)}, u32[]{:S(2)}, u32[]{:S(2)}) collective-permute-start(bf16[128,1024]{1,0:T(8,128)(2,1)S(1)} %get-tuple-element.32), channel_id=1, source_target_pairs={{24,0},{28,4},{25,1},{29,5},{26,2},{30,6},{27,3},{31,7}} | collective-permute-start | bytes 786440 | tf_op jit(solution)/shard_map/ppermute | solution.py:30
  53.4 22.7 %collective-permute-start.9 = (bf16[128,1024]{1,0:T(8,128)(2,1)S(1)}, bf16[128,1024]{1,0:T(8,128)(2,1)S(1)}, u32[]{:S(2)}, u32[]{:S(2)}) collective-permute-start(bf16[128,1024]{1,0:T(8,128)(2,1)S(1)} %get-tuple-element.33), channel_id=1, source_target_pairs={{20,0},{24,4},{28,8},{21,1},{25,5},{29,9},{22,2},{26,6},{30,10},{2... | collective-permute-start | bytes 786440 | tf_op jit(solution)/shard_map/ppermute | solution.py:30
  54.7 22.0 %collective-permute-start.8 = (bf16[128,1024]{1,0:T(8,128)(2,1)S(1)}, bf16[128,1024]{1,0:T(8,128)(2,1)S(1)}, u32[]{:S(2)}, u32[]{:S(2)}) collective-permute-start(bf16[128,1024]{1,0:T(8,128)(2,1)S(1)} %get-tuple-element.34), channel_id=1, source_target_pairs={{16,0},{20,4},{24,8},{28,12},{17,1},{21,5},{25,9},{29,13},{18,2},{... | collective-permute-start | bytes 786440 | tf_op jit(solution)/shard_map/ppermute | solution.py:30
  56.0 20.7 %collective-permute-start.7 = (bf16[128,1024]{1,0:T(8,128)(2,1)S(1)}, bf16[128,1024]{1,0:T(8,128)(2,1)S(1)}, u32[]{:S(2)}, u32[]{:S(2)}) collective-permute-start(bf16[128,1024]{1,0:T(8,128)(2,1)S(1)} %get-tuple-element.35), channel_id=1, source_target_pairs={{12,0},{16,4},{20,8},{24,12},{28,16},{13,1},{17,5},{21,9},{25,13},... | collective-permute-start | bytes 786440 | tf_op jit(solution)/shard_map/ppermute | solution.py:30
  57.3 19.4 %collective-permute-start.6 = (bf16[128,1024]{1,0:T(8,128)(2,1)S(1)}, bf16[128,1024]{1,0:T(8,128)(2,1)S(1)}, u32[]{:S(2)}, u32[]{:S(2)}) collective-permute-start(bf16[128,1024]{1,0:T(8,128)(2,1)S(1)} %get-tuple-element.36), channel_id=1, source_target_pairs={{8,0},{12,4},{16,8},{20,12},{24,16},{28,20},{9,1},{13,5},{17,9},{2... | collective-permute-start | bytes 786440 | tf_op jit(solution)/shard_map/ppermute | solution.py:30
  64.4 12.3 %collective-permute-start.5 = (bf16[128,1024]{1,0:T(8,128)(2,1)S(1)}, bf16[128,1024]{1,0:T(8,128)(2,1)S(1)}, u32[]{:S(2)}, u32[]{:S(2)}) collective-permute-start(bf16[128,1024]{1,0:T(8,128)(2,1)S(1)} %get-tuple-element.31), channel_id=1, source_target_pairs={{4,0},{8,4},{12,8},{16,12},{20,16},{24,20},{28,24},{5,1},{9,5},{13... | collective-permute-start | bytes 786440 | tf_op jit(solution)/shard_map/ppermute | solution.py:30
  91.2 5.4 %collective-permute-start.11 = (f32[128]{0:T(128)S(1)}, f32[128]{0:T(128)S(1)}, u32[]{:S(2)}, u32[]{:S(2)}) collective-permute-start(f32[128]{0:T(128)S(1)} %get-tuple-element.22), channel_id=1, source_target_pairs={{0,1},{1,2},{2,3},{3,0},{4,5},{5,6},{6,7},{7,4},{8,9},{9,10},{10,1... | collective-permute-start | bytes 1544 | tf_op jit(solution)/shard_map/ppermute | solution.py:74
  92.6 4.4 %collective-permute-start.12 = (f32[128]{0:T(128)S(1)}, f32[128]{0:T(128)S(1)}, u32[]{:S(2)}, u32[]{:S(2)}) collective-permute-start(f32[128]{0:T(128)S(1)} %get-tuple-element.22), channel_id=1, source_target_pairs={{0,2},{1,3},{2,0},{3,1},{4,6},{5,7},{6,4},{7,5},{8,10},{9,11},{10,... | collective-permute-start | bytes 1544 | tf_op jit(solution)/shard_map/ppermute | solution.py:74
  95.1 3.5 %collective-permute-start.13 = (f32[128]{0:T(128)S(1)}, f32[128]{0:T(128)S(1)}, u32[]{:S(2)}, u32[]{:S(2)}) collective-permute-start(f32[128]{0:T(128)S(1)} %get-tuple-element.22), channel_id=1, source_target_pairs={{0,3},{1,0},{2,1},{3,2},{4,7},{5,4},{6,5},{7,6},{8,11},{9,8},{10,9... | collective-permute-start | bytes 1544 | tf_op jit(solution)/shard_map/ppermute | solution.py:74
  101.8 7.5 %collective-permute-start.14 = (bf16[127,1024]{1,0:T(8,128)(2,1)}, bf16[127,1024]{1,0:T(8,128)(2,1)S(1)}, u32[]{:S(2)}, u32[]{:S(2)}) collective-permute-start(bf16[127,1024]{1,0:T(8,128)(2,1)} %slice.55), channel_id=1, source_target_pairs={{4,0},{8,4},{12,8},{16,12},{20,16},{24,20},{28,24},{5,1},{9,5},{13... | collective-permute-start | bytes 780296 | tf_op jit(solution)/shard_map/ppermute | solution.py:30
  119.1 7.8 %collective-permute-start.16 = (bf16[136,1024]{1,0:T(8,128)(2,1)S(1)}, bf16[136,1024]{1,0:T(8,128)(2,1)S(1)}, u32[]{:S(2)}, u32[]{:S(2)}) collective-permute-start(bf16[136,1024]{1,0:T(8,128)(2,1)S(1)} %pad_maximum_fusion), channel_id=1, source_target_pairs={{0,4},{4,0},{8,12},{12,8},{16,20},{20,16},{24,28},{28,24},{1,5},{5... | collective-permute-start | bytes 835592 | tf_op jit(solution)/shard_map/ppermute | solution.py:62
  127.0 9.7 %collective-permute-start.17 = (bf16[136,1024]{1,0:T(8,128)(2,1)S(1)}, bf16[136,1024]{1,0:T(8,128)(2,1)S(1)}, u32[]{:S(2)}, u32[]{:S(2)}) collective-permute-start(bf16[136,1024]{1,0:T(8,128)(2,1)S(1)} %add_convert_fusion.1), channel_id=1, source_target_pairs={{0,8},{4,12},{8,0},{12,4},{16,24},{20,28},{24,16},{28,20},{1,9},{5... | collective-permute-start | bytes 835592 | tf_op jit(solution)/shard_map/ppermute | solution.py:62
  129.5 3.1 %collective-permute-start.15 = (bf16[6,1024]{1,0:T(8,128)(2,1)S(1)}, bf16[6,1024]{1,0:T(8,128)(2,1)S(1)}, u32[]{:S(2)}, u32[]{:S(2)}) collective-permute-start(bf16[6,1024]{1,0:T(8,128)(2,1)S(1)} %slice.57), channel_id=1, source_target_pairs={{4,0},{8,4},{12,8},{16,12},{20,16},{24,20},{28,24},{5,1},{9,5},{13... | collective-permute-start | bytes 36872 | tf_op jit(solution)/shard_map/ppermute | solution.py:30
  136.7 10.1 %collective-permute-start.18 = (bf16[136,1024]{1,0:T(8,128)(2,1)S(1)}, bf16[136,1024]{1,0:T(8,128)(2,1)}, u32[]{:S(2)}, u32[]{:S(2)}) collective-permute-start(bf16[136,1024]{1,0:T(8,128)(2,1)S(1)} %add_convert_fusion), channel_id=1, source_target_pairs={{0,16},{4,20},{8,24},{12,28},{16,0},{20,4},{24,8},{28,12},{1,17},{... | collective-permute-start | bytes 835592 | tf_op jit(solution)/shard_map/ppermute | solution.py:62
  (15 other events, 56.3 us)
Sparse Core Ops, SparseCore 0:
  9.9 31.8 all-gather.2
  44.2 36.2 all-gather.4
  96.6 45.9 reduce-scatter.1

commit v8 on v7

--- a/solution.py
+++ b/solution.py
@@ -90,26 +90,27 @@
     )
     scores = jnp.where(visible > 0.5, scores, -jnp.inf)
     row_max = jnp.max(scores, axis=1, keepdims=True)
-    logsum = row_max + jnp.log(jnp.sum(jnp.exp(scores - row_max), axis=1, keepdims=True))
-    return jnp.exp(scores - logsum).astype(jnp.bfloat16)
-
-
-def value_block(scale_factor, q_ref, k_ref, cot_ref, vis_ref, dv_ref):
+    raised = jnp.exp(scores - row_max)
+    return (raised * (1.0 / jnp.sum(raised, axis=1, keepdims=True))).astype(jnp.bfloat16)
+
+
+def value_block(scale_factor, q_ref, k_ref, cot_ref, vis_ref, dv_ref, w_ref):
     contract_first = (((0,), (0,)), ((), ()))
     weights = head_weights(scale_factor, q_ref[...], k_ref[...], vis_ref[...])
+    w_ref[0] = weights
     dv_ref[...] = lax.dot_general(
         weights, cot_ref[...], contract_first, preferred_element_type=jnp.float32
     ).astype(jnp.bfloat16)
 
 
-def attention_block(scale_factor, q_ref, k_ref, v_ref, cot_ref, vis_ref, dk_ref, att_ref, dq_ref):
+def attention_block(scale_factor, q_ref, k_ref, v_ref, cot_ref, w_ref, dk_ref, att_ref, dq_ref):
     contract_last = (((1,), (1,)), ((), ()))
     contract_first = (((0,), (0,)), ((), ()))
     query_head = q_ref[...]
     key_head = k_ref[...]
     value_head = v_ref[...]
     cotangent_head = cot_ref[...]
-    weights = head_weights(scale_factor, query_head, key_head, vis_ref[...])
+    weights = w_ref[0]
     attended = jnp.dot(weights, value_head, preferred_element_type=jnp.float32)
     weight_grad = lax.dot_general(
         cotangent_head, value_head, contract_last, preferred_element_type=jnp.float32
@@ -128,38 +129,42 @@
 def head_specs(local_rows, total_rows):
     local_spec = pl.BlockSpec((local_rows, HD), lambda h: (0, h))
     whole_spec = pl.BlockSpec((total_rows, HD), lambda h: (0, h))
-    mask_spec = pl.BlockSpec((local_rows, total_rows), lambda h: (0, 0))
-    return local_spec, whole_spec, mask_spec
+    weight_spec = pl.BlockSpec((1, local_rows, total_rows), lambda h: (h, 0, 0))
+    return local_spec, whole_spec, weight_spec
 
 
 def head_values_grad(queries, keys_whole, cotangent, visible, scale_factor):
     local_rows, width_local = queries.shape
     total_rows = keys_whole.shape[0]
-    local_spec, whole_spec, mask_spec = head_specs(local_rows, total_rows)
+    local_spec, whole_spec, weight_spec = head_specs(local_rows, total_rows)
+    mask_spec = pl.BlockSpec((local_rows, total_rows), lambda h: (0, 0))
     return pl.pallas_call(
         functools.partial(value_block, scale_factor),
         grid=(width_local // HD,),
         in_specs=[local_spec, whole_spec, local_spec, mask_spec],
-        out_specs=whole_spec,
-        out_shape=jax.ShapeDtypeStruct((total_rows, width_local), jnp.bfloat16),
+        out_specs=[whole_spec, weight_spec],
+        out_shape=[
+            jax.ShapeDtypeStruct((total_rows, width_local), jnp.bfloat16),
+            jax.ShapeDtypeStruct((width_local // HD, local_rows, total_rows), jnp.bfloat16),
+        ],
     )(queries, keys_whole, cotangent, visible)
 
 
-def head_attention(queries, keys_whole, values_whole, cotangent, visible, scale_factor):
+def head_attention(queries, keys_whole, values_whole, cotangent, weights, scale_factor):
     local_rows, width_local = queries.shape
     total_rows = keys_whole.shape[0]
-    local_spec, whole_spec, mask_spec = head_specs(local_rows, total_rows)
+    local_spec, whole_spec, weight_spec = head_specs(local_rows, total_rows)
     return pl.pallas_call(
         functools.partial(attention_block, scale_factor),
         grid=(width_local // HD,),
-        in_specs=[local_spec, whole_spec, whole_spec, local_spec, mask_spec],
+        in_specs=[local_spec, whole_spec, whole_spec, local_spec, weight_spec],
         out_specs=[whole_spec, local_spec, local_spec],
         out_shape=[
             jax.ShapeDtypeStruct((total_rows, width_local), jnp.bfloat16),
             jax.ShapeDtypeStruct((local_rows, width_local), jnp.float32),
             jax.ShapeDtypeStruct((local_rows, width_local), jnp.bfloat16),
         ],
-    )(queries, keys_whole, values_whole, cotangent, visible)
+    )(queries, keys_whole, values_whole, cotangent, weights)
 
 
 def shards(
@@ -207,7 +212,7 @@
     query_seg = lax.dynamic_slice_in_dim(segments, position, local_rows, 0)
     visible = (key_pos[None, :] <= query_pos[:, None]) & (segments[None, :] == query_seg[:, None])
     mask = visible.astype(jnp.float32)
-    value_part = head_values_grad(queries, keys_whole, cotangent, mask, scale_factor)
+    value_part, weights_all = head_values_grad(queries, keys_whole, cotangent, mask, scale_factor)
     value_grad = lax.dynamic_slice_in_dim(value_part, position, local_rows, 0).astype(jnp.float32)
     for distance in range(1, reach + 1):
         block_start = ((ctx_index - distance) % ctx_count) * local_rows
@@ -215,7 +220,7 @@
         value_grad = value_grad + passed_along(leaving, "ctx", -distance).astype(jnp.float32)
     values_whole = lax.all_gather(normed, "ctx", axis=0, tiled=True)
     key_part, attended_all, queries_grad = head_attention(
-        queries, keys_whole, values_whole, cotangent, mask, scale_factor
+        queries, keys_whole, values_whole, cotangent, weights_all, scale_factor
     )
     result = (second_wide + attended_all).astype(jnp.bfloat16)
     key_part, value_grad = lax.optimization_barrier((key_part, value_grad))

time: 158 us -> 160 us (1.013)
  waiting for transfers between devices: 41.1 us -> 49.5 us
  starting transfers between devices: 39.4 us -> 35.2 us
  Pallas kernels: 19.3 us -> 17.5 us
    ppermute x10, waiting for transfers between devices: 19.4 us -> 27.1 us  [passed_along(): lax.ppermute(value, axis, [(source, source + steps) for source in range(l...]
    ppermute x3, waiting for transfers between devices: 10.1 us -> 13.8 us  [butterfly_total(): lax.ppermute(rounded, axis, pairs).astype(value.dtype)]
    ppermute x3, starting transfers between devices: 11.3 us -> 7.67 us  [butterfly_total(): lax.ppermute(rounded, axis, pairs).astype(value.dtype)]
    all_gather x1, waiting for transfers between devices: 2.56 us -> 0.02 us  [shards(): values_whole = lax.all_gather(normed, 'ctx', axis=0, tiled=True)]
    pallas_call x1, Pallas kernels: 10.5 us -> 8.77 us  [head_attention(): pl.pallas_call(functools.partial(attention_block, scale_factor), grid=(wi...]
  transfers between devices with their start and end apart: 22 -> 22, of which waited for: 15 -> 15; matrix products, arithmetic and copies ran while one was open for 26% -> 25% of each run, Pallas kernels for 6% -> 6%
where the time goes in v8:
time: 160 us; the launch traced here: 159 us
  waiting for transfers between devices  49.5 us (31%)
  starting transfers between devices  35.2 us (22%)
  matrix products  19.6 us (12%)
  Pallas kernels  17.5 us (11%)
  between operations  14.5 us (9%)
  other arithmetic  12.9 us (8%)
  local copies, waits for them, and re-layouts  9.71 us (6%)
    ppermute x10, waiting for transfers between devices, passed_along(): lax.ppermute(value, axis, [(source, source + steps) for source in range(l...  27.1 us
    conv_general_dilated x6, matrix products, depthwise(): lax.conv_general_dilated(padded[None], tap_rows[:, None, :], (1,), 'VALID...  19.6 us
    ppermute x10, starting transfers between devices, passed_along(): lax.ppermute(value, axis, [(source, source + steps) for source in range(l...  17.2 us
    ppermute x3, waiting for transfers between devices, butterfly_total(): lax.ppermute(rounded, axis, pairs).astype(value.dtype)  13.8 us
    ppermute x6, starting transfers between devices, exchange_total(): arrived = lax.ppermute(value, axis, pairs)  10.2 us
    pallas_call x1, Pallas kernels, head_attention(): pl.pallas_call(functools.partial(attention_block, scale_factor), grid=(wi...  8.77 us
    pallas_call x1, Pallas kernels, head_values_grad(): pl.pallas_call(functools.partial(value_block, scale_factor), grid=(width_...  8.75 us
    ppermute x3, starting transfers between devices, butterfly_total(): lax.ppermute(rounded, axis, pairs).astype(value.dtype)  7.67 us
  transfers between devices with their start and end apart: 22, of which 15 were waited for; matrix products, arithmetic and copies ran while one was open for 25% of the time, Pallas kernels for 6%

profile of v8, /device:TPU:0, one launch (start us, length us, event | category | flops | bytes accessed | tf_op | source)
XLA Modules:
  0.0 158.9 jit_solution(10908532749542486256)
XLA Ops:
  9.1 2.4 %collective-permute-start = (bf16[6,1024]{1,0:T(8,128)(2,1)S(1)}, bf16[6,1024]{1,0:T(8,128)(2,1)S(1)}, u32[]{:S(2)}, u32[]{:S(2)}) collective-permute-start(bf16[6,1024]{1,0:T(8,128)(2,1)S(1)} %slice.58), channel_id=1, source_target_pairs={{0,4},{4,8},{8,12},{12,16},{16,20},{20,24},{24,28},{1,5},{5,9},{9,... | collective-permute-start | bytes 36872 | tf_op jit(solution)/shard_map/ppermute | solution.py:30
  11.4 2.8 %rev.12 = f32[7,1024]{1,0:T(8,128)S(1)} reverse(f32[7,1024]{1,0:T(8,128)} %param.15), dimensions={0} | reverse | bytes 57344 | tf_op jit(solution)/shard_map/rev | solution.py:194
  16.5 4.5 %collective-permute-start.1 = (bf16[127,1024]{1,0:T(8,128)(2,1)S(1)}, bf16[127,1024]{1,0:T(8,128)(2,1)S(1)}, u32[]{:S(2)}, u32[]{:S(2)}) collective-permute-start(bf16[127,1024]{1,0:T(8,128)(2,1)S(1)} %slice.56), channel_id=1, source_target_pairs={{0,4},{4,8},{8,12},{12,16},{16,20},{20,24},{24,28},{1,5},{5,9},{9,... | collective-permute-start | bytes 780296 | tf_op jit(solution)/shard_map/ppermute | solution.py:30
  22.3 5.8 %fusion.8 = f32[1,128,1024]{2,0,1:T(1,128)S(1)} fusion(f32[1,255,1024]{2,1,0:T(8,128)S(1)} %maximum_bitcast_fusion, f32[128,1,1024]{2,0,1:T(8,128)S(1)} %bitcast.58), kind=kOutput, calls=%fused_computation.35 | convolution fusion | flops 201326592 | bytes 2093056 | tf_op jit(solution)/shard_map/conv_general_dilated | solution.py:34
  28.4 1.6 %collective-permute-start.2 = (f32[128]{0:T(128)S(1)}, f32[128]{0:T(128)S(1)}, u32[]{:S(2)}, u32[]{:S(2)}) collective-permute-start(f32[128]{0:T(128)S(1)} %get-tuple-element.31), channel_id=1, source_target_pairs={{0,1},{1,2},{2,3},{3,0},{4,5},{5,6},{6,7},{7,4},{8,9},{9,10},{10,1... | collective-permute-start | bytes 1544 | tf_op jit(solution)/shard_map/ppermute | solution.py:74
  30.0 2.6 %collective-permute-start.3 = (f32[128]{0:T(128)S(1)}, f32[128]{0:T(128)S(1)}, u32[]{:S(2)}, u32[]{:S(2)}) collective-permute-start(f32[128]{0:T(128)S(1)} %get-tuple-element.31), channel_id=1, source_target_pairs={{0,2},{1,3},{2,0},{3,1},{4,6},{5,7},{6,4},{7,5},{8,10},{9,11},{10,... | collective-permute-start | bytes 1544 | tf_op jit(solution)/shard_map/ppermute | solution.py:74
  34.4 1.7 %collective-permute-done.4 = f32[128]{0:T(128)S(1)} collective-permute-done((f32[128]{0:T(128)S(1)}, f32[128]{0:T(128)S(1)}, u32[]{:S(2)}, u32[]{:S(2)}) %collective-permute-start.4) | collective-permute-done | bytes 544 | tf_op jit(solution)/shard_map/ppermute | solution.py:74
  38.3 3.1 %all-gather.3.cloned.1.call-done.k_ref = bf16[1024,1024]{1,0:T(8,128)(2,1)} async-done(((bf16[128,1024]{1,0:T(8,128)(2,1)}), bf16[1024,1024]{1,0:T(8,128)(2,1)}) %all-gather.3.cloned.1.call-update) | async-done | bytes 2097168 | tf_op jit(solution)/shard_map/all_gather | solution.py:208
  41.4 8.7 %shard_map.203 = (bf16[1024,1024]{1,0:T(8,128)(2,1)}, bf16[8,128,1024]{2,1,0:T(8,128)(2,1)}) custom-call(bf16[128,1024]{1,0:T(8,128)(2,1)} %q_ref.3, bf16[1024,1024]{1,0:T(8,128)(2,1)} %all-gather.3.cloned.1.call-done.k_ref, bf16[128,1024]{1,0:T(8,128)(2,1)} %cot_ref.3, f32[128,1024]{1,0:T(8,128)} %fusion.33.vis_ref), custom_call_target="tpu_custom_call" | custom-call | tf_op jit(solution)/shard_map/pallas_call | solution.py:141
  58.2 5.5 %collective-permute-done.10 = bf16[128,1024]{1,0:T(8,128)(2,1)S(1)} collective-permute-done((bf16[128,1024]{1,0:T(8,128)(2,1)S(1)}, bf16[128,1024]{1,0:T(8,128)(2,1)S(1)}, u32[]{:S(2)}, u32[]{:S(2)}) %collective-permute-start.10) | collective-permute-done | bytes 262176 | tf_op jit(solution)/shard_map/ppermute | solution.py:30
  65.0 7.1 %collective-permute-done.6 = bf16[128,1024]{1,0:T(8,128)(2,1)S(1)} collective-permute-done((bf16[128,1024]{1,0:T(8,128)(2,1)S(1)}, bf16[128,1024]{1,0:T(8,128)(2,1)S(1)}, u32[]{:S(2)}, u32[]{:S(2)}) %collective-permute-start.6) | collective-permute-done | bytes 262176 | tf_op jit(solution)/shard_map/ppermute | solution.py:30
  72.1 3.8 %collective-permute-done.7 = bf16[128,1024]{1,0:T(8,128)(2,1)S(1)} collective-permute-done((bf16[128,1024]{1,0:T(8,128)(2,1)S(1)}, bf16[128,1024]{1,0:T(8,128)(2,1)S(1)}, u32[]{:S(2)}, u32[]{:S(2)}) %collective-permute-start.7) | collective-permute-done | bytes 262176 | tf_op jit(solution)/shard_map/ppermute | solution.py:30
  75.9 7.8 %collective-permute-done.8 = bf16[128,1024]{1,0:T(8,128)(2,1)S(1)} collective-permute-done((bf16[128,1024]{1,0:T(8,128)(2,1)S(1)}, bf16[128,1024]{1,0:T(8,128)(2,1)S(1)}, u32[]{:S(2)}, u32[]{:S(2)}) %collective-permute-start.8) | collective-permute-done | bytes 262176 | tf_op jit(solution)/shard_map/ppermute | solution.py:30
  85.3 8.8 %shard_map.204 = (bf16[1024,1024]{1,0:T(8,128)(2,1)}, f32[128,1024]{1,0:T(8,128)}, bf16[128,1024]{1,0:T(8,128)(2,1)}) custom-call(bf16[128,1024]{1,0:T(8,128)(2,1)} %q_ref.3, bf16[1024,1024]{1,0:T(8,128)(2,1)} %all-gather.3.cloned.1.call-done.k_ref, bf16[1024,1024]{1,0:T(8,128)(2,1)} %all-gather.5.cloned.1.call-done.v_ref, bf16[128,1024]{1,0:T(8,128)(2,1)} %cot_ref.3, ...), custom_call_target="tpu_custom_call" | custom-call | tf_op jit(solution)/shard_map/pallas_call | solution.py:157
  95.0 3.1 %collective-permute-start.12 = (f32[128]{0:T(128)S(1)}, f32[128]{0:T(128)S(1)}, u32[]{:S(2)}, u32[]{:S(2)}) collective-permute-start(f32[128]{0:T(128)S(1)} %get-tuple-element.26), channel_id=1, source_target_pairs={{0,2},{1,3},{2,0},{3,1},{4,6},{5,7},{6,4},{7,5},{8,10},{9,11},{10,... | collective-permute-start | bytes 1544 | tf_op jit(solution)/shard_map/ppermute | solution.py:74
  99.7 1.9 %collective-permute-done.13 = f32[128]{0:T(128)S(1)} collective-permute-done((f32[128]{0:T(128)S(1)}, f32[128]{0:T(128)S(1)}, u32[]{:S(2)}, u32[]{:S(2)}) %collective-permute-start.13) | collective-permute-done | bytes 544 | tf_op jit(solution)/shard_map/ppermute | solution.py:74
  101.7 2.3 %fusion.25 = (bf16[128,1024]{1,0:T(8,128)(2,1)}, f32[128,1024]{1,0:T(8,128)S(1)}, bf16[128,1024]{1,0:T(8,128)(2,1)}) fusion(f32[1,128,1024]{2,0,1:T(1,128)S(1)} %fusion.8, f32[128]{0:T(128)S(1)} %fusion.42, bf16[128,1024]{1,0:T(8,128)(2,1)S(1)} %get-tuple-element.32, f32[128,1024]{1,0:T(8,128)S(1)} %convert_add_fusion.4, f32[1024]{0:T(1024)S(1)} %copy-done.14, ...), kind=kLoop, calls=%fused_computation.58 | loop fusion | flops 1441792 | bytes 3150848 | tf_op jit(solution)/shard_map/convert_element_type | solution.py:241
  106.1 5.8 %fusion.6 = bf16[1,128,1024]{2,0,1:T(2,128)(2,1)S(1)} fusion(f32[1,255,1024]{2,1,0:T(8,128)S(1)} %copy-done.4, f32[128,1,1024]{2,0,1:T(8,128)S(1)} %bitcast.54), kind=kOutput, calls=%fused_computation.33 | convolution fusion | flops 201326592 | bytes 1830912 | tf_op jit(solution)/shard_map/conv_general_dilated | solution.py:34
  113.1 5.8 %fusion = f32[1,128,1024]{2,0,1:T(1,128)S(1)} fusion(f32[1,255,1024]{2,1,0:T(8,128)S(1)} %maximum_bitcast_fusion.1, f32[128,1,1024]{2,0,1:T(8,128)S(1)} %bitcast.57), kind=kOutput, calls=%fused_computation.9 | convolution fusion | flops 201326592 | bytes 2093056 | tf_op jit(solution)/shard_map/conv_general_dilated | solution.py:34
  121.5 3.8 %collective-permute-start.16 = (bf16[136,1024]{1,0:T(8,128)(2,1)S(1)}, bf16[136,1024]{1,0:T(8,128)(2,1)S(1)}, u32[]{:S(2)}, u32[]{:S(2)}) collective-permute-start(bf16[136,1024]{1,0:T(8,128)(2,1)S(1)} %pad_maximum_fusion), channel_id=1, source_target_pairs={{0,4},{4,0},{8,12},{12,8},{16,20},{20,16},{24,28},{28,24},{1,5},{5... | collective-permute-start | bytes 835592 | tf_op jit(solution)/shard_map/ppermute | solution.py:62
  126.6 3.0 %collective-permute-start.17 = (bf16[136,1024]{1,0:T(8,128)(2,1)S(1)}, bf16[136,1024]{1,0:T(8,128)(2,1)S(1)}, u32[]{:S(2)}, u32[]{:S(2)}) collective-permute-start(bf16[136,1024]{1,0:T(8,128)(2,1)S(1)} %add_convert_fusion.1), channel_id=1, source_target_pairs={{0,8},{4,12},{8,0},{12,4},{16,24},{20,28},{24,16},{28,20},{1,9},{5... | collective-permute-start | bytes 835592 | tf_op jit(solution)/shard_map/ppermute | solution.py:62
  130.9 1.8 %collective-permute-done.15 = bf16[6,1024]{1,0:T(8,128)(2,1)S(1)} collective-permute-done((bf16[6,1024]{1,0:T(8,128)(2,1)S(1)}, bf16[6,1024]{1,0:T(8,128)(2,1)S(1)}, u32[]{:S(2)}, u32[]{:S(2)}) %collective-permute-start.15) | collective-permute-done | bytes 12320 | tf_op jit(solution)/shard_map/ppermute | solution.py:30
  133.6 3.2 %collective-permute-done.17 = bf16[136,1024]{1,0:T(8,128)(2,1)S(1)} collective-permute-done((bf16[136,1024]{1,0:T(8,128)(2,1)S(1)}, bf16[136,1024]{1,0:T(8,128)(2,1)S(1)}, u32[]{:S(2)}, u32[]{:S(2)}) %collective-permute-start.17) | collective-permute-done | bytes 278560 | tf_op jit(solution)/shard_map/ppermute | solution.py:62
  139.9 9.4 %collective-permute-done.18 = bf16[136,1024]{1,0:T(8,128)(2,1)} collective-permute-done((bf16[136,1024]{1,0:T(8,128)(2,1)S(1)}, bf16[136,1024]{1,0:T(8,128)(2,1)}, u32[]{:S(2)}, u32[]{:S(2)}) %collective-permute-start.18) | collective-permute-done | bytes 278560 | tf_op jit(solution)/shard_map/ppermute | solution.py:62
  (128 shorter events, 38.2 us)
Async XLA Ops:
  7.2 34.2 %all-gather.3.cloned.1.call-start = ((), (), s32[]{:S(2)}) async-start(), calls=%async_computation.1 | async-start | bytes 2359296 | tf_op jit(solution)/shard_map/all_gather | solution.py:208
  7.9 77.4 %all-gather.5.cloned.1.call-start = ((), (), s32[]{:S(2)}) async-start(), calls=%async_computation.2 | async-start | bytes 2359296 | tf_op jit(solution)/shard_map/all_gather | solution.py:221
  9.1 5.2 %collective-permute-start = (bf16[6,1024]{1,0:T(8,128)(2,1)S(1)}, bf16[6,1024]{1,0:T(8,128)(2,1)S(1)}, u32[]{:S(2)}, u32[]{:S(2)}) collective-permute-start(bf16[6,1024]{1,0:T(8,128)(2,1)S(1)} %slice.58), channel_id=1, source_target_pairs={{0,4},{4,8},{8,12},{12,16},{16,20},{20,24},{24,28},{1,5},{5,9},{9,... | collective-permute-start | bytes 36872 | tf_op jit(solution)/shard_map/ppermute | solution.py:30
  16.5 5.7 %collective-permute-start.1 = (bf16[127,1024]{1,0:T(8,128)(2,1)S(1)}, bf16[127,1024]{1,0:T(8,128)(2,1)S(1)}, u32[]{:S(2)}, u32[]{:S(2)}) collective-permute-start(bf16[127,1024]{1,0:T(8,128)(2,1)S(1)} %slice.56), channel_id=1, source_target_pairs={{0,4},{4,8},{8,12},{12,16},{16,20},{20,24},{24,28},{1,5},{5,9},{9,... | collective-permute-start | bytes 780296 | tf_op jit(solution)/shard_map/ppermute | solution.py:30
  22.3 13.9 %copy-start.14 = (f32[1024]{0:T(1024)S(1)}, f32[1024]{0:T(1024)}, u32[]{:S(2)}) copy-start(f32[1024]{0:T(1024)} %param.19) | copy-start | bytes 12292
  28.1 9.1 %copy-start.16 = (s32[1024]{0:T(1024)S(1)}, s32[1024]{0:T(1024)}, u32[]{:S(2)}) copy-start(s32[1024]{0:T(1024)} %param.22) | copy-start | bytes 12292
  28.4 5.6 %collective-permute-start.2 = (f32[128]{0:T(128)S(1)}, f32[128]{0:T(128)S(1)}, u32[]{:S(2)}, u32[]{:S(2)}) collective-permute-start(f32[128]{0:T(128)S(1)} %get-tuple-element.31), channel_id=1, source_target_pairs={{0,1},{1,2},{2,3},{3,0},{4,5},{5,6},{6,7},{7,4},{8,9},{9,10},{10,1... | collective-permute-start | bytes 1544 | tf_op jit(solution)/shard_map/ppermute | solution.py:74
  30.0 4.4 %collective-permute-start.3 = (f32[128]{0:T(128)S(1)}, f32[128]{0:T(128)S(1)}, u32[]{:S(2)}, u32[]{:S(2)}) collective-permute-start(f32[128]{0:T(128)S(1)} %get-tuple-element.31), channel_id=1, source_target_pairs={{0,2},{1,3},{2,0},{3,1},{4,6},{5,7},{6,4},{7,5},{8,10},{9,11},{10,... | collective-permute-start | bytes 1544 | tf_op jit(solution)/shard_map/ppermute | solution.py:74
  32.6 3.5 %collective-permute-start.4 = (f32[128]{0:T(128)S(1)}, f32[128]{0:T(128)S(1)}, u32[]{:S(2)}, u32[]{:S(2)}) collective-permute-start(f32[128]{0:T(128)S(1)} %get-tuple-element.31), channel_id=1, source_target_pairs={{0,3},{1,0},{2,1},{3,2},{4,7},{5,4},{6,5},{7,6},{8,11},{9,8},{10,9... | collective-permute-start | bytes 1544 | tf_op jit(solution)/shard_map/ppermute | solution.py:74
  37.0 115.3 %reduce-scatter.2.cloned.1.call-start = ((), (), s32[]{:S(2)}) async-start(), calls=%async_computation.3 | async-start | bytes 2359296 | tf_op jit(solution)/shard_map/reduce_scatter | solution.py:227
  51.7 12.0 %collective-permute-start.10 = (bf16[128,1024]{1,0:T(8,128)(2,1)S(1)}, bf16[128,1024]{1,0:T(8,128)(2,1)S(1)}, u32[]{:S(2)}, u32[]{:S(2)}) collective-permute-start(bf16[128,1024]{1,0:T(8,128)(2,1)S(1)} %get-tuple-element.36), channel_id=1, source_target_pairs={{24,0},{28,4},{25,1},{29,5},{26,2},{30,6},{27,3},{31,7}} | collective-permute-start | bytes 786440 | tf_op jit(solution)/shard_map/ppermute | solution.py:30
  53.0 12.0 %collective-permute-start.5 = (bf16[128,1024]{1,0:T(8,128)(2,1)S(1)}, bf16[128,1024]{1,0:T(8,128)(2,1)S(1)}, u32[]{:S(2)}, u32[]{:S(2)}) collective-permute-start(bf16[128,1024]{1,0:T(8,128)(2,1)S(1)} %get-tuple-element.35), channel_id=1, source_target_pairs={{4,0},{8,4},{12,8},{16,12},{20,16},{24,20},{28,24},{5,1},{9,5},{13... | collective-permute-start | bytes 786440 | tf_op jit(solution)/shard_map/ppermute | solution.py:30
  54.3 17.8 %collective-permute-start.6 = (bf16[128,1024]{1,0:T(8,128)(2,1)S(1)}, bf16[128,1024]{1,0:T(8,128)(2,1)S(1)}, u32[]{:S(2)}, u32[]{:S(2)}) collective-permute-start(bf16[128,1024]{1,0:T(8,128)(2,1)S(1)} %get-tuple-element.40), channel_id=1, source_target_pairs={{8,0},{12,4},{16,8},{20,12},{24,16},{28,20},{9,1},{13,5},{17,9},{2... | collective-permute-start | bytes 786440 | tf_op jit(solution)/shard_map/ppermute | solution.py:30
  55.6 20.3 %collective-permute-start.7 = (bf16[128,1024]{1,0:T(8,128)(2,1)S(1)}, bf16[128,1024]{1,0:T(8,128)(2,1)S(1)}, u32[]{:S(2)}, u32[]{:S(2)}) collective-permute-start(bf16[128,1024]{1,0:T(8,128)(2,1)S(1)} %get-tuple-element.39), channel_id=1, source_target_pairs={{12,0},{16,4},{20,8},{24,12},{28,16},{13,1},{17,5},{21,9},{25,13},... | collective-permute-start | bytes 786440 | tf_op jit(solution)/shard_map/ppermute | solution.py:30
  56.9 26.8 %collective-permute-start.8 = (bf16[128,1024]{1,0:T(8,128)(2,1)S(1)}, bf16[128,1024]{1,0:T(8,128)(2,1)S(1)}, u32[]{:S(2)}, u32[]{:S(2)}) collective-permute-start(bf16[128,1024]{1,0:T(8,128)(2,1)S(1)} %get-tuple-element.38), channel_id=1, source_target_pairs={{16,0},{20,4},{24,8},{28,12},{17,1},{21,5},{25,9},{29,13},{18,2},{... | collective-permute-start | bytes 786440 | tf_op jit(solution)/shard_map/ppermute | solution.py:30
  63.7 20.4 %collective-permute-start.9 = (bf16[128,1024]{1,0:T(8,128)(2,1)S(1)}, bf16[128,1024]{1,0:T(8,128)(2,1)S(1)}, u32[]{:S(2)}, u32[]{:S(2)}) collective-permute-start(bf16[128,1024]{1,0:T(8,128)(2,1)S(1)} %get-tuple-element.37), channel_id=1, source_target_pairs={{20,0},{24,4},{28,8},{21,1},{25,5},{29,9},{22,2},{26,6},{30,10},{2... | collective-permute-start | bytes 786440 | tf_op jit(solution)/shard_map/ppermute | solution.py:30
  94.3 5.4 %collective-permute-start.11 = (f32[128]{0:T(128)S(1)}, f32[128]{0:T(128)S(1)}, u32[]{:S(2)}, u32[]{:S(2)}) collective-permute-start(f32[128]{0:T(128)S(1)} %get-tuple-element.26), channel_id=1, source_target_pairs={{0,1},{1,2},{2,3},{3,0},{4,5},{5,6},{6,7},{7,4},{8,9},{9,10},{10,1... | collective-permute-start | bytes 1544 | tf_op jit(solution)/shard_map/ppermute | solution.py:74
  95.0 4.6 %collective-permute-start.12 = (f32[128]{0:T(128)S(1)}, f32[128]{0:T(128)S(1)}, u32[]{:S(2)}, u32[]{:S(2)}) collective-permute-start(f32[128]{0:T(128)S(1)} %get-tuple-element.26), channel_id=1, source_target_pairs={{0,2},{1,3},{2,0},{3,1},{4,6},{5,7},{6,4},{7,5},{8,10},{9,11},{10,... | collective-permute-start | bytes 1544 | tf_op jit(solution)/shard_map/ppermute | solution.py:74
  98.1 3.5 %collective-permute-start.13 = (f32[128]{0:T(128)S(1)}, f32[128]{0:T(128)S(1)}, u32[]{:S(2)}, u32[]{:S(2)}) collective-permute-start(f32[128]{0:T(128)S(1)} %get-tuple-element.26), channel_id=1, source_target_pairs={{0,3},{1,0},{2,1},{3,2},{4,7},{5,4},{6,5},{7,6},{8,11},{9,8},{10,9... | collective-permute-start | bytes 1544 | tf_op jit(solution)/shard_map/ppermute | solution.py:74
  104.8 7.5 %collective-permute-start.14 = (bf16[127,1024]{1,0:T(8,128)(2,1)}, bf16[127,1024]{1,0:T(8,128)(2,1)S(1)}, u32[]{:S(2)}, u32[]{:S(2)}) collective-permute-start(bf16[127,1024]{1,0:T(8,128)(2,1)} %slice.55), channel_id=1, source_target_pairs={{4,0},{8,4},{12,8},{16,12},{20,16},{24,20},{28,24},{5,1},{9,5},{13... | collective-permute-start | bytes 780296 | tf_op jit(solution)/shard_map/ppermute | solution.py:30
  121.5 5.0 %collective-permute-start.16 = (bf16[136,1024]{1,0:T(8,128)(2,1)S(1)}, bf16[136,1024]{1,0:T(8,128)(2,1)S(1)}, u32[]{:S(2)}, u32[]{:S(2)}) collective-permute-start(bf16[136,1024]{1,0:T(8,128)(2,1)S(1)} %pad_maximum_fusion), channel_id=1, source_target_pairs={{0,4},{4,0},{8,12},{12,8},{16,20},{20,16},{24,28},{28,24},{1,5},{5... | collective-permute-start | bytes 835592 | tf_op jit(solution)/shard_map/ppermute | solution.py:62
  126.6 10.1 %collective-permute-start.17 = (bf16[136,1024]{1,0:T(8,128)(2,1)S(1)}, bf16[136,1024]{1,0:T(8,128)(2,1)S(1)}, u32[]{:S(2)}, u32[]{:S(2)}) collective-permute-start(bf16[136,1024]{1,0:T(8,128)(2,1)S(1)} %add_convert_fusion.1), channel_id=1, source_target_pairs={{0,8},{4,12},{8,0},{12,4},{16,24},{20,28},{24,16},{28,20},{1,9},{5... | collective-permute-start | bytes 835592 | tf_op jit(solution)/shard_map/ppermute | solution.py:62
  129.6 3.1 %collective-permute-start.15 = (bf16[6,1024]{1,0:T(8,128)(2,1)S(1)}, bf16[6,1024]{1,0:T(8,128)(2,1)S(1)}, u32[]{:S(2)}, u32[]{:S(2)}) collective-permute-start(bf16[6,1024]{1,0:T(8,128)(2,1)S(1)} %slice.57), channel_id=1, source_target_pairs={{4,0},{8,4},{12,8},{16,12},{20,16},{24,20},{28,24},{5,1},{9,5},{13... | collective-permute-start | bytes 36872 | tf_op jit(solution)/shard_map/ppermute | solution.py:30
  136.9 12.4 %collective-permute-start.18 = (bf16[136,1024]{1,0:T(8,128)(2,1)S(1)}, bf16[136,1024]{1,0:T(8,128)(2,1)}, u32[]{:S(2)}, u32[]{:S(2)}) collective-permute-start(bf16[136,1024]{1,0:T(8,128)(2,1)S(1)} %add_convert_fusion), channel_id=1, source_target_pairs={{0,16},{4,20},{8,24},{12,28},{16,0},{20,4},{24,8},{28,12},{1,17},{... | collective-permute-start | bytes 835592 | tf_op jit(solution)/shard_map/ppermute | solution.py:62
  (16 other events, 52.6 us)
Sparse Core Ops, SparseCore 0:
  9.9 31.4 all-gather.2
  43.9 33.6 all-gather.4
  99.0 49.1 reduce-scatter.1

commit v9 on v7

--- a/solution.py
+++ b/solution.py
@@ -208,11 +208,12 @@
     visible = (key_pos[None, :] <= query_pos[:, None]) & (segments[None, :] == query_seg[:, None])
     mask = visible.astype(jnp.float32)
     value_part = head_values_grad(queries, keys_whole, cotangent, mask, scale_factor)
-    value_grad = lax.dynamic_slice_in_dim(value_part, position, local_rows, 0).astype(jnp.float32)
-    for distance in range(1, reach + 1):
-        block_start = ((ctx_index - distance) % ctx_count) * local_rows
-        leaving = lax.dynamic_slice_in_dim(value_part, block_start, local_rows, 0)
-        value_grad = value_grad + passed_along(leaving, "ctx", -distance).astype(jnp.float32)
+    value_grad = (
+        lax.all_to_all(value_part, "ctx", 0, 0, tiled=True)
+        .reshape(ctx_count, local_rows, width_local)
+        .astype(jnp.float32)
+        .sum(axis=0)
+    )
     values_whole = lax.all_gather(normed, "ctx", axis=0, tiled=True)
     key_part, attended_all, queries_grad = head_attention(
         queries, keys_whole, values_whole, cotangent, mask, scale_factor

time: 158 us -> 154 us (0.975)
  waiting for transfers between devices: 41.1 us -> 51.7 us
  starting transfers between devices: 39.4 us -> 29.7 us
  other arithmetic: 12.9 us -> 9.97 us
    all_gather x1, waiting for transfers between devices: 2.56 us -> 26.8 us  [shards(): values_whole = lax.all_gather(normed, 'ctx', axis=0, tiled=True)]
    ppermute x10 -> x4, waiting for transfers between devices: 19.4 us -> 2.58 us  [passed_along(): lax.ppermute(value, axis, [(source, source + steps) for source in range(l...]
    ppermute x10 -> x4, starting transfers between devices: 17.2 us -> 9.57 us  [passed_along(): lax.ppermute(value, axis, [(source, source + steps) for source in range(l...]
    ppermute x3, starting transfers between devices: 11.3 us -> 4.21 us  [butterfly_total(): lax.ppermute(rounded, axis, pairs).astype(value.dtype)]
    all_to_all x0 -> x1, starting transfers between devices: none -> 5.84 us  [shards(): lax.all_to_all(value_part, 'ctx', 0, 0, tiled=True)]
    ppermute x3, waiting for transfers between devices: 10.1 us -> 13.4 us  [butterfly_total(): lax.ppermute(rounded, axis, pairs).astype(value.dtype)]
  transfers between devices with their start and end apart: 22 -> 17, of which waited for: 15 -> 11; matrix products, arithmetic and copies ran while one was open for 26% -> 23% of each run, Pallas kernels for 6% -> 13%
where the time goes in v9:
time: 154 us; the launch traced here: 153 us
  waiting for transfers between devices  51.7 us (34%)
  starting transfers between devices  29.7 us (19%)
  matrix products  19.6 us (13%)
  Pallas kernels  19.3 us (13%)
  between operations  14.4 us (9%)
  other arithmetic  9.97 us (6%)
  local copies, waits for them, and re-layouts  8.45 us (5%)
    all_gather x1, waiting for transfers between devices, shards(): values_whole = lax.all_gather(normed, 'ctx', axis=0, tiled=True)  26.8 us
    conv_general_dilated x6, matrix products, depthwise(): lax.conv_general_dilated(padded[None], tap_rows[:, None, :], (1,), 'VALID...  19.6 us
    ppermute x3, waiting for transfers between devices, butterfly_total(): lax.ppermute(rounded, axis, pairs).astype(value.dtype)  13.4 us
    pallas_call x1, Pallas kernels, head_attention(): pl.pallas_call(functools.partial(attention_block, scale_factor), grid=(wi...  10.5 us
    ppermute x6, starting transfers between devices, exchange_total(): arrived = lax.ppermute(value, axis, pairs)  9.94 us
    ppermute x4, starting transfers between devices, passed_along(): lax.ppermute(value, axis, [(source, source + steps) for source in range(l...  9.57 us
    pallas_call x1, Pallas kernels, head_values_grad(): pl.pallas_call(functools.partial(value_block, scale_factor), grid=(width_...  8.79 us
    all_to_all x1, starting transfers between devices, shards(): lax.all_to_all(value_part, 'ctx', 0, 0, tiled=True)  5.84 us
  transfers between devices with their start and end apart: 17, of which 11 were waited for; matrix products, arithmetic and copies ran while one was open for 23% of the time, Pallas kernels for 13%

profile of v9, /device:TPU:0, one launch (start us, length us, event | category | flops | bytes accessed | tf_op | source)
XLA Modules:
  0.0 153.2 jit_solution(14502516230156199407)
XLA Ops:
  9.1 2.4 %collective-permute-start = (bf16[6,1024]{1,0:T(8,128)(2,1)S(1)}, bf16[6,1024]{1,0:T(8,128)(2,1)S(1)}, u32[]{:S(2)}, u32[]{:S(2)}) collective-permute-start(bf16[6,1024]{1,0:T(8,128)(2,1)S(1)} %slice.58), channel_id=1, source_target_pairs={{0,4},{4,8},{8,12},{12,16},{16,20},{20,24},{24,28},{1,5},{5,9},{9,... | collective-permute-start | bytes 36872 | tf_op jit(solution)/shard_map/ppermute | solution.py:30
  11.4 2.8 %rev.12 = f32[7,1024]{1,0:T(8,128)S(1)} reverse(f32[7,1024]{1,0:T(8,128)} %param.15), dimensions={0} | reverse | bytes 57344 | tf_op jit(solution)/shard_map/rev | solution.py:189
  15.9 4.7 %collective-permute-start.1 = (bf16[127,1024]{1,0:T(8,128)(2,1)S(1)}, bf16[127,1024]{1,0:T(8,128)(2,1)S(1)}, u32[]{:S(2)}, u32[]{:S(2)}) collective-permute-start(bf16[127,1024]{1,0:T(8,128)(2,1)S(1)} %slice.56), channel_id=1, source_target_pairs={{0,4},{4,8},{8,12},{12,16},{16,20},{20,24},{24,28},{1,5},{5,9},{9,... | collective-permute-start | bytes 780296 | tf_op jit(solution)/shard_map/ppermute | solution.py:30
  21.9 5.8 %fusion.8 = f32[1,128,1024]{2,0,1:T(1,128)S(1)} fusion(f32[1,255,1024]{2,1,0:T(8,128)S(1)} %maximum_bitcast_fusion, f32[128,1,1024]{2,0,1:T(8,128)S(1)} %bitcast.60), kind=kOutput, calls=%fused_computation.36 | convolution fusion | flops 201326592 | bytes 2093056 | tf_op jit(solution)/shard_map/conv_general_dilated | solution.py:34
  28.7 1.6 %collective-permute-start.2 = (f32[128]{0:T(128)S(1)}, f32[128]{0:T(128)S(1)}, u32[]{:S(2)}, u32[]{:S(2)}) collective-permute-start(f32[128]{0:T(128)S(1)} %get-tuple-element.27), channel_id=1, source_target_pairs={{0,1},{1,2},{2,3},{3,0},{4,5},{5,6},{6,7},{7,4},{8,9},{9,10},{10,1... | collective-permute-start | bytes 1544 | tf_op jit(solution)/shard_map/ppermute | solution.py:74
  30.3 2.6 %collective-permute-start.3 = (f32[128]{0:T(128)S(1)}, f32[128]{0:T(128)S(1)}, u32[]{:S(2)}, u32[]{:S(2)}) collective-permute-start(f32[128]{0:T(128)S(1)} %get-tuple-element.27), channel_id=1, source_target_pairs={{0,2},{1,3},{2,0},{3,1},{4,6},{5,7},{6,4},{7,5},{8,10},{9,11},{10,... | collective-permute-start | bytes 1544 | tf_op jit(solution)/shard_map/ppermute | solution.py:74
  32.9 1.3 collective-permute-start.4
  34.8 1.7 %collective-permute-done.4 = f32[128]{0:T(128)S(1)} collective-permute-done((f32[128]{0:T(128)S(1)}, f32[128]{0:T(128)S(1)}, u32[]{:S(2)}, u32[]{:S(2)}) %collective-permute-start.4) | collective-permute-done | bytes 544 | tf_op jit(solution)/shard_map/ppermute | solution.py:74
  38.5 3.2 %all-gather.3.cloned.1.call-done.k_ref = bf16[1024,1024]{1,0:T(8,128)(2,1)} async-done(((bf16[128,1024]{1,0:T(8,128)(2,1)}), bf16[1024,1024]{1,0:T(8,128)(2,1)}) %all-gather.3.cloned.1.call-update) | async-done | bytes 2097168 | tf_op jit(solution)/shard_map/all_gather | solution.py:203
  41.7 8.8 %shard_map.204 = bf16[1024,1024]{1,0:T(8,128)(2,1)} custom-call(bf16[128,1024]{1,0:T(8,128)(2,1)} %q_ref.3, bf16[1024,1024]{1,0:T(8,128)(2,1)} %all-gather.3.cloned.1.call-done.k_ref, bf16[128,1024]{1,0:T(8,128)(2,1)} %cot_ref.3, f32[128,1024]{1,0:T(8,128)} %fusion.33.vis_ref), custom_call_target="tpu_custom_call" | custom-call | tf_op jit(solution)/shard_map/pallas_call | solution.py:139
  50.5 5.8 %all-to-all-start = ((bf16[8,128,1024]{2,1,0:T(8,128)(2,1)}), bf16[8,128,1024]{2,1,0:T(8,128)(2,1)S(1)}, u32[]{:S(2)}, u32[]{:S(2)}) async-start(bf16[8,128,1024]{2,1,0:T(8,128)(2,1)} %bitcast.55), calls=%async_computation | async-start | bytes 4194304 | tf_op jit(solution)/shard_map/all_to_all | solution.py:212
  56.4 26.8 %all-gather.5.cloned.1.call-done.v_ref = bf16[1024,1024]{1,0:T(8,128)(2,1)} async-done(((bf16[128,1024]{1,0:T(8,128)(2,1)}), bf16[1024,1024]{1,0:T(8,128)(2,1)}) %all-gather.5.cloned.1.call-update) | async-done | bytes 2097168 | tf_op jit(solution)/shard_map/all_gather | solution.py:217
  83.2 10.5 %shard_map.203 = (bf16[1024,1024]{1,0:T(8,128)(2,1)}, f32[128,1024]{1,0:T(8,128)}, bf16[128,1024]{1,0:T(8,128)(2,1)}) custom-call(bf16[128,1024]{1,0:T(8,128)(2,1)} %q_ref.3, bf16[1024,1024]{1,0:T(8,128)(2,1)} %all-gather.3.cloned.1.call-done.k_ref, bf16[1024,1024]{1,0:T(8,128)(2,1)} %all-gather.5.cloned.1.call-done.v_ref, bf16[128,1024]{1,0:T(8,128)(2,1)} %cot_ref.3, ...), custom_call_target="tpu_custom_call" | custom-call | tf_op jit(solution)/shard_map/pallas_call | solution.py:152
  95.2 2.9 %collective-permute-start.6 = (f32[128]{0:T(128)S(1)}, f32[128]{0:T(128)S(1)}, u32[]{:S(2)}, u32[]{:S(2)}) collective-permute-start(f32[128]{0:T(128)S(1)} %get-tuple-element.22), channel_id=1, source_target_pairs={{0,2},{1,3},{2,0},{3,1},{4,6},{5,7},{6,4},{7,5},{8,10},{9,11},{10,... | collective-permute-start | bytes 1544 | tf_op jit(solution)/shard_map/ppermute | solution.py:74
  99.7 2.0 %collective-permute-done.7 = f32[128]{0:T(128)S(1)} collective-permute-done((f32[128]{0:T(128)S(1)}, f32[128]{0:T(128)S(1)}, u32[]{:S(2)}, u32[]{:S(2)}) %collective-permute-start.7) | collective-permute-done | bytes 544 | tf_op jit(solution)/shard_map/ppermute | solution.py:74
  103.8 1.3 collective-permute-start.8
  105.1 5.8 %fusion.6 = bf16[1,128,1024]{2,0,1:T(2,128)(2,1)S(1)} fusion(f32[1,255,1024]{2,1,0:T(8,128)S(1)} %copy-done.9, f32[128,1,1024]{2,0,1:T(8,128)S(1)} %bitcast.56), kind=kOutput, calls=%fused_computation.34 | convolution fusion | flops 201326592 | bytes 1830912 | tf_op jit(solution)/shard_map/conv_general_dilated | solution.py:34
  111.9 5.8 %fusion = f32[1,128,1024]{2,0,1:T(1,128)S(1)} fusion(f32[1,255,1024]{2,1,0:T(8,128)S(1)} %maximum_bitcast_fusion.1, f32[128,1,1024]{2,0,1:T(8,128)S(1)} %bitcast.59), kind=kOutput, calls=%fused_computation.10 | convolution fusion | flops 201326592 | bytes 2093056 | tf_op jit(solution)/shard_map/conv_general_dilated | solution.py:34
  122.8 1.7 %collective-permute-start.11 = (bf16[136,1024]{1,0:T(8,128)(2,1)S(1)}, bf16[136,1024]{1,0:T(8,128)(2,1)S(1)}, u32[]{:S(2)}, u32[]{:S(2)}) collective-permute-start(bf16[136,1024]{1,0:T(8,128)(2,1)S(1)} %add_convert_fusion.1), channel_id=1, source_target_pairs={{0,8},{4,12},{8,0},{12,4},{16,24},{20,28},{24,16},{28,20},{1,9},{5... | collective-permute-start | bytes 835592 | tf_op jit(solution)/shard_map/ppermute | solution.py:62
  124.5 1.3 collective-permute-start.9
  125.8 1.8 %collective-permute-done.9 = bf16[6,1024]{1,0:T(8,128)(2,1)S(1)} collective-permute-done((bf16[6,1024]{1,0:T(8,128)(2,1)S(1)}, bf16[6,1024]{1,0:T(8,128)(2,1)S(1)}, u32[]{:S(2)}, u32[]{:S(2)}) %collective-permute-start.9) | collective-permute-done | bytes 12320 | tf_op jit(solution)/shard_map/ppermute | solution.py:30
  128.5 3.6 %collective-permute-done.11 = bf16[136,1024]{1,0:T(8,128)(2,1)S(1)} collective-permute-done((bf16[136,1024]{1,0:T(8,128)(2,1)S(1)}, bf16[136,1024]{1,0:T(8,128)(2,1)S(1)}, u32[]{:S(2)}, u32[]{:S(2)}) %collective-permute-start.11) | collective-permute-done | bytes 278560 | tf_op jit(solution)/shard_map/ppermute | solution.py:62
  132.2 1.5 %collective-permute-start.12 = (bf16[136,1024]{1,0:T(8,128)(2,1)S(1)}, bf16[136,1024]{1,0:T(8,128)(2,1)S(1)}, u32[]{:S(2)}, u32[]{:S(2)}) collective-permute-start(bf16[136,1024]{1,0:T(8,128)(2,1)S(1)} %add_convert_fusion), channel_id=1, source_target_pairs={{0,16},{4,20},{8,24},{12,28},{16,0},{20,4},{24,8},{28,12},{1,17},{... | collective-permute-start | bytes 835592 | tf_op jit(solution)/shard_map/ppermute | solution.py:62
  135.9 8.6 %collective-permute-done.12 = bf16[136,1024]{1,0:T(8,128)(2,1)S(1)} collective-permute-done((bf16[136,1024]{1,0:T(8,128)(2,1)S(1)}, bf16[136,1024]{1,0:T(8,128)(2,1)S(1)}, u32[]{:S(2)}, u32[]{:S(2)}) %collective-permute-start.12) | collective-permute-done | bytes 278560 | tf_op jit(solution)/shard_map/ppermute | solution.py:62
  (129 shorter events, 24.6 us)
Async XLA Ops:
  7.2 34.5 %all-gather.3.cloned.1.call-start = ((), (), s32[]{:S(2)}) async-start(), calls=%async_computation.2 | async-start | bytes 2359296 | tf_op jit(solution)/shard_map/all_gather | solution.py:203
  7.9 75.3 %all-gather.5.cloned.1.call-start = ((), (), s32[]{:S(2)}) async-start(), calls=%async_computation.3 | async-start | bytes 2359296 | tf_op jit(solution)/shard_map/all_gather | solution.py:217
  9.1 5.2 %collective-permute-start = (bf16[6,1024]{1,0:T(8,128)(2,1)S(1)}, bf16[6,1024]{1,0:T(8,128)(2,1)S(1)}, u32[]{:S(2)}, u32[]{:S(2)}) collective-permute-start(bf16[6,1024]{1,0:T(8,128)(2,1)S(1)} %slice.58), channel_id=1, source_target_pairs={{0,4},{4,8},{8,12},{12,16},{16,20},{20,24},{24,28},{1,5},{5,9},{9,... | collective-permute-start | bytes 36872 | tf_op jit(solution)/shard_map/ppermute | solution.py:30
  15.9 5.8 %collective-permute-start.1 = (bf16[127,1024]{1,0:T(8,128)(2,1)S(1)}, bf16[127,1024]{1,0:T(8,128)(2,1)S(1)}, u32[]{:S(2)}, u32[]{:S(2)}) collective-permute-start(bf16[127,1024]{1,0:T(8,128)(2,1)S(1)} %slice.56), channel_id=1, source_target_pairs={{0,4},{4,8},{8,12},{12,16},{16,20},{20,24},{24,28},{1,5},{5,9},{9,... | collective-permute-start | bytes 780296 | tf_op jit(solution)/shard_map/ppermute | solution.py:30
  21.9 6.6 %copy-start.6 = (bf16[128,1024]{1,0:T(8,128)(2,1)S(1)}, bf16[128,1024]{1,0:T(8,128)(2,1)}, u32[]{:S(2)}) copy-start(bf16[128,1024]{1,0:T(8,128)(2,1)} %param.16) | copy-start | bytes 786436
  21.9 14.6 %copy-start.20 = (f32[1024]{0:T(1024)S(1)}, f32[1024]{0:T(1024)}, u32[]{:S(2)}) copy-start(f32[1024]{0:T(1024)} %param.19) | copy-start | bytes 12292
  27.7 9.7 %copy-start.22 = (s32[1024]{0:T(1024)S(1)}, s32[1024]{0:T(1024)}, u32[]{:S(2)}) copy-start(s32[1024]{0:T(1024)} %param.22) | copy-start | bytes 12292
  28.7 5.6 %collective-permute-start.2 = (f32[128]{0:T(128)S(1)}, f32[128]{0:T(128)S(1)}, u32[]{:S(2)}, u32[]{:S(2)}) collective-permute-start(f32[128]{0:T(128)S(1)} %get-tuple-element.27), channel_id=1, source_target_pairs={{0,1},{1,2},{2,3},{3,0},{4,5},{5,6},{6,7},{7,4},{8,9},{9,10},{10,1... | collective-permute-start | bytes 1544 | tf_op jit(solution)/shard_map/ppermute | solution.py:74
  30.3 4.4 %collective-permute-start.3 = (f32[128]{0:T(128)S(1)}, f32[128]{0:T(128)S(1)}, u32[]{:S(2)}, u32[]{:S(2)}) collective-permute-start(f32[128]{0:T(128)S(1)} %get-tuple-element.27), channel_id=1, source_target_pairs={{0,2},{1,3},{2,0},{3,1},{4,6},{5,7},{6,4},{7,5},{8,10},{9,11},{10,... | collective-permute-start | bytes 1544 | tf_op jit(solution)/shard_map/ppermute | solution.py:74
  32.9 3.5 %collective-permute-start.4 = (f32[128]{0:T(128)S(1)}, f32[128]{0:T(128)S(1)}, u32[]{:S(2)}, u32[]{:S(2)}) collective-permute-start(f32[128]{0:T(128)S(1)} %get-tuple-element.27), channel_id=1, source_target_pairs={{0,3},{1,0},{2,1},{3,2},{4,7},{5,4},{6,5},{7,6},{8,11},{9,8},{10,9... | collective-permute-start | bytes 1544 | tf_op jit(solution)/shard_map/ppermute | solution.py:74
  50.5 43.2 %all-to-all-start = ((bf16[8,128,1024]{2,1,0:T(8,128)(2,1)}), bf16[8,128,1024]{2,1,0:T(8,128)(2,1)S(1)}, u32[]{:S(2)}, u32[]{:S(2)}) async-start(bf16[8,128,1024]{2,1,0:T(8,128)(2,1)} %bitcast.55), calls=%async_computation | async-start | bytes 4194304 | tf_op jit(solution)/shard_map/all_to_all | solution.py:212
  56.3 90.3 %reduce-scatter.2.cloned.1.call-start = ((), (), s32[]{:S(2)}) async-start(), calls=%async_computation.4 | async-start | bytes 2359296 | tf_op jit(solution)/shard_map/reduce_scatter | solution.py:223
  94.0 7.7 %copy-start = (bf16[128,1024]{1,0:T(8,128)(2,1)S(1)}, bf16[128,1024]{1,0:T(8,128)(2,1)}, u32[]{:S(2)}) copy-start(bf16[128,1024]{1,0:T(8,128)(2,1)} %cot_ref.3) | copy-start | bytes 786436
  94.1 7.7 %copy-start.3 = (f32[1,128,1024]{2,0,1:T(1,128)S(1)}, f32[1,128,1024]{2,0,1:T(1,128)}, u32[]{:S(2)}) copy-start(f32[1,128,1024]{2,0,1:T(1,128)} %copy-done.2) | copy-start | bytes 1572868
  94.1 7.7 %copy-start.19 = (f32[128,1024]{1,0:T(8,128)S(1)}, f32[128,1024]{1,0:T(8,128)}, u32[]{:S(2)}) copy-start(f32[128,1024]{1,0:T(8,128)} %get-tuple-element.16) | copy-start | bytes 1572868
  94.3 5.4 %collective-permute-start.5 = (f32[128]{0:T(128)S(1)}, f32[128]{0:T(128)S(1)}, u32[]{:S(2)}, u32[]{:S(2)}) collective-permute-start(f32[128]{0:T(128)S(1)} %get-tuple-element.22), channel_id=1, source_target_pairs={{0,1},{1,2},{2,3},{3,0},{4,5},{5,6},{6,7},{7,4},{8,9},{9,10},{10,1... | collective-permute-start | bytes 1544 | tf_op jit(solution)/shard_map/ppermute | solution.py:74
  95.2 4.4 %collective-permute-start.6 = (f32[128]{0:T(128)S(1)}, f32[128]{0:T(128)S(1)}, u32[]{:S(2)}, u32[]{:S(2)}) collective-permute-start(f32[128]{0:T(128)S(1)} %get-tuple-element.22), channel_id=1, source_target_pairs={{0,2},{1,3},{2,0},{3,1},{4,6},{5,7},{6,4},{7,5},{8,10},{9,11},{10,... | collective-permute-start | bytes 1544 | tf_op jit(solution)/shard_map/ppermute | solution.py:74
  98.2 3.5 %collective-permute-start.7 = (f32[128]{0:T(128)S(1)}, f32[128]{0:T(128)S(1)}, u32[]{:S(2)}, u32[]{:S(2)}) collective-permute-start(f32[128]{0:T(128)S(1)} %get-tuple-element.22), channel_id=1, source_target_pairs={{0,3},{1,0},{2,1},{3,2},{4,7},{5,4},{6,5},{7,6},{8,11},{9,8},{10,9... | collective-permute-start | bytes 1544 | tf_op jit(solution)/shard_map/ppermute | solution.py:74
  103.8 7.5 %collective-permute-start.8 = (bf16[127,1024]{1,0:T(8,128)(2,1)}, bf16[127,1024]{1,0:T(8,128)(2,1)S(1)}, u32[]{:S(2)}, u32[]{:S(2)}) collective-permute-start(bf16[127,1024]{1,0:T(8,128)(2,1)} %slice.55), channel_id=1, source_target_pairs={{4,0},{8,4},{12,8},{16,12},{20,16},{24,20},{28,24},{5,1},{9,5},{13... | collective-permute-start | bytes 780296 | tf_op jit(solution)/shard_map/ppermute | solution.py:30
  120.5 2.2 %collective-permute-start.10 = (bf16[136,1024]{1,0:T(8,128)(2,1)S(1)}, bf16[136,1024]{1,0:T(8,128)(2,1)S(1)}, u32[]{:S(2)}, u32[]{:S(2)}) collective-permute-start(bf16[136,1024]{1,0:T(8,128)(2,1)S(1)} %pad_maximum_fusion), channel_id=1, source_target_pairs={{0,4},{4,0},{8,12},{12,8},{16,20},{20,16},{24,28},{28,24},{1,5},{5... | collective-permute-start | bytes 835592 | tf_op jit(solution)/shard_map/ppermute | solution.py:62
  122.8 9.3 %collective-permute-start.11 = (bf16[136,1024]{1,0:T(8,128)(2,1)S(1)}, bf16[136,1024]{1,0:T(8,128)(2,1)S(1)}, u32[]{:S(2)}, u32[]{:S(2)}) collective-permute-start(bf16[136,1024]{1,0:T(8,128)(2,1)S(1)} %add_convert_fusion.1), channel_id=1, source_target_pairs={{0,8},{4,12},{8,0},{12,4},{16,24},{20,28},{24,16},{28,20},{1,9},{5... | collective-permute-start | bytes 835592 | tf_op jit(solution)/shard_map/ppermute | solution.py:62
  124.5 3.1 %collective-permute-start.9 = (bf16[6,1024]{1,0:T(8,128)(2,1)S(1)}, bf16[6,1024]{1,0:T(8,128)(2,1)S(1)}, u32[]{:S(2)}, u32[]{:S(2)}) collective-permute-start(bf16[6,1024]{1,0:T(8,128)(2,1)S(1)} %slice.57), channel_id=1, source_target_pairs={{4,0},{8,4},{12,8},{16,12},{20,16},{24,20},{28,24},{5,1},{9,5},{13... | collective-permute-start | bytes 36872 | tf_op jit(solution)/shard_map/ppermute | solution.py:30
  127.6 6.1 %copy-start.21 = (f32[7,1024]{1,0:T(8,128)S(1)}, f32[7,1024]{1,0:T(8,128)}, u32[]{:S(2)}) copy-start(f32[7,1024]{1,0:T(8,128)} %param.15) | copy-start | bytes 86020
  132.2 12.4 %collective-permute-start.12 = (bf16[136,1024]{1,0:T(8,128)(2,1)S(1)}, bf16[136,1024]{1,0:T(8,128)(2,1)S(1)}, u32[]{:S(2)}, u32[]{:S(2)}) collective-permute-start(bf16[136,1024]{1,0:T(8,128)(2,1)S(1)} %add_convert_fusion), channel_id=1, source_target_pairs={{0,16},{4,20},{8,24},{12,28},{16,0},{20,4},{24,8},{28,12},{1,17},{... | collective-permute-start | bytes 835592 | tf_op jit(solution)/shard_map/ppermute | solution.py:62
  (17 other events, 51.4 us)
Sparse Core Ops, SparseCore 0:
  9.9 31.7 all-gather.2
  44.1 38.9 all-gather.4
  98.8 43.5 reduce-scatter.1

commit v10 on v9

--- a/solution.py
+++ b/solution.py
@@ -215,17 +215,6 @@
         .sum(axis=0)
     )
     values_whole = lax.all_gather(normed, "ctx", axis=0, tiled=True)
-    key_part, attended_all, queries_grad = head_attention(
-        queries, keys_whole, values_whole, cotangent, mask, scale_factor
-    )
-    result = (second_wide + attended_all).astype(jnp.bfloat16)
-    key_part, value_grad = lax.optimization_barrier((key_part, value_grad))
-    matchers_grad = lax.psum_scatter(
-        key_part,
-        "ctx",
-        scatter_dimension=0,
-        tiled=True,
-    )
     gain_part = value_grad * scaling
     projected = channel_total(jnp.sum(gain_part * second_wide, axis=1))
     scaling_part = jnp.sum(value_grad * second_wide * inverse_rms[:, None], axis=0)
@@ -238,6 +227,17 @@
     dconv_two = second_grad * valves.astype(jnp.float32)
     back_two = neighbor_rows(dconv_two[: KM - 1], -1)
     dinner_two = depthwise(jnp.concatenate([dconv_two, back_two], axis=0), kernel)
+    values_whole, _ = lax.optimization_barrier((values_whole, dinner_two))
+    key_part, attended_all, queries_grad = head_attention(
+        queries, keys_whole, values_whole, cotangent, mask, scale_factor
+    )
+    result = (second_wide + attended_all).astype(jnp.bfloat16)
+    matchers_grad = lax.psum_scatter(
+        key_part,
+        "ctx",
+        scatter_dimension=0,
+        tiled=True,
+    )
     intake_grad = (dinner_two * first_wide).astype(jnp.bfloat16)
     kernel_part = depthwise(padded_two, dconv_two)[::-1]
     first_grad = second_grad + dinner_two * intake.astype(jnp.float32)

time: 154 us -> 177 us (1.15)
  waiting for transfers between devices: 51.7 us -> 68.2 us
  local copies, waits for them, and re-layouts: 8.45 us -> 14.9 us
  starting transfers between devices: 29.7 us -> 27.3 us
    all_gather x1, waiting for transfers between devices: 26.8 us -> 9.41 us  [shards(): values_whole = lax.all_gather(normed, 'ctx', axis=0, tiled=True)]
    reduce_scatter x1, waiting for transfers between devices: 0.01 us -> 16.3 us  [shards(): lax.psum_scatter(key_part, 'ctx', scatter_dimension=0, tiled=True)]
    all_gather x1, waiting for transfers between devices: 3.23 us -> 18.5 us  [shards(): keys_whole = lax.all_gather(matchers, 'ctx', axis=0, tiled=True)]
    all_to_all x1, waiting for transfers between devices: 0.01 us -> 6.36 us  [shards(): lax.all_to_all(value_part, 'ctx', 0, 0, tiled=True)]
    rev x1, local copies, waits for them, and re-layouts: 0.24 us -> 4.73 us  [shards(): conv_two = depthwise(padded_two, kernel[::-1])]
    ppermute x3, waiting for transfers between devices: 13.4 us -> 11.2 us  [butterfly_total(): lax.ppermute(rounded, axis, pairs).astype(value.dtype)]
    all_to_all x1, starting transfers between devices: 5.84 us -> 3.6 us  [shards(): lax.all_to_all(value_part, 'ctx', 0, 0, tiled=True)]
    unnamed x50 -> x48, local copies, waits for them, and re-layouts: 2.44 us -> 3.71 us
  transfers between devices with their start and end apart: 17 -> 17, of which waited for: 11 -> 12; matrix products, arithmetic and copies ran while one was open for 23% -> 23% of each run, Pallas kernels for 13% -> 5%
where the time goes in v10:
time: 177 us; the launch traced here: 176 us
  waiting for transfers between devices  68.2 us (39%)
  starting transfers between devices  27.3 us (15%)
  matrix products  20.8 us (12%)
  Pallas kernels  19.3 us (11%)
  local copies, waits for them, and re-layouts  14.9 us (8%)
  between operations  14.4 us (8%)
  other arithmetic  11.1 us (6%)
    conv_general_dilated x6, matrix products, depthwise(): lax.conv_general_dilated(padded[None], tap_rows[:, None, :], (1,), 'VALID...  20.8 us
    all_gather x1, waiting for transfers between devices, shards(): keys_whole = lax.all_gather(matchers, 'ctx', axis=0, tiled=True)  18.5 us
    reduce_scatter x1, waiting for transfers between devices, shards(): lax.psum_scatter(key_part, 'ctx', scatter_dimension=0, tiled=True)  16.3 us
    ppermute x3, waiting for transfers between devices, butterfly_total(): lax.ppermute(rounded, axis, pairs).astype(value.dtype)  11.2 us
    ppermute x6, starting transfers between devices, exchange_total(): arrived = lax.ppermute(value, axis, pairs)  10.8 us
    pallas_call x1, Pallas kernels, head_attention(): pl.pallas_call(functools.partial(attention_block, scale_factor), grid=(wi...  10.5 us
    ppermute x4, starting transfers between devices, passed_along(): lax.ppermute(value, axis, [(source, source + steps) for source in range(l...  9.44 us
    all_gather x1, waiting for transfers between devices, shards(): values_whole = lax.all_gather(normed, 'ctx', axis=0, tiled=True)  9.41 us
  transfers between devices with their start and end apart: 17, of which 12 were waited for; matrix products, arithmetic and copies ran while one was open for 23% of the time, Pallas kernels for 5%

profile of v10, /device:TPU:0, one launch (start us, length us, event | category | flops | bytes accessed | tf_op | source)
XLA Modules:
  0.0 176.0 jit_solution(10376065559766531447)
XLA Ops:
  9.0 2.4 %collective-permute-start = (bf16[6,1024]{1,0:T(8,128)(2,1)S(1)}, bf16[6,1024]{1,0:T(8,128)(2,1)S(1)}, u32[]{:S(2)}, u32[]{:S(2)}) collective-permute-start(bf16[6,1024]{1,0:T(8,128)(2,1)S(1)} %slice.58), channel_id=1, source_target_pairs={{0,4},{4,8},{8,12},{12,16},{16,20},{20,24},{24,28},{1,5},{5,9},{9,... | collective-permute-start | bytes 36872 | tf_op jit(solution)/shard_map/ppermute | solution.py:30
  11.4 2.8 %rev.12 = f32[7,1024]{1,0:T(8,128)S(1)} reverse(f32[7,1024]{1,0:T(8,128)} %param.15), dimensions={0} | reverse | bytes 57344 | tf_op jit(solution)/shard_map/rev | solution.py:189
  17.2 4.5 %collective-permute-start.1 = (bf16[127,1024]{1,0:T(8,128)(2,1)S(1)}, bf16[127,1024]{1,0:T(8,128)(2,1)S(1)}, u32[]{:S(2)}, u32[]{:S(2)}) collective-permute-start(bf16[127,1024]{1,0:T(8,128)(2,1)S(1)} %slice.56), channel_id=1, source_target_pairs={{0,4},{4,8},{8,12},{12,16},{16,20},{20,24},{24,28},{1,5},{5,9},{9,... | collective-permute-start | bytes 780296 | tf_op jit(solution)/shard_map/ppermute | solution.py:30
  22.7 18.5 %all-gather.3.cloned.1.call-done.k_ref = bf16[1024,1024]{1,0:T(8,128)(2,1)} async-done(((bf16[128,1024]{1,0:T(8,128)(2,1)}), bf16[1024,1024]{1,0:T(8,128)(2,1)}) %all-gather.3.cloned.1.call-update) | async-done | bytes 2097168 | tf_op jit(solution)/shard_map/all_gather | solution.py:203
  41.2 8.7 %shard_map.203 = bf16[1024,1024]{1,0:T(8,128)(2,1)} custom-call(bf16[128,1024]{1,0:T(8,128)(2,1)} %q_ref.3, bf16[1024,1024]{1,0:T(8,128)(2,1)} %all-gather.3.cloned.1.call-done.k_ref, bf16[128,1024]{1,0:T(8,128)(2,1)} %cot_ref.3, f32[128,1024]{1,0:T(8,128)} %fusion.33.vis_ref), custom_call_target="tpu_custom_call" | custom-call | tf_op jit(solution)/shard_map/pallas_call | solution.py:139
  49.9 3.6 %all-to-all-start = ((bf16[8,128,1024]{2,1,0:T(8,128)(2,1)}), bf16[8,128,1024]{2,1,0:T(8,128)(2,1)S(1)}, u32[]{:S(2)}, u32[]{:S(2)}) async-start(bf16[8,128,1024]{2,1,0:T(8,128)(2,1)} %bitcast.58), calls=%async_computation | async-start | bytes 4194304 | tf_op jit(solution)/shard_map/all_to_all | solution.py:212
  53.6 4.7 %rev.13 = f32[128,1024]{1,0:T(8,128)} reverse(f32[128,1024]{1,0:T(8,128)} %param.18), dimensions={0} | reverse | bytes 1048576 | tf_op jit(solution)/shard_map/rev | solution.py:195
  59.4 5.8 %fusion.8 = f32[1,128,1024]{2,0,1:T(1,128)S(1)} fusion(f32[1,255,1024]{2,1,0:T(8,128)S(1)} %maximum_bitcast_fusion, f32[128,1,1024]{2,0,1:T(8,128)S(1)} %bitcast.63), kind=kOutput, calls=%fused_computation.36 | convolution fusion | flops 201326592 | bytes 2093056 | tf_op jit(solution)/shard_map/conv_general_dilated | solution.py:34
  66.2 1.5 collective-permute-start.2
  67.7 2.4 %collective-permute-start.3 = (f32[128]{0:T(128)S(1)}, f32[128]{0:T(128)S(1)}, u32[]{:S(2)}, u32[]{:S(2)}) collective-permute-start(f32[128]{0:T(128)S(1)} %get-tuple-element.25), channel_id=1, source_target_pairs={{0,2},{1,3},{2,0},{3,1},{4,6},{5,7},{6,4},{7,5},{8,10},{9,11},{10,... | collective-permute-start | bytes 1544 | tf_op jit(solution)/shard_map/ppermute | solution.py:74
  72.2 1.5 collective-permute-done.4
  73.7 6.4 %all-to-all-done = bf16[8,128,1024]{2,1,0:T(8,128)(2,1)S(1)} async-done(((bf16[8,128,1024]{2,1,0:T(8,128)(2,1)}), bf16[8,128,1024]{2,1,0:T(8,128)(2,1)S(1)}, u32[]{:S(2)}, u32[]{:S(2)}) %all-to-all-start) | async-done | bytes 2097184 | tf_op jit(solution)/shard_map/all_to_all | solution.py:212
  80.7 1.5 collective-permute-start.5
  82.2 2.4 %collective-permute-start.6 = (f32[128]{0:T(128)S(1)}, f32[128]{0:T(128)S(1)}, u32[]{:S(2)}, u32[]{:S(2)}) collective-permute-start(f32[128]{0:T(128)S(1)} %get-tuple-element.20), channel_id=1, source_target_pairs={{0,2},{1,3},{2,0},{3,1},{4,6},{5,7},{6,4},{7,5},{8,10},{9,11},{10,... | collective-permute-start | bytes 1544 | tf_op jit(solution)/shard_map/ppermute | solution.py:74
  88.2 2.1 %fusion.25 = (bf16[128,1024]{1,0:T(8,128)(2,1)}, f32[128,1024]{1,0:T(8,128)S(1)}, bf16[128,1024]{1,0:T(8,128)(2,1)}) fusion(f32[1,128,1024]{2,0,1:T(1,128)} %copy-done.3, f32[128]{0:T(128)S(1)} %fusion.42, bf16[128,1024]{1,0:T(8,128)(2,1)S(1)} %get-tuple-element.26, f32[128,1024]{1,0:T(8,128)S(1)} %convert_reduce_fusion, f32[1024]{0:T(1024)S(1)} %copy-done.20, ...), kind=kLoop, calls=%fused_computation.60 | loop fusion | flops 1572864 | bytes 2626560 | tf_op jit(solution)/shard_map/convert_element_type | solution.py:226
  92.6 5.8 %fusion.6 = bf16[1,128,1024]{2,0,1:T(2,128)(2,1)S(1)} fusion(f32[1,255,1024]{2,1,0:T(8,128)S(1)} %copy-done.9, f32[128,1,1024]{2,0,1:T(8,128)S(1)} %bitcast.59), kind=kOutput, calls=%fused_computation.34 | convolution fusion | flops 201326592 | bytes 1830912 | tf_op jit(solution)/shard_map/conv_general_dilated | solution.py:34
  99.9 7.0 %fusion = f32[1,128,1024]{2,0,1:T(1,128)S(1)} fusion(f32[1,255,1024]{2,1,0:T(8,128)S(1)} %maximum_bitcast_fusion.1, f32[128,1,1024]{2,0,1:T(8,128)} %bitcast.62), kind=kOutput, calls=%fused_computation.10 | convolution fusion | flops 201326592 | bytes 2093056 | tf_op jit(solution)/shard_map/conv_general_dilated | solution.py:34
  108.1 9.4 %all-gather.5.cloned.1.call-done.v_ref = bf16[1024,1024]{1,0:T(8,128)(2,1)} async-done(((bf16[128,1024]{1,0:T(8,128)(2,1)}), bf16[1024,1024]{1,0:T(8,128)(2,1)}) %all-gather.5.cloned.1.call-update) | async-done | bytes 2097168 | tf_op jit(solution)/shard_map/all_gather | solution.py:217
  117.5 10.5 %shard_map.204 = (bf16[1024,1024]{1,0:T(8,128)(2,1)}, f32[128,1024]{1,0:T(8,128)}, bf16[128,1024]{1,0:T(8,128)(2,1)}) custom-call(bf16[128,1024]{1,0:T(8,128)(2,1)} %q_ref.3, bf16[1024,1024]{1,0:T(8,128)(2,1)} %all-gather.3.cloned.1.call-done.k_ref, bf16[1024,1024]{1,0:T(8,128)(2,1)} %all-gather.5.cloned.1.call-done.v_ref, bf16[128,1024]{1,0:T(8,128)(2,1)} %cot_ref.3, ...), custom_call_target="tpu_custom_call" | custom-call | tf_op jit(solution)/shard_map/pallas_call | solution.py:152
  132.3 1.6 collective-permute-start.11
  135.1 1.8 %collective-permute-done.9 = bf16[6,1024]{1,0:T(8,128)(2,1)S(1)} collective-permute-done((bf16[6,1024]{1,0:T(8,128)(2,1)S(1)}, bf16[6,1024]{1,0:T(8,128)(2,1)S(1)}, u32[]{:S(2)}, u32[]{:S(2)}) %collective-permute-start.9) | collective-permute-done | bytes 12320 | tf_op jit(solution)/shard_map/ppermute | solution.py:30
  136.9 4.3 %collective-permute-done.11 = bf16[136,1024]{1,0:T(8,128)(2,1)S(1)} collective-permute-done((bf16[136,1024]{1,0:T(8,128)(2,1)S(1)}, bf16[136,1024]{1,0:T(8,128)(2,1)S(1)}, u32[]{:S(2)}, u32[]{:S(2)}) %collective-permute-start.11) | collective-permute-done | bytes 278560 | tf_op jit(solution)/shard_map/ppermute | solution.py:62
  144.4 5.6 %collective-permute-done.12 = bf16[136,1024]{1,0:T(8,128)(2,1)S(1)} collective-permute-done((bf16[136,1024]{1,0:T(8,128)(2,1)S(1)}, bf16[136,1024]{1,0:T(8,128)(2,1)S(1)}, u32[]{:S(2)}, u32[]{:S(2)}) %collective-permute-start.12) | collective-permute-done | bytes 278560 | tf_op jit(solution)/shard_map/ppermute | solution.py:62
  153.1 16.3 %reduce-scatter.2.cloned.1.call-done = bf16[128,1024]{1,0:T(8,128)(2,1)} async-done(((bf16[1024,1024]{1,0:T(8,128)(2,1)}), bf16[128,1024]{1,0:T(8,128)(2,1)}) %reduce-scatter.2.cloned.1.call-update) | async-done | bytes 262160 | tf_op jit(solution)/shard_map/reduce_scatter | solution.py:235
  (126 shorter events, 30.5 us)
Async XLA Ops:
  7.2 34.0 %all-gather.3.cloned.1.call-start = ((), (), s32[]{:S(2)}) async-start(), calls=%async_computation.2 | async-start | bytes 2359296 | tf_op jit(solution)/shard_map/all_gather | solution.py:203
  9.0 5.9 %collective-permute-start = (bf16[6,1024]{1,0:T(8,128)(2,1)S(1)}, bf16[6,1024]{1,0:T(8,128)(2,1)S(1)}, u32[]{:S(2)}, u32[]{:S(2)}) collective-permute-start(bf16[6,1024]{1,0:T(8,128)(2,1)S(1)} %slice.58), channel_id=1, source_target_pairs={{0,4},{4,8},{8,12},{12,16},{16,20},{20,24},{24,28},{1,5},{5,9},{9,... | collective-permute-start | bytes 36872 | tf_op jit(solution)/shard_map/ppermute | solution.py:30
  17.2 41.2 %collective-permute-start.1 = (bf16[127,1024]{1,0:T(8,128)(2,1)S(1)}, bf16[127,1024]{1,0:T(8,128)(2,1)S(1)}, u32[]{:S(2)}, u32[]{:S(2)}) collective-permute-start(bf16[127,1024]{1,0:T(8,128)(2,1)S(1)} %slice.56), channel_id=1, source_target_pairs={{0,4},{4,8},{8,12},{12,16},{16,20},{20,24},{24,28},{1,5},{5,9},{9,... | collective-permute-start | bytes 780296 | tf_op jit(solution)/shard_map/ppermute | solution.py:30
  49.9 30.2 %all-to-all-start = ((bf16[8,128,1024]{2,1,0:T(8,128)(2,1)}), bf16[8,128,1024]{2,1,0:T(8,128)(2,1)S(1)}, u32[]{:S(2)}, u32[]{:S(2)}) async-start(bf16[8,128,1024]{2,1,0:T(8,128)(2,1)} %bitcast.58), calls=%async_computation | async-start | bytes 4194304 | tf_op jit(solution)/shard_map/all_to_all | solution.py:212
  53.5 63.9 %all-gather.5.cloned.1.call-start = ((), (), s32[]{:S(2)}) async-start(), calls=%async_computation.3 | async-start | bytes 2359296 | tf_op jit(solution)/shard_map/all_gather | solution.py:217
  65.2 15.3 %copy-start.20 = (f32[1024]{0:T(1024)S(1)}, f32[1024]{0:T(1024)}, u32[]{:S(2)}) copy-start(f32[1024]{0:T(1024)} %param.19) | copy-start | bytes 12292
  66.0 22.2 %copy-start = (bf16[128,1024]{1,0:T(8,128)(2,1)S(1)}, bf16[128,1024]{1,0:T(8,128)(2,1)}, u32[]{:S(2)}) copy-start(bf16[128,1024]{1,0:T(8,128)(2,1)} %cot_ref.3) | copy-start | bytes 786436
  66.2 5.4 %collective-permute-start.2 = (f32[128]{0:T(128)S(1)}, f32[128]{0:T(128)S(1)}, u32[]{:S(2)}, u32[]{:S(2)}) collective-permute-start(f32[128]{0:T(128)S(1)} %get-tuple-element.25), channel_id=1, source_target_pairs={{0,1},{1,2},{2,3},{3,0},{4,5},{5,6},{6,7},{7,4},{8,9},{9,10},{10,1... | collective-permute-start | bytes 1544 | tf_op jit(solution)/shard_map/ppermute | solution.py:74
  67.7 4.4 %collective-permute-start.3 = (f32[128]{0:T(128)S(1)}, f32[128]{0:T(128)S(1)}, u32[]{:S(2)}, u32[]{:S(2)}) collective-permute-start(f32[128]{0:T(128)S(1)} %get-tuple-element.25), channel_id=1, source_target_pairs={{0,2},{1,3},{2,0},{3,1},{4,6},{5,7},{6,4},{7,5},{8,10},{9,11},{10,... | collective-permute-start | bytes 1544 | tf_op jit(solution)/shard_map/ppermute | solution.py:74
  70.1 3.5 %collective-permute-start.4 = (f32[128]{0:T(128)S(1)}, f32[128]{0:T(128)S(1)}, u32[]{:S(2)}, u32[]{:S(2)}) collective-permute-start(f32[128]{0:T(128)S(1)} %get-tuple-element.25), channel_id=1, source_target_pairs={{0,3},{1,0},{2,1},{3,2},{4,7},{5,4},{6,5},{7,6},{8,11},{9,8},{10,9... | collective-permute-start | bytes 1544 | tf_op jit(solution)/shard_map/ppermute | solution.py:74
  80.4 10.0 %copy-start.7 = (bf16[128,1024]{1,0:T(8,128)(2,1)S(1)}, bf16[128,1024]{1,0:T(8,128)(2,1)}, u32[]{:S(2)}) copy-start(bf16[128,1024]{1,0:T(8,128)(2,1)} %param.16) | copy-start | bytes 786436
  80.7 5.4 %collective-permute-start.5 = (f32[128]{0:T(128)S(1)}, f32[128]{0:T(128)S(1)}, u32[]{:S(2)}, u32[]{:S(2)}) collective-permute-start(f32[128]{0:T(128)S(1)} %get-tuple-element.20), channel_id=1, source_target_pairs={{0,1},{1,2},{2,3},{3,0},{4,5},{5,6},{6,7},{7,4},{8,9},{9,10},{10,1... | collective-permute-start | bytes 1544 | tf_op jit(solution)/shard_map/ppermute | solution.py:74
  82.2 4.4 %collective-permute-start.6 = (f32[128]{0:T(128)S(1)}, f32[128]{0:T(128)S(1)}, u32[]{:S(2)}, u32[]{:S(2)}) collective-permute-start(f32[128]{0:T(128)S(1)} %get-tuple-element.20), channel_id=1, source_target_pairs={{0,2},{1,3},{2,0},{3,1},{4,6},{5,7},{6,4},{7,5},{8,10},{9,11},{10,... | collective-permute-start | bytes 1544 | tf_op jit(solution)/shard_map/ppermute | solution.py:74
  84.6 3.5 %collective-permute-start.7 = (f32[128]{0:T(128)S(1)}, f32[128]{0:T(128)S(1)}, u32[]{:S(2)}, u32[]{:S(2)}) collective-permute-start(f32[128]{0:T(128)S(1)} %get-tuple-element.20), channel_id=1, source_target_pairs={{0,3},{1,0},{2,1},{3,2},{4,7},{5,4},{6,5},{7,6},{8,11},{9,8},{10,9... | collective-permute-start | bytes 1544 | tf_op jit(solution)/shard_map/ppermute | solution.py:74
  90.4 79.1 %reduce-scatter.2.cloned.1.call-start = ((), (), s32[]{:S(2)}) async-start(), calls=%async_computation.4 | async-start | bytes 2359296 | tf_op jit(solution)/shard_map/reduce_scatter | solution.py:235
  91.3 7.5 %collective-permute-start.8 = (bf16[127,1024]{1,0:T(8,128)(2,1)}, bf16[127,1024]{1,0:T(8,128)(2,1)}, u32[]{:S(2)}, u32[]{:S(2)}) collective-permute-start(bf16[127,1024]{1,0:T(8,128)(2,1)} %slice.55), channel_id=1, source_target_pairs={{4,0},{8,4},{12,8},{16,12},{20,16},{24,20},{28,24},{5,1},{9,5},{13... | collective-permute-start | bytes 780296 | tf_op jit(solution)/shard_map/ppermute | solution.py:30
  99.9 7.0 %copy-start.5 = (f32[1,128,1024]{2,0,1:T(1,128)S(1)}, f32[1,128,1024]{2,0,1:T(1,128)}, u32[]{:S(2)}) copy-start(f32[1,128,1024]{2,0,1:T(1,128)} %copy-done.4) | copy-start | bytes 1572868
  130.5 1.6 collective-permute-start.10
  132.3 8.9 %collective-permute-start.11 = (bf16[136,1024]{1,0:T(8,128)(2,1)S(1)}, bf16[136,1024]{1,0:T(8,128)(2,1)S(1)}, u32[]{:S(2)}, u32[]{:S(2)}) collective-permute-start(bf16[136,1024]{1,0:T(8,128)(2,1)S(1)} %add_convert_fusion.1), channel_id=1, source_target_pairs={{0,8},{4,12},{8,0},{12,4},{16,24},{20,28},{24,16},{28,20},{1,9},{5... | collective-permute-start | bytes 835592 | tf_op jit(solution)/shard_map/ppermute | solution.py:62
  133.8 3.1 %collective-permute-start.9 = (bf16[6,1024]{1,0:T(8,128)(2,1)S(1)}, bf16[6,1024]{1,0:T(8,128)(2,1)S(1)}, u32[]{:S(2)}, u32[]{:S(2)}) collective-permute-start(bf16[6,1024]{1,0:T(8,128)(2,1)S(1)} %slice.57), channel_id=1, source_target_pairs={{4,0},{8,4},{12,8},{16,12},{20,16},{24,20},{28,24},{5,1},{9,5},{13... | collective-permute-start | bytes 36872 | tf_op jit(solution)/shard_map/ppermute | solution.py:30
  141.2 8.8 %collective-permute-start.12 = (bf16[136,1024]{1,0:T(8,128)(2,1)S(1)}, bf16[136,1024]{1,0:T(8,128)(2,1)S(1)}, u32[]{:S(2)}, u32[]{:S(2)}) collective-permute-start(bf16[136,1024]{1,0:T(8,128)(2,1)S(1)} %add_convert_fusion), channel_id=1, source_target_pairs={{0,16},{4,20},{8,24},{12,28},{16,0},{20,4},{24,8},{28,12},{1,17},{... | collective-permute-start | bytes 835592 | tf_op jit(solution)/shard_map/ppermute | solution.py:62
  144.3 7.8 %copy-start.2 = (bf16[128,1024]{1,0:T(8,128)(2,1)S(1)}, bf16[128,1024]{1,0:T(8,128)(2,1)}, u32[]{:S(2)}) copy-start(bf16[128,1024]{1,0:T(8,128)(2,1)} %param.12) | copy-start | bytes 786436
  144.3 7.8 %copy-start.10 = (bf16[128,1024]{1,0:T(8,128)(2,1)S(1)}, bf16[128,1024]{1,0:T(8,128)(2,1)}, u32[]{:S(2)}) copy-start(bf16[128,1024]{1,0:T(8,128)(2,1)} %param.14) | copy-start | bytes 786436
  144.4 7.7 %copy-start.18 = (f32[128,1024]{1,0:T(8,128)S(1)}, f32[128,1024]{1,0:T(8,128)}, u32[]{:S(2)}) copy-start(f32[128,1024]{1,0:T(8,128)} %get-tuple-element.16) | copy-start | bytes 1572868
  (16 other events, 38.9 us)
Sparse Core Ops, SparseCore 0:
  9.9 31.2 all-gather.2
  90.5 26.9 all-gather.4
  128.2 41.2 reduce-scatter.1

commit v11 on v10

--- a/solution.py
+++ b/solution.py
@@ -207,7 +207,8 @@
     query_seg = lax.dynamic_slice_in_dim(segments, position, local_rows, 0)
     visible = (key_pos[None, :] <= query_pos[:, None]) & (segments[None, :] == query_seg[:, None])
     mask = visible.astype(jnp.float32)
-    value_part = head_values_grad(queries, keys_whole, cotangent, mask, scale_factor)
+    held_queries, normed = lax.optimization_barrier((queries, normed))
+    value_part = head_values_grad(held_queries, keys_whole, cotangent, mask, scale_factor)
     value_grad = (
         lax.all_to_all(value_part, "ctx", 0, 0, tiled=True)
         .reshape(ctx_count, local_rows, width_local)
@@ -223,11 +224,7 @@
         + inverse_rms[:, None] * gain_part
         - second_wide * (inverse_rms**3 * projected / D)[:, None]
     )
-    valves_grad = (second_grad * conv_two).astype(jnp.bfloat16)
-    dconv_two = second_grad * valves.astype(jnp.float32)
-    back_two = neighbor_rows(dconv_two[: KM - 1], -1)
-    dinner_two = depthwise(jnp.concatenate([dconv_two, back_two], axis=0), kernel)
-    values_whole, _ = lax.optimization_barrier((values_whole, dinner_two))
+    values_whole, _ = lax.optimization_barrier((values_whole, second_grad))
     key_part, attended_all, queries_grad = head_attention(
         queries, keys_whole, values_whole, cotangent, mask, scale_factor
     )
@@ -238,6 +235,10 @@
         scatter_dimension=0,
         tiled=True,
     )
+    valves_grad = (second_grad * conv_two).astype(jnp.bfloat16)
+    dconv_two = second_grad * valves.astype(jnp.float32)
+    back_two = neighbor_rows(dconv_two[: KM - 1], -1)
+    dinner_two = depthwise(jnp.concatenate([dconv_two, back_two], axis=0), kernel)
     intake_grad = (dinner_two * first_wide).astype(jnp.bfloat16)
     kernel_part = depthwise(padded_two, dconv_two)[::-1]
     first_grad = second_grad + dinner_two * intake.astype(jnp.float32)

time: 177 us -> 161 us (0.910)
  waiting for transfers between devices: 68.2 us -> 57.3 us
  local copies, waits for them, and re-layouts: 14.9 us -> 8 us
  starting transfers between devices: 27.3 us -> 29.3 us
    all_to_all x1, waiting for transfers between devices: 6.36 us -> 28.7 us  [shards(): lax.all_to_all(value_part, 'ctx', 0, 0, tiled=True)]
    all_gather x1, waiting for transfers between devices: 18.5 us -> 3.36 us  [shards(): keys_whole = lax.all_gather(matchers, 'ctx', axis=0, tiled=True)]
    reduce_scatter x1, waiting for transfers between devices: 16.3 us -> 3.14 us  [shards(): lax.psum_scatter(key_part, 'ctx', scatter_dimension=0, tiled=True)]
    all_gather x1, waiting for transfers between devices: 9.41 us -> 0.02 us  [shards(): values_whole = lax.all_gather(normed, 'ctx', axis=0, tiled=True)]
    rev x1, local copies, waits for them, and re-layouts: 4.73 us -> 0.24 us  [shards(): conv_two = depthwise(padded_two, kernel[::-1])]
    ppermute x3, waiting for transfers between devices: 11.2 us -> 13.5 us  [butterfly_total(): lax.ppermute(rounded, axis, pairs).astype(value.dtype)]
    ppermute x3, starting transfers between devices: 3.34 us -> 5.25 us  [butterfly_total(): lax.ppermute(rounded, axis, pairs).astype(value.dtype)]
    unnamed x48 -> x50, local copies, waits for them, and re-layouts: 3.71 us -> 2.7 us
  transfers between devices with their start and end apart: 17 -> 17, of which waited for: 12 -> 10; matrix products, arithmetic and copies ran while one was open for 23% -> 23% of each run, Pallas kernels for 5% -> 7%
where the time goes in v11:
time: 161 us; the launch traced here: 160 us
  waiting for transfers between devices  57.3 us (36%)
  starting transfers between devices  29.3 us (18%)
  matrix products  19.7 us (12%)
  Pallas kernels  19.4 us (12%)
  between operations  14.4 us (9%)
  other arithmetic  12.1 us (8%)
  local copies, waits for them, and re-layouts  8 us (5%)
    all_to_all x1, waiting for transfers between devices, shards(): lax.all_to_all(value_part, 'ctx', 0, 0, tiled=True)  28.7 us
    conv_general_dilated x6, matrix products, depthwise(): lax.conv_general_dilated(padded[None], tap_rows[:, None, :], (1,), 'VALID...  19.7 us
    ppermute x3, waiting for transfers between devices, butterfly_total(): lax.ppermute(rounded, axis, pairs).astype(value.dtype)  13.5 us
    pallas_call x1, Pallas kernels, head_attention(): pl.pallas_call(functools.partial(attention_block, scale_factor), grid=(wi...  10.6 us
    ppermute x6, starting transfers between devices, exchange_total(): arrived = lax.ppermute(value, axis, pairs)  9.47 us
    ppermute x4, starting transfers between devices, passed_along(): lax.ppermute(value, axis, [(source, source + steps) for source in range(l...  9.45 us
    pallas_call x1, Pallas kernels, head_values_grad(): pl.pallas_call(functools.partial(value_block, scale_factor), grid=(width_...  8.77 us
    ppermute x6, waiting for transfers between devices, exchange_total(): arrived = lax.ppermute(value, axis, pairs)  5.45 us
  transfers between devices with their start and end apart: 17, of which 10 were waited for; matrix products, arithmetic and copies ran while one was open for 23% of the time, Pallas kernels for 7%

profile of v11, /device:TPU:0, one launch (start us, length us, event | category | flops | bytes accessed | tf_op | source)
XLA Modules:
  0.0 160.1 jit_solution(18158007807739001269)
XLA Ops:
  9.0 2.4 %collective-permute-start = (bf16[6,1024]{1,0:T(8,128)(2,1)S(1)}, bf16[6,1024]{1,0:T(8,128)(2,1)S(1)}, u32[]{:S(2)}, u32[]{:S(2)}) collective-permute-start(bf16[6,1024]{1,0:T(8,128)(2,1)S(1)} %slice.58), channel_id=1, source_target_pairs={{0,4},{4,8},{8,12},{12,16},{16,20},{20,24},{24,28},{1,5},{5,9},{9,... | collective-permute-start | bytes 36872 | tf_op jit(solution)/shard_map/ppermute | solution.py:30
  11.4 2.8 %rev.12 = f32[7,1024]{1,0:T(8,128)S(1)} reverse(f32[7,1024]{1,0:T(8,128)} %param.15), dimensions={0} | reverse | bytes 57344 | tf_op jit(solution)/shard_map/rev | solution.py:189
  16.4 4.5 %collective-permute-start.1 = (bf16[127,1024]{1,0:T(8,128)(2,1)S(1)}, bf16[127,1024]{1,0:T(8,128)(2,1)S(1)}, u32[]{:S(2)}, u32[]{:S(2)}) collective-permute-start(bf16[127,1024]{1,0:T(8,128)(2,1)S(1)} %slice.56), channel_id=1, source_target_pairs={{0,4},{4,8},{8,12},{12,16},{16,20},{20,24},{24,28},{1,5},{5,9},{9,... | collective-permute-start | bytes 780296 | tf_op jit(solution)/shard_map/ppermute | solution.py:30
  22.6 5.8 %fusion.8 = f32[1,128,1024]{2,0,1:T(1,128)S(1)} fusion(f32[1,255,1024]{2,1,0:T(8,128)S(1)} %maximum_bitcast_fusion, f32[128,1,1024]{2,0,1:T(8,128)S(1)} %bitcast.60), kind=kOutput, calls=%fused_computation.36 | convolution fusion | flops 201326592 | bytes 2093056 | tf_op jit(solution)/shard_map/conv_general_dilated | solution.py:34
  29.4 1.6 %collective-permute-start.2 = (f32[128]{0:T(128)S(1)}, f32[128]{0:T(128)S(1)}, u32[]{:S(2)}, u32[]{:S(2)}) collective-permute-start(f32[128]{0:T(128)S(1)} %get-tuple-element.29), channel_id=1, source_target_pairs={{0,1},{1,2},{2,3},{3,0},{4,5},{5,6},{6,7},{7,4},{8,9},{9,10},{10,1... | collective-permute-start | bytes 1544 | tf_op jit(solution)/shard_map/ppermute | solution.py:74
  31.1 2.6 %collective-permute-start.3 = (f32[128]{0:T(128)S(1)}, f32[128]{0:T(128)S(1)}, u32[]{:S(2)}, u32[]{:S(2)}) collective-permute-start(f32[128]{0:T(128)S(1)} %get-tuple-element.29), channel_id=1, source_target_pairs={{0,2},{1,3},{2,0},{3,1},{4,6},{5,7},{6,4},{7,5},{8,10},{9,11},{10,... | collective-permute-start | bytes 1544 | tf_op jit(solution)/shard_map/ppermute | solution.py:74
  35.5 1.7 %collective-permute-done.4 = f32[128]{0:T(128)S(1)} collective-permute-done((f32[128]{0:T(128)S(1)}, f32[128]{0:T(128)S(1)}, u32[]{:S(2)}, u32[]{:S(2)}) %collective-permute-start.4) | collective-permute-done | bytes 544 | tf_op jit(solution)/shard_map/ppermute | solution.py:74
  38.1 3.4 %all-gather.3.cloned.1.call-done.k_ref = bf16[1024,1024]{1,0:T(8,128)(2,1)} async-done(((bf16[128,1024]{1,0:T(8,128)(2,1)}), bf16[1024,1024]{1,0:T(8,128)(2,1)}) %all-gather.3.cloned.1.call-update) | async-done | bytes 2097168 | tf_op jit(solution)/shard_map/all_gather | solution.py:203
  41.5 8.8 %shard_map.203 = bf16[1024,1024]{1,0:T(8,128)(2,1)} custom-call(bf16[128,1024]{1,0:T(8,128)(2,1)} %q_ref.2, bf16[1024,1024]{1,0:T(8,128)(2,1)} %all-gather.3.cloned.1.call-done.k_ref, bf16[128,1024]{1,0:T(8,128)(2,1)} %cot_ref.3, f32[128,1024]{1,0:T(8,128)} %fusion.33.vis_ref), custom_call_target="tpu_custom_call" | custom-call | tf_op jit(solution)/shard_map/pallas_call | solution.py:139
  50.2 5.0 %all-to-all-start = ((bf16[8,128,1024]{2,1,0:T(8,128)(2,1)}), bf16[8,128,1024]{2,1,0:T(8,128)(2,1)S(1)}, u32[]{:S(2)}, u32[]{:S(2)}) async-start(bf16[8,128,1024]{2,1,0:T(8,128)(2,1)} %bitcast.55), calls=%async_computation | async-start | bytes 4194304 | tf_op jit(solution)/shard_map/all_to_all | solution.py:213
  56.1 28.7 %all-to-all-done = bf16[8,128,1024]{2,1,0:T(8,128)(2,1)S(1)} async-done(((bf16[8,128,1024]{2,1,0:T(8,128)(2,1)}), bf16[8,128,1024]{2,1,0:T(8,128)(2,1)S(1)}, u32[]{:S(2)}, u32[]{:S(2)}) %all-to-all-start) | async-done | bytes 2097184 | tf_op jit(solution)/shard_map/all_to_all | solution.py:213
  85.8 3.3 %collective-permute-start.6 = (f32[128]{0:T(128)S(1)}, f32[128]{0:T(128)S(1)}, u32[]{:S(2)}, u32[]{:S(2)}) collective-permute-start(f32[128]{0:T(128)S(1)} %get-tuple-element.24), channel_id=1, source_target_pairs={{0,2},{1,3},{2,0},{3,1},{4,6},{5,7},{6,4},{7,5},{8,10},{9,11},{10,... | collective-permute-start | bytes 1544 | tf_op jit(solution)/shard_map/ppermute | solution.py:74
  89.2 1.4 collective-permute-done.5
  90.7 1.9 %collective-permute-done.7 = f32[128]{0:T(128)S(1)} collective-permute-done((f32[128]{0:T(128)S(1)}, f32[128]{0:T(128)S(1)}, u32[]{:S(2)}, u32[]{:S(2)}) %collective-permute-start.7) | collective-permute-done | bytes 544 | tf_op jit(solution)/shard_map/ppermute | solution.py:74
  92.7 2.2 %fusion.25 = (bf16[128,1024]{1,0:T(8,128)(2,1)}, f32[128,1024]{1,0:T(8,128)S(1)}) fusion(f32[1,128,1024]{2,0,1:T(1,128)} %copy-done.3, f32[128]{0:T(128)S(1)} %fusion.42, bf16[128,1024]{1,0:T(8,128)(2,1)S(1)} %get-tuple-element.30, f32[128,1024]{1,0:T(8,128)S(1)} %convert_reduce_fusion, f32[1024]{0:T(1024)S(1)} %copy-done.20, f32[128]{0:T(128)S(1)} %add_rsqrt_fusion, ...), kind=kLoop, calls=%fused_computation.59 | loop fusion | flops 1179648 | bytes 2364416 | tf_op jit(solution)/shard_map/convert_element_type | solution.py:238
  96.3 5.8 %fusion.6 = bf16[1,128,1024]{2,0,1:T(2,128)(2,1)S(1)} fusion(f32[1,255,1024]{2,1,0:T(8,128)S(1)} %copy-done.9, f32[128,1,1024]{2,0,1:T(8,128)S(1)} %bitcast.56), kind=kOutput, calls=%fused_computation.34 | convolution fusion | flops 201326592 | bytes 1830912 | tf_op jit(solution)/shard_map/conv_general_dilated | solution.py:34
  102.6 10.6 %shard_map.204 = (bf16[1024,1024]{1,0:T(8,128)(2,1)}, f32[128,1024]{1,0:T(8,128)}, bf16[128,1024]{1,0:T(8,128)(2,1)}) custom-call(bf16[128,1024]{1,0:T(8,128)(2,1)} %q_ref.2, bf16[1024,1024]{1,0:T(8,128)(2,1)} %all-gather.3.cloned.1.call-done.k_ref, bf16[1024,1024]{1,0:T(8,128)(2,1)} %all-gather.5.cloned.1.call-done.v_ref, bf16[128,1024]{1,0:T(8,128)(2,1)} %cot_ref.3, ...), custom_call_target="tpu_custom_call" | custom-call | tf_op jit(solution)/shard_map/pallas_call | solution.py:152
  114.2 5.8 %fusion = f32[1,128,1024]{2,0,1:T(1,128)S(1)} fusion(f32[1,255,1024]{2,1,0:T(8,128)S(1)} %maximum_bitcast_fusion.1, f32[128,1,1024]{2,0,1:T(8,128)S(1)} %bitcast.59), kind=kOutput, calls=%fused_computation.10 | convolution fusion | flops 201326592 | bytes 2093056 | tf_op jit(solution)/shard_map/conv_general_dilated | solution.py:34
  125.1 1.8 %collective-permute-done.9 = bf16[6,1024]{1,0:T(8,128)(2,1)S(1)} collective-permute-done((bf16[6,1024]{1,0:T(8,128)(2,1)S(1)}, bf16[6,1024]{1,0:T(8,128)(2,1)S(1)}, u32[]{:S(2)}, u32[]{:S(2)}) %collective-permute-start.9) | collective-permute-done | bytes 12320 | tf_op jit(solution)/shard_map/ppermute | solution.py:30
  127.0 2.0 %collective-permute-start.11 = (bf16[136,1024]{1,0:T(8,128)(2,1)S(1)}, bf16[136,1024]{1,0:T(8,128)(2,1)}, u32[]{:S(2)}, u32[]{:S(2)}) collective-permute-start(bf16[136,1024]{1,0:T(8,128)(2,1)S(1)} %add_convert_fusion.1), channel_id=1, source_target_pairs={{0,8},{4,12},{8,0},{12,4},{16,24},{20,28},{24,16},{28,20},{1,9},{5... | collective-permute-start | bytes 835592 | tf_op jit(solution)/shard_map/ppermute | solution.py:62
  130.7 7.5 %collective-permute-done.11 = bf16[136,1024]{1,0:T(8,128)(2,1)} collective-permute-done((bf16[136,1024]{1,0:T(8,128)(2,1)S(1)}, bf16[136,1024]{1,0:T(8,128)(2,1)}, u32[]{:S(2)}, u32[]{:S(2)}) %collective-permute-start.11) | collective-permute-done | bytes 278560 | tf_op jit(solution)/shard_map/ppermute | solution.py:62
  139.2 2.1 %collective-permute-start.12 = (bf16[136,1024]{1,0:T(8,128)(2,1)S(1)}, bf16[136,1024]{1,0:T(8,128)(2,1)S(1)}, u32[]{:S(2)}, u32[]{:S(2)}) collective-permute-start(bf16[136,1024]{1,0:T(8,128)(2,1)S(1)} %add_convert_fusion), channel_id=1, source_target_pairs={{0,16},{4,20},{8,24},{12,28},{16,0},{20,4},{24,8},{28,12},{1,17},{... | collective-permute-start | bytes 835592 | tf_op jit(solution)/shard_map/ppermute | solution.py:62
  142.3 6.0 %collective-permute-done.12 = bf16[136,1024]{1,0:T(8,128)(2,1)S(1)} collective-permute-done((bf16[136,1024]{1,0:T(8,128)(2,1)S(1)}, bf16[136,1024]{1,0:T(8,128)(2,1)S(1)}, u32[]{:S(2)}, u32[]{:S(2)}) %collective-permute-start.12) | collective-permute-done | bytes 278560 | tf_op jit(solution)/shard_map/ppermute | solution.py:62
  150.5 3.1 %reduce-scatter.2.cloned.1.call-done = bf16[128,1024]{1,0:T(8,128)(2,1)} async-done(((bf16[1024,1024]{1,0:T(8,128)(2,1)}), bf16[128,1024]{1,0:T(8,128)(2,1)}) %reduce-scatter.2.cloned.1.call-update) | async-done | bytes 262160 | tf_op jit(solution)/shard_map/reduce_scatter | solution.py:232
  (129 shorter events, 25.1 us)
Async XLA Ops:
  7.2 34.3 %all-gather.3.cloned.1.call-start = ((), (), s32[]{:S(2)}) async-start(), calls=%async_computation.2 | async-start | bytes 2359296 | tf_op jit(solution)/shard_map/all_gather | solution.py:203
  9.0 5.2 %collective-permute-start = (bf16[6,1024]{1,0:T(8,128)(2,1)S(1)}, bf16[6,1024]{1,0:T(8,128)(2,1)S(1)}, u32[]{:S(2)}, u32[]{:S(2)}) collective-permute-start(bf16[6,1024]{1,0:T(8,128)(2,1)S(1)} %slice.58), channel_id=1, source_target_pairs={{0,4},{4,8},{8,12},{12,16},{16,20},{20,24},{24,28},{1,5},{5,9},{9,... | collective-permute-start | bytes 36872 | tf_op jit(solution)/shard_map/ppermute | solution.py:30
  16.4 6.0 %collective-permute-start.1 = (bf16[127,1024]{1,0:T(8,128)(2,1)S(1)}, bf16[127,1024]{1,0:T(8,128)(2,1)S(1)}, u32[]{:S(2)}, u32[]{:S(2)}) collective-permute-start(bf16[127,1024]{1,0:T(8,128)(2,1)S(1)} %slice.56), channel_id=1, source_target_pairs={{0,4},{4,8},{8,12},{12,16},{16,20},{20,24},{24,28},{1,5},{5,9},{9,... | collective-permute-start | bytes 780296 | tf_op jit(solution)/shard_map/ppermute | solution.py:30
  22.6 6.6 %copy-start.6 = (bf16[128,1024]{1,0:T(8,128)(2,1)S(1)}, bf16[128,1024]{1,0:T(8,128)(2,1)}, u32[]{:S(2)}) copy-start(bf16[128,1024]{1,0:T(8,128)(2,1)} %param.16) | copy-start | bytes 786436
  22.6 14.7 %copy-start.20 = (f32[1024]{0:T(1024)S(1)}, f32[1024]{0:T(1024)}, u32[]{:S(2)}) copy-start(f32[1024]{0:T(1024)} %param.19) | copy-start | bytes 12292
  29.4 5.6 %collective-permute-start.2 = (f32[128]{0:T(128)S(1)}, f32[128]{0:T(128)S(1)}, u32[]{:S(2)}, u32[]{:S(2)}) collective-permute-start(f32[128]{0:T(128)S(1)} %get-tuple-element.29), channel_id=1, source_target_pairs={{0,1},{1,2},{2,3},{3,0},{4,5},{5,6},{6,7},{7,4},{8,9},{9,10},{10,1... | collective-permute-start | bytes 1544 | tf_op jit(solution)/shard_map/ppermute | solution.py:74
  31.1 4.4 %collective-permute-start.3 = (f32[128]{0:T(128)S(1)}, f32[128]{0:T(128)S(1)}, u32[]{:S(2)}, u32[]{:S(2)}) collective-permute-start(f32[128]{0:T(128)S(1)} %get-tuple-element.29), channel_id=1, source_target_pairs={{0,2},{1,3},{2,0},{3,1},{4,6},{5,7},{6,4},{7,5},{8,10},{9,11},{10,... | collective-permute-start | bytes 1544 | tf_op jit(solution)/shard_map/ppermute | solution.py:74
  33.6 3.5 %collective-permute-start.4 = (f32[128]{0:T(128)S(1)}, f32[128]{0:T(128)S(1)}, u32[]{:S(2)}, u32[]{:S(2)}) collective-permute-start(f32[128]{0:T(128)S(1)} %get-tuple-element.29), channel_id=1, source_target_pairs={{0,3},{1,0},{2,1},{3,2},{4,7},{5,4},{6,5},{7,6},{8,11},{9,8},{10,9... | collective-permute-start | bytes 1544 | tf_op jit(solution)/shard_map/ppermute | solution.py:74
  50.2 34.5 %all-to-all-start = ((bf16[8,128,1024]{2,1,0:T(8,128)(2,1)}), bf16[8,128,1024]{2,1,0:T(8,128)(2,1)S(1)}, u32[]{:S(2)}, u32[]{:S(2)}) async-start(bf16[8,128,1024]{2,1,0:T(8,128)(2,1)} %bitcast.55), calls=%async_computation | async-start | bytes 4194304 | tf_op jit(solution)/shard_map/all_to_all | solution.py:213
  55.3 37.5 %copy-start = (bf16[128,1024]{1,0:T(8,128)(2,1)S(1)}, bf16[128,1024]{1,0:T(8,128)(2,1)}, u32[]{:S(2)}) copy-start(bf16[128,1024]{1,0:T(8,128)(2,1)} %cot_ref.3) | copy-start | bytes 786436
  55.3 47.3 %all-gather.5.cloned.1.call-start = ((), (), s32[]{:S(2)}) async-start(), calls=%async_computation.3 | async-start | bytes 2359296 | tf_op jit(solution)/shard_map/all_gather | solution.py:218
  56.0 97.6 %reduce-scatter.2.cloned.1.call-start = ((), (), s32[]{:S(2)}) async-start(), calls=%async_computation.4 | async-start | bytes 2359296 | tf_op jit(solution)/shard_map/reduce_scatter | solution.py:232
  85.1 9.8 %copy-start.7 = (bf16[128,1024]{1,0:T(8,128)(2,1)S(1)}, bf16[128,1024]{1,0:T(8,128)(2,1)}, u32[]{:S(2)}) copy-start(bf16[128,1024]{1,0:T(8,128)(2,1)} %param.16) | copy-start | bytes 786436
  85.3 5.4 %collective-permute-start.5 = (f32[128]{0:T(128)S(1)}, f32[128]{0:T(128)S(1)}, u32[]{:S(2)}, u32[]{:S(2)}) collective-permute-start(f32[128]{0:T(128)S(1)} %get-tuple-element.24), channel_id=1, source_target_pairs={{0,1},{1,2},{2,3},{3,0},{4,5},{5,6},{6,7},{7,4},{8,9},{9,10},{10,1... | collective-permute-start | bytes 1544 | tf_op jit(solution)/shard_map/ppermute | solution.py:74
  85.8 4.9 %collective-permute-start.6 = (f32[128]{0:T(128)S(1)}, f32[128]{0:T(128)S(1)}, u32[]{:S(2)}, u32[]{:S(2)}) collective-permute-start(f32[128]{0:T(128)S(1)} %get-tuple-element.24), channel_id=1, source_target_pairs={{0,2},{1,3},{2,0},{3,1},{4,6},{5,7},{6,4},{7,5},{8,10},{9,11},{10,... | collective-permute-start | bytes 1544 | tf_op jit(solution)/shard_map/ppermute | solution.py:74
  89.1 3.5 %collective-permute-start.7 = (f32[128]{0:T(128)S(1)}, f32[128]{0:T(128)S(1)}, u32[]{:S(2)}, u32[]{:S(2)}) collective-permute-start(f32[128]{0:T(128)S(1)} %get-tuple-element.24), channel_id=1, source_target_pairs={{0,3},{1,0},{2,1},{3,2},{4,7},{5,4},{6,5},{7,6},{8,11},{9,8},{10,9... | collective-permute-start | bytes 1544 | tf_op jit(solution)/shard_map/ppermute | solution.py:74
  95.0 18.2 %collective-permute-start.8 = (bf16[127,1024]{1,0:T(8,128)(2,1)S(1)}, bf16[127,1024]{1,0:T(8,128)(2,1)S(1)}, u32[]{:S(2)}, u32[]{:S(2)}) collective-permute-start(bf16[127,1024]{1,0:T(8,128)(2,1)S(1)} %slice.55), channel_id=1, source_target_pairs={{4,0},{8,4},{12,8},{16,12},{20,16},{24,20},{28,24},{5,1},{9,5},{13... | collective-permute-start | bytes 780296 | tf_op jit(solution)/shard_map/ppermute | solution.py:30
  122.6 4.3 %collective-permute-start.10 = (bf16[136,1024]{1,0:T(8,128)(2,1)S(1)}, bf16[136,1024]{1,0:T(8,128)(2,1)S(1)}, u32[]{:S(2)}, u32[]{:S(2)}) collective-permute-start(bf16[136,1024]{1,0:T(8,128)(2,1)S(1)} %pad_maximum_fusion), channel_id=1, source_target_pairs={{0,4},{4,0},{8,12},{12,8},{16,20},{20,16},{24,28},{28,24},{1,5},{5... | collective-permute-start | bytes 835592 | tf_op jit(solution)/shard_map/ppermute | solution.py:62
  123.8 3.1 %collective-permute-start.9 = (bf16[6,1024]{1,0:T(8,128)(2,1)S(1)}, bf16[6,1024]{1,0:T(8,128)(2,1)S(1)}, u32[]{:S(2)}, u32[]{:S(2)}) collective-permute-start(bf16[6,1024]{1,0:T(8,128)(2,1)S(1)} %slice.57), channel_id=1, source_target_pairs={{4,0},{8,4},{12,8},{16,12},{20,16},{24,20},{28,24},{5,1},{9,5},{13... | collective-permute-start | bytes 36872 | tf_op jit(solution)/shard_map/ppermute | solution.py:30
  127.0 11.2 %collective-permute-start.11 = (bf16[136,1024]{1,0:T(8,128)(2,1)S(1)}, bf16[136,1024]{1,0:T(8,128)(2,1)}, u32[]{:S(2)}, u32[]{:S(2)}) collective-permute-start(bf16[136,1024]{1,0:T(8,128)(2,1)S(1)} %add_convert_fusion.1), channel_id=1, source_target_pairs={{0,8},{4,12},{8,0},{12,4},{16,24},{20,28},{24,16},{28,20},{1,9},{5... | collective-permute-start | bytes 835592 | tf_op jit(solution)/shard_map/ppermute | solution.py:62
  130.2 11.1 %copy-start.2 = (bf16[128,1024]{1,0:T(8,128)(2,1)S(1)}, bf16[128,1024]{1,0:T(8,128)(2,1)}, u32[]{:S(2)}) copy-start(bf16[128,1024]{1,0:T(8,128)(2,1)} %param.12) | copy-start | bytes 786436
  130.2 11.1 %copy-start.10 = (bf16[128,1024]{1,0:T(8,128)(2,1)S(1)}, bf16[128,1024]{1,0:T(8,128)(2,1)}, u32[]{:S(2)}) copy-start(bf16[128,1024]{1,0:T(8,128)(2,1)} %param.14) | copy-start | bytes 786436
  130.2 11.1 %copy-start.19 = (f32[128,1024]{1,0:T(8,128)S(1)}, f32[128,1024]{1,0:T(8,128)}, u32[]{:S(2)}) copy-start(f32[128,1024]{1,0:T(8,128)} %get-tuple-element.20) | copy-start | bytes 1572868
  139.2 9.1 %collective-permute-start.12 = (bf16[136,1024]{1,0:T(8,128)(2,1)S(1)}, bf16[136,1024]{1,0:T(8,128)(2,1)S(1)}, u32[]{:S(2)}, u32[]{:S(2)}) collective-permute-start(bf16[136,1024]{1,0:T(8,128)(2,1)S(1)} %add_convert_fusion), channel_id=1, source_target_pairs={{0,16},{4,20},{8,24},{12,28},{16,0},{20,4},{24,8},{28,12},{1,17},{... | collective-permute-start | bytes 835592 | tf_op jit(solution)/shard_map/ppermute | solution.py:62
  (17 other events, 43.6 us)
Sparse Core Ops, SparseCore 0:
  9.9 31.5 all-gather.2
  58.6 37.1 all-gather.4
  113.3 40.2 reduce-scatter.1

commit v12 on v8

--- a/solution.py
+++ b/solution.py
@@ -88,7 +88,7 @@
         lax.dot_general(query_head, key_head, contract_last, preferred_element_type=jnp.float32)
         * scale_factor
     )
-    scores = jnp.where(visible > 0.5, scores, -jnp.inf)
+    scores = jnp.where(visible, scores, -jnp.inf)
     row_max = jnp.max(scores, axis=1, keepdims=True)
     raised = jnp.exp(scores - row_max)
     return (raised * (1.0 / jnp.sum(raised, axis=1, keepdims=True))).astype(jnp.bfloat16)
@@ -96,51 +96,59 @@
 
 def value_block(scale_factor, q_ref, k_ref, cot_ref, vis_ref, dv_ref, w_ref):
     contract_first = (((0,), (0,)), ((), ()))
-    weights = head_weights(scale_factor, q_ref[...], k_ref[...], vis_ref[...])
-    w_ref[0] = weights
-    dv_ref[...] = lax.dot_general(
-        weights, cot_ref[...], contract_first, preferred_element_type=jnp.float32
-    ).astype(jnp.bfloat16)
+    visible = vis_ref[...] > 0.5
+    for head in range(w_ref.shape[0]):
+        columns = slice(head * HD, (head + 1) * HD)
+        weights = head_weights(scale_factor, q_ref[:, columns], k_ref[:, columns], visible)
+        w_ref[head] = weights
+        dv_ref[:, columns] = lax.dot_general(
+            weights, cot_ref[:, columns], contract_first, preferred_element_type=jnp.float32
+        ).astype(jnp.bfloat16)
 
 
 def attention_block(scale_factor, q_ref, k_ref, v_ref, cot_ref, w_ref, dk_ref, att_ref, dq_ref):
     contract_last = (((1,), (1,)), ((), ()))
     contract_first = (((0,), (0,)), ((), ()))
-    query_head = q_ref[...]
-    key_head = k_ref[...]
-    value_head = v_ref[...]
-    cotangent_head = cot_ref[...]
-    weights = w_ref[0]
-    attended = jnp.dot(weights, value_head, preferred_element_type=jnp.float32)
-    weight_grad = lax.dot_general(
-        cotangent_head, value_head, contract_last, preferred_element_type=jnp.float32
-    )
-    row_delta = jnp.sum(cotangent_head.astype(jnp.float32) * attended, axis=1, keepdims=True)
-    dscore = (scale_factor * weights.astype(jnp.float32) * (weight_grad - row_delta)).astype(
-        jnp.bfloat16
-    )
-    att_ref[...] = attended
-    dq_ref[...] = jnp.dot(dscore, key_head, preferred_element_type=jnp.float32).astype(jnp.bfloat16)
-    dk_ref[...] = lax.dot_general(
-        dscore, query_head, contract_first, preferred_element_type=jnp.float32
-    ).astype(jnp.bfloat16)
-
-
-def head_specs(local_rows, total_rows):
-    local_spec = pl.BlockSpec((local_rows, HD), lambda h: (0, h))
-    whole_spec = pl.BlockSpec((total_rows, HD), lambda h: (0, h))
-    weight_spec = pl.BlockSpec((1, local_rows, total_rows), lambda h: (h, 0, 0))
-    return local_spec, whole_spec, weight_spec
+    for head in range(w_ref.shape[0]):
+        columns = slice(head * HD, (head + 1) * HD)
+        query_head = q_ref[:, columns]
+        key_head = k_ref[:, columns]
+        value_head = v_ref[:, columns]
+        cotangent_head = cot_ref[:, columns]
+        weights = w_ref[head]
+        attended = jnp.dot(weights, value_head, preferred_element_type=jnp.float32)
+        weight_grad = lax.dot_general(
+            cotangent_head, value_head, contract_last, preferred_element_type=jnp.float32
+        )
+        row_delta = jnp.sum(cotangent_head.astype(jnp.float32) * attended, axis=1, keepdims=True)
+        dscore = (scale_factor * weights.astype(jnp.float32) * (weight_grad - row_delta)).astype(
+            jnp.bfloat16
+        )
+        att_ref[:, columns] = attended
+        dq_ref[:, columns] = jnp.dot(
+            dscore, key_head, preferred_element_type=jnp.float32
+        ).astype(jnp.bfloat16)
+        dk_ref[:, columns] = lax.dot_general(
+            dscore, query_head, contract_first, preferred_element_type=jnp.float32
+        ).astype(jnp.bfloat16)
+
+
+def head_specs(local_rows, total_rows, width_local):
+    group = 2 if (width_local // HD) % 2 == 0 else 1
+    local_spec = pl.BlockSpec((local_rows, group * HD), lambda h: (0, h))
+    whole_spec = pl.BlockSpec((total_rows, group * HD), lambda h: (0, h))
+    weight_spec = pl.BlockSpec((group, local_rows, total_rows), lambda h: (h, 0, 0))
+    return local_spec, whole_spec, weight_spec, width_local // (group * HD)
 
 
 def head_values_grad(queries, keys_whole, cotangent, visible, scale_factor):
     local_rows, width_local = queries.shape
     total_rows = keys_whole.shape[0]
-    local_spec, whole_spec, weight_spec = head_specs(local_rows, total_rows)
+    local_spec, whole_spec, weight_spec, steps = head_specs(local_rows, total_rows, width_local)
     mask_spec = pl.BlockSpec((local_rows, total_rows), lambda h: (0, 0))
     return pl.pallas_call(
         functools.partial(value_block, scale_factor),
-        grid=(width_local // HD,),
+        grid=(steps,),
         in_specs=[local_spec, whole_spec, local_spec, mask_spec],
         out_specs=[whole_spec, weight_spec],
         out_shape=[
@@ -153,10 +161,10 @@
 def head_attention(queries, keys_whole, values_whole, cotangent, weights, scale_factor):
     local_rows, width_local = queries.shape
     total_rows = keys_whole.shape[0]
-    local_spec, whole_spec, weight_spec = head_specs(local_rows, total_rows)
+    local_spec, whole_spec, weight_spec, steps = head_specs(local_rows, total_rows, width_local)
     return pl.pallas_call(
         functools.partial(attention_block, scale_factor),
-        grid=(width_local // HD,),
+        grid=(steps,),
         in_specs=[local_spec, whole_spec, whole_spec, local_spec, weight_spec],
         out_specs=[whole_spec, local_spec, local_spec],
         out_shape=[
@@ -213,11 +221,12 @@
     visible = (key_pos[None, :] <= query_pos[:, None]) & (segments[None, :] == query_seg[:, None])
     mask = visible.astype(jnp.float32)
     value_part, weights_all = head_values_grad(queries, keys_whole, cotangent, mask, scale_factor)
-    value_grad = lax.dynamic_slice_in_dim(value_part, position, local_rows, 0).astype(jnp.float32)
-    for distance in range(1, reach + 1):
-        block_start = ((ctx_index - distance) % ctx_count) * local_rows
-        leaving = lax.dynamic_slice_in_dim(value_part, block_start, local_rows, 0)
-        value_grad = value_grad + passed_along(leaving, "ctx", -distance).astype(jnp.float32)
+    value_grad = (
+        lax.all_to_all(value_part, "ctx", 0, 0, tiled=True)
+        .reshape(ctx_count, local_rows, width_local)
+        .astype(jnp.float32)
+        .sum(axis=0)
+    )
     values_whole = lax.all_gather(normed, "ctx", axis=0, tiled=True)
     key_part, attended_all, queries_grad = head_attention(
         queries, keys_whole, values_whole, cotangent, weights_all, scale_factor

time: 160 us -> 155 us (0.969)
  other arithmetic: 12.9 us -> 9.98 us
  Pallas kernels: 17.5 us -> 15 us
  waiting for transfers between devices: 49.5 us -> 51.2 us
  local copies, waits for them, and re-layouts: 9.71 us -> 8.06 us
    all_gather x1, waiting for transfers between devices: 0.02 us -> 27.3 us  [shards(): values_whole = lax.all_gather(normed, 'ctx', axis=0, tiled=True)]
    ppermute x10 -> x4, waiting for transfers between devices: 27.1 us -> 2.59 us  [passed_along(): lax.ppermute(value, axis, [(source, source + steps) for source in range(l...]
    ppermute x10 -> x4, starting transfers between devices: 17.2 us -> 9.45 us  [passed_along(): lax.ppermute(value, axis, [(source, source + steps) for source in range(l...]
    all_to_all x0 -> x1, starting transfers between devices: none -> 6.11 us  [shards(): lax.all_to_all(value_part, 'ctx', 0, 0, tiled=True)]
    pallas_call x2, Pallas kernels: 17.5 us -> 15 us  [the longest x1 7.72 us: head_values_grad(): pl.pallas_call(functools.partial(value_block, scale_factor), grid=(steps,...]
    ppermute x3, starting transfers between devices: 7.67 us -> 9.73 us  [butterfly_total(): lax.ppermute(rounded, axis, pairs).astype(value.dtype)]
  transfers between devices with their start and end apart: 22 -> 17, of which waited for: 15 -> 12; matrix products, arithmetic and copies ran while one was open for 25% -> 22% of each run, Pallas kernels for 6% -> 10%
where the time goes in v12:
time: 155 us; the launch traced here: 154 us
  waiting for transfers between devices  51.2 us (33%)
  starting transfers between devices  36 us (23%)
  matrix products  19.7 us (13%)
  Pallas kernels  15 us (10%)
  between operations  14.4 us (9%)
  other arithmetic  9.98 us (6%)
  local copies, waits for them, and re-layouts  8.06 us (5%)
    all_gather x1, waiting for transfers between devices, shards(): values_whole = lax.all_gather(normed, 'ctx', axis=0, tiled=True)  27.3 us
    conv_general_dilated x6, matrix products, depthwise(): lax.conv_general_dilated(padded[None], tap_rows[:, None, :], (1,), 'VALID...  19.7 us
    ppermute x3, waiting for transfers between devices, butterfly_total(): lax.ppermute(rounded, axis, pairs).astype(value.dtype)  13.8 us
    ppermute x6, starting transfers between devices, exchange_total(): arrived = lax.ppermute(value, axis, pairs)  10.6 us
    ppermute x3, starting transfers between devices, butterfly_total(): lax.ppermute(rounded, axis, pairs).astype(value.dtype)  9.73 us
    ppermute x4, starting transfers between devices, passed_along(): lax.ppermute(value, axis, [(source, source + steps) for source in range(l...  9.45 us
    pallas_call x1, Pallas kernels, head_values_grad(): pl.pallas_call(functools.partial(value_block, scale_factor), grid=(steps,...  7.72 us
    pallas_call x1, Pallas kernels, head_attention(): pl.pallas_call(functools.partial(attention_block, scale_factor), grid=(st...  7.27 us
  transfers between devices with their start and end apart: 17, of which 12 were waited for; matrix products, arithmetic and copies ran while one was open for 22% of the time, Pallas kernels for 10%

profile of v12, /device:TPU:0, one launch (start us, length us, event | category | flops | bytes accessed | tf_op | source)
XLA Modules:
  0.0 154.3 jit_solution(8640942585699332155)
XLA Ops:
  9.1 2.4 %collective-permute-start = (bf16[6,1024]{1,0:T(8,128)(2,1)S(1)}, bf16[6,1024]{1,0:T(8,128)(2,1)S(1)}, u32[]{:S(2)}, u32[]{:S(2)}) collective-permute-start(bf16[6,1024]{1,0:T(8,128)(2,1)S(1)} %slice.58), channel_id=1, source_target_pairs={{0,4},{4,8},{8,12},{12,16},{16,20},{20,24},{24,28},{1,5},{5,9},{9,... | collective-permute-start | bytes 36872 | tf_op jit(solution)/shard_map/ppermute | solution.py:30
  11.4 2.8 %rev.12 = f32[7,1024]{1,0:T(8,128)S(1)} reverse(f32[7,1024]{1,0:T(8,128)} %param.15), dimensions={0} | reverse | bytes 57344 | tf_op jit(solution)/shard_map/rev | solution.py:202
  16.5 4.5 %collective-permute-start.1 = (bf16[127,1024]{1,0:T(8,128)(2,1)S(1)}, bf16[127,1024]{1,0:T(8,128)(2,1)S(1)}, u32[]{:S(2)}, u32[]{:S(2)}) collective-permute-start(bf16[127,1024]{1,0:T(8,128)(2,1)S(1)} %slice.56), channel_id=1, source_target_pairs={{0,4},{4,8},{8,12},{12,16},{16,20},{20,24},{24,28},{1,5},{5,9},{9,... | collective-permute-start | bytes 780296 | tf_op jit(solution)/shard_map/ppermute | solution.py:30
  22.3 5.8 %fusion.8 = f32[1,128,1024]{2,0,1:T(1,128)S(1)} fusion(f32[1,255,1024]{2,1,0:T(8,128)S(1)} %maximum_bitcast_fusion, f32[128,1,1024]{2,0,1:T(8,128)S(1)} %bitcast.60), kind=kOutput, calls=%fused_computation.36 | convolution fusion | flops 201326592 | bytes 2093056 | tf_op jit(solution)/shard_map/conv_general_dilated | solution.py:34
  29.1 1.6 %collective-permute-start.2 = (f32[128]{0:T(128)S(1)}, f32[128]{0:T(128)S(1)}, u32[]{:S(2)}, u32[]{:S(2)}) collective-permute-start(f32[128]{0:T(128)S(1)} %get-tuple-element.31), channel_id=1, source_target_pairs={{0,1},{1,2},{2,3},{3,0},{4,5},{5,6},{6,7},{7,4},{8,9},{9,10},{10,1... | collective-permute-start | bytes 1544 | tf_op jit(solution)/shard_map/ppermute | solution.py:74
  30.8 2.6 %collective-permute-start.3 = (f32[128]{0:T(128)S(1)}, f32[128]{0:T(128)S(1)}, u32[]{:S(2)}, u32[]{:S(2)}) collective-permute-start(f32[128]{0:T(128)S(1)} %get-tuple-element.31), channel_id=1, source_target_pairs={{0,2},{1,3},{2,0},{3,1},{4,6},{5,7},{6,4},{7,5},{8,10},{9,11},{10,... | collective-permute-start | bytes 1544 | tf_op jit(solution)/shard_map/ppermute | solution.py:74
  33.3 1.3 collective-permute-start.4
  35.2 1.7 %collective-permute-done.4 = f32[128]{0:T(128)S(1)} collective-permute-done((f32[128]{0:T(128)S(1)}, f32[128]{0:T(128)S(1)}, u32[]{:S(2)}, u32[]{:S(2)}) %collective-permute-start.4) | collective-permute-done | bytes 544 | tf_op jit(solution)/shard_map/ppermute | solution.py:74
  38.9 2.6 %all-gather.3.cloned.1.call-done.k_ref = bf16[1024,1024]{1,0:T(8,128)(2,1)} async-done(((bf16[128,1024]{1,0:T(8,128)(2,1)}), bf16[1024,1024]{1,0:T(8,128)(2,1)}) %all-gather.3.cloned.1.call-update) | async-done | bytes 2097168 | tf_op jit(solution)/shard_map/all_gather | solution.py:216
  41.4 7.7 %shard_map.203 = (bf16[1024,1024]{1,0:T(8,128)(2,1)}, bf16[8,128,1024]{2,1,0:T(8,128)(2,1)}) custom-call(bf16[128,1024]{1,0:T(8,128)(2,1)} %q_ref.3, bf16[1024,1024]{1,0:T(8,128)(2,1)} %all-gather.3.cloned.1.call-done.k_ref, bf16[128,1024]{1,0:T(8,128)(2,1)} %cot_ref.3, f32[128,1024]{1,0:T(8,128)} %fusion.33.vis_ref), custom_call_target="tpu_custom_call" | custom-call | tf_op jit(solution)/shard_map/pallas_call | solution.py:149
  49.1 6.1 %all-to-all-start = ((bf16[8,128,1024]{2,1,0:T(8,128)(2,1)}), bf16[8,128,1024]{2,1,0:T(8,128)(2,1)S(1)}, u32[]{:S(2)}, u32[]{:S(2)}) async-start(bf16[8,128,1024]{2,1,0:T(8,128)(2,1)} %bitcast.57), calls=%async_computation | async-start | bytes 4194304 | tf_op jit(solution)/shard_map/all_to_all | solution.py:225
  55.3 27.3 %all-gather.5.cloned.1.call-done.v_ref = bf16[1024,1024]{1,0:T(8,128)(2,1)} async-done(((bf16[128,1024]{1,0:T(8,128)(2,1)}), bf16[1024,1024]{1,0:T(8,128)(2,1)}) %all-gather.5.cloned.1.call-update) | async-done | bytes 2097168 | tf_op jit(solution)/shard_map/all_gather | solution.py:230
  82.6 7.3 %shard_map.204 = (bf16[1024,1024]{1,0:T(8,128)(2,1)}, f32[128,1024]{1,0:T(8,128)}, bf16[128,1024]{1,0:T(8,128)(2,1)}) custom-call(bf16[128,1024]{1,0:T(8,128)(2,1)} %q_ref.3, bf16[1024,1024]{1,0:T(8,128)(2,1)} %all-gather.3.cloned.1.call-done.k_ref, bf16[1024,1024]{1,0:T(8,128)(2,1)} %all-gather.5.cloned.1.call-done.v_ref, bf16[128,1024]{1,0:T(8,128)(2,1)} %cot_ref.3, ...), custom_call_target="tpu_custom_call" | custom-call | tf_op jit(solution)/shard_map/pallas_call | solution.py:165
  91.6 2.6 %collective-permute-start.6 = (f32[128]{0:T(128)S(1)}, f32[128]{0:T(128)S(1)}, u32[]{:S(2)}, u32[]{:S(2)}) collective-permute-start(f32[128]{0:T(128)S(1)} %get-tuple-element.26), channel_id=1, source_target_pairs={{0,2},{1,3},{2,0},{3,1},{4,6},{5,7},{6,4},{7,5},{8,10},{9,11},{10,... | collective-permute-start | bytes 1544 | tf_op jit(solution)/shard_map/ppermute | solution.py:74
  96.1 1.7 %collective-permute-done.7 = f32[128]{0:T(128)S(1)} collective-permute-done((f32[128]{0:T(128)S(1)}, f32[128]{0:T(128)S(1)}, u32[]{:S(2)}, u32[]{:S(2)}) %collective-permute-start.7) | collective-permute-done | bytes 544 | tf_op jit(solution)/shard_map/ppermute | solution.py:74
  99.2 1.3 collective-permute-start.8
  100.5 5.8 %fusion.6 = bf16[1,128,1024]{2,0,1:T(2,128)(2,1)S(1)} fusion(f32[1,255,1024]{2,1,0:T(8,128)S(1)} %copy-done.9, f32[128,1,1024]{2,0,1:T(8,128)S(1)} %bitcast.55), kind=kOutput, calls=%fused_computation.34 | convolution fusion | flops 201326592 | bytes 1830912 | tf_op jit(solution)/shard_map/conv_general_dilated | solution.py:34
  107.3 5.8 %fusion = f32[1,128,1024]{2,0,1:T(1,128)S(1)} fusion(f32[1,255,1024]{2,1,0:T(8,128)S(1)} %maximum_bitcast_fusion.1, f32[128,1,1024]{2,0,1:T(8,128)S(1)} %bitcast.59), kind=kOutput, calls=%fused_computation.10 | convolution fusion | flops 201326592 | bytes 2093056 | tf_op jit(solution)/shard_map/conv_general_dilated | solution.py:34
  115.8 4.9 %collective-permute-start.10 = (bf16[136,1024]{1,0:T(8,128)(2,1)S(1)}, bf16[136,1024]{1,0:T(8,128)(2,1)S(1)}, u32[]{:S(2)}, u32[]{:S(2)}) collective-permute-start(bf16[136,1024]{1,0:T(8,128)(2,1)S(1)} %pad_maximum_fusion), channel_id=1, source_target_pairs={{0,4},{4,0},{8,12},{12,8},{16,20},{20,16},{24,28},{28,24},{1,5},{5... | collective-permute-start | bytes 835592 | tf_op jit(solution)/shard_map/ppermute | solution.py:62
  122.0 3.3 %collective-permute-start.11 = (bf16[136,1024]{1,0:T(8,128)(2,1)S(1)}, bf16[136,1024]{1,0:T(8,128)(2,1)S(1)}, u32[]{:S(2)}, u32[]{:S(2)}) collective-permute-start(bf16[136,1024]{1,0:T(8,128)(2,1)S(1)} %add_convert_fusion.1), channel_id=1, source_target_pairs={{0,8},{4,12},{8,0},{12,4},{16,24},{20,28},{24,16},{28,20},{1,9},{5... | collective-permute-start | bytes 835592 | tf_op jit(solution)/shard_map/ppermute | solution.py:62
  126.5 1.8 %collective-permute-done.9 = bf16[6,1024]{1,0:T(8,128)(2,1)S(1)} collective-permute-done((bf16[6,1024]{1,0:T(8,128)(2,1)S(1)}, bf16[6,1024]{1,0:T(8,128)(2,1)S(1)}, u32[]{:S(2)}, u32[]{:S(2)}) %collective-permute-start.9) | collective-permute-done | bytes 12320 | tf_op jit(solution)/shard_map/ppermute | solution.py:30
  129.2 4.0 %collective-permute-done.11 = bf16[136,1024]{1,0:T(8,128)(2,1)S(1)} collective-permute-done((bf16[136,1024]{1,0:T(8,128)(2,1)S(1)}, bf16[136,1024]{1,0:T(8,128)(2,1)S(1)}, u32[]{:S(2)}, u32[]{:S(2)}) %collective-permute-start.11) | collective-permute-done | bytes 278560 | tf_op jit(solution)/shard_map/ppermute | solution.py:62
  133.4 1.5 collective-permute-start.12
  137.1 8.6 %collective-permute-done.12 = bf16[136,1024]{1,0:T(8,128)(2,1)S(1)} collective-permute-done((bf16[136,1024]{1,0:T(8,128)(2,1)S(1)}, bf16[136,1024]{1,0:T(8,128)(2,1)S(1)}, u32[]{:S(2)}, u32[]{:S(2)}) %collective-permute-start.12) | collective-permute-done | bytes 278560 | tf_op jit(solution)/shard_map/ppermute | solution.py:62
  (129 shorter events, 25.0 us)
Async XLA Ops:
  7.2 34.2 %all-gather.3.cloned.1.call-start = ((), (), s32[]{:S(2)}) async-start(), calls=%async_computation.2 | async-start | bytes 2359296 | tf_op jit(solution)/shard_map/all_gather | solution.py:216
  7.9 74.7 %all-gather.5.cloned.1.call-start = ((), (), s32[]{:S(2)}) async-start(), calls=%async_computation.3 | async-start | bytes 2359296 | tf_op jit(solution)/shard_map/all_gather | solution.py:230
  9.1 5.2 %collective-permute-start = (bf16[6,1024]{1,0:T(8,128)(2,1)S(1)}, bf16[6,1024]{1,0:T(8,128)(2,1)S(1)}, u32[]{:S(2)}, u32[]{:S(2)}) collective-permute-start(bf16[6,1024]{1,0:T(8,128)(2,1)S(1)} %slice.58), channel_id=1, source_target_pairs={{0,4},{4,8},{8,12},{12,16},{16,20},{20,24},{24,28},{1,5},{5,9},{9,... | collective-permute-start | bytes 36872 | tf_op jit(solution)/shard_map/ppermute | solution.py:30
  16.5 5.7 %collective-permute-start.1 = (bf16[127,1024]{1,0:T(8,128)(2,1)S(1)}, bf16[127,1024]{1,0:T(8,128)(2,1)S(1)}, u32[]{:S(2)}, u32[]{:S(2)}) collective-permute-start(bf16[127,1024]{1,0:T(8,128)(2,1)S(1)} %slice.56), channel_id=1, source_target_pairs={{0,4},{4,8},{8,12},{12,16},{16,20},{20,24},{24,28},{1,5},{5,9},{9,... | collective-permute-start | bytes 780296 | tf_op jit(solution)/shard_map/ppermute | solution.py:30
  22.3 6.6 %copy-start.6 = (bf16[128,1024]{1,0:T(8,128)(2,1)S(1)}, bf16[128,1024]{1,0:T(8,128)(2,1)}, u32[]{:S(2)}) copy-start(bf16[128,1024]{1,0:T(8,128)(2,1)} %param.16) | copy-start | bytes 786436
  22.3 14.6 %copy-start.20 = (f32[1024]{0:T(1024)S(1)}, f32[1024]{0:T(1024)}, u32[]{:S(2)}) copy-start(f32[1024]{0:T(1024)} %param.19) | copy-start | bytes 12292
  28.1 9.7 %copy-start.22 = (s32[1024]{0:T(1024)S(1)}, s32[1024]{0:T(1024)}, u32[]{:S(2)}) copy-start(s32[1024]{0:T(1024)} %param.22) | copy-start | bytes 12292
  29.1 5.6 %collective-permute-start.2 = (f32[128]{0:T(128)S(1)}, f32[128]{0:T(128)S(1)}, u32[]{:S(2)}, u32[]{:S(2)}) collective-permute-start(f32[128]{0:T(128)S(1)} %get-tuple-element.31), channel_id=1, source_target_pairs={{0,1},{1,2},{2,3},{3,0},{4,5},{5,6},{6,7},{7,4},{8,9},{9,10},{10,1... | collective-permute-start | bytes 1544 | tf_op jit(solution)/shard_map/ppermute | solution.py:74
  30.8 4.4 %collective-permute-start.3 = (f32[128]{0:T(128)S(1)}, f32[128]{0:T(128)S(1)}, u32[]{:S(2)}, u32[]{:S(2)}) collective-permute-start(f32[128]{0:T(128)S(1)} %get-tuple-element.31), channel_id=1, source_target_pairs={{0,2},{1,3},{2,0},{3,1},{4,6},{5,7},{6,4},{7,5},{8,10},{9,11},{10,... | collective-permute-start | bytes 1544 | tf_op jit(solution)/shard_map/ppermute | solution.py:74
  33.3 3.5 %collective-permute-start.4 = (f32[128]{0:T(128)S(1)}, f32[128]{0:T(128)S(1)}, u32[]{:S(2)}, u32[]{:S(2)}) collective-permute-start(f32[128]{0:T(128)S(1)} %get-tuple-element.31), channel_id=1, source_target_pairs={{0,3},{1,0},{2,1},{3,2},{4,7},{5,4},{6,5},{7,6},{8,11},{9,8},{10,9... | collective-permute-start | bytes 1544 | tf_op jit(solution)/shard_map/ppermute | solution.py:74
  49.1 40.7 %all-to-all-start = ((bf16[8,128,1024]{2,1,0:T(8,128)(2,1)}), bf16[8,128,1024]{2,1,0:T(8,128)(2,1)S(1)}, u32[]{:S(2)}, u32[]{:S(2)}) async-start(bf16[8,128,1024]{2,1,0:T(8,128)(2,1)} %bitcast.57), calls=%async_computation | async-start | bytes 4194304 | tf_op jit(solution)/shard_map/all_to_all | solution.py:225
  55.3 92.5 %reduce-scatter.2.cloned.1.call-start = ((), (), s32[]{:S(2)}) async-start(), calls=%async_computation.4 | async-start | bytes 2359296 | tf_op jit(solution)/shard_map/reduce_scatter | solution.py:236
  90.2 7.7 %copy-start = (bf16[128,1024]{1,0:T(8,128)(2,1)S(1)}, bf16[128,1024]{1,0:T(8,128)(2,1)}, u32[]{:S(2)}) copy-start(bf16[128,1024]{1,0:T(8,128)(2,1)} %cot_ref.3) | copy-start | bytes 786436
  90.2 7.7 %copy-start.3 = (f32[1,128,1024]{2,0,1:T(1,128)S(1)}, f32[1,128,1024]{2,0,1:T(1,128)}, u32[]{:S(2)}) copy-start(f32[1,128,1024]{2,0,1:T(1,128)} %copy-done.2) | copy-start | bytes 1572868
  90.2 7.7 %copy-start.19 = (f32[128,1024]{1,0:T(8,128)S(1)}, f32[128,1024]{1,0:T(8,128)}, u32[]{:S(2)}) copy-start(f32[128,1024]{1,0:T(8,128)} %get-tuple-element.19) | copy-start | bytes 1572868
  90.4 5.4 %collective-permute-start.5 = (f32[128]{0:T(128)S(1)}, f32[128]{0:T(128)S(1)}, u32[]{:S(2)}, u32[]{:S(2)}) collective-permute-start(f32[128]{0:T(128)S(1)} %get-tuple-element.26), channel_id=1, source_target_pairs={{0,1},{1,2},{2,3},{3,0},{4,5},{5,6},{6,7},{7,4},{8,9},{9,10},{10,1... | collective-permute-start | bytes 1544 | tf_op jit(solution)/shard_map/ppermute | solution.py:74
  91.6 4.4 %collective-permute-start.6 = (f32[128]{0:T(128)S(1)}, f32[128]{0:T(128)S(1)}, u32[]{:S(2)}, u32[]{:S(2)}) collective-permute-start(f32[128]{0:T(128)S(1)} %get-tuple-element.26), channel_id=1, source_target_pairs={{0,2},{1,3},{2,0},{3,1},{4,6},{5,7},{6,4},{7,5},{8,10},{9,11},{10,... | collective-permute-start | bytes 1544 | tf_op jit(solution)/shard_map/ppermute | solution.py:74
  94.3 3.5 %collective-permute-start.7 = (f32[128]{0:T(128)S(1)}, f32[128]{0:T(128)S(1)}, u32[]{:S(2)}, u32[]{:S(2)}) collective-permute-start(f32[128]{0:T(128)S(1)} %get-tuple-element.26), channel_id=1, source_target_pairs={{0,3},{1,0},{2,1},{3,2},{4,7},{5,4},{6,5},{7,6},{8,11},{9,8},{10,9... | collective-permute-start | bytes 1544 | tf_op jit(solution)/shard_map/ppermute | solution.py:74
  99.2 7.6 %collective-permute-start.8 = (bf16[127,1024]{1,0:T(8,128)(2,1)S(1)}, bf16[127,1024]{1,0:T(8,128)(2,1)S(1)}, u32[]{:S(2)}, u32[]{:S(2)}) collective-permute-start(bf16[127,1024]{1,0:T(8,128)(2,1)S(1)} %slice.55), channel_id=1, source_target_pairs={{4,0},{8,4},{12,8},{16,12},{20,16},{24,20},{28,24},{5,1},{9,5},{13... | collective-permute-start | bytes 780296 | tf_op jit(solution)/shard_map/ppermute | solution.py:30
  115.8 6.1 %collective-permute-start.10 = (bf16[136,1024]{1,0:T(8,128)(2,1)S(1)}, bf16[136,1024]{1,0:T(8,128)(2,1)S(1)}, u32[]{:S(2)}, u32[]{:S(2)}) collective-permute-start(bf16[136,1024]{1,0:T(8,128)(2,1)S(1)} %pad_maximum_fusion), channel_id=1, source_target_pairs={{0,4},{4,0},{8,12},{12,8},{16,20},{20,16},{24,28},{28,24},{1,5},{5... | collective-permute-start | bytes 835592 | tf_op jit(solution)/shard_map/ppermute | solution.py:62
  122.0 11.3 %collective-permute-start.11 = (bf16[136,1024]{1,0:T(8,128)(2,1)S(1)}, bf16[136,1024]{1,0:T(8,128)(2,1)S(1)}, u32[]{:S(2)}, u32[]{:S(2)}) collective-permute-start(bf16[136,1024]{1,0:T(8,128)(2,1)S(1)} %add_convert_fusion.1), channel_id=1, source_target_pairs={{0,8},{4,12},{8,0},{12,4},{16,24},{20,28},{24,16},{28,20},{1,9},{5... | collective-permute-start | bytes 835592 | tf_op jit(solution)/shard_map/ppermute | solution.py:62
  125.2 3.1 %collective-permute-start.9 = (bf16[6,1024]{1,0:T(8,128)(2,1)S(1)}, bf16[6,1024]{1,0:T(8,128)(2,1)S(1)}, u32[]{:S(2)}, u32[]{:S(2)}) collective-permute-start(bf16[6,1024]{1,0:T(8,128)(2,1)S(1)} %slice.57), channel_id=1, source_target_pairs={{4,0},{8,4},{12,8},{16,12},{20,16},{24,20},{28,24},{5,1},{9,5},{13... | collective-permute-start | bytes 36872 | tf_op jit(solution)/shard_map/ppermute | solution.py:30
  128.4 6.5 %copy-start.21 = (f32[7,1024]{1,0:T(8,128)S(1)}, f32[7,1024]{1,0:T(8,128)}, u32[]{:S(2)}) copy-start(f32[7,1024]{1,0:T(8,128)} %param.15) | copy-start | bytes 86020
  133.4 12.3 %collective-permute-start.12 = (bf16[136,1024]{1,0:T(8,128)(2,1)S(1)}, bf16[136,1024]{1,0:T(8,128)(2,1)S(1)}, u32[]{:S(2)}, u32[]{:S(2)}) collective-permute-start(bf16[136,1024]{1,0:T(8,128)(2,1)S(1)} %add_convert_fusion), channel_id=1, source_target_pairs={{0,16},{4,20},{8,24},{12,28},{16,0},{20,4},{24,8},{28,12},{1,17},{... | collective-permute-start | bytes 835592 | tf_op jit(solution)/shard_map/ppermute | solution.py:62
  (17 other events, 47.5 us)
Sparse Core Ops, SparseCore 0:
  9.9 31.4 all-gather.2
  43.9 38.6 all-gather.4
  95.6 49.5 reduce-scatter.1

commit v13 on v12

--- a/solution.py
+++ b/solution.py
@@ -213,7 +213,9 @@
     normed = (second_wide * inverse_rms[:, None] * scaling).astype(jnp.bfloat16)
     ctx_count = lax.axis_size("ctx")
     ctx_index = lax.axis_index("ctx")
-    keys_whole = lax.all_gather(matchers, "ctx", axis=0, tiled=True)
+    keys_whole = lax.all_to_all(
+        jnp.tile(matchers, (ctx_count, 1)), "ctx", 0, 0, tiled=True
+    )
     reach = min(ctx_count - 1, (3 * total_rows // 4 - 1 + local_rows - 1) // local_rows)
     query_pos = position + jnp.arange(local_rows, dtype=jnp.int32)
     key_pos = jnp.arange(total_rows, dtype=jnp.int32)

time: 155 us -> 165 us (1.065)
  blocking collectives: 0 us -> 35.7 us
  waiting for transfers between devices: 51.2 us -> 25 us
  starting transfers between devices: 36 us -> 27.4 us
  local copies, waits for them, and re-layouts: 8.06 us -> 16.3 us
    all_to_all x0 -> x1, blocking collectives: none -> 35.7 us  [shards(): lax.all_to_all(value_part, 'ctx', 0, 0, tiled=True)]
    all_gather x1, waiting for transfers between devices: 27.3 us -> 0.02 us  [shards(): values_whole = lax.all_gather(normed, 'ctx', axis=0, tiled=True)]
    ppermute x3, starting transfers between devices: 9.73 us -> 3.23 us  [butterfly_total(): lax.ppermute(rounded, axis, pairs).astype(value.dtype)]
    all_to_all x1, waiting for transfers between devices: 0.01 us -> 4.95 us  [shards(): lax.all_to_all(jnp.tile(matchers, (ctx_count, 1)), 'ctx', 0, 0, tiled=True)]
    rev x1, local copies, waits for them, and re-layouts: 0.24 us -> 4.73 us  [shards(): conv_two = depthwise(padded_two, kernel[::-1])]
    all_gather x1 -> x0, waiting for transfers between devices: 2.55 us -> none  [shards(): keys_whole = lax.all_gather(matchers, 'ctx', axis=0, tiled=True)]
    all_to_all x1, starting transfers between devices: 6.11 us -> 3.6 us  [shards(): lax.all_to_all(jnp.tile(matchers, (ctx_count, 1)), 'ctx', 0, 0, tiled=True)]
  transfers between devices with their start and end apart: 17 -> 16, of which waited for: 12 -> 9; matrix products, arithmetic and copies ran while one was open for 22% -> 24% of each run, Pallas kernels for 10% -> 5%
where the time goes in v13:
time: 165 us; the launch traced here: 164 us
  blocking collectives  35.7 us (22%)
  starting transfers between devices  27.4 us (17%)
  waiting for transfers between devices  25 us (15%)
  matrix products  19.6 us (12%)
  local copies, waits for them, and re-layouts  16.3 us (10%)
  Pallas kernels  15 us (9%)
  between operations  14.7 us (9%)
  other arithmetic  9.97 us (6%)
    all_to_all x1, blocking collectives, shards(): lax.all_to_all(value_part, 'ctx', 0, 0, tiled=True)  35.7 us
    conv_general_dilated x6, matrix products, depthwise(): lax.conv_general_dilated(padded[None], tap_rows[:, None, :], (1,), 'VALID...  19.6 us
    ppermute x3, waiting for transfers between devices, butterfly_total(): lax.ppermute(rounded, axis, pairs).astype(value.dtype)  14.2 us
    ppermute x6, starting transfers between devices, exchange_total(): arrived = lax.ppermute(value, axis, pairs)  11 us
    ppermute x4, starting transfers between devices, passed_along(): lax.ppermute(value, axis, [(source, source + steps) for source in range(l...  9.44 us
    pallas_call x1, Pallas kernels, head_values_grad(): pl.pallas_call(functools.partial(value_block, scale_factor), grid=(steps,...  7.76 us
    pallas_call x1, Pallas kernels, head_attention(): pl.pallas_call(functools.partial(attention_block, scale_factor), grid=(st...  7.29 us
    all_to_all x1, waiting for transfers between devices, shards(): lax.all_to_all(jnp.tile(matchers, (ctx_count, 1)), 'ctx', 0, 0, tiled=True)  4.95 us
  transfers between devices with their start and end apart: 16, of which 9 were waited for; matrix products, arithmetic and copies ran while one was open for 24% of the time, Pallas kernels for 5%

profile of v13, /device:TPU:0, one launch (start us, length us, event | category | flops | bytes accessed | tf_op | source)
XLA Modules:
  0.0 163.7 jit_solution(1621858003373399093)
XLA Ops:
  8.3 2.4 %collective-permute-start = (bf16[6,1024]{1,0:T(8,128)(2,1)S(1)}, bf16[6,1024]{1,0:T(8,128)(2,1)S(1)}, u32[]{:S(2)}, u32[]{:S(2)}) collective-permute-start(bf16[6,1024]{1,0:T(8,128)(2,1)S(1)} %slice.58), channel_id=1, source_target_pairs={{0,4},{4,8},{8,12},{12,16},{16,20},{20,24},{24,28},{1,5},{5,9},{9,... | collective-permute-start | bytes 36872 | tf_op jit(solution)/shard_map/ppermute | solution.py:30
  10.7 2.8 %rev.12 = f32[7,1024]{1,0:T(8,128)S(1)} reverse(f32[7,1024]{1,0:T(8,128)} %param.15), dimensions={0} | reverse | bytes 57344 | tf_op jit(solution)/shard_map/rev | solution.py:202
  16.4 4.5 %collective-permute-start.1 = (bf16[127,1024]{1,0:T(8,128)(2,1)}, bf16[127,1024]{1,0:T(8,128)(2,1)S(1)}, u32[]{:S(2)}, u32[]{:S(2)}) collective-permute-start(bf16[127,1024]{1,0:T(8,128)(2,1)} %slice.56), channel_id=1, source_target_pairs={{0,4},{4,8},{8,12},{12,16},{16,20},{20,24},{24,28},{1,5},{5,9},{9,... | collective-permute-start | bytes 780296 | tf_op jit(solution)/shard_map/ppermute | solution.py:30
  20.9 1.6 tile.2
  22.5 3.6 %all-to-all-start = ((bf16[8,128,1024]{2,1,0:T(8,128)(2,1)}), bf16[8,128,1024]{2,1,0:T(8,128)(2,1)S(1)}, u32[]{:S(2)}, u32[]{:S(2)}) async-start(bf16[8,128,1024]{2,1,0:T(8,128)(2,1)} %tile.2), calls=%async_computation | async-start | bytes 4194304 | tf_op jit(solution)/shard_map/all_to_all | solution.py:216
  26.2 4.7 %rev.13 = f32[128,1024]{1,0:T(8,128)} reverse(f32[128,1024]{1,0:T(8,128)} %param.18), dimensions={0} | reverse | bytes 1048576 | tf_op jit(solution)/shard_map/rev | solution.py:208
  32.0 5.8 %fusion.8 = f32[1,128,1024]{2,0,1:T(1,128)S(1)} fusion(f32[1,255,1024]{2,1,0:T(8,128)S(1)} %maximum_bitcast_fusion, f32[128,1,1024]{2,0,1:T(8,128)S(1)} %bitcast.63), kind=kOutput, calls=%fused_computation.36 | convolution fusion | flops 201326592 | bytes 2093056 | tf_op jit(solution)/shard_map/conv_general_dilated | solution.py:34
  38.0 1.6 collective-permute-start.2
  39.6 2.6 %collective-permute-start.3 = (f32[128]{0:T(128)S(1)}, f32[128]{0:T(128)S(1)}, u32[]{:S(2)}, u32[]{:S(2)}) collective-permute-start(f32[128]{0:T(128)S(1)} %get-tuple-element.31), channel_id=1, source_target_pairs={{0,2},{1,3},{2,0},{3,1},{4,6},{5,7},{6,4},{7,5},{8,10},{9,11},{10,... | collective-permute-start | bytes 1544 | tf_op jit(solution)/shard_map/ppermute | solution.py:74
  44.1 1.7 %collective-permute-done.4 = f32[128]{0:T(128)S(1)} collective-permute-done((f32[128]{0:T(128)S(1)}, f32[128]{0:T(128)S(1)}, u32[]{:S(2)}, u32[]{:S(2)}) %collective-permute-start.4) | collective-permute-done | bytes 544 | tf_op jit(solution)/shard_map/ppermute | solution.py:74
  47.8 4.9 %all-to-all-done = bf16[8,128,1024]{2,1,0:T(8,128)(2,1)S(1)} async-done(((bf16[8,128,1024]{2,1,0:T(8,128)(2,1)}), bf16[8,128,1024]{2,1,0:T(8,128)(2,1)S(1)}, u32[]{:S(2)}, u32[]{:S(2)}) %all-to-all-start) | async-done | bytes 2097184 | tf_op jit(solution)/shard_map/all_to_all | solution.py:216
  52.8 1.4 copy-done
  54.1 7.8 %shard_map.203 = (bf16[1024,1024]{1,0:T(8,128)(2,1)}, bf16[8,128,1024]{2,1,0:T(8,128)(2,1)}) custom-call(bf16[128,1024]{1,0:T(8,128)(2,1)} %q_ref.3, bf16[1024,1024]{1,0:T(8,128)(2,1)} %bitcast.56, bf16[128,1024]{1,0:T(8,128)(2,1)} %cot_ref.3, f32[128,1024]{1,0:T(8,128)} %fusion.33.vis_ref), custom_call_target="tpu_custom_call" | custom-call | tf_op jit(solution)/shard_map/pallas_call | solution.py:149
  61.9 35.7 %all_to_all.17 = bf16[8,128,1024]{2,1,0:T(8,128)(2,1)S(1)} all-to-all(bf16[8,128,1024]{2,1,0:T(8,128)(2,1)} %bitcast.60), channel_id=1, replica_groups=mesh['ctx'=8,'tp'=4] {'ctx'}, dimensions={0} | all-to-all | bytes 4194304 | tf_op jit(solution)/shard_map/all_to_all | solution.py:227
  98.0 7.3 %shard_map.204 = (bf16[1024,1024]{1,0:T(8,128)(2,1)}, f32[128,1024]{1,0:T(8,128)}, bf16[128,1024]{1,0:T(8,128)(2,1)}) custom-call(bf16[128,1024]{1,0:T(8,128)(2,1)} %q_ref.3, bf16[1024,1024]{1,0:T(8,128)(2,1)} %bitcast.57, bf16[1024,1024]{1,0:T(8,128)(2,1)} %all-gather.2.cloned.1.call-done.v_ref, bf16[128,1024]{1,0:T(8,128)(2,1)} %cot_ref.3, ...), custom_call_target="tpu_custom_call" | custom-call | tf_op jit(solution)/shard_map/pallas_call | solution.py:165
  105.5 1.6 collective-permute-start.5
  107.1 2.4 %collective-permute-start.6 = (f32[128]{0:T(128)S(1)}, f32[128]{0:T(128)S(1)}, u32[]{:S(2)}, u32[]{:S(2)}) collective-permute-start(f32[128]{0:T(128)S(1)} %get-tuple-element.26), channel_id=1, source_target_pairs={{0,2},{1,3},{2,0},{3,1},{4,6},{5,7},{6,4},{7,5},{8,10},{9,11},{10,... | collective-permute-start | bytes 1544 | tf_op jit(solution)/shard_map/ppermute | solution.py:74
  109.5 1.4 collective-permute-start.7
  111.6 1.5 collective-permute-done.7
  115.7 5.8 %fusion.6 = bf16[1,128,1024]{2,0,1:T(2,128)(2,1)S(1)} fusion(f32[1,255,1024]{2,1,0:T(8,128)S(1)} %copy-done.8, f32[128,1,1024]{2,0,1:T(8,128)S(1)} %bitcast.58), kind=kOutput, calls=%fused_computation.34 | convolution fusion | flops 201326592 | bytes 1830912 | tf_op jit(solution)/shard_map/conv_general_dilated | solution.py:34
  122.5 5.8 %fusion = f32[1,128,1024]{2,0,1:T(1,128)S(1)} fusion(f32[1,255,1024]{2,1,0:T(8,128)S(1)} %maximum_bitcast_fusion.1, f32[128,1,1024]{2,0,1:T(8,128)S(1)} %bitcast.62), kind=kOutput, calls=%fused_computation.10 | convolution fusion | flops 201326592 | bytes 2093056 | tf_op jit(solution)/shard_map/conv_general_dilated | solution.py:34
  135.5 1.8 %collective-permute-done.9 = bf16[6,1024]{1,0:T(8,128)(2,1)S(1)} collective-permute-done((bf16[6,1024]{1,0:T(8,128)(2,1)S(1)}, bf16[6,1024]{1,0:T(8,128)(2,1)S(1)}, u32[]{:S(2)}, u32[]{:S(2)}) %collective-permute-start.9) | collective-permute-done | bytes 12320 | tf_op jit(solution)/shard_map/ppermute | solution.py:30
  138.2 4.2 %collective-permute-done.11 = bf16[136,1024]{1,0:T(8,128)(2,1)S(1)} collective-permute-done((bf16[136,1024]{1,0:T(8,128)(2,1)S(1)}, bf16[136,1024]{1,0:T(8,128)(2,1)S(1)}, u32[]{:S(2)}, u32[]{:S(2)}) %collective-permute-start.11) | collective-permute-done | bytes 278560 | tf_op jit(solution)/shard_map/ppermute | solution.py:62
  146.0 8.8 %collective-permute-done.12 = bf16[136,1024]{1,0:T(8,128)(2,1)S(1)} collective-permute-done((bf16[136,1024]{1,0:T(8,128)(2,1)S(1)}, bf16[136,1024]{1,0:T(8,128)(2,1)S(1)}, u32[]{:S(2)}, u32[]{:S(2)}) %collective-permute-start.12) | collective-permute-done | bytes 278560 | tf_op jit(solution)/shard_map/ppermute | solution.py:62
  (128 shorter events, 27.5 us)
Async XLA Ops:
  8.3 5.2 %collective-permute-start = (bf16[6,1024]{1,0:T(8,128)(2,1)S(1)}, bf16[6,1024]{1,0:T(8,128)(2,1)S(1)}, u32[]{:S(2)}, u32[]{:S(2)}) collective-permute-start(bf16[6,1024]{1,0:T(8,128)(2,1)S(1)} %slice.58), channel_id=1, source_target_pairs={{0,4},{4,8},{8,12},{12,16},{16,20},{20,24},{24,28},{1,5},{5,9},{9,... | collective-permute-start | bytes 36872 | tf_op jit(solution)/shard_map/ppermute | solution.py:30
  16.4 14.6 %collective-permute-start.1 = (bf16[127,1024]{1,0:T(8,128)(2,1)}, bf16[127,1024]{1,0:T(8,128)(2,1)S(1)}, u32[]{:S(2)}, u32[]{:S(2)}) collective-permute-start(bf16[127,1024]{1,0:T(8,128)(2,1)} %slice.56), channel_id=1, source_target_pairs={{0,4},{4,8},{8,12},{12,16},{16,20},{20,24},{24,28},{1,5},{5,9},{9,... | collective-permute-start | bytes 780296 | tf_op jit(solution)/shard_map/ppermute | solution.py:30
  22.5 30.2 %all-to-all-start = ((bf16[8,128,1024]{2,1,0:T(8,128)(2,1)}), bf16[8,128,1024]{2,1,0:T(8,128)(2,1)S(1)}, u32[]{:S(2)}, u32[]{:S(2)}) async-start(bf16[8,128,1024]{2,1,0:T(8,128)(2,1)} %tile.2), calls=%async_computation | async-start | bytes 4194304 | tf_op jit(solution)/shard_map/all_to_all | solution.py:216
  26.1 71.9 %all-gather.2.cloned.1.call-start = ((), (), s32[]{:S(2)}) async-start(), calls=%async_computation.3 | async-start | bytes 2359296 | tf_op jit(solution)/shard_map/all_gather | solution.py:232
  31.1 6.6 %copy-start.7 = (f32[1,255,1024]{2,1,0:T(8,128)}, f32[1,255,1024]{2,1,0:T(8,128)S(1)}, u32[]{:S(2)}) copy-start(f32[1,255,1024]{2,1,0:T(8,128)S(1)} %maximum_bitcast_fusion) | copy-start | bytes 3133444
  32.0 5.8 %copy-start.5 = (bf16[128,1024]{1,0:T(8,128)(2,1)S(1)}, bf16[128,1024]{1,0:T(8,128)(2,1)}, u32[]{:S(2)}) copy-start(bf16[128,1024]{1,0:T(8,128)(2,1)} %param.16) | copy-start | bytes 786436
  32.0 13.8 %copy-start.20 = (f32[1024]{0:T(1024)S(1)}, f32[1024]{0:T(1024)}, u32[]{:S(2)}) copy-start(f32[1024]{0:T(1024)} %param.19) | copy-start | bytes 12292
  37.8 9.0 %copy-start.22 = (s32[1024]{0:T(1024)S(1)}, s32[1024]{0:T(1024)}, u32[]{:S(2)}) copy-start(s32[1024]{0:T(1024)} %param.22) | copy-start | bytes 12292
  38.0 5.6 %collective-permute-start.2 = (f32[128]{0:T(128)S(1)}, f32[128]{0:T(128)S(1)}, u32[]{:S(2)}, u32[]{:S(2)}) collective-permute-start(f32[128]{0:T(128)S(1)} %get-tuple-element.31), channel_id=1, source_target_pairs={{0,1},{1,2},{2,3},{3,0},{4,5},{5,6},{6,7},{7,4},{8,9},{9,10},{10,1... | collective-permute-start | bytes 1544 | tf_op jit(solution)/shard_map/ppermute | solution.py:74
  39.6 4.4 %collective-permute-start.3 = (f32[128]{0:T(128)S(1)}, f32[128]{0:T(128)S(1)}, u32[]{:S(2)}, u32[]{:S(2)}) collective-permute-start(f32[128]{0:T(128)S(1)} %get-tuple-element.31), channel_id=1, source_target_pairs={{0,2},{1,3},{2,0},{3,1},{4,6},{5,7},{6,4},{7,5},{8,10},{9,11},{10,... | collective-permute-start | bytes 1544 | tf_op jit(solution)/shard_map/ppermute | solution.py:74
  42.2 3.5 %collective-permute-start.4 = (f32[128]{0:T(128)S(1)}, f32[128]{0:T(128)S(1)}, u32[]{:S(2)}, u32[]{:S(2)}) collective-permute-start(f32[128]{0:T(128)S(1)} %get-tuple-element.31), channel_id=1, source_target_pairs={{0,3},{1,0},{2,1},{3,2},{4,7},{5,4},{6,5},{7,6},{8,11},{9,8},{10,9... | collective-permute-start | bytes 1544 | tf_op jit(solution)/shard_map/ppermute | solution.py:74
  46.7 110.2 %reduce-scatter.2.cloned.1.call-start = ((), (), s32[]{:S(2)}) async-start(), calls=%async_computation.4 | async-start | bytes 2359296 | tf_op jit(solution)/shard_map/reduce_scatter | solution.py:238
  105.3 7.8 %copy-start.1 = (bf16[128,1024]{1,0:T(8,128)(2,1)S(1)}, bf16[128,1024]{1,0:T(8,128)(2,1)}, u32[]{:S(2)}) copy-start(bf16[128,1024]{1,0:T(8,128)(2,1)} %cot_ref.3) | copy-start | bytes 786436
  105.3 7.8 %copy-start.18 = (f32[128,1024]{1,0:T(8,128)S(1)}, f32[128,1024]{1,0:T(8,128)}, u32[]{:S(2)}) copy-start(f32[128,1024]{1,0:T(8,128)} %get-tuple-element.19) | copy-start | bytes 1572868
  105.5 5.5 %collective-permute-start.5 = (f32[128]{0:T(128)S(1)}, f32[128]{0:T(128)S(1)}, u32[]{:S(2)}, u32[]{:S(2)}) collective-permute-start(f32[128]{0:T(128)S(1)} %get-tuple-element.26), channel_id=1, source_target_pairs={{0,1},{1,2},{2,3},{3,0},{4,5},{5,6},{6,7},{7,4},{8,9},{9,10},{10,1... | collective-permute-start | bytes 1544 | tf_op jit(solution)/shard_map/ppermute | solution.py:74
  107.1 4.4 %collective-permute-start.6 = (f32[128]{0:T(128)S(1)}, f32[128]{0:T(128)S(1)}, u32[]{:S(2)}, u32[]{:S(2)}) collective-permute-start(f32[128]{0:T(128)S(1)} %get-tuple-element.26), channel_id=1, source_target_pairs={{0,2},{1,3},{2,0},{3,1},{4,6},{5,7},{6,4},{7,5},{8,10},{9,11},{10,... | collective-permute-start | bytes 1544 | tf_op jit(solution)/shard_map/ppermute | solution.py:74
  109.5 3.5 %collective-permute-start.7 = (f32[128]{0:T(128)S(1)}, f32[128]{0:T(128)S(1)}, u32[]{:S(2)}, u32[]{:S(2)}) collective-permute-start(f32[128]{0:T(128)S(1)} %get-tuple-element.26), channel_id=1, source_target_pairs={{0,3},{1,0},{2,1},{3,2},{4,7},{5,4},{6,5},{7,6},{8,11},{9,8},{10,9... | collective-permute-start | bytes 1544 | tf_op jit(solution)/shard_map/ppermute | solution.py:74
  114.4 7.6 %collective-permute-start.8 = (bf16[127,1024]{1,0:T(8,128)(2,1)S(1)}, bf16[127,1024]{1,0:T(8,128)(2,1)S(1)}, u32[]{:S(2)}, u32[]{:S(2)}) collective-permute-start(bf16[127,1024]{1,0:T(8,128)(2,1)S(1)} %slice.55), channel_id=1, source_target_pairs={{4,0},{8,4},{12,8},{16,12},{20,16},{24,20},{28,24},{5,1},{9,5},{13... | collective-permute-start | bytes 780296 | tf_op jit(solution)/shard_map/ppermute | solution.py:30
  131.0 2.4 %collective-permute-start.10 = (bf16[136,1024]{1,0:T(8,128)(2,1)S(1)}, bf16[136,1024]{1,0:T(8,128)(2,1)S(1)}, u32[]{:S(2)}, u32[]{:S(2)}) collective-permute-start(bf16[136,1024]{1,0:T(8,128)(2,1)S(1)} %pad_maximum_fusion), channel_id=1, source_target_pairs={{0,4},{4,0},{8,12},{12,8},{16,20},{20,16},{24,28},{28,24},{1,5},{5... | collective-permute-start | bytes 835592 | tf_op jit(solution)/shard_map/ppermute | solution.py:62
  133.4 9.0 %collective-permute-start.11 = (bf16[136,1024]{1,0:T(8,128)(2,1)S(1)}, bf16[136,1024]{1,0:T(8,128)(2,1)S(1)}, u32[]{:S(2)}, u32[]{:S(2)}) collective-permute-start(bf16[136,1024]{1,0:T(8,128)(2,1)S(1)} %add_convert_fusion.1), channel_id=1, source_target_pairs={{0,8},{4,12},{8,0},{12,4},{16,24},{20,28},{24,16},{28,20},{1,9},{5... | collective-permute-start | bytes 835592 | tf_op jit(solution)/shard_map/ppermute | solution.py:62
  134.2 3.1 %collective-permute-start.9 = (bf16[6,1024]{1,0:T(8,128)(2,1)S(1)}, bf16[6,1024]{1,0:T(8,128)(2,1)S(1)}, u32[]{:S(2)}, u32[]{:S(2)}) collective-permute-start(bf16[6,1024]{1,0:T(8,128)(2,1)S(1)} %slice.57), channel_id=1, source_target_pairs={{4,0},{8,4},{12,8},{16,12},{20,16},{24,20},{28,24},{5,1},{9,5},{13... | collective-permute-start | bytes 36872 | tf_op jit(solution)/shard_map/ppermute | solution.py:30
  137.3 6.5 %copy-start.21 = (f32[7,1024]{1,0:T(8,128)S(1)}, f32[7,1024]{1,0:T(8,128)}, u32[]{:S(2)}) copy-start(f32[7,1024]{1,0:T(8,128)} %param.15) | copy-start | bytes 86020
  137.3 6.5 %copy-start.23 = (pred[8,17]{0,1:T(8,128)(4,1)S(1)}, pred[8,17]{0,1:T(8,128)(4,1)}, u32[]{:S(2)}) copy-start(pred[8,17]{0,1:T(8,128)(4,1)} %constant.100) | copy-start | bytes 412
  142.5 12.2 %collective-permute-start.12 = (bf16[136,1024]{1,0:T(8,128)(2,1)S(1)}, bf16[136,1024]{1,0:T(8,128)(2,1)S(1)}, u32[]{:S(2)}, u32[]{:S(2)}) collective-permute-start(bf16[136,1024]{1,0:T(8,128)(2,1)S(1)} %add_convert_fusion), channel_id=1, source_target_pairs={{0,16},{4,20},{8,24},{12,28},{16,0},{20,4},{24,8},{28,12},{1,17},{... | collective-permute-start | bytes 835592 | tf_op jit(solution)/shard_map/ppermute | solution.py:62
  (16 other events, 37.1 us)
Sparse Core Ops, SparseCore 0:
  46.8 38.8 all-gather.1
  111.1 41.5 reduce-scatter.1

commit v14 on v12

--- a/solution.py
+++ b/solution.py
@@ -221,13 +221,14 @@
     visible = (key_pos[None, :] <= query_pos[:, None]) & (segments[None, :] == query_seg[:, None])
     mask = visible.astype(jnp.float32)
     value_part, weights_all = head_values_grad(queries, keys_whole, cotangent, mask, scale_factor)
+    values_whole = lax.all_gather(normed, "ctx", axis=0, tiled=True)
+    value_part, values_whole = lax.optimization_barrier((value_part, values_whole))
     value_grad = (
         lax.all_to_all(value_part, "ctx", 0, 0, tiled=True)
         .reshape(ctx_count, local_rows, width_local)
         .astype(jnp.float32)
         .sum(axis=0)
     )
-    values_whole = lax.all_gather(normed, "ctx", axis=0, tiled=True)
     key_part, attended_all, queries_grad = head_attention(
         queries, keys_whole, values_whole, cotangent, weights_all, scale_factor
     )

time: 155 us -> 161 us (1.039)
  waiting for transfers between devices: 51.2 us -> 66 us
  starting transfers between devices: 36 us -> 27.4 us
    all_to_all x1, waiting for transfers between devices: 0.01 us -> 19.2 us  [shards(): lax.all_to_all(value_part, 'ctx', 0, 0, tiled=True)]
    ppermute x3, starting transfers between devices: 9.73 us -> 3.3 us  [butterfly_total(): lax.ppermute(rounded, axis, pairs).astype(value.dtype)]
    all_gather x1, waiting for transfers between devices: 27.3 us -> 22.7 us  [shards(): values_whole = lax.all_gather(normed, 'ctx', axis=0, tiled=True)]
    all_to_all x1, starting transfers between devices: 6.11 us -> 3.6 us  [shards(): lax.all_to_all(value_part, 'ctx', 0, 0, tiled=True)]
  transfers between devices with their start and end apart: 17 -> 17, of which waited for: 12 -> 12; matrix products, arithmetic and copies ran while one was open for 22% -> 22% of each run, Pallas kernels for 10% -> 9%
where the time goes in v14:
time: 161 us
  waiting for transfers between devices  66 us (41%)
  starting transfers between devices  27.4 us (17%)
  matrix products  19.7 us (12%)
  Pallas kernels  15 us (9%)
  between operations  14.4 us (9%)
  other arithmetic  9.98 us (6%)
  local copies, waits for them, and re-layouts  8.04 us (5%)
    all_gather x1, waiting for transfers between devices, shards(): values_whole = lax.all_gather(normed, 'ctx', axis=0, tiled=True)  22.7 us
    conv_general_dilated x6, matrix products, depthwise(): lax.conv_general_dilated(padded[None], tap_rows[:, None, :], (1,), 'VALID...  19.7 us
    all_to_all x1, waiting for transfers between devices, shards(): lax.all_to_all(value_part, 'ctx', 0, 0, tiled=True)  19.2 us
    ppermute x3, waiting for transfers between devices, butterfly_total(): lax.ppermute(rounded, axis, pairs).astype(value.dtype)  14.2 us
    ppermute x6, starting transfers between devices, exchange_total(): arrived = lax.ppermute(value, axis, pairs)  10.9 us
    ppermute x4, starting transfers between devices, passed_along(): lax.ppermute(value, axis, [(source, source + steps) for source in range(l...  9.45 us
    pallas_call x1, Pallas kernels, head_values_grad(): pl.pallas_call(functools.partial(value_block, scale_factor), grid=(steps,...  7.72 us
    pallas_call x1, Pallas kernels, head_attention(): pl.pallas_call(functools.partial(attention_block, scale_factor), grid=(st...  7.3 us
  transfers between devices with their start and end apart: 17, of which 12 were waited for; matrix products, arithmetic and copies ran while one was open for 22% of the time, Pallas kernels for 9%

profile of v14, /device:TPU:0, one launch (start us, length us, event | category | flops | bytes accessed | tf_op | source)
XLA Modules:
  0.0 160.5 jit_solution(2990353823354594950)
XLA Ops:
  9.1 2.4 %collective-permute-start = (bf16[6,1024]{1,0:T(8,128)(2,1)S(1)}, bf16[6,1024]{1,0:T(8,128)(2,1)S(1)}, u32[]{:S(2)}, u32[]{:S(2)}) collective-permute-start(bf16[6,1024]{1,0:T(8,128)(2,1)S(1)} %slice.58), channel_id=1, source_target_pairs={{0,4},{4,8},{8,12},{12,16},{16,20},{20,24},{24,28},{1,5},{5,9},{9,... | collective-permute-start | bytes 36872 | tf_op jit(solution)/shard_map/ppermute | solution.py:30
  11.4 2.8 %rev.12 = f32[7,1024]{1,0:T(8,128)S(1)} reverse(f32[7,1024]{1,0:T(8,128)} %param.15), dimensions={0} | reverse | bytes 57344 | tf_op jit(solution)/shard_map/rev | solution.py:202
  16.5 4.5 %collective-permute-start.1 = (bf16[127,1024]{1,0:T(8,128)(2,1)S(1)}, bf16[127,1024]{1,0:T(8,128)(2,1)S(1)}, u32[]{:S(2)}, u32[]{:S(2)}) collective-permute-start(bf16[127,1024]{1,0:T(8,128)(2,1)S(1)} %slice.56), channel_id=1, source_target_pairs={{0,4},{4,8},{8,12},{12,16},{16,20},{20,24},{24,28},{1,5},{5,9},{9,... | collective-permute-start | bytes 780296 | tf_op jit(solution)/shard_map/ppermute | solution.py:30
  22.3 5.8 %fusion.8 = f32[1,128,1024]{2,0,1:T(1,128)S(1)} fusion(f32[1,255,1024]{2,1,0:T(8,128)S(1)} %maximum_bitcast_fusion, f32[128,1,1024]{2,0,1:T(8,128)S(1)} %bitcast.60), kind=kOutput, calls=%fused_computation.36 | convolution fusion | flops 201326592 | bytes 2093056 | tf_op jit(solution)/shard_map/conv_general_dilated | solution.py:34
  29.1 1.6 %collective-permute-start.2 = (f32[128]{0:T(128)S(1)}, f32[128]{0:T(128)S(1)}, u32[]{:S(2)}, u32[]{:S(2)}) collective-permute-start(f32[128]{0:T(128)S(1)} %get-tuple-element.35), channel_id=1, source_target_pairs={{0,1},{1,2},{2,3},{3,0},{4,5},{5,6},{6,7},{7,4},{8,9},{9,10},{10,1... | collective-permute-start | bytes 1544 | tf_op jit(solution)/shard_map/ppermute | solution.py:74
  30.8 2.6 %collective-permute-start.3 = (f32[128]{0:T(128)S(1)}, f32[128]{0:T(128)S(1)}, u32[]{:S(2)}, u32[]{:S(2)}) collective-permute-start(f32[128]{0:T(128)S(1)} %get-tuple-element.35), channel_id=1, source_target_pairs={{0,2},{1,3},{2,0},{3,1},{4,6},{5,7},{6,4},{7,5},{8,10},{9,11},{10,... | collective-permute-start | bytes 1544 | tf_op jit(solution)/shard_map/ppermute | solution.py:74
  33.3 1.3 collective-permute-start.4
  35.2 1.7 %collective-permute-done.4 = f32[128]{0:T(128)S(1)} collective-permute-done((f32[128]{0:T(128)S(1)}, f32[128]{0:T(128)S(1)}, u32[]{:S(2)}, u32[]{:S(2)}) %collective-permute-start.4) | collective-permute-done | bytes 544 | tf_op jit(solution)/shard_map/ppermute | solution.py:74
  38.9 2.6 %all-gather.3.cloned.1.call-done.k_ref = bf16[1024,1024]{1,0:T(8,128)(2,1)} async-done(((bf16[128,1024]{1,0:T(8,128)(2,1)}), bf16[1024,1024]{1,0:T(8,128)(2,1)}) %all-gather.3.cloned.1.call-update) | async-done | bytes 2097168 | tf_op jit(solution)/shard_map/all_gather | solution.py:216
  41.4 7.7 %shard_map.203 = (bf16[1024,1024]{1,0:T(8,128)(2,1)}, bf16[8,128,1024]{2,1,0:T(8,128)(2,1)}) custom-call(bf16[128,1024]{1,0:T(8,128)(2,1)} %q_ref.3, bf16[1024,1024]{1,0:T(8,128)(2,1)} %all-gather.3.cloned.1.call-done.k_ref, bf16[128,1024]{1,0:T(8,128)(2,1)} %cot_ref.3, f32[128,1024]{1,0:T(8,128)} %fusion.33.vis_ref), custom_call_target="tpu_custom_call" | custom-call | tf_op jit(solution)/shard_map/pallas_call | solution.py:149
  49.1 22.7 %all-gather.5.cloned.1.call-done.v_ref = bf16[1024,1024]{1,0:T(8,128)(2,1)} async-done(((bf16[128,1024]{1,0:T(8,128)(2,1)}), bf16[1024,1024]{1,0:T(8,128)(2,1)}) %all-gather.5.cloned.1.call-update) | async-done | bytes 2097168 | tf_op jit(solution)/shard_map/all_gather | solution.py:224
  71.8 3.6 %all-to-all-start = ((bf16[8,128,1024]{2,1,0:T(8,128)(2,1)}), bf16[8,128,1024]{2,1,0:T(8,128)(2,1)S(1)}, u32[]{:S(2)}, u32[]{:S(2)}) async-start(bf16[8,128,1024]{2,1,0:T(8,128)(2,1)} %bitcast.57), calls=%async_computation | async-start | bytes 4194304 | tf_op jit(solution)/shard_map/all_to_all | solution.py:227
  75.5 7.3 %shard_map.204 = (bf16[1024,1024]{1,0:T(8,128)(2,1)}, f32[128,1024]{1,0:T(8,128)}, bf16[128,1024]{1,0:T(8,128)(2,1)}) custom-call(bf16[128,1024]{1,0:T(8,128)(2,1)} %q_ref.3, bf16[1024,1024]{1,0:T(8,128)(2,1)} %all-gather.3.cloned.1.call-done.k_ref, bf16[1024,1024]{1,0:T(8,128)(2,1)} %all-gather.5.cloned.1.call-done.v_ref, bf16[128,1024]{1,0:T(8,128)(2,1)} %cot_ref.3, ...), custom_call_target="tpu_custom_call" | custom-call | tf_op jit(solution)/shard_map/pallas_call | solution.py:165
  82.8 19.2 %all-to-all-done = bf16[8,128,1024]{2,1,0:T(8,128)(2,1)S(1)} async-done(((bf16[8,128,1024]{2,1,0:T(8,128)(2,1)}), bf16[8,128,1024]{2,1,0:T(8,128)(2,1)S(1)}, u32[]{:S(2)}, u32[]{:S(2)}) %all-to-all-start) | async-done | bytes 2097184 | tf_op jit(solution)/shard_map/all_to_all | solution.py:227
  102.6 1.5 collective-permute-start.5
  104.1 2.4 %collective-permute-start.6 = (f32[128]{0:T(128)S(1)}, f32[128]{0:T(128)S(1)}, u32[]{:S(2)}, u32[]{:S(2)}) collective-permute-start(f32[128]{0:T(128)S(1)} %get-tuple-element.30), channel_id=1, source_target_pairs={{0,2},{1,3},{2,0},{3,1},{4,6},{5,7},{6,4},{7,5},{8,10},{9,11},{10,... | collective-permute-start | bytes 1544 | tf_op jit(solution)/shard_map/ppermute | solution.py:74
  106.5 1.4 collective-permute-start.7
  108.6 1.5 collective-permute-done.7
  112.7 5.8 %fusion.6 = bf16[1,128,1024]{2,0,1:T(2,128)(2,1)S(1)} fusion(f32[1,255,1024]{2,1,0:T(8,128)S(1)} %copy-done.9, f32[128,1,1024]{2,0,1:T(8,128)S(1)} %bitcast.55), kind=kOutput, calls=%fused_computation.34 | convolution fusion | flops 201326592 | bytes 1830912 | tf_op jit(solution)/shard_map/conv_general_dilated | solution.py:34
  119.6 5.8 %fusion = f32[1,128,1024]{2,0,1:T(1,128)S(1)} fusion(f32[1,255,1024]{2,1,0:T(8,128)S(1)} %maximum_bitcast_fusion.1, f32[128,1,1024]{2,0,1:T(8,128)S(1)} %bitcast.59), kind=kOutput, calls=%fused_computation.10 | convolution fusion | flops 201326592 | bytes 2093056 | tf_op jit(solution)/shard_map/conv_general_dilated | solution.py:34
  132.6 1.8 %collective-permute-done.9 = bf16[6,1024]{1,0:T(8,128)(2,1)S(1)} collective-permute-done((bf16[6,1024]{1,0:T(8,128)(2,1)S(1)}, bf16[6,1024]{1,0:T(8,128)(2,1)S(1)}, u32[]{:S(2)}, u32[]{:S(2)}) %collective-permute-start.9) | collective-permute-done | bytes 12320 | tf_op jit(solution)/shard_map/ppermute | solution.py:30
  135.3 4.2 %collective-permute-done.11 = bf16[136,1024]{1,0:T(8,128)(2,1)S(1)} collective-permute-done((bf16[136,1024]{1,0:T(8,128)(2,1)S(1)}, bf16[136,1024]{1,0:T(8,128)(2,1)S(1)}, u32[]{:S(2)}, u32[]{:S(2)}) %collective-permute-start.11) | collective-permute-done | bytes 278560 | tf_op jit(solution)/shard_map/ppermute | solution.py:62
  139.5 1.3 collective-permute-start.12
  143.0 8.8 %collective-permute-done.12 = bf16[136,1024]{1,0:T(8,128)(2,1)S(1)} collective-permute-done((bf16[136,1024]{1,0:T(8,128)(2,1)S(1)}, bf16[136,1024]{1,0:T(8,128)(2,1)S(1)}, u32[]{:S(2)}, u32[]{:S(2)}) %collective-permute-start.12) | collective-permute-done | bytes 278560 | tf_op jit(solution)/shard_map/ppermute | solution.py:62
  (129 shorter events, 25.9 us)
Async XLA Ops:
  7.2 34.2 %all-gather.3.cloned.1.call-start = ((), (), s32[]{:S(2)}) async-start(), calls=%async_computation.2 | async-start | bytes 2359296 | tf_op jit(solution)/shard_map/all_gather | solution.py:216
  7.9 63.9 %all-gather.5.cloned.1.call-start = ((), (), s32[]{:S(2)}) async-start(), calls=%async_computation.3 | async-start | bytes 2359296 | tf_op jit(solution)/shard_map/all_gather | solution.py:224
  9.1 5.2 %collective-permute-start = (bf16[6,1024]{1,0:T(8,128)(2,1)S(1)}, bf16[6,1024]{1,0:T(8,128)(2,1)S(1)}, u32[]{:S(2)}, u32[]{:S(2)}) collective-permute-start(bf16[6,1024]{1,0:T(8,128)(2,1)S(1)} %slice.58), channel_id=1, source_target_pairs={{0,4},{4,8},{8,12},{12,16},{16,20},{20,24},{24,28},{1,5},{5,9},{9,... | collective-permute-start | bytes 36872 | tf_op jit(solution)/shard_map/ppermute | solution.py:30
  16.5 5.7 %collective-permute-start.1 = (bf16[127,1024]{1,0:T(8,128)(2,1)S(1)}, bf16[127,1024]{1,0:T(8,128)(2,1)S(1)}, u32[]{:S(2)}, u32[]{:S(2)}) collective-permute-start(bf16[127,1024]{1,0:T(8,128)(2,1)S(1)} %slice.56), channel_id=1, source_target_pairs={{0,4},{4,8},{8,12},{12,16},{16,20},{20,24},{24,28},{1,5},{5,9},{9,... | collective-permute-start | bytes 780296 | tf_op jit(solution)/shard_map/ppermute | solution.py:30
  22.3 6.6 %copy-start.6 = (bf16[128,1024]{1,0:T(8,128)(2,1)S(1)}, bf16[128,1024]{1,0:T(8,128)(2,1)}, u32[]{:S(2)}) copy-start(bf16[128,1024]{1,0:T(8,128)(2,1)} %param.16) | copy-start | bytes 786436
  22.3 14.6 %copy-start.20 = (f32[1024]{0:T(1024)S(1)}, f32[1024]{0:T(1024)}, u32[]{:S(2)}) copy-start(f32[1024]{0:T(1024)} %param.19) | copy-start | bytes 12292
  28.1 9.7 %copy-start.22 = (s32[1024]{0:T(1024)S(1)}, s32[1024]{0:T(1024)}, u32[]{:S(2)}) copy-start(s32[1024]{0:T(1024)} %param.22) | copy-start | bytes 12292
  29.1 5.6 %collective-permute-start.2 = (f32[128]{0:T(128)S(1)}, f32[128]{0:T(128)S(1)}, u32[]{:S(2)}, u32[]{:S(2)}) collective-permute-start(f32[128]{0:T(128)S(1)} %get-tuple-element.35), channel_id=1, source_target_pairs={{0,1},{1,2},{2,3},{3,0},{4,5},{5,6},{6,7},{7,4},{8,9},{9,10},{10,1... | collective-permute-start | bytes 1544 | tf_op jit(solution)/shard_map/ppermute | solution.py:74
  30.8 4.4 %collective-permute-start.3 = (f32[128]{0:T(128)S(1)}, f32[128]{0:T(128)S(1)}, u32[]{:S(2)}, u32[]{:S(2)}) collective-permute-start(f32[128]{0:T(128)S(1)} %get-tuple-element.35), channel_id=1, source_target_pairs={{0,2},{1,3},{2,0},{3,1},{4,6},{5,7},{6,4},{7,5},{8,10},{9,11},{10,... | collective-permute-start | bytes 1544 | tf_op jit(solution)/shard_map/ppermute | solution.py:74
  33.3 3.5 %collective-permute-start.4 = (f32[128]{0:T(128)S(1)}, f32[128]{0:T(128)S(1)}, u32[]{:S(2)}, u32[]{:S(2)}) collective-permute-start(f32[128]{0:T(128)S(1)} %get-tuple-element.35), channel_id=1, source_target_pairs={{0,3},{1,0},{2,1},{3,2},{4,7},{5,4},{6,5},{7,6},{8,11},{9,8},{10,9... | collective-permute-start | bytes 1544 | tf_op jit(solution)/shard_map/ppermute | solution.py:74
  71.8 30.2 %all-to-all-start = ((bf16[8,128,1024]{2,1,0:T(8,128)(2,1)}), bf16[8,128,1024]{2,1,0:T(8,128)(2,1)S(1)}, u32[]{:S(2)}, u32[]{:S(2)}) async-start(bf16[8,128,1024]{2,1,0:T(8,128)(2,1)} %bitcast.57), calls=%async_computation | async-start | bytes 4194304 | tf_op jit(solution)/shard_map/all_to_all | solution.py:227
  75.4 78.6 %reduce-scatter.2.cloned.1.call-start = ((), (), s32[]{:S(2)}) async-start(), calls=%async_computation.4 | async-start | bytes 2359296 | tf_op jit(solution)/shard_map/reduce_scatter | solution.py:237
  102.3 7.8 %copy-start = (bf16[128,1024]{1,0:T(8,128)(2,1)S(1)}, bf16[128,1024]{1,0:T(8,128)(2,1)}, u32[]{:S(2)}) copy-start(bf16[128,1024]{1,0:T(8,128)(2,1)} %cot_ref.3) | copy-start | bytes 786436
  102.4 7.8 %copy-start.3 = (f32[1,128,1024]{2,0,1:T(1,128)S(1)}, f32[1,128,1024]{2,0,1:T(1,128)}, u32[]{:S(2)}) copy-start(f32[1,128,1024]{2,0,1:T(1,128)} %copy-done.2) | copy-start | bytes 1572868
  102.4 7.8 %copy-start.19 = (f32[128,1024]{1,0:T(8,128)S(1)}, f32[128,1024]{1,0:T(8,128)}, u32[]{:S(2)}) copy-start(f32[128,1024]{1,0:T(8,128)} %get-tuple-element.23) | copy-start | bytes 1572868
  102.6 5.5 %collective-permute-start.5 = (f32[128]{0:T(128)S(1)}, f32[128]{0:T(128)S(1)}, u32[]{:S(2)}, u32[]{:S(2)}) collective-permute-start(f32[128]{0:T(128)S(1)} %get-tuple-element.30), channel_id=1, source_target_pairs={{0,1},{1,2},{2,3},{3,0},{4,5},{5,6},{6,7},{7,4},{8,9},{9,10},{10,1... | collective-permute-start | bytes 1544 | tf_op jit(solution)/shard_map/ppermute | solution.py:74
  104.1 4.4 %collective-permute-start.6 = (f32[128]{0:T(128)S(1)}, f32[128]{0:T(128)S(1)}, u32[]{:S(2)}, u32[]{:S(2)}) collective-permute-start(f32[128]{0:T(128)S(1)} %get-tuple-element.30), channel_id=1, source_target_pairs={{0,2},{1,3},{2,0},{3,1},{4,6},{5,7},{6,4},{7,5},{8,10},{9,11},{10,... | collective-permute-start | bytes 1544 | tf_op jit(solution)/shard_map/ppermute | solution.py:74
  106.5 3.5 %collective-permute-start.7 = (f32[128]{0:T(128)S(1)}, f32[128]{0:T(128)S(1)}, u32[]{:S(2)}, u32[]{:S(2)}) collective-permute-start(f32[128]{0:T(128)S(1)} %get-tuple-element.30), channel_id=1, source_target_pairs={{0,3},{1,0},{2,1},{3,2},{4,7},{5,4},{6,5},{7,6},{8,11},{9,8},{10,9... | collective-permute-start | bytes 1544 | tf_op jit(solution)/shard_map/ppermute | solution.py:74
  111.4 7.6 %collective-permute-start.8 = (bf16[127,1024]{1,0:T(8,128)(2,1)S(1)}, bf16[127,1024]{1,0:T(8,128)(2,1)S(1)}, u32[]{:S(2)}, u32[]{:S(2)}) collective-permute-start(bf16[127,1024]{1,0:T(8,128)(2,1)S(1)} %slice.55), channel_id=1, source_target_pairs={{4,0},{8,4},{12,8},{16,12},{20,16},{24,20},{28,24},{5,1},{9,5},{13... | collective-permute-start | bytes 780296 | tf_op jit(solution)/shard_map/ppermute | solution.py:30
  128.0 2.4 %collective-permute-start.10 = (bf16[136,1024]{1,0:T(8,128)(2,1)S(1)}, bf16[136,1024]{1,0:T(8,128)(2,1)S(1)}, u32[]{:S(2)}, u32[]{:S(2)}) collective-permute-start(bf16[136,1024]{1,0:T(8,128)(2,1)S(1)} %pad_maximum_fusion), channel_id=1, source_target_pairs={{0,4},{4,0},{8,12},{12,8},{16,20},{20,16},{24,28},{28,24},{1,5},{5... | collective-permute-start | bytes 835592 | tf_op jit(solution)/shard_map/ppermute | solution.py:62
  130.5 9.0 %collective-permute-start.11 = (bf16[136,1024]{1,0:T(8,128)(2,1)S(1)}, bf16[136,1024]{1,0:T(8,128)(2,1)S(1)}, u32[]{:S(2)}, u32[]{:S(2)}) collective-permute-start(bf16[136,1024]{1,0:T(8,128)(2,1)S(1)} %add_convert_fusion.1), channel_id=1, source_target_pairs={{0,8},{4,12},{8,0},{12,4},{16,24},{20,28},{24,16},{28,20},{1,9},{5... | collective-permute-start | bytes 835592 | tf_op jit(solution)/shard_map/ppermute | solution.py:62
  131.3 3.1 %collective-permute-start.9 = (bf16[6,1024]{1,0:T(8,128)(2,1)S(1)}, bf16[6,1024]{1,0:T(8,128)(2,1)S(1)}, u32[]{:S(2)}, u32[]{:S(2)}) collective-permute-start(bf16[6,1024]{1,0:T(8,128)(2,1)S(1)} %slice.57), channel_id=1, source_target_pairs={{4,0},{8,4},{12,8},{16,12},{20,16},{24,20},{28,24},{5,1},{9,5},{13... | collective-permute-start | bytes 36872 | tf_op jit(solution)/shard_map/ppermute | solution.py:30
  134.4 6.5 %copy-start.21 = (f32[7,1024]{1,0:T(8,128)S(1)}, f32[7,1024]{1,0:T(8,128)}, u32[]{:S(2)}) copy-start(f32[7,1024]{1,0:T(8,128)} %param.15) | copy-start | bytes 86020
  139.5 12.3 %collective-permute-start.12 = (bf16[136,1024]{1,0:T(8,128)(2,1)S(1)}, bf16[136,1024]{1,0:T(8,128)(2,1)S(1)}, u32[]{:S(2)}, u32[]{:S(2)}) collective-permute-start(bf16[136,1024]{1,0:T(8,128)(2,1)S(1)} %add_convert_fusion), channel_id=1, source_target_pairs={{0,16},{4,20},{8,24},{12,28},{16,0},{20,4},{24,8},{28,12},{1,17},{... | collective-permute-start | bytes 835592 | tf_op jit(solution)/shard_map/ppermute | solution.py:62
  (17 other events, 47.2 us)
Sparse Core Ops, SparseCore 0:
  9.9 31.4 all-gather.2
  43.9 27.8 all-gather.4
  108.1 41.6 reduce-scatter.1

commit v15 on v9

--- a/solution.py
+++ b/solution.py
@@ -220,11 +220,12 @@
     )
     result = (second_wide + attended_all).astype(jnp.bfloat16)
     key_part, value_grad = lax.optimization_barrier((key_part, value_grad))
-    matchers_grad = lax.psum_scatter(
-        key_part,
-        "ctx",
-        scatter_dimension=0,
-        tiled=True,
+    matchers_grad = (
+        lax.all_to_all(key_part, "ctx", 0, 0, tiled=True)
+        .reshape(ctx_count, local_rows, width_local)
+        .astype(jnp.float32)
+        .sum(axis=0)
+        .astype(jnp.bfloat16)
     )
     gain_part = value_grad * scaling
     projected = channel_total(jnp.sum(gain_part * second_wide, axis=1))
@@ -241,6 +242,7 @@
     intake_grad = (dinner_two * first_wide).astype(jnp.bfloat16)
     kernel_part = depthwise(padded_two, dconv_two)[::-1]
     first_grad = second_grad + dinner_two * intake.astype(jnp.float32)
+    matchers_grad, first_grad = lax.optimization_barrier((matchers_grad, first_grad))
     shutter_grad = (first_grad * conv_one).astype(jnp.bfloat16)
     dconv_one = first_grad * shutter.astype(jnp.float32)
     back_one = neighbor_rows(dconv_one[: KS - 1], -1)

time: 154 us -> 176 us (1.14)
  starting transfers between devices: 29.7 us -> 45.6 us
  other arithmetic: 9.97 us -> 15.3 us
  waiting for transfers between devices: 51.7 us -> 47.7 us
  local copies, waits for them, and re-layouts: 8.45 us -> 11.2 us
  matrix products: 19.6 us -> 21.4 us
    ppermute x3, starting transfers between devices: 4.21 us -> 16.1 us  [butterfly_total(): lax.ppermute(rounded, axis, pairs).astype(value.dtype)]
    all_to_all x0 -> x1, starting transfers between devices: none -> 4.01 us  [shards(): lax.all_to_all(key_part, 'ctx', 0, 0, tiled=True)]
    ppermute x3, waiting for transfers between devices: 13.4 us -> 9.8 us  [butterfly_total(): lax.ppermute(rounded, axis, pairs).astype(value.dtype)]
    all_to_all x0 -> x1, waiting for transfers between devices: none -> 3.13 us  [shards(): lax.all_to_all(key_part, 'ctx', 0, 0, tiled=True)]
    ppermute x6, waiting for transfers between devices: 4.99 us -> 2.1 us  [exchange_total(): arrived = lax.ppermute(value, axis, pairs)]
    rev x1, local copies, waits for them, and re-layouts: 0.34 us -> 3.19 us  [shards(): kernel_part = depthwise(padded_two, dconv_two)[::-1]]
  transfers between devices with their start and end apart: 17 -> 17, of which waited for: 11 -> 9; matrix products, arithmetic and copies ran while one was open for 23% -> 22% of each run, Pallas kernels for 13% -> 11%
where the time goes in v15:
time: 176 us; the launch traced here: 175 us
  waiting for transfers between devices  47.7 us (27%)
  starting transfers between devices  45.6 us (26%)
  matrix products  21.4 us (12%)
  Pallas kernels  19.3 us (11%)
  other arithmetic  15.3 us (9%)
  between operations  14.7 us (8%)
  local copies, waits for them, and re-layouts  11.2 us (6%)
    all_gather x1, waiting for transfers between devices, shards(): values_whole = lax.all_gather(normed, 'ctx', axis=0, tiled=True)  26.8 us
    conv_general_dilated x6, matrix products, depthwise(): lax.conv_general_dilated(padded[None], tap_rows[:, None, :], (1,), 'VALID...  21.4 us
    ppermute x3, starting transfers between devices, butterfly_total(): lax.ppermute(rounded, axis, pairs).astype(value.dtype)  16.1 us
    pallas_call x1, Pallas kernels, head_attention(): pl.pallas_call(functools.partial(attention_block, scale_factor), grid=(wi...  10.5 us
    ppermute x6, starting transfers between devices, exchange_total(): arrived = lax.ppermute(value, axis, pairs)  9.91 us
    ppermute x3, waiting for transfers between devices, butterfly_total(): lax.ppermute(rounded, axis, pairs).astype(value.dtype)  9.8 us
    ppermute x4, starting transfers between devices, passed_along(): lax.ppermute(value, axis, [(source, source + steps) for source in range(l...  9.62 us
    pallas_call x1, Pallas kernels, head_values_grad(): pl.pallas_call(functools.partial(value_block, scale_factor), grid=(width_...  8.8 us
  transfers between devices with their start and end apart: 17, of which 9 were waited for; matrix products, arithmetic and copies ran while one was open for 22% of the time, Pallas kernels for 11%

profile of v15, /device:TPU:0, one launch (start us, length us, event | category | flops | bytes accessed | tf_op | source)
XLA Modules:
  0.0 175.2 jit_solution(7197960482926149602)
XLA Ops:
  9.1 2.4 %collective-permute-start = (bf16[6,1024]{1,0:T(8,128)(2,1)S(1)}, bf16[6,1024]{1,0:T(8,128)(2,1)S(1)}, u32[]{:S(2)}, u32[]{:S(2)}) collective-permute-start(bf16[6,1024]{1,0:T(8,128)(2,1)S(1)} %slice.58), channel_id=1, source_target_pairs={{0,4},{4,8},{8,12},{12,16},{16,20},{20,24},{24,28},{1,5},{5,9},{9,... | collective-permute-start | bytes 36872 | tf_op jit(solution)/shard_map/ppermute | solution.py:30
  11.4 2.8 %rev.12 = f32[7,1024]{1,0:T(8,128)S(1)} reverse(f32[7,1024]{1,0:T(8,128)} %param.15), dimensions={0} | reverse | bytes 57344 | tf_op jit(solution)/shard_map/rev | solution.py:189
  16.5 4.5 %collective-permute-start.1 = (bf16[127,1024]{1,0:T(8,128)(2,1)S(1)}, bf16[127,1024]{1,0:T(8,128)(2,1)S(1)}, u32[]{:S(2)}, u32[]{:S(2)}) collective-permute-start(bf16[127,1024]{1,0:T(8,128)(2,1)S(1)} %slice.56), channel_id=1, source_target_pairs={{0,4},{4,8},{8,12},{12,16},{16,20},{20,24},{24,28},{1,5},{5,9},{9,... | collective-permute-start | bytes 780296 | tf_op jit(solution)/shard_map/ppermute | solution.py:30
  22.4 5.8 %fusion.8 = f32[1,128,1024]{2,0,1:T(1,128)S(1)} fusion(f32[1,255,1024]{2,1,0:T(8,128)S(1)} %maximum_bitcast_fusion, f32[128,1,1024]{2,0,1:T(8,128)S(1)} %bitcast.61), kind=kOutput, calls=%fused_computation.36 | convolution fusion | flops 201326592 | bytes 2093056 | tf_op jit(solution)/shard_map/conv_general_dilated | solution.py:34
  30.5 2.6 %collective-permute-start.3 = (f32[128]{0:T(128)S(1)}, f32[128]{0:T(128)S(1)}, u32[]{:S(2)}, u32[]{:S(2)}) collective-permute-start(f32[128]{0:T(128)S(1)} %get-tuple-element.29), channel_id=1, source_target_pairs={{0,2},{1,3},{2,0},{3,1},{4,6},{5,7},{6,4},{7,5},{8,10},{9,11},{10,... | collective-permute-start | bytes 1544 | tf_op jit(solution)/shard_map/ppermute | solution.py:74
  35.0 1.7 collective-permute-done.4
  38.6 2.8 %all-gather.3.cloned.1.call-done.k_ref = bf16[1024,1024]{1,0:T(8,128)(2,1)} async-done(((bf16[128,1024]{1,0:T(8,128)(2,1)}), bf16[1024,1024]{1,0:T(8,128)(2,1)}) %all-gather.3.cloned.1.call-update) | async-done | bytes 2097168 | tf_op jit(solution)/shard_map/all_gather | solution.py:203
  41.4 8.8 %shard_map.204 = bf16[1024,1024]{1,0:T(8,128)(2,1)} custom-call(bf16[128,1024]{1,0:T(8,128)(2,1)} %q_ref.3, bf16[1024,1024]{1,0:T(8,128)(2,1)} %all-gather.3.cloned.1.call-done.k_ref, bf16[128,1024]{1,0:T(8,128)(2,1)} %cot_ref.3, f32[128,1024]{1,0:T(8,128)} %fusion.33.vis_ref), custom_call_target="tpu_custom_call" | custom-call | tf_op jit(solution)/shard_map/pallas_call | solution.py:139
  50.2 5.9 %all-to-all-start = ((bf16[8,128,1024]{2,1,0:T(8,128)(2,1)}), bf16[8,128,1024]{2,1,0:T(8,128)(2,1)S(1)}, u32[]{:S(2)}, u32[]{:S(2)}) async-start(bf16[8,128,1024]{2,1,0:T(8,128)(2,1)} %bitcast.55), calls=%async_computation | async-start | bytes 4194304 | tf_op jit(solution)/shard_map/all_to_all | solution.py:212
  56.1 26.8 %all-gather.5.cloned.1.call-done.v_ref = bf16[1024,1024]{1,0:T(8,128)(2,1)} async-done(((bf16[128,1024]{1,0:T(8,128)(2,1)}), bf16[1024,1024]{1,0:T(8,128)(2,1)}) %all-gather.5.cloned.1.call-update) | async-done | bytes 2097168 | tf_op jit(solution)/shard_map/all_gather | solution.py:217
  82.9 10.5 %shard_map.203 = (bf16[1024,1024]{1,0:T(8,128)(2,1)}, f32[128,1024]{1,0:T(8,128)}, bf16[128,1024]{1,0:T(8,128)(2,1)}) custom-call(bf16[128,1024]{1,0:T(8,128)(2,1)} %q_ref.3, bf16[1024,1024]{1,0:T(8,128)(2,1)} %all-gather.3.cloned.1.call-done.k_ref, bf16[1024,1024]{1,0:T(8,128)(2,1)} %all-gather.5.cloned.1.call-done.v_ref, bf16[128,1024]{1,0:T(8,128)(2,1)} %cot_ref.3, ...), custom_call_target="tpu_custom_call" | custom-call | tf_op jit(solution)/shard_map/pallas_call | solution.py:152
  94.9 2.9 %collective-permute-start.6 = (f32[128]{0:T(128)S(1)}, f32[128]{0:T(128)S(1)}, u32[]{:S(2)}, u32[]{:S(2)}) collective-permute-start(f32[128]{0:T(128)S(1)} %get-tuple-element.26), channel_id=1, source_target_pairs={{0,2},{1,3},{2,0},{3,1},{4,6},{5,7},{6,4},{7,5},{8,10},{9,11},{10,... | collective-permute-start | bytes 1544 | tf_op jit(solution)/shard_map/ppermute | solution.py:74
  98.3 4.0 %all-to-all-start.1 = ((bf16[8,128,1024]{2,1,0:T(8,128)(2,1)}), bf16[8,128,1024]{2,1,0:T(8,128)(2,1)S(1)}, u32[]{:S(2)}, u32[]{:S(2)}) async-start(bf16[8,128,1024]{2,1,0:T(8,128)(2,1)} %bitcast.58), calls=%async_computation.1 | async-start | bytes 4194304 | tf_op jit(solution)/shard_map/all_to_all | solution.py:224
  102.6 2.5 %fusion.25 = (bf16[128,1024]{1,0:T(8,128)(2,1)}, f32[128,1024]{1,0:T(8,128)S(1)}, bf16[128,1024]{1,0:T(8,128)(2,1)}) fusion(f32[1,128,1024]{2,0,1:T(1,128)} %copy-done.4, f32[128]{0:T(128)S(1)} %fusion.42, bf16[128,1024]{1,0:T(8,128)(2,1)S(1)} %get-tuple-element.30, f32[128,1024]{1,0:T(8,128)S(1)} %convert_reduce_fusion, f32[1024]{0:T(1024)S(1)} %copy-done.18, ...), kind=kLoop, calls=%fused_computation.59 | loop fusion | flops 1441792 | bytes 3150848 | tf_op jit(solution)/shard_map/convert_element_type | solution.py:238
  108.1 5.8 %fusion.6 = bf16[1,128,1024]{2,0,1:T(2,128)(2,1)S(1)} fusion(f32[1,255,1024]{2,1,0:T(8,128)S(1)} %copy-done.9, f32[128,1,1024]{2,0,1:T(8,128)S(1)} %bitcast.56), kind=kOutput, calls=%fused_computation.34 | convolution fusion | flops 201326592 | bytes 1830912 | tf_op jit(solution)/shard_map/conv_general_dilated | solution.py:34
  114.7 3.2 %rev.14 = bf16[128,1024]{1,0:T(8,128)(2,1)S(1)} reverse(bf16[128,1024]{1,0:T(8,128)(2,1)} %bitcast.59), dimensions={0} | reverse | bytes 524288 | tf_op jit(solution)/shard_map/rev | solution.py:243
  119.1 5.8 %fusion = f32[1,128,1024]{2,0,1:T(1,128)S(1)} fusion(f32[1,255,1024]{2,1,0:T(8,128)S(1)} %maximum_bitcast_fusion.1, f32[128,1,1024]{2,0,1:T(8,128)S(1)} %bitcast.60), kind=kOutput, calls=%fused_computation.10 | convolution fusion | flops 201326592 | bytes 2093056 | tf_op jit(solution)/shard_map/conv_general_dilated | solution.py:34
  125.9 3.1 %all-to-all-done.1 = bf16[8,128,1024]{2,1,0:T(8,128)(2,1)S(1)} async-done(((bf16[8,128,1024]{2,1,0:T(8,128)(2,1)}), bf16[8,128,1024]{2,1,0:T(8,128)(2,1)S(1)}, u32[]{:S(2)}, u32[]{:S(2)}) %all-to-all-start.1) | async-done | bytes 2097184 | tf_op jit(solution)/shard_map/all_to_all | solution.py:224
  130.2 2.8 %fusion.27 = bf16[1,7,1024]{2,0,1:T(2,128)(2,1)S(1)} fusion(f32[128,1,1024]{2,0,1:T(8,128)S(1)} %bitcast.57, f32[1,134,1024]{2,1,0:T(8,128)} %copy-done.15), kind=kOutput, calls=%fused_computation.62 | convolution fusion | flops 11010048 | bytes 1087488 | tf_op jit(solution)/shard_map/conv_general_dilated | solution.py:34
  133.3 9.8 %collective-permute-start.10 = (bf16[136,1024]{1,0:T(8,128)(2,1)S(1)}, bf16[136,1024]{1,0:T(8,128)(2,1)S(1)}, u32[]{:S(2)}, u32[]{:S(2)}) collective-permute-start(bf16[136,1024]{1,0:T(8,128)(2,1)S(1)} %pad_maximum_fusion), channel_id=1, source_target_pairs={{0,4},{4,0},{8,12},{12,8},{16,20},{20,16},{24,28},{28,24},{1,5},{5... | collective-permute-start | bytes 835592 | tf_op jit(solution)/shard_map/ppermute | solution.py:62
  146.2 2.0 %collective-permute-start.11 = (bf16[136,1024]{1,0:T(8,128)(2,1)S(1)}, bf16[136,1024]{1,0:T(8,128)(2,1)}, u32[]{:S(2)}, u32[]{:S(2)}) collective-permute-start(bf16[136,1024]{1,0:T(8,128)(2,1)S(1)} %add_convert_fusion.1), channel_id=1, source_target_pairs={{0,8},{4,12},{8,0},{12,4},{16,24},{20,28},{24,16},{28,20},{1,9},{5... | collective-permute-start | bytes 835592 | tf_op jit(solution)/shard_map/ppermute | solution.py:62
  149.9 4.2 %collective-permute-done.11 = bf16[136,1024]{1,0:T(8,128)(2,1)} collective-permute-done((bf16[136,1024]{1,0:T(8,128)(2,1)S(1)}, bf16[136,1024]{1,0:T(8,128)(2,1)}, u32[]{:S(2)}, u32[]{:S(2)}) %collective-permute-start.11) | collective-permute-done | bytes 278560 | tf_op jit(solution)/shard_map/ppermute | solution.py:62
  155.2 4.4 %collective-permute-start.12 = (bf16[136,1024]{1,0:T(8,128)(2,1)S(1)}, bf16[136,1024]{1,0:T(8,128)(2,1)S(1)}, u32[]{:S(2)}, u32[]{:S(2)}) collective-permute-start(bf16[136,1024]{1,0:T(8,128)(2,1)S(1)} %add_convert_fusion), channel_id=1, source_target_pairs={{0,16},{4,20},{8,24},{12,28},{16,0},{20,4},{24,8},{28,12},{1,17},{... | collective-permute-start | bytes 835592 | tf_op jit(solution)/shard_map/ppermute | solution.py:62
  160.6 5.6 %collective-permute-done.12 = bf16[136,1024]{1,0:T(8,128)(2,1)S(1)} collective-permute-done((bf16[136,1024]{1,0:T(8,128)(2,1)S(1)}, bf16[136,1024]{1,0:T(8,128)(2,1)S(1)}, u32[]{:S(2)}, u32[]{:S(2)}) %collective-permute-start.12) | collective-permute-done | bytes 278560 | tf_op jit(solution)/shard_map/ppermute | solution.py:62
  (125 shorter events, 29.9 us)
Async XLA Ops:
  7.2 34.2 %all-gather.3.cloned.1.call-start = ((), (), s32[]{:S(2)}) async-start(), calls=%async_computation.2 | async-start | bytes 2359296 | tf_op jit(solution)/shard_map/all_gather | solution.py:203
  7.9 75.0 %all-gather.5.cloned.1.call-start = ((), (), s32[]{:S(2)}) async-start(), calls=%async_computation.3 | async-start | bytes 2359296 | tf_op jit(solution)/shard_map/all_gather | solution.py:217
  9.1 5.2 %collective-permute-start = (bf16[6,1024]{1,0:T(8,128)(2,1)S(1)}, bf16[6,1024]{1,0:T(8,128)(2,1)S(1)}, u32[]{:S(2)}, u32[]{:S(2)}) collective-permute-start(bf16[6,1024]{1,0:T(8,128)(2,1)S(1)} %slice.58), channel_id=1, source_target_pairs={{0,4},{4,8},{8,12},{12,16},{16,20},{20,24},{24,28},{1,5},{5,9},{9,... | collective-permute-start | bytes 36872 | tf_op jit(solution)/shard_map/ppermute | solution.py:30
  16.4 11.7 %copy-start = (bf16[128,1024]{1,0:T(8,128)(2,1)}, bf16[128,1024]{1,0:T(8,128)(2,1)S(1)}, u32[]{:S(2)}) copy-start(bf16[128,1024]{1,0:T(8,128)(2,1)S(1)} %get-tuple-element.32) | copy-start | bytes 786436
  16.5 5.7 %collective-permute-start.1 = (bf16[127,1024]{1,0:T(8,128)(2,1)S(1)}, bf16[127,1024]{1,0:T(8,128)(2,1)S(1)}, u32[]{:S(2)}, u32[]{:S(2)}) collective-permute-start(bf16[127,1024]{1,0:T(8,128)(2,1)S(1)} %slice.56), channel_id=1, source_target_pairs={{0,4},{4,8},{8,12},{12,16},{16,20},{20,24},{24,28},{1,5},{5,9},{9,... | collective-permute-start | bytes 780296 | tf_op jit(solution)/shard_map/ppermute | solution.py:30
  22.3 5.8 %copy-start.7 = (bf16[128,1024]{1,0:T(8,128)(2,1)S(1)}, bf16[128,1024]{1,0:T(8,128)(2,1)}, u32[]{:S(2)}) copy-start(bf16[128,1024]{1,0:T(8,128)(2,1)} %param.16) | copy-start | bytes 786436
  22.4 14.4 %copy-start.18 = (f32[1024]{0:T(1024)S(1)}, f32[1024]{0:T(1024)}, u32[]{:S(2)}) copy-start(f32[1024]{0:T(1024)} %param.19) | copy-start | bytes 12292
  28.2 9.4 %copy-start.20 = (s32[1024]{0:T(1024)S(1)}, s32[1024]{0:T(1024)}, u32[]{:S(2)}) copy-start(s32[1024]{0:T(1024)} %param.22) | copy-start | bytes 12292
  28.9 5.6 %collective-permute-start.2 = (f32[128]{0:T(128)S(1)}, f32[128]{0:T(128)S(1)}, u32[]{:S(2)}, u32[]{:S(2)}) collective-permute-start(f32[128]{0:T(128)S(1)} %get-tuple-element.29), channel_id=1, source_target_pairs={{0,1},{1,2},{2,3},{3,0},{4,5},{5,6},{6,7},{7,4},{8,9},{9,10},{10,1... | collective-permute-start | bytes 1544 | tf_op jit(solution)/shard_map/ppermute | solution.py:74
  30.5 4.4 %collective-permute-start.3 = (f32[128]{0:T(128)S(1)}, f32[128]{0:T(128)S(1)}, u32[]{:S(2)}, u32[]{:S(2)}) collective-permute-start(f32[128]{0:T(128)S(1)} %get-tuple-element.29), channel_id=1, source_target_pairs={{0,2},{1,3},{2,0},{3,1},{4,6},{5,7},{6,4},{7,5},{8,10},{9,11},{10,... | collective-permute-start | bytes 1544 | tf_op jit(solution)/shard_map/ppermute | solution.py:74
  33.1 3.5 %collective-permute-start.4 = (f32[128]{0:T(128)S(1)}, f32[128]{0:T(128)S(1)}, u32[]{:S(2)}, u32[]{:S(2)}) collective-permute-start(f32[128]{0:T(128)S(1)} %get-tuple-element.29), channel_id=1, source_target_pairs={{0,3},{1,0},{2,1},{3,2},{4,7},{5,4},{6,5},{7,6},{8,11},{9,8},{10,9... | collective-permute-start | bytes 1544 | tf_op jit(solution)/shard_map/ppermute | solution.py:74
  50.2 43.2 %all-to-all-start = ((bf16[8,128,1024]{2,1,0:T(8,128)(2,1)}), bf16[8,128,1024]{2,1,0:T(8,128)(2,1)S(1)}, u32[]{:S(2)}, u32[]{:S(2)}) async-start(bf16[8,128,1024]{2,1,0:T(8,128)(2,1)} %bitcast.55), calls=%async_computation | async-start | bytes 4194304 | tf_op jit(solution)/shard_map/all_to_all | solution.py:212
  93.9 8.5 %collective-permute-start.5 = (f32[128]{0:T(128)S(1)}, f32[128]{0:T(128)S(1)}, u32[]{:S(2)}, u32[]{:S(2)}) collective-permute-start(f32[128]{0:T(128)S(1)} %get-tuple-element.26), channel_id=1, source_target_pairs={{0,1},{1,2},{2,3},{3,0},{4,5},{5,6},{6,7},{7,4},{8,9},{9,10},{10,1... | collective-permute-start | bytes 1544 | tf_op jit(solution)/shard_map/ppermute | solution.py:74
  94.9 7.5 %collective-permute-start.6 = (f32[128]{0:T(128)S(1)}, f32[128]{0:T(128)S(1)}, u32[]{:S(2)}, u32[]{:S(2)}) collective-permute-start(f32[128]{0:T(128)S(1)} %get-tuple-element.26), channel_id=1, source_target_pairs={{0,2},{1,3},{2,0},{3,1},{4,6},{5,7},{6,4},{7,5},{8,10},{9,11},{10,... | collective-permute-start | bytes 1544 | tf_op jit(solution)/shard_map/ppermute | solution.py:74
  97.9 4.6 %collective-permute-start.7 = (f32[128]{0:T(128)S(1)}, f32[128]{0:T(128)S(1)}, u32[]{:S(2)}, u32[]{:S(2)}) collective-permute-start(f32[128]{0:T(128)S(1)} %get-tuple-element.26), channel_id=1, source_target_pairs={{0,3},{1,0},{2,1},{3,2},{4,7},{5,4},{6,5},{7,6},{8,11},{9,8},{10,9... | collective-permute-start | bytes 1544 | tf_op jit(solution)/shard_map/ppermute | solution.py:74
  98.3 30.7 %all-to-all-start.1 = ((bf16[8,128,1024]{2,1,0:T(8,128)(2,1)}), bf16[8,128,1024]{2,1,0:T(8,128)(2,1)S(1)}, u32[]{:S(2)}, u32[]{:S(2)}) async-start(bf16[8,128,1024]{2,1,0:T(8,128)(2,1)} %bitcast.58), calls=%async_computation.1 | async-start | bytes 4194304 | tf_op jit(solution)/shard_map/all_to_all | solution.py:224
  106.8 11.1 %collective-permute-start.8 = (bf16[127,1024]{1,0:T(8,128)(2,1)}, bf16[127,1024]{1,0:T(8,128)(2,1)}, u32[]{:S(2)}, u32[]{:S(2)}) collective-permute-start(bf16[127,1024]{1,0:T(8,128)(2,1)} %slice.55), channel_id=1, source_target_pairs={{4,0},{8,4},{12,8},{16,12},{20,16},{24,20},{28,24},{5,1},{9,5},{13... | collective-permute-start | bytes 780296 | tf_op jit(solution)/shard_map/ppermute | solution.py:30
  133.3 12.8 %collective-permute-start.10 = (bf16[136,1024]{1,0:T(8,128)(2,1)S(1)}, bf16[136,1024]{1,0:T(8,128)(2,1)S(1)}, u32[]{:S(2)}, u32[]{:S(2)}) collective-permute-start(bf16[136,1024]{1,0:T(8,128)(2,1)S(1)} %pad_maximum_fusion), channel_id=1, source_target_pairs={{0,4},{4,0},{8,12},{12,8},{16,20},{20,16},{24,28},{28,24},{1,5},{5... | collective-permute-start | bytes 835592 | tf_op jit(solution)/shard_map/ppermute | solution.py:62
  143.0 3.1 %collective-permute-start.9 = (bf16[6,1024]{1,0:T(8,128)(2,1)S(1)}, bf16[6,1024]{1,0:T(8,128)(2,1)S(1)}, u32[]{:S(2)}, u32[]{:S(2)}) collective-permute-start(bf16[6,1024]{1,0:T(8,128)(2,1)S(1)} %slice.57), channel_id=1, source_target_pairs={{4,0},{8,4},{12,8},{16,12},{20,16},{24,20},{28,24},{5,1},{9,5},{13... | collective-permute-start | bytes 36872 | tf_op jit(solution)/shard_map/ppermute | solution.py:30
  146.2 7.9 %collective-permute-start.11 = (bf16[136,1024]{1,0:T(8,128)(2,1)S(1)}, bf16[136,1024]{1,0:T(8,128)(2,1)}, u32[]{:S(2)}, u32[]{:S(2)}) collective-permute-start(bf16[136,1024]{1,0:T(8,128)(2,1)S(1)} %add_convert_fusion.1), channel_id=1, source_target_pairs={{0,8},{4,12},{8,0},{12,4},{16,24},{20,28},{24,16},{28,20},{1,9},{5... | collective-permute-start | bytes 835592 | tf_op jit(solution)/shard_map/ppermute | solution.py:62
  149.4 10.1 %copy-start.3 = (bf16[128,1024]{1,0:T(8,128)(2,1)S(1)}, bf16[128,1024]{1,0:T(8,128)(2,1)}, u32[]{:S(2)}) copy-start(bf16[128,1024]{1,0:T(8,128)(2,1)} %param.12) | copy-start | bytes 786436
  149.4 10.1 %copy-start.6 = (f32[1,128,1024]{2,0,1:T(1,128)S(1)}, f32[1,128,1024]{2,0,1:T(1,128)}, u32[]{:S(2)}) copy-start(f32[1,128,1024]{2,0,1:T(1,128)} %copy-done.5) | copy-start | bytes 1572868
  149.4 10.1 %copy-start.14 = (bf16[128,1024]{1,0:T(8,128)(2,1)S(1)}, bf16[128,1024]{1,0:T(8,128)(2,1)}, u32[]{:S(2)}) copy-start(bf16[128,1024]{1,0:T(8,128)(2,1)} %param.14) | copy-start | bytes 786436
  155.2 11.0 %collective-permute-start.12 = (bf16[136,1024]{1,0:T(8,128)(2,1)S(1)}, bf16[136,1024]{1,0:T(8,128)(2,1)S(1)}, u32[]{:S(2)}, u32[]{:S(2)}) collective-permute-start(bf16[136,1024]{1,0:T(8,128)(2,1)S(1)} %add_convert_fusion), channel_id=1, source_target_pairs={{0,16},{4,20},{8,24},{12,28},{16,0},{20,4},{24,8},{28,12},{1,17},{... | collective-permute-start | bytes 835592 | tf_op jit(solution)/shard_map/ppermute | solution.py:62
  (15 other events, 41.9 us)
Sparse Core Ops, SparseCore 0:
  9.9 31.4 all-gather.2
  43.9 38.9 all-gather.4

commit v16 on v9

--- a/solution.py
+++ b/solution.py
@@ -73,7 +73,7 @@
         pairs = [(source, (source + shift) % count) for source in range(count)]
         arrived = lax.ppermute(value, axis, pairs)
         stacked = lax.dynamic_update_index_in_dim(stacked, arrived, (index - shift) % count, 0)
-    return jnp.sum(stacked, axis=0)
+    return jnp.sum(stacked.astype(jnp.float32), axis=0)
 
 
 def channel_total(partial_value):
@@ -249,11 +249,14 @@
     stencil_part = depthwise(padded_one, dconv_one)[::-1]
     stream_grad = (first_grad + dinner_one * feeder.astype(jnp.float32)).astype(jnp.bfloat16)
     filter_sum = butterfly_total(
-        jnp.concatenate([kernel_part, scaling_part[None], stencil_part], axis=0), "ctx", jnp.bfloat16
+        jnp.concatenate([kernel_part, scaling_part[None]], axis=0), "ctx", jnp.bfloat16
     )
     kernel_sum = filter_sum[:KM]
     scaling_sum = filter_sum[KM]
-    stencil_sum = filter_sum[KM + 1 :]
+    if lax.axis_size("ctx") <= 8:
+        stencil_sum = exchange_total(stencil_part.astype(jnp.bfloat16), "ctx")
+    else:
+        stencil_sum = butterfly_total(stencil_part, "ctx", jnp.bfloat16)
     normalizer = math.sqrt(total_rows)
     return (
         result,

time: 154 us -> 163 us (1.058)
  starting transfers between devices: 29.7 us -> 36.4 us
  waiting for transfers between devices: 51.7 us -> 53.8 us
    ppermute x6 -> x13, starting transfers between devices: 9.94 us -> 18.7 us  [exchange_total(): arrived = lax.ppermute(value, axis, pairs)]
    ppermute x3, starting transfers between devices: 4.21 us -> 2.18 us  [butterfly_total(): lax.ppermute(rounded, axis, pairs).astype(value.dtype)]
    ppermute x6 -> x13, waiting for transfers between devices: 4.99 us -> 6.45 us  [exchange_total(): arrived = lax.ppermute(value, axis, pairs)]
  transfers between devices with their start and end apart: 17 -> 24, of which waited for: 11 -> 11; matrix products, arithmetic and copies ran while one was open for 23% -> 22% of each run, Pallas kernels for 13% -> 12%
where the time goes in v16:
time: 163 us; the launch traced here: 162 us
  waiting for transfers between devices  53.8 us (33%)
  starting transfers between devices  36.4 us (22%)
  matrix products  19.7 us (12%)
  Pallas kernels  19.3 us (12%)
  between operations  14.6 us (9%)
  other arithmetic  9.98 us (6%)
  local copies, waits for them, and re-layouts  7.85 us (5%)
    all_gather x1, waiting for transfers between devices, shards(): values_whole = lax.all_gather(normed, 'ctx', axis=0, tiled=True)  26.7 us
    conv_general_dilated x6, matrix products, depthwise(): lax.conv_general_dilated(padded[None], tap_rows[:, None, :], (1,), 'VALID...  19.7 us
    ppermute x13, starting transfers between devices, exchange_total(): arrived = lax.ppermute(value, axis, pairs)  18.7 us
    ppermute x3, waiting for transfers between devices, butterfly_total(): lax.ppermute(rounded, axis, pairs).astype(value.dtype)  14.2 us
    pallas_call x1, Pallas kernels, head_attention(): pl.pallas_call(functools.partial(attention_block, scale_factor), grid=(wi...  10.5 us
    ppermute x4, starting transfers between devices, passed_along(): lax.ppermute(value, axis, [(source, source + steps) for source in range(l...  9.59 us
    pallas_call x1, Pallas kernels, head_values_grad(): pl.pallas_call(functools.partial(value_block, scale_factor), grid=(width_...  8.79 us
    ppermute x13, waiting for transfers between devices, exchange_total(): arrived = lax.ppermute(value, axis, pairs)  6.45 us
  transfers between devices with their start and end apart: 24, of which 11 were waited for; matrix products, arithmetic and copies ran while one was open for 22% of the time, Pallas kernels for 12%

profile of v16, /device:TPU:0, one launch (start us, length us, event | category | flops | bytes accessed | tf_op | source)
XLA Modules:
  0.0 161.6 jit_solution(17794031796965187675)
XLA Ops:
  9.1 2.4 %collective-permute-start = (bf16[6,1024]{1,0:T(8,128)(2,1)S(1)}, bf16[6,1024]{1,0:T(8,128)(2,1)S(1)}, u32[]{:S(2)}, u32[]{:S(2)}) collective-permute-start(bf16[6,1024]{1,0:T(8,128)(2,1)S(1)} %slice.52), channel_id=1, source_target_pairs={{0,4},{4,8},{8,12},{12,16},{16,20},{20,24},{24,28},{1,5},{5,9},{9,... | collective-permute-start | bytes 36872 | tf_op jit(solution)/shard_map/ppermute | solution.py:30
  11.4 2.8 %rev.12 = f32[7,1024]{1,0:T(8,128)S(1)} reverse(f32[7,1024]{1,0:T(8,128)} %param.15), dimensions={0} | reverse | bytes 57344 | tf_op jit(solution)/shard_map/rev | solution.py:189
  15.9 4.7 %collective-permute-start.1 = (bf16[127,1024]{1,0:T(8,128)(2,1)S(1)}, bf16[127,1024]{1,0:T(8,128)(2,1)S(1)}, u32[]{:S(2)}, u32[]{:S(2)}) collective-permute-start(bf16[127,1024]{1,0:T(8,128)(2,1)S(1)} %slice.50), channel_id=1, source_target_pairs={{0,4},{4,8},{8,12},{12,16},{16,20},{20,24},{24,28},{1,5},{5,9},{9,... | collective-permute-start | bytes 780296 | tf_op jit(solution)/shard_map/ppermute | solution.py:30
  21.9 5.8 %fusion.8 = f32[1,128,1024]{2,0,1:T(1,128)S(1)} fusion(f32[1,255,1024]{2,1,0:T(8,128)S(1)} %maximum_bitcast_fusion, f32[128,1,1024]{2,0,1:T(8,128)S(1)} %bitcast.76), kind=kOutput, calls=%fused_computation.36 | convolution fusion | flops 201326592 | bytes 2093056 | tf_op jit(solution)/shard_map/conv_general_dilated | solution.py:34
  28.7 1.6 %collective-permute-start.2 = (f32[128]{0:T(128)S(1)}, f32[128]{0:T(128)S(1)}, u32[]{:S(2)}, u32[]{:S(2)}) collective-permute-start(f32[128]{0:T(128)S(1)} %get-tuple-element.27), channel_id=1, source_target_pairs={{0,1},{1,2},{2,3},{3,0},{4,5},{5,6},{6,7},{7,4},{8,9},{9,10},{10,1... | collective-permute-start | bytes 1544 | tf_op jit(solution)/shard_map/ppermute | solution.py:74
  30.3 2.6 %collective-permute-start.3 = (f32[128]{0:T(128)S(1)}, f32[128]{0:T(128)S(1)}, u32[]{:S(2)}, u32[]{:S(2)}) collective-permute-start(f32[128]{0:T(128)S(1)} %get-tuple-element.27), channel_id=1, source_target_pairs={{0,2},{1,3},{2,0},{3,1},{4,6},{5,7},{6,4},{7,5},{8,10},{9,11},{10,... | collective-permute-start | bytes 1544 | tf_op jit(solution)/shard_map/ppermute | solution.py:74
  34.8 1.7 %collective-permute-done.4 = f32[128]{0:T(128)S(1)} collective-permute-done((f32[128]{0:T(128)S(1)}, f32[128]{0:T(128)S(1)}, u32[]{:S(2)}, u32[]{:S(2)}) %collective-permute-start.4) | collective-permute-done | bytes 544 | tf_op jit(solution)/shard_map/ppermute | solution.py:74
  38.4 3.3 %all-gather.3.cloned.1.call-done.k_ref = bf16[1024,1024]{1,0:T(8,128)(2,1)} async-done(((bf16[128,1024]{1,0:T(8,128)(2,1)}), bf16[1024,1024]{1,0:T(8,128)(2,1)}) %all-gather.3.cloned.1.call-update) | async-done | bytes 2097168 | tf_op jit(solution)/shard_map/all_gather | solution.py:203
  41.7 8.8 %shard_map.204 = bf16[1024,1024]{1,0:T(8,128)(2,1)} custom-call(bf16[128,1024]{1,0:T(8,128)(2,1)} %q_ref.3, bf16[1024,1024]{1,0:T(8,128)(2,1)} %all-gather.3.cloned.1.call-done.k_ref, bf16[128,1024]{1,0:T(8,128)(2,1)} %cot_ref.3, f32[128,1024]{1,0:T(8,128)} %fusion.33.vis_ref), custom_call_target="tpu_custom_call" | custom-call | tf_op jit(solution)/shard_map/pallas_call | solution.py:139
  50.5 5.8 %all-to-all-start = ((bf16[8,128,1024]{2,1,0:T(8,128)(2,1)}), bf16[8,128,1024]{2,1,0:T(8,128)(2,1)S(1)}, u32[]{:S(2)}, u32[]{:S(2)}) async-start(bf16[8,128,1024]{2,1,0:T(8,128)(2,1)} %bitcast.71), calls=%async_computation | async-start | bytes 4194304 | tf_op jit(solution)/shard_map/all_to_all | solution.py:212
  56.5 26.7 %all-gather.5.cloned.1.call-done.v_ref = bf16[1024,1024]{1,0:T(8,128)(2,1)} async-done(((bf16[128,1024]{1,0:T(8,128)(2,1)}), bf16[1024,1024]{1,0:T(8,128)(2,1)}) %all-gather.5.cloned.1.call-update) | async-done | bytes 2097168 | tf_op jit(solution)/shard_map/all_gather | solution.py:217
  83.1 10.5 %shard_map.203 = (bf16[1024,1024]{1,0:T(8,128)(2,1)}, f32[128,1024]{1,0:T(8,128)}, bf16[128,1024]{1,0:T(8,128)(2,1)}) custom-call(bf16[128,1024]{1,0:T(8,128)(2,1)} %q_ref.3, bf16[1024,1024]{1,0:T(8,128)(2,1)} %all-gather.3.cloned.1.call-done.k_ref, bf16[1024,1024]{1,0:T(8,128)(2,1)} %all-gather.5.cloned.1.call-done.v_ref, bf16[128,1024]{1,0:T(8,128)(2,1)} %cot_ref.3, ...), custom_call_target="tpu_custom_call" | custom-call | tf_op jit(solution)/shard_map/pallas_call | solution.py:152
  95.2 2.9 %collective-permute-start.6 = (f32[128]{0:T(128)S(1)}, f32[128]{0:T(128)S(1)}, u32[]{:S(2)}, u32[]{:S(2)}) collective-permute-start(f32[128]{0:T(128)S(1)} %get-tuple-element.22), channel_id=1, source_target_pairs={{0,2},{1,3},{2,0},{3,1},{4,6},{5,7},{6,4},{7,5},{8,10},{9,11},{10,... | collective-permute-start | bytes 1544 | tf_op jit(solution)/shard_map/ppermute | solution.py:74
  99.7 2.0 %collective-permute-done.7 = f32[128]{0:T(128)S(1)} collective-permute-done((f32[128]{0:T(128)S(1)}, f32[128]{0:T(128)S(1)}, u32[]{:S(2)}, u32[]{:S(2)}) %collective-permute-start.7) | collective-permute-done | bytes 544 | tf_op jit(solution)/shard_map/ppermute | solution.py:74
  105.1 5.8 %fusion.6 = bf16[1,128,1024]{2,0,1:T(2,128)(2,1)S(1)} fusion(f32[1,255,1024]{2,1,0:T(8,128)S(1)} %copy-done.9, f32[128,1,1024]{2,0,1:T(8,128)S(1)} %bitcast.72), kind=kOutput, calls=%fused_computation.34 | convolution fusion | flops 201326592 | bytes 1830912 | tf_op jit(solution)/shard_map/conv_general_dilated | solution.py:34
  112.7 5.8 %fusion = f32[1,128,1024]{2,0,1:T(1,128)S(1)} fusion(f32[1,255,1024]{2,1,0:T(8,128)S(1)} %maximum_bitcast_fusion.1, f32[128,1,1024]{2,0,1:T(8,128)S(1)} %bitcast.75), kind=kOutput, calls=%fused_computation.10 | convolution fusion | flops 201326592 | bytes 2093056 | tf_op jit(solution)/shard_map/conv_general_dilated | solution.py:34
  121.6 1.6 collective-permute-start.11
  123.7 2.0 %collective-permute-start.13 = (bf16[7,1024]{1,0:T(8,128)(2,1)S(1)}, bf16[7,1024]{1,0:T(8,128)(2,1)S(1)}, u32[]{:S(2)}, u32[]{:S(2)}) collective-permute-start(bf16[7,1024]{1,0:T(8,128)(2,1)S(1)} %rev.14), channel_id=1, source_target_pairs={{0,16},{4,20},{8,24},{12,28},{16,0},{20,4},{24,8},{28,12},{1,17},{... | collective-permute-start | bytes 43016 | tf_op jit(solution)/shard_map/ppermute | solution.py:74
  127.2 1.7 %collective-permute-done.9 = bf16[6,1024]{1,0:T(8,128)(2,1)S(1)} collective-permute-done((bf16[6,1024]{1,0:T(8,128)(2,1)S(1)}, bf16[6,1024]{1,0:T(8,128)(2,1)S(1)}, u32[]{:S(2)}, u32[]{:S(2)}) %collective-permute-start.9) | collective-permute-done | bytes 12320 | tf_op jit(solution)/shard_map/ppermute | solution.py:30
  128.9 1.8 %collective-permute-start.14 = (bf16[7,1024]{1,0:T(8,128)(2,1)S(1)}, bf16[7,1024]{1,0:T(8,128)(2,1)S(1)}, u32[]{:S(2)}, u32[]{:S(2)}) collective-permute-start(bf16[7,1024]{1,0:T(8,128)(2,1)S(1)} %rev.14), channel_id=1, source_target_pairs={{0,20},{4,24},{8,28},{12,0},{16,4},{20,8},{24,12},{28,16},{1,21},{... | collective-permute-start | bytes 43016 | tf_op jit(solution)/shard_map/ppermute | solution.py:74
  133.9 2.3 %collective-permute-start.15 = (bf16[7,1024]{1,0:T(8,128)(2,1)S(1)}, bf16[7,1024]{1,0:T(8,128)(2,1)S(1)}, u32[]{:S(2)}, u32[]{:S(2)}) collective-permute-start(bf16[7,1024]{1,0:T(8,128)(2,1)S(1)} %rev.14), channel_id=1, source_target_pairs={{0,24},{4,28},{8,0},{12,4},{16,8},{20,12},{24,16},{28,20},{1,25},{... | collective-permute-start | bytes 43016 | tf_op jit(solution)/shard_map/ppermute | solution.py:74
  136.5 1.4 collective-permute-done.15
  137.9 7.3 %collective-permute-done.18 = bf16[129,1024]{1,0:T(8,128)(2,1)S(1)} collective-permute-done((bf16[129,1024]{1,0:T(8,128)(2,1)S(1)}, bf16[129,1024]{1,0:T(8,128)(2,1)S(1)}, u32[]{:S(2)}, u32[]{:S(2)}) %collective-permute-start.18) | collective-permute-done | bytes 264224 | tf_op jit(solution)/shard_map/ppermute | solution.py:62
  146.7 6.9 %collective-permute-done.19 = bf16[129,1024]{1,0:T(8,128)(2,1)S(1)} collective-permute-done((bf16[129,1024]{1,0:T(8,128)(2,1)S(1)}, bf16[129,1024]{1,0:T(8,128)(2,1)S(1)}, u32[]{:S(2)}, u32[]{:S(2)}) %collective-permute-start.19) | collective-permute-done | bytes 264224 | tf_op jit(solution)/shard_map/ppermute | solution.py:62
  (153 shorter events, 28.9 us)
Async XLA Ops:
  7.2 34.5 %all-gather.3.cloned.1.call-start = ((), (), s32[]{:S(2)}) async-start(), calls=%async_computation.2 | async-start | bytes 2359296 | tf_op jit(solution)/shard_map/all_gather | solution.py:203
  7.9 75.2 %all-gather.5.cloned.1.call-start = ((), (), s32[]{:S(2)}) async-start(), calls=%async_computation.3 | async-start | bytes 2359296 | tf_op jit(solution)/shard_map/all_gather | solution.py:217
  9.1 5.2 %collective-permute-start = (bf16[6,1024]{1,0:T(8,128)(2,1)S(1)}, bf16[6,1024]{1,0:T(8,128)(2,1)S(1)}, u32[]{:S(2)}, u32[]{:S(2)}) collective-permute-start(bf16[6,1024]{1,0:T(8,128)(2,1)S(1)} %slice.52), channel_id=1, source_target_pairs={{0,4},{4,8},{8,12},{12,16},{16,20},{20,24},{24,28},{1,5},{5,9},{9,... | collective-permute-start | bytes 36872 | tf_op jit(solution)/shard_map/ppermute | solution.py:30
  15.9 5.8 %collective-permute-start.1 = (bf16[127,1024]{1,0:T(8,128)(2,1)S(1)}, bf16[127,1024]{1,0:T(8,128)(2,1)S(1)}, u32[]{:S(2)}, u32[]{:S(2)}) collective-permute-start(bf16[127,1024]{1,0:T(8,128)(2,1)S(1)} %slice.50), channel_id=1, source_target_pairs={{0,4},{4,8},{8,12},{12,16},{16,20},{20,24},{24,28},{1,5},{5,9},{9,... | collective-permute-start | bytes 780296 | tf_op jit(solution)/shard_map/ppermute | solution.py:30
  28.7 5.6 %collective-permute-start.2 = (f32[128]{0:T(128)S(1)}, f32[128]{0:T(128)S(1)}, u32[]{:S(2)}, u32[]{:S(2)}) collective-permute-start(f32[128]{0:T(128)S(1)} %get-tuple-element.27), channel_id=1, source_target_pairs={{0,1},{1,2},{2,3},{3,0},{4,5},{5,6},{6,7},{7,4},{8,9},{9,10},{10,1... | collective-permute-start | bytes 1544 | tf_op jit(solution)/shard_map/ppermute | solution.py:74
  30.3 4.4 %collective-permute-start.3 = (f32[128]{0:T(128)S(1)}, f32[128]{0:T(128)S(1)}, u32[]{:S(2)}, u32[]{:S(2)}) collective-permute-start(f32[128]{0:T(128)S(1)} %get-tuple-element.27), channel_id=1, source_target_pairs={{0,2},{1,3},{2,0},{3,1},{4,6},{5,7},{6,4},{7,5},{8,10},{9,11},{10,... | collective-permute-start | bytes 1544 | tf_op jit(solution)/shard_map/ppermute | solution.py:74
  32.9 3.5 %collective-permute-start.4 = (f32[128]{0:T(128)S(1)}, f32[128]{0:T(128)S(1)}, u32[]{:S(2)}, u32[]{:S(2)}) collective-permute-start(f32[128]{0:T(128)S(1)} %get-tuple-element.27), channel_id=1, source_target_pairs={{0,3},{1,0},{2,1},{3,2},{4,7},{5,4},{6,5},{7,6},{8,11},{9,8},{10,9... | collective-permute-start | bytes 1544 | tf_op jit(solution)/shard_map/ppermute | solution.py:74
  50.5 43.2 %all-to-all-start = ((bf16[8,128,1024]{2,1,0:T(8,128)(2,1)}), bf16[8,128,1024]{2,1,0:T(8,128)(2,1)S(1)}, u32[]{:S(2)}, u32[]{:S(2)}) async-start(bf16[8,128,1024]{2,1,0:T(8,128)(2,1)} %bitcast.71), calls=%async_computation | async-start | bytes 4194304 | tf_op jit(solution)/shard_map/all_to_all | solution.py:212
  56.3 98.8 %reduce-scatter.2.cloned.1.call-start = ((), (), s32[]{:S(2)}) async-start(), calls=%async_computation.4 | async-start | bytes 2359296 | tf_op jit(solution)/shard_map/reduce_scatter | solution.py:223
  94.2 5.4 %collective-permute-start.5 = (f32[128]{0:T(128)S(1)}, f32[128]{0:T(128)S(1)}, u32[]{:S(2)}, u32[]{:S(2)}) collective-permute-start(f32[128]{0:T(128)S(1)} %get-tuple-element.22), channel_id=1, source_target_pairs={{0,1},{1,2},{2,3},{3,0},{4,5},{5,6},{6,7},{7,4},{8,9},{9,10},{10,1... | collective-permute-start | bytes 1544 | tf_op jit(solution)/shard_map/ppermute | solution.py:74
  95.2 4.5 %collective-permute-start.6 = (f32[128]{0:T(128)S(1)}, f32[128]{0:T(128)S(1)}, u32[]{:S(2)}, u32[]{:S(2)}) collective-permute-start(f32[128]{0:T(128)S(1)} %get-tuple-element.22), channel_id=1, source_target_pairs={{0,2},{1,3},{2,0},{3,1},{4,6},{5,7},{6,4},{7,5},{8,10},{9,11},{10,... | collective-permute-start | bytes 1544 | tf_op jit(solution)/shard_map/ppermute | solution.py:74
  98.2 3.5 %collective-permute-start.7 = (f32[128]{0:T(128)S(1)}, f32[128]{0:T(128)S(1)}, u32[]{:S(2)}, u32[]{:S(2)}) collective-permute-start(f32[128]{0:T(128)S(1)} %get-tuple-element.22), channel_id=1, source_target_pairs={{0,3},{1,0},{2,1},{3,2},{4,7},{5,4},{6,5},{7,6},{8,11},{9,8},{10,9... | collective-permute-start | bytes 1544 | tf_op jit(solution)/shard_map/ppermute | solution.py:74
  103.8 8.8 %collective-permute-start.8 = (bf16[127,1024]{1,0:T(8,128)(2,1)}, bf16[127,1024]{1,0:T(8,128)(2,1)S(1)}, u32[]{:S(2)}, u32[]{:S(2)}) collective-permute-start(bf16[127,1024]{1,0:T(8,128)(2,1)} %slice.49), channel_id=1, source_target_pairs={{4,0},{8,4},{12,8},{16,12},{20,16},{24,20},{28,24},{5,1},{9,5},{13... | collective-permute-start | bytes 780296 | tf_op jit(solution)/shard_map/ppermute | solution.py:30
  111.3 14.5 %collective-permute-start.17 = (bf16[129,1024]{1,0:T(8,128)(2,1)S(1)}, bf16[129,1024]{1,0:T(8,128)(2,1)S(1)}, u32[]{:S(2)}, u32[]{:S(2)}) collective-permute-start(bf16[129,1024]{1,0:T(8,128)(2,1)S(1)} %pad_maximum_fusion), channel_id=1, source_target_pairs={{0,4},{4,0},{8,12},{12,8},{16,20},{20,16},{24,28},{28,24},{1,5},{5... | collective-permute-start | bytes 792584 | tf_op jit(solution)/shard_map/ppermute | solution.py:62
  121.2 12.7 %collective-permute-start.10 = (bf16[7,1024]{1,0:T(8,128)(2,1)S(1)}, bf16[7,1024]{1,0:T(8,128)(2,1)S(1)}, u32[]{:S(2)}, u32[]{:S(2)}) collective-permute-start(bf16[7,1024]{1,0:T(8,128)(2,1)S(1)} %rev.14), channel_id=1, source_target_pairs={{0,4},{4,8},{8,12},{12,16},{16,20},{20,24},{24,28},{28,0},{1,5},{5... | collective-permute-start | bytes 43016 | tf_op jit(solution)/shard_map/ppermute | solution.py:74
  121.6 14.6 %collective-permute-start.11 = (bf16[7,1024]{1,0:T(8,128)(2,1)S(1)}, bf16[7,1024]{1,0:T(8,128)(2,1)S(1)}, u32[]{:S(2)}, u32[]{:S(2)}) collective-permute-start(bf16[7,1024]{1,0:T(8,128)(2,1)S(1)} %rev.14), channel_id=1, source_target_pairs={{0,8},{4,12},{8,16},{12,20},{16,24},{20,28},{24,0},{28,4},{1,9},{5... | collective-permute-start | bytes 43016 | tf_op jit(solution)/shard_map/ppermute | solution.py:74
  123.2 13.0 %collective-permute-start.12 = (bf16[7,1024]{1,0:T(8,128)(2,1)S(1)}, bf16[7,1024]{1,0:T(8,128)(2,1)S(1)}, u32[]{:S(2)}, u32[]{:S(2)}) collective-permute-start(bf16[7,1024]{1,0:T(8,128)(2,1)S(1)} %rev.14), channel_id=1, source_target_pairs={{0,12},{4,16},{8,20},{12,24},{16,28},{20,0},{24,4},{28,8},{1,13},{... | collective-permute-start | bytes 43016 | tf_op jit(solution)/shard_map/ppermute | solution.py:74
  123.7 12.7 %collective-permute-start.13 = (bf16[7,1024]{1,0:T(8,128)(2,1)S(1)}, bf16[7,1024]{1,0:T(8,128)(2,1)S(1)}, u32[]{:S(2)}, u32[]{:S(2)}) collective-permute-start(bf16[7,1024]{1,0:T(8,128)(2,1)S(1)} %rev.14), channel_id=1, source_target_pairs={{0,16},{4,20},{8,24},{12,28},{16,0},{20,4},{24,8},{28,12},{1,17},{... | collective-permute-start | bytes 43016 | tf_op jit(solution)/shard_map/ppermute | solution.py:74
  125.8 3.1 %collective-permute-start.9 = (bf16[6,1024]{1,0:T(8,128)(2,1)S(1)}, bf16[6,1024]{1,0:T(8,128)(2,1)S(1)}, u32[]{:S(2)}, u32[]{:S(2)}) collective-permute-start(bf16[6,1024]{1,0:T(8,128)(2,1)S(1)} %slice.51), channel_id=1, source_target_pairs={{4,0},{8,4},{12,8},{16,12},{20,16},{24,20},{28,24},{5,1},{9,5},{13... | collective-permute-start | bytes 36872 | tf_op jit(solution)/shard_map/ppermute | solution.py:30
  128.9 7.6 %collective-permute-start.14 = (bf16[7,1024]{1,0:T(8,128)(2,1)S(1)}, bf16[7,1024]{1,0:T(8,128)(2,1)S(1)}, u32[]{:S(2)}, u32[]{:S(2)}) collective-permute-start(bf16[7,1024]{1,0:T(8,128)(2,1)S(1)} %rev.14), channel_id=1, source_target_pairs={{0,20},{4,24},{8,28},{12,0},{16,4},{20,8},{24,12},{28,16},{1,21},{... | collective-permute-start | bytes 43016 | tf_op jit(solution)/shard_map/ppermute | solution.py:74
  133.9 4.1 %collective-permute-start.15 = (bf16[7,1024]{1,0:T(8,128)(2,1)S(1)}, bf16[7,1024]{1,0:T(8,128)(2,1)S(1)}, u32[]{:S(2)}, u32[]{:S(2)}) collective-permute-start(bf16[7,1024]{1,0:T(8,128)(2,1)S(1)} %rev.14), channel_id=1, source_target_pairs={{0,24},{4,28},{8,0},{12,4},{16,8},{20,12},{24,16},{28,20},{1,25},{... | collective-permute-start | bytes 43016 | tf_op jit(solution)/shard_map/ppermute | solution.py:74
  136.2 1.8 %collective-permute-start.16 = (bf16[7,1024]{1,0:T(8,128)(2,1)S(1)}, bf16[7,1024]{1,0:T(8,128)(2,1)S(1)}, u32[]{:S(2)}, u32[]{:S(2)}) collective-permute-start(bf16[7,1024]{1,0:T(8,128)(2,1)S(1)} %rev.14), channel_id=1, source_target_pairs={{0,28},{4,0},{8,4},{12,8},{16,12},{20,16},{24,20},{28,24},{1,29},{... | collective-permute-start | bytes 43016 | tf_op jit(solution)/shard_map/ppermute | solution.py:74
  136.2 9.1 %collective-permute-start.18 = (bf16[129,1024]{1,0:T(8,128)(2,1)S(1)}, bf16[129,1024]{1,0:T(8,128)(2,1)S(1)}, u32[]{:S(2)}, u32[]{:S(2)}) collective-permute-start(bf16[129,1024]{1,0:T(8,128)(2,1)S(1)} %add_convert_fusion.1), channel_id=1, source_target_pairs={{0,8},{4,12},{8,0},{12,4},{16,24},{20,28},{24,16},{28,20},{1,9},{5... | collective-permute-start | bytes 792584 | tf_op jit(solution)/shard_map/ppermute | solution.py:62
  145.3 8.3 %collective-permute-start.19 = (bf16[129,1024]{1,0:T(8,128)(2,1)S(1)}, bf16[129,1024]{1,0:T(8,128)(2,1)S(1)}, u32[]{:S(2)}, u32[]{:S(2)}) collective-permute-start(bf16[129,1024]{1,0:T(8,128)(2,1)S(1)} %add_convert_fusion), channel_id=1, source_target_pairs={{0,16},{4,20},{8,24},{12,28},{16,0},{20,4},{24,8},{28,12},{1,17},{... | collective-permute-start | bytes 792584 | tf_op jit(solution)/shard_map/ppermute | solution.py:62
  (24 other events, 101.8 us)
Sparse Core Ops, SparseCore 0:
  9.9 31.7 all-gather.2
  44.1 38.9 all-gather.4
  98.8 40.6 reduce-scatter.1

commit v17 on v9

--- a/solution.py
+++ b/solution.py
@@ -38,7 +38,7 @@
         "VALID",
         dimension_numbers=("NWC", "WIO", "NWC"),
         feature_group_count=padded.shape[1],
-        precision=lax.Precision.HIGHEST,
+        precision=lax.Precision.DEFAULT,
     )[0]
 
 

time: 154 us -> 155 us (level)
  matrix products: 19.6 us -> 23 us
  waiting for transfers between devices: 51.7 us -> 49.3 us
    conv_general_dilated x6, matrix products: 19.6 us -> 23 us  [depthwise(): lax.conv_general_dilated(padded[None], tap_rows[:, None, :], (1,), 'VALID...]
    all_gather x1, waiting for transfers between devices: 3.23 us -> 0.84 us  [shards(): keys_whole = lax.all_gather(matchers, 'ctx', axis=0, tiled=True)]
    all_to_all x1, starting transfers between devices: 5.84 us -> 7.64 us  [shards(): lax.all_to_all(value_part, 'ctx', 0, 0, tiled=True)]
  transfers between devices with their start and end apart: 17 -> 17, of which waited for: 11 -> 12; matrix products, arithmetic and copies ran while one was open for 23% -> 24% of each run, Pallas kernels for 13% -> 13%
where the time goes in v17:
time: 155 us; the launch traced here: 154 us
  waiting for transfers between devices  49.3 us (32%)
  starting transfers between devices  30.2 us (19%)
  matrix products  23 us (15%)
  Pallas kernels  19.3 us (12%)
  between operations  14.4 us (9%)
  other arithmetic  9.77 us (6%)
  local copies, waits for them, and re-layouts  7.66 us (5%)
    all_gather x1, waiting for transfers between devices, shards(): values_whole = lax.all_gather(normed, 'ctx', axis=0, tiled=True)  26.6 us
    conv_general_dilated x6, matrix products, depthwise(): lax.conv_general_dilated(padded[None], tap_rows[:, None, :], (1,), 'VALID...  23 us
    ppermute x3, waiting for transfers between devices, butterfly_total(): lax.ppermute(rounded, axis, pairs).astype(value.dtype)  13.7 us
    pallas_call x1, Pallas kernels, head_attention(): pl.pallas_call(functools.partial(attention_block, scale_factor), grid=(wi...  10.5 us
    ppermute x6, starting transfers between devices, exchange_total(): arrived = lax.ppermute(value, axis, pairs)  10.1 us
    ppermute x4, starting transfers between devices, passed_along(): lax.ppermute(value, axis, [(source, source + steps) for source in range(l...  9.59 us
    pallas_call x1, Pallas kernels, head_values_grad(): pl.pallas_call(functools.partial(value_block, scale_factor), grid=(width_...  8.79 us
    all_to_all x1, starting transfers between devices, shards(): lax.all_to_all(value_part, 'ctx', 0, 0, tiled=True)  7.64 us
  transfers between devices with their start and end apart: 17, of which 12 were waited for; matrix products, arithmetic and copies ran while one was open for 24% of the time, Pallas kernels for 13%

profile of v17, /device:TPU:0, one launch (start us, length us, event | category | flops | bytes accessed | tf_op | source)
XLA Modules:
  0.0 153.6 jit_solution(13951368617888970971)
XLA Ops:
  9.1 2.4 %collective-permute-start = (bf16[6,1024]{1,0:T(8,128)(2,1)S(1)}, bf16[6,1024]{1,0:T(8,128)(2,1)S(1)}, u32[]{:S(2)}, u32[]{:S(2)}) collective-permute-start(bf16[6,1024]{1,0:T(8,128)(2,1)S(1)} %slice.58), channel_id=1, source_target_pairs={{0,4},{4,8},{8,12},{12,16},{16,20},{20,24},{24,28},{1,5},{5,9},{9,... | collective-permute-start | bytes 36872 | tf_op jit(solution)/shard_map/ppermute | solution.py:30
  11.4 2.8 %rev.12 = bf16[7,1024]{1,0:T(8,128)(2,1)S(1)} reverse(f32[7,1024]{1,0:T(8,128)} %param.15), dimensions={0} | reverse | bytes 43008 | tf_op jit(solution)/shard_map/rev | solution.py:189
  16.5 4.7 %collective-permute-start.1 = (bf16[127,1024]{1,0:T(8,128)(2,1)S(1)}, bf16[127,1024]{1,0:T(8,128)(2,1)S(1)}, u32[]{:S(2)}, u32[]{:S(2)}) collective-permute-start(bf16[127,1024]{1,0:T(8,128)(2,1)S(1)} %slice.56), channel_id=1, source_target_pairs={{0,4},{4,8},{8,12},{12,16},{16,20},{20,24},{24,28},{1,5},{5,9},{9,... | collective-permute-start | bytes 780296 | tf_op jit(solution)/shard_map/ppermute | solution.py:30
  22.4 7.3 %fusion.8 = f32[1,128,1024]{2,0,1:T(1,128)S(1)} fusion(bf16[1,255,1024]{2,1,0:T(8,128)(2,1)S(1)} %maximum_bitcast_fusion, bf16[128,1,1024]{2,0,1:T(8,128)(2,1)S(1)} %bitcast.62), kind=kOutput, calls=%fused_computation.36 | convolution fusion | flops 33554432 | bytes 1308672 | tf_op jit(solution)/shard_map/conv_general_dilated | solution.py:34
  30.8 1.6 %collective-permute-start.2 = (f32[128]{0:T(128)S(1)}, f32[128]{0:T(128)S(1)}, u32[]{:S(2)}, u32[]{:S(2)}) collective-permute-start(f32[128]{0:T(128)S(1)} %get-tuple-element.27), channel_id=1, source_target_pairs={{0,1},{1,2},{2,3},{3,0},{4,5},{5,6},{6,7},{7,4},{8,9},{9,10},{10,1... | collective-permute-start | bytes 1544 | tf_op jit(solution)/shard_map/ppermute | solution.py:74
  32.4 2.6 %collective-permute-start.3 = (f32[128]{0:T(128)S(1)}, f32[128]{0:T(128)S(1)}, u32[]{:S(2)}, u32[]{:S(2)}) collective-permute-start(f32[128]{0:T(128)S(1)} %get-tuple-element.27), channel_id=1, source_target_pairs={{0,2},{1,3},{2,0},{3,1},{4,6},{5,7},{6,4},{7,5},{8,10},{9,11},{10,... | collective-permute-start | bytes 1544 | tf_op jit(solution)/shard_map/ppermute | solution.py:74
  35.0 1.3 collective-permute-start.4
  36.9 1.7 %collective-permute-done.4 = f32[128]{0:T(128)S(1)} collective-permute-done((f32[128]{0:T(128)S(1)}, f32[128]{0:T(128)S(1)}, u32[]{:S(2)}, u32[]{:S(2)}) %collective-permute-start.4) | collective-permute-done | bytes 544 | tf_op jit(solution)/shard_map/ppermute | solution.py:74
  41.4 8.8 %shard_map.204 = bf16[1024,1024]{1,0:T(8,128)(2,1)} custom-call(bf16[128,1024]{1,0:T(8,128)(2,1)} %q_ref.3, bf16[1024,1024]{1,0:T(8,128)(2,1)} %all-gather.3.cloned.1.call-done.k_ref, bf16[128,1024]{1,0:T(8,128)(2,1)} %cot_ref.3, f32[128,1024]{1,0:T(8,128)} %fusion.33.vis_ref), custom_call_target="tpu_custom_call" | custom-call | tf_op jit(solution)/shard_map/pallas_call | solution.py:139
  50.2 7.6 %all-to-all-start = ((bf16[8,128,1024]{2,1,0:T(8,128)(2,1)}), bf16[8,128,1024]{2,1,0:T(8,128)(2,1)S(1)}, u32[]{:S(2)}, u32[]{:S(2)}) async-start(bf16[8,128,1024]{2,1,0:T(8,128)(2,1)} %bitcast.56), calls=%async_computation | async-start | bytes 4194304 | tf_op jit(solution)/shard_map/all_to_all | solution.py:212
  57.8 26.6 %all-gather.5.cloned.1.call-done.v_ref = bf16[1024,1024]{1,0:T(8,128)(2,1)} async-done(((bf16[128,1024]{1,0:T(8,128)(2,1)}), bf16[1024,1024]{1,0:T(8,128)(2,1)}) %all-gather.5.cloned.1.call-update) | async-done | bytes 2097168 | tf_op jit(solution)/shard_map/all_gather | solution.py:217
  84.5 10.5 %shard_map.203 = (bf16[1024,1024]{1,0:T(8,128)(2,1)}, f32[128,1024]{1,0:T(8,128)}, bf16[128,1024]{1,0:T(8,128)(2,1)}) custom-call(bf16[128,1024]{1,0:T(8,128)(2,1)} %q_ref.3, bf16[1024,1024]{1,0:T(8,128)(2,1)} %all-gather.3.cloned.1.call-done.k_ref, bf16[1024,1024]{1,0:T(8,128)(2,1)} %all-gather.5.cloned.1.call-done.v_ref, bf16[128,1024]{1,0:T(8,128)(2,1)} %cot_ref.3, ...), custom_call_target="tpu_custom_call" | custom-call | tf_op jit(solution)/shard_map/pallas_call | solution.py:152
  96.6 2.9 %collective-permute-start.6 = (f32[128]{0:T(128)S(1)}, f32[128]{0:T(128)S(1)}, u32[]{:S(2)}, u32[]{:S(2)}) collective-permute-start(f32[128]{0:T(128)S(1)} %get-tuple-element.22), channel_id=1, source_target_pairs={{0,2},{1,3},{2,0},{3,1},{4,6},{5,7},{6,4},{7,5},{8,10},{9,11},{10,... | collective-permute-start | bytes 1544 | tf_op jit(solution)/shard_map/ppermute | solution.py:74
  101.1 1.9 %collective-permute-done.7 = f32[128]{0:T(128)S(1)} collective-permute-done((f32[128]{0:T(128)S(1)}, f32[128]{0:T(128)S(1)}, u32[]{:S(2)}, u32[]{:S(2)}) %collective-permute-start.7) | collective-permute-done | bytes 544 | tf_op jit(solution)/shard_map/ppermute | solution.py:74
  104.3 1.3 collective-permute-start.8
  105.6 7.4 %fusion.6 = bf16[1,128,1024]{2,0,1:T(2,128)(2,1)S(1)} fusion(bf16[1,255,1024]{2,1,0:T(8,128)(2,1)S(1)} %copy-done.16, bf16[128,1,1024]{2,0,1:T(8,128)(2,1)S(1)} %bitcast.60), kind=kOutput, calls=%fused_computation.34 | convolution fusion | flops 33554432 | bytes 1046528 | tf_op jit(solution)/shard_map/conv_general_dilated | solution.py:34
  114.1 5.8 %fusion = f32[1,128,1024]{2,0,1:T(1,128)S(1)} fusion(bf16[1,255,1024]{2,1,0:T(8,128)(2,1)S(1)} %maximum_bitcast_fusion.1, f32[128,1,1024]{2,0,1:T(8,128)S(1)} %bitcast.61), kind=kOutput, calls=%fused_computation.10 | convolution fusion | flops 33554432 | bytes 1570816 | tf_op jit(solution)/shard_map/conv_general_dilated | solution.py:34
  121.1 1.2 fusion.27
  122.6 1.2 collective-permute-start.10
  123.8 1.2 collective-permute-done.10
  125.9 1.3 collective-permute-start.9
  127.2 1.8 %collective-permute-done.9 = bf16[6,1024]{1,0:T(8,128)(2,1)S(1)} collective-permute-done((bf16[6,1024]{1,0:T(8,128)(2,1)S(1)}, bf16[6,1024]{1,0:T(8,128)(2,1)S(1)}, u32[]{:S(2)}, u32[]{:S(2)}) %collective-permute-start.9) | collective-permute-done | bytes 12320 | tf_op jit(solution)/shard_map/ppermute | solution.py:30
  129.4 4.7 %collective-permute-done.11 = bf16[136,1024]{1,0:T(8,128)(2,1)S(1)} collective-permute-done((bf16[136,1024]{1,0:T(8,128)(2,1)S(1)}, bf16[136,1024]{1,0:T(8,128)(2,1)S(1)}, u32[]{:S(2)}, u32[]{:S(2)}) %collective-permute-start.11) | collective-permute-done | bytes 278560 | tf_op jit(solution)/shard_map/ppermute | solution.py:62
  137.1 7.9 %collective-permute-done.12 = bf16[136,1024]{1,0:T(8,128)(2,1)S(1)} collective-permute-done((bf16[136,1024]{1,0:T(8,128)(2,1)S(1)}, bf16[136,1024]{1,0:T(8,128)(2,1)S(1)}, u32[]{:S(2)}, u32[]{:S(2)}) %collective-permute-start.12) | collective-permute-done | bytes 278560 | tf_op jit(solution)/shard_map/ppermute | solution.py:62
  (124 shorter events, 22.9 us)
Async XLA Ops:
  7.2 34.2 %all-gather.3.cloned.1.call-start = ((), (), s32[]{:S(2)}) async-start(), calls=%async_computation.2 | async-start | bytes 2359296 | tf_op jit(solution)/shard_map/all_gather | solution.py:203
  7.9 76.5 %all-gather.5.cloned.1.call-start = ((), (), s32[]{:S(2)}) async-start(), calls=%async_computation.3 | async-start | bytes 2359296 | tf_op jit(solution)/shard_map/all_gather | solution.py:217
  9.1 5.2 %collective-permute-start = (bf16[6,1024]{1,0:T(8,128)(2,1)S(1)}, bf16[6,1024]{1,0:T(8,128)(2,1)S(1)}, u32[]{:S(2)}, u32[]{:S(2)}) collective-permute-start(bf16[6,1024]{1,0:T(8,128)(2,1)S(1)} %slice.58), channel_id=1, source_target_pairs={{0,4},{4,8},{8,12},{12,16},{16,20},{20,24},{24,28},{1,5},{5,9},{9,... | collective-permute-start | bytes 36872 | tf_op jit(solution)/shard_map/ppermute | solution.py:30
  16.5 5.8 %collective-permute-start.1 = (bf16[127,1024]{1,0:T(8,128)(2,1)S(1)}, bf16[127,1024]{1,0:T(8,128)(2,1)S(1)}, u32[]{:S(2)}, u32[]{:S(2)}) collective-permute-start(bf16[127,1024]{1,0:T(8,128)(2,1)S(1)} %slice.56), channel_id=1, source_target_pairs={{0,4},{4,8},{8,12},{12,16},{16,20},{20,24},{24,28},{1,5},{5,9},{9,... | collective-permute-start | bytes 780296 | tf_op jit(solution)/shard_map/ppermute | solution.py:30
  22.4 8.2 %copy-start.8 = (bf16[128,1024]{1,0:T(8,128)(2,1)S(1)}, bf16[128,1024]{1,0:T(8,128)(2,1)}, u32[]{:S(2)}) copy-start(bf16[128,1024]{1,0:T(8,128)(2,1)} %param.16) | copy-start | bytes 786436
  22.4 16.2 %copy-start.20 = (f32[1024]{0:T(1024)S(1)}, f32[1024]{0:T(1024)}, u32[]{:S(2)}) copy-start(f32[1024]{0:T(1024)} %param.19) | copy-start | bytes 12292
  29.8 9.7 %copy-start.22 = (s32[1024]{0:T(1024)S(1)}, s32[1024]{0:T(1024)}, u32[]{:S(2)}) copy-start(s32[1024]{0:T(1024)} %param.22) | copy-start | bytes 12292
  30.8 5.6 %collective-permute-start.2 = (f32[128]{0:T(128)S(1)}, f32[128]{0:T(128)S(1)}, u32[]{:S(2)}, u32[]{:S(2)}) collective-permute-start(f32[128]{0:T(128)S(1)} %get-tuple-element.27), channel_id=1, source_target_pairs={{0,1},{1,2},{2,3},{3,0},{4,5},{5,6},{6,7},{7,4},{8,9},{9,10},{10,1... | collective-permute-start | bytes 1544 | tf_op jit(solution)/shard_map/ppermute | solution.py:74
  32.4 4.4 %collective-permute-start.3 = (f32[128]{0:T(128)S(1)}, f32[128]{0:T(128)S(1)}, u32[]{:S(2)}, u32[]{:S(2)}) collective-permute-start(f32[128]{0:T(128)S(1)} %get-tuple-element.27), channel_id=1, source_target_pairs={{0,2},{1,3},{2,0},{3,1},{4,6},{5,7},{6,4},{7,5},{8,10},{9,11},{10,... | collective-permute-start | bytes 1544 | tf_op jit(solution)/shard_map/ppermute | solution.py:74
  35.0 3.5 %collective-permute-start.4 = (f32[128]{0:T(128)S(1)}, f32[128]{0:T(128)S(1)}, u32[]{:S(2)}, u32[]{:S(2)}) collective-permute-start(f32[128]{0:T(128)S(1)} %get-tuple-element.27), channel_id=1, source_target_pairs={{0,3},{1,0},{2,1},{3,2},{4,7},{5,4},{6,5},{7,6},{8,11},{9,8},{10,9... | collective-permute-start | bytes 1544 | tf_op jit(solution)/shard_map/ppermute | solution.py:74
  50.2 44.8 %all-to-all-start = ((bf16[8,128,1024]{2,1,0:T(8,128)(2,1)}), bf16[8,128,1024]{2,1,0:T(8,128)(2,1)S(1)}, u32[]{:S(2)}, u32[]{:S(2)}) async-start(bf16[8,128,1024]{2,1,0:T(8,128)(2,1)} %bitcast.56), calls=%async_computation | async-start | bytes 4194304 | tf_op jit(solution)/shard_map/all_to_all | solution.py:212
  57.8 89.3 %reduce-scatter.2.cloned.1.call-start = ((), (), s32[]{:S(2)}) async-start(), calls=%async_computation.4 | async-start | bytes 2359296 | tf_op jit(solution)/shard_map/reduce_scatter | solution.py:223
  95.4 7.7 %copy-start = (bf16[128,1024]{1,0:T(8,128)(2,1)S(1)}, bf16[128,1024]{1,0:T(8,128)(2,1)}, u32[]{:S(2)}) copy-start(bf16[128,1024]{1,0:T(8,128)(2,1)} %cot_ref.3) | copy-start | bytes 786436
  95.4 7.7 %copy-start.5 = (f32[1,128,1024]{2,0,1:T(1,128)S(1)}, f32[1,128,1024]{2,0,1:T(1,128)}, u32[]{:S(2)}) copy-start(f32[1,128,1024]{2,0,1:T(1,128)} %copy-done.4) | copy-start | bytes 1572868
  95.6 5.4 %collective-permute-start.5 = (f32[128]{0:T(128)S(1)}, f32[128]{0:T(128)S(1)}, u32[]{:S(2)}, u32[]{:S(2)}) collective-permute-start(f32[128]{0:T(128)S(1)} %get-tuple-element.22), channel_id=1, source_target_pairs={{0,1},{1,2},{2,3},{3,0},{4,5},{5,6},{6,7},{7,4},{8,9},{9,10},{10,1... | collective-permute-start | bytes 1544 | tf_op jit(solution)/shard_map/ppermute | solution.py:74
  96.6 4.4 %collective-permute-start.6 = (f32[128]{0:T(128)S(1)}, f32[128]{0:T(128)S(1)}, u32[]{:S(2)}, u32[]{:S(2)}) collective-permute-start(f32[128]{0:T(128)S(1)} %get-tuple-element.22), channel_id=1, source_target_pairs={{0,2},{1,3},{2,0},{3,1},{4,6},{5,7},{6,4},{7,5},{8,10},{9,11},{10,... | collective-permute-start | bytes 1544 | tf_op jit(solution)/shard_map/ppermute | solution.py:74
  99.5 3.5 %collective-permute-start.7 = (f32[128]{0:T(128)S(1)}, f32[128]{0:T(128)S(1)}, u32[]{:S(2)}, u32[]{:S(2)}) collective-permute-start(f32[128]{0:T(128)S(1)} %get-tuple-element.22), channel_id=1, source_target_pairs={{0,3},{1,0},{2,1},{3,2},{4,7},{5,4},{6,5},{7,6},{8,11},{9,8},{10,9... | collective-permute-start | bytes 1544 | tf_op jit(solution)/shard_map/ppermute | solution.py:74
  104.3 9.2 %collective-permute-start.8 = (bf16[127,1024]{1,0:T(8,128)(2,1)S(1)}, bf16[127,1024]{1,0:T(8,128)(2,1)S(1)}, u32[]{:S(2)}, u32[]{:S(2)}) collective-permute-start(bf16[127,1024]{1,0:T(8,128)(2,1)S(1)} %bitcast.59), channel_id=1, source_target_pairs={{4,0},{8,4},{12,8},{16,12},{20,16},{24,20},{28,24},{5,1},{9,5},{13... | collective-permute-start | bytes 780296 | tf_op jit(solution)/shard_map/ppermute | solution.py:30
  122.6 2.4 %collective-permute-start.10 = (bf16[136,1024]{1,0:T(8,128)(2,1)S(1)}, bf16[136,1024]{1,0:T(8,128)(2,1)S(1)}, u32[]{:S(2)}, u32[]{:S(2)}) collective-permute-start(bf16[136,1024]{1,0:T(8,128)(2,1)S(1)} %pad_maximum_fusion), channel_id=1, source_target_pairs={{0,4},{4,0},{8,12},{12,8},{16,20},{20,16},{24,28},{28,24},{1,5},{5... | collective-permute-start | bytes 835592 | tf_op jit(solution)/shard_map/ppermute | solution.py:62
  125.0 9.9 %copy-start.21 = (f32[7,1024]{1,0:T(8,128)S(1)}, f32[7,1024]{1,0:T(8,128)}, u32[]{:S(2)}) copy-start(f32[7,1024]{1,0:T(8,128)} %param.15) | copy-start | bytes 86020
  125.0 9.8 %copy-start.23 = (pred[8,17]{0,1:T(8,128)(4,1)S(1)}, pred[8,17]{0,1:T(8,128)(4,1)}, u32[]{:S(2)}) copy-start(pred[8,17]{0,1:T(8,128)(4,1)} %constant.100) | copy-start | bytes 412
  125.1 9.0 %collective-permute-start.11 = (bf16[136,1024]{1,0:T(8,128)(2,1)S(1)}, bf16[136,1024]{1,0:T(8,128)(2,1)S(1)}, u32[]{:S(2)}, u32[]{:S(2)}) collective-permute-start(bf16[136,1024]{1,0:T(8,128)(2,1)S(1)} %add_convert_fusion.1), channel_id=1, source_target_pairs={{0,8},{4,12},{8,0},{12,4},{16,24},{20,28},{24,16},{28,20},{1,9},{5... | collective-permute-start | bytes 835592 | tf_op jit(solution)/shard_map/ppermute | solution.py:62
  125.9 3.1 %collective-permute-start.9 = (bf16[6,1024]{1,0:T(8,128)(2,1)S(1)}, bf16[6,1024]{1,0:T(8,128)(2,1)S(1)}, u32[]{:S(2)}, u32[]{:S(2)}) collective-permute-start(bf16[6,1024]{1,0:T(8,128)(2,1)S(1)} %slice.57), channel_id=1, source_target_pairs={{4,0},{8,4},{12,8},{16,12},{20,16},{24,20},{28,24},{5,1},{9,5},{13... | collective-permute-start | bytes 36872 | tf_op jit(solution)/shard_map/ppermute | solution.py:30
  134.1 10.8 %collective-permute-start.12 = (bf16[136,1024]{1,0:T(8,128)(2,1)S(1)}, bf16[136,1024]{1,0:T(8,128)(2,1)S(1)}, u32[]{:S(2)}, u32[]{:S(2)}) collective-permute-start(bf16[136,1024]{1,0:T(8,128)(2,1)S(1)} %add_convert_fusion), channel_id=1, source_target_pairs={{0,16},{4,20},{8,24},{12,28},{16,0},{20,4},{24,8},{28,12},{1,17},{... | collective-permute-start | bytes 835592 | tf_op jit(solution)/shard_map/ppermute | solution.py:62
  (17 other events, 53.7 us)
Sparse Core Ops, SparseCore 0:
  9.9 31.4 all-gather.2
  43.8 40.5 all-gather.4
  100.2 41.7 reduce-scatter.1

commit v18 on v9

--- a/solution.py
+++ b/solution.py
@@ -208,13 +208,20 @@
     visible = (key_pos[None, :] <= query_pos[:, None]) & (segments[None, :] == query_seg[:, None])
     mask = visible.astype(jnp.float32)
     value_part = head_values_grad(queries, keys_whole, cotangent, mask, scale_factor)
+    exchanged = lax.all_to_all(
+        jnp.concatenate([value_part, jnp.tile(normed, (ctx_count, 1))], axis=1),
+        "ctx",
+        0,
+        0,
+        tiled=True,
+    )
     value_grad = (
-        lax.all_to_all(value_part, "ctx", 0, 0, tiled=True)
+        exchanged[:, :width_local]
         .reshape(ctx_count, local_rows, width_local)
         .astype(jnp.float32)
         .sum(axis=0)
     )
-    values_whole = lax.all_gather(normed, "ctx", axis=0, tiled=True)
+    values_whole = exchanged[:, width_local:]
     key_part, attended_all, queries_grad = head_attention(
         queries, keys_whole, values_whole, cotangent, mask, scale_factor
     )

time: 154 us -> 177 us (1.15)
  blocking collectives: 0 us -> 52.1 us
  waiting for transfers between devices: 51.7 us -> 25.2 us
  starting transfers between devices: 29.7 us -> 22.2 us
  other arithmetic: 9.97 us -> 11.8 us
    all_to_all x0 -> x1, blocking collectives: none -> 52.1 us  [shards(): lax.all_to_all(jnp.concatenate([value_part, jnp.tile(normed, (ctx_count,...]
    all_gather x1 -> x0, waiting for transfers between devices: 26.8 us -> none  [shards(): values_whole = lax.all_gather(normed, 'ctx', axis=0, tiled=True)]
    all_to_all x1 -> x0, starting transfers between devices: 5.84 us -> none  [shards(): lax.all_to_all(value_part, 'ctx', 0, 0, tiled=True)]
    all_gather x1, waiting for transfers between devices: 3.23 us -> 5.76 us  [shards(): keys_whole = lax.all_gather(matchers, 'ctx', axis=0, tiled=True)]
    ppermute x3, starting transfers between devices: 4.21 us -> 2.23 us  [butterfly_total(): lax.ppermute(rounded, axis, pairs).astype(value.dtype)]
    slice x0 -> x1, local copies, waits for them, and re-layouts: none -> 1.79 us  [shards(): exchanged[:, :width_local].reshape(ctx_count, local_rows, width_local)]
  transfers between devices with their start and end apart: 17 -> 15, of which waited for: 11 -> 10; matrix products, arithmetic and copies ran while one was open for 23% -> 21% of each run, Pallas kernels for 13% -> 0%
where the time goes in v18:
time: 177 us; the launch traced here: 176 us
  blocking collectives  52.1 us (29%)
  waiting for transfers between devices  25.2 us (14%)
  starting transfers between devices  22.2 us (13%)
  matrix products  20.9 us (12%)
  Pallas kernels  19.3 us (11%)
  between operations  14.7 us (8%)
  other arithmetic  11.8 us (7%)
  local copies, waits for them, and re-layouts  9.67 us (5%)
    all_to_all x1, blocking collectives, shards(): lax.all_to_all(jnp.concatenate([value_part, jnp.tile(normed, (ctx_count,...  52.1 us
    conv_general_dilated x6, matrix products, depthwise(): lax.conv_general_dilated(padded[None], tap_rows[:, None, :], (1,), 'VALID...  20.9 us
    ppermute x3, waiting for transfers between devices, butterfly_total(): lax.ppermute(rounded, axis, pairs).astype(value.dtype)  12.6 us
    pallas_call x1, Pallas kernels, head_attention(): pl.pallas_call(functools.partial(attention_block, scale_factor), grid=(wi...  10.6 us
    ppermute x6, starting transfers between devices, exchange_total(): arrived = lax.ppermute(value, axis, pairs)  10.5 us
    ppermute x4, starting transfers between devices, passed_along(): lax.ppermute(value, axis, [(source, source + steps) for source in range(l...  9.45 us
    pallas_call x1, Pallas kernels, head_values_grad(): pl.pallas_call(functools.partial(value_block, scale_factor), grid=(width_...  8.75 us
    all_gather x1, waiting for transfers between devices, shards(): keys_whole = lax.all_gather(matchers, 'ctx', axis=0, tiled=True)  5.76 us
  transfers between devices with their start and end apart: 15, of which 10 were waited for; matrix products, arithmetic and copies ran while one was open for 21% of the time, Pallas kernels for 0%

profile of v18, /device:TPU:0, one launch (start us, length us, event | category | flops | bytes accessed | tf_op | source)
XLA Modules:
  0.0 175.9 jit_solution(5969410382749956074)
XLA Ops:
  9.1 2.4 %collective-permute-start = (bf16[6,1024]{1,0:T(8,128)(2,1)S(1)}, bf16[6,1024]{1,0:T(8,128)(2,1)S(1)}, u32[]{:S(2)}, u32[]{:S(2)}) collective-permute-start(bf16[6,1024]{1,0:T(8,128)(2,1)S(1)} %slice.68), channel_id=1, source_target_pairs={{0,4},{4,8},{8,12},{12,16},{16,20},{20,24},{24,28},{1,5},{5,9},{9,... | collective-permute-start | bytes 36872 | tf_op jit(solution)/shard_map/ppermute | solution.py:30
  11.4 2.8 %rev.12 = f32[7,1024]{1,0:T(8,128)S(1)} reverse(f32[7,1024]{1,0:T(8,128)} %param.15), dimensions={0} | reverse | bytes 57344 | tf_op jit(solution)/shard_map/rev | solution.py:189
  15.9 4.5 %collective-permute-start.1 = (bf16[127,1024]{1,0:T(8,128)(2,1)S(1)}, bf16[127,1024]{1,0:T(8,128)(2,1)S(1)}, u32[]{:S(2)}, u32[]{:S(2)}) collective-permute-start(bf16[127,1024]{1,0:T(8,128)(2,1)S(1)} %slice.66), channel_id=1, source_target_pairs={{0,4},{4,8},{8,12},{12,16},{16,20},{20,24},{24,28},{1,5},{5,9},{9,... | collective-permute-start | bytes 780296 | tf_op jit(solution)/shard_map/ppermute | solution.py:30
  22.0 5.8 %fusion.8 = f32[1,128,1024]{2,0,1:T(1,128)S(1)} fusion(f32[1,255,1024]{2,1,0:T(8,128)S(1)} %maximum_bitcast_fusion, f32[128,1,1024]{2,0,1:T(8,128)S(1)} %bitcast.65), kind=kOutput, calls=%fused_computation.37 | convolution fusion | flops 201326592 | bytes 2093056 | tf_op jit(solution)/shard_map/conv_general_dilated | solution.py:34
  28.1 1.6 collective-permute-start.2
  29.7 2.6 %collective-permute-start.3 = (f32[128]{0:T(128)S(1)}, f32[128]{0:T(128)S(1)}, u32[]{:S(2)}, u32[]{:S(2)}) collective-permute-start(f32[128]{0:T(128)S(1)} %get-tuple-element.27), channel_id=1, source_target_pairs={{0,2},{1,3},{2,0},{3,1},{4,6},{5,7},{6,4},{7,5},{8,10},{9,11},{10,... | collective-permute-start | bytes 1544 | tf_op jit(solution)/shard_map/ppermute | solution.py:74
  32.3 1.3 collective-permute-start.4
  34.1 1.7 collective-permute-done.4
  36.0 5.8 %all-gather.2.cloned.1.call-done.k_ref = bf16[1024,1024]{1,0:T(8,128)(2,1)} async-done(((bf16[128,1024]{1,0:T(8,128)(2,1)}), bf16[1024,1024]{1,0:T(8,128)(2,1)}) %all-gather.2.cloned.1.call-update) | async-done | bytes 2097168 | tf_op jit(solution)/shard_map/all_gather | solution.py:203
  41.8 8.8 %shard_map.203 = bf16[1024,1024]{1,0:T(8,128)(2,1)} custom-call(bf16[128,1024]{1,0:T(8,128)(2,1)} %q_ref.3, bf16[1024,1024]{1,0:T(8,128)(2,1)} %all-gather.2.cloned.1.call-done.k_ref, bf16[128,1024]{1,0:T(8,128)(2,1)} %cot_ref.3, f32[128,1024]{1,0:T(8,128)} %fusion.33.vis_ref), custom_call_target="tpu_custom_call" | custom-call | tf_op jit(solution)/shard_map/pallas_call | solution.py:139
  50.8 1.3 copy-done
  52.6 52.1 %all_to_all.9 = bf16[8,128,2048]{2,1,0:T(8,128)(2,1)S(1)} all-to-all(bf16[8,128,2048]{2,1,0:T(8,128)(2,1)S(1)} %pad_maximum_fusion), channel_id=1, replica_groups=mesh['ctx'=8,'tp'=4] {'ctx'}, dimensions={0} | all-to-all | bytes 8388608 | tf_op jit(solution)/shard_map/all_to_all | solution.py:211
  104.7 1.8 %fusion.50 = (bf16[1024,1024]{1,0:T(8,128)(2,1)S(1)}, bf16[1024,1024]{1,0:T(8,128)(2,1)}) fusion(bf16[1024,2048]{1,0:T(8,128)(2,1)S(1)} %bitcast.58), kind=kLoop, calls=%fused_computation.92 | loop fusion | bytes 8388608 | tf_op jit(solution)/shard_map/slice | solution.py:219
  106.8 10.6 %shard_map.204 = (bf16[1024,1024]{1,0:T(8,128)(2,1)}, f32[128,1024]{1,0:T(8,128)}, bf16[128,1024]{1,0:T(8,128)(2,1)}) custom-call(bf16[128,1024]{1,0:T(8,128)(2,1)} %q_ref.3, bf16[1024,1024]{1,0:T(8,128)(2,1)} %all-gather.2.cloned.1.call-done.k_ref, bf16[1024,1024]{1,0:T(8,128)(2,1)} %get-tuple-element.32.v_ref, bf16[128,1024]{1,0:T(8,128)(2,1)} %cot_ref.3, ...), custom_call_target="tpu_custom_call" | custom-call | tf_op jit(solution)/shard_map/pallas_call | solution.py:152
  118.6 2.8 %collective-permute-start.6 = (f32[128]{0:T(128)S(1)}, f32[128]{0:T(128)S(1)}, u32[]{:S(2)}, u32[]{:S(2)}) collective-permute-start(f32[128]{0:T(128)S(1)} %get-tuple-element.22), channel_id=1, source_target_pairs={{0,2},{1,3},{2,0},{3,1},{4,6},{5,7},{6,4},{7,5},{8,10},{9,11},{10,... | collective-permute-start | bytes 1544 | tf_op jit(solution)/shard_map/ppermute | solution.py:74
  123.1 1.9 %collective-permute-done.7 = f32[128]{0:T(128)S(1)} collective-permute-done((f32[128]{0:T(128)S(1)}, f32[128]{0:T(128)S(1)}, u32[]{:S(2)}, u32[]{:S(2)}) %collective-permute-start.7) | collective-permute-done | bytes 544 | tf_op jit(solution)/shard_map/ppermute | solution.py:74
  125.0 2.3 %fusion.25 = (bf16[128,1024]{1,0:T(8,128)(2,1)}, f32[128,1024]{1,0:T(8,128)S(1)}, bf16[128,1024]{1,0:T(8,128)(2,1)}) fusion(f32[1,128,1024]{2,0,1:T(1,128)S(1)} %fusion.8, f32[128]{0:T(128)S(1)} %fusion.42, bf16[128,1024]{1,0:T(8,128)(2,1)S(1)} %get-tuple-element.28, f32[128,1024]{1,0:T(8,128)S(1)} %convert_reduce_fusion, f32[1024]{0:T(1024)S(1)} %copy-done.14, ...), kind=kLoop, calls=%fused_computation.60 | loop fusion | flops 1441792 | bytes 3150848 | tf_op jit(solution)/shard_map/convert_element_type | solution.py:244
  127.4 1.3 collective-permute-start.8
  128.7 5.8 %fusion.6 = bf16[1,128,1024]{2,0,1:T(2,128)(2,1)S(1)} fusion(f32[1,255,1024]{2,1,0:T(8,128)S(1)} %copy-done.5, f32[128,1,1024]{2,0,1:T(8,128)S(1)} %bitcast.61), kind=kOutput, calls=%fused_computation.35 | convolution fusion | flops 201326592 | bytes 1830912 | tf_op jit(solution)/shard_map/conv_general_dilated | solution.py:34
  136.1 7.0 %fusion = f32[1,128,1024]{2,0,1:T(1,128)S(1)} fusion(f32[1,255,1024]{2,1,0:T(8,128)S(1)} %maximum_bitcast_fusion.1, f32[128,1,1024]{2,0,1:T(8,128)} %bitcast.64), kind=kOutput, calls=%fused_computation.11 | convolution fusion | flops 201326592 | bytes 2093056 | tf_op jit(solution)/shard_map/conv_general_dilated | solution.py:34
  148.9 1.3 collective-permute-start.9
  150.2 1.8 %collective-permute-done.9 = bf16[6,1024]{1,0:T(8,128)(2,1)S(1)} collective-permute-done((bf16[6,1024]{1,0:T(8,128)(2,1)S(1)}, bf16[6,1024]{1,0:T(8,128)(2,1)S(1)}, u32[]{:S(2)}, u32[]{:S(2)}) %collective-permute-start.9) | collective-permute-done | bytes 12320 | tf_op jit(solution)/shard_map/ppermute | solution.py:30
  152.9 5.0 %collective-permute-done.11 = bf16[136,1024]{1,0:T(8,128)(2,1)S(1)} collective-permute-done((bf16[136,1024]{1,0:T(8,128)(2,1)S(1)}, bf16[136,1024]{1,0:T(8,128)(2,1)S(1)}, u32[]{:S(2)}, u32[]{:S(2)}) %collective-permute-start.11) | collective-permute-done | bytes 278560 | tf_op jit(solution)/shard_map/ppermute | solution.py:62
  160.5 6.4 %collective-permute-done.12 = bf16[136,1024]{1,0:T(8,128)(2,1)S(1)} collective-permute-done((bf16[136,1024]{1,0:T(8,128)(2,1)S(1)}, bf16[136,1024]{1,0:T(8,128)(2,1)S(1)}, u32[]{:S(2)}, u32[]{:S(2)}) %collective-permute-start.12) | collective-permute-done | bytes 278560 | tf_op jit(solution)/shard_map/ppermute | solution.py:62
  (116 shorter events, 22.8 us)
Async XLA Ops:
  7.2 34.6 %all-gather.2.cloned.1.call-start = ((), (), s32[]{:S(2)}) async-start(), calls=%async_computation.2 | async-start | bytes 2359296 | tf_op jit(solution)/shard_map/all_gather | solution.py:203
  7.9 161.1 %reduce-scatter.2.cloned.1.call-start = ((), (), s32[]{:S(2)}) async-start(), calls=%async_computation.3 | async-start | bytes 2359296 | tf_op jit(solution)/shard_map/reduce_scatter | solution.py:230
  9.1 5.2 %collective-permute-start = (bf16[6,1024]{1,0:T(8,128)(2,1)S(1)}, bf16[6,1024]{1,0:T(8,128)(2,1)S(1)}, u32[]{:S(2)}, u32[]{:S(2)}) collective-permute-start(bf16[6,1024]{1,0:T(8,128)(2,1)S(1)} %slice.68), channel_id=1, source_target_pairs={{0,4},{4,8},{8,12},{12,16},{16,20},{20,24},{24,28},{1,5},{5,9},{9,... | collective-permute-start | bytes 36872 | tf_op jit(solution)/shard_map/ppermute | solution.py:30
  15.6 4.9 %copy-start.13 = (f32[128,1024]{1,0:T(8,128)S(1)}, f32[128,1024]{1,0:T(8,128)}, u32[]{:S(2)}) copy-start(f32[128,1024]{1,0:T(8,128)} %param.18) | copy-start | bytes 1572868
  15.6 5.2 %copy-start.16 = (s32[1024]{0:T(1024)S(1)}, s32[1024]{0:T(1024)}, u32[]{:S(2)}) copy-start(s32[1024]{0:T(1024)} %param.22) | copy-start | bytes 12292
  15.9 5.9 %collective-permute-start.1 = (bf16[127,1024]{1,0:T(8,128)(2,1)S(1)}, bf16[127,1024]{1,0:T(8,128)(2,1)S(1)}, u32[]{:S(2)}, u32[]{:S(2)}) collective-permute-start(bf16[127,1024]{1,0:T(8,128)(2,1)S(1)} %slice.66), channel_id=1, source_target_pairs={{0,4},{4,8},{8,12},{12,16},{16,20},{20,24},{24,28},{1,5},{5,9},{9,... | collective-permute-start | bytes 780296 | tf_op jit(solution)/shard_map/ppermute | solution.py:30
  22.0 5.8 %copy-start.4 = (f32[1,255,1024]{2,1,0:T(8,128)}, f32[1,255,1024]{2,1,0:T(8,128)S(1)}, u32[]{:S(2)}) copy-start(f32[1,255,1024]{2,1,0:T(8,128)S(1)} %maximum_bitcast_fusion) | copy-start | bytes 3133444
  22.0 5.8 %copy-start.3 = (bf16[128,1024]{1,0:T(8,128)(2,1)S(1)}, bf16[128,1024]{1,0:T(8,128)(2,1)}, u32[]{:S(2)}) copy-start(bf16[128,1024]{1,0:T(8,128)(2,1)} %param.16) | copy-start | bytes 786436
  22.0 13.8 %copy-start.14 = (f32[1024]{0:T(1024)S(1)}, f32[1024]{0:T(1024)}, u32[]{:S(2)}) copy-start(f32[1024]{0:T(1024)} %param.19) | copy-start | bytes 12292
  28.1 5.6 %collective-permute-start.2 = (f32[128]{0:T(128)S(1)}, f32[128]{0:T(128)S(1)}, u32[]{:S(2)}, u32[]{:S(2)}) collective-permute-start(f32[128]{0:T(128)S(1)} %get-tuple-element.27), channel_id=1, source_target_pairs={{0,1},{1,2},{2,3},{3,0},{4,5},{5,6},{6,7},{7,4},{8,9},{9,10},{10,1... | collective-permute-start | bytes 1544 | tf_op jit(solution)/shard_map/ppermute | solution.py:74
  29.7 4.4 %collective-permute-start.3 = (f32[128]{0:T(128)S(1)}, f32[128]{0:T(128)S(1)}, u32[]{:S(2)}, u32[]{:S(2)}) collective-permute-start(f32[128]{0:T(128)S(1)} %get-tuple-element.27), channel_id=1, source_target_pairs={{0,2},{1,3},{2,0},{3,1},{4,6},{5,7},{6,4},{7,5},{8,10},{9,11},{10,... | collective-permute-start | bytes 1544 | tf_op jit(solution)/shard_map/ppermute | solution.py:74
  32.3 3.5 %collective-permute-start.4 = (f32[128]{0:T(128)S(1)}, f32[128]{0:T(128)S(1)}, u32[]{:S(2)}, u32[]{:S(2)}) collective-permute-start(f32[128]{0:T(128)S(1)} %get-tuple-element.27), channel_id=1, source_target_pairs={{0,3},{1,0},{2,1},{3,2},{4,7},{5,4},{6,5},{7,6},{8,11},{9,8},{10,9... | collective-permute-start | bytes 1544 | tf_op jit(solution)/shard_map/ppermute | solution.py:74
  117.4 7.6 %copy-start.1 = (bf16[128,1024]{1,0:T(8,128)(2,1)S(1)}, bf16[128,1024]{1,0:T(8,128)(2,1)}, u32[]{:S(2)}) copy-start(bf16[128,1024]{1,0:T(8,128)(2,1)} %cot_ref.3) | copy-start | bytes 786436
  117.6 5.4 %collective-permute-start.5 = (f32[128]{0:T(128)S(1)}, f32[128]{0:T(128)S(1)}, u32[]{:S(2)}, u32[]{:S(2)}) collective-permute-start(f32[128]{0:T(128)S(1)} %get-tuple-element.22), channel_id=1, source_target_pairs={{0,1},{1,2},{2,3},{3,0},{4,5},{5,6},{6,7},{7,4},{8,9},{9,10},{10,1... | collective-permute-start | bytes 1544 | tf_op jit(solution)/shard_map/ppermute | solution.py:74
  118.6 4.4 %collective-permute-start.6 = (f32[128]{0:T(128)S(1)}, f32[128]{0:T(128)S(1)}, u32[]{:S(2)}, u32[]{:S(2)}) collective-permute-start(f32[128]{0:T(128)S(1)} %get-tuple-element.22), channel_id=1, source_target_pairs={{0,2},{1,3},{2,0},{3,1},{4,6},{5,7},{6,4},{7,5},{8,10},{9,11},{10,... | collective-permute-start | bytes 1544 | tf_op jit(solution)/shard_map/ppermute | solution.py:74
  121.4 3.5 %collective-permute-start.7 = (f32[128]{0:T(128)S(1)}, f32[128]{0:T(128)S(1)}, u32[]{:S(2)}, u32[]{:S(2)}) collective-permute-start(f32[128]{0:T(128)S(1)} %get-tuple-element.22), channel_id=1, source_target_pairs={{0,3},{1,0},{2,1},{3,2},{4,7},{5,4},{6,5},{7,6},{8,11},{9,8},{10,9... | collective-permute-start | bytes 1544 | tf_op jit(solution)/shard_map/ppermute | solution.py:74
  127.4 7.5 %collective-permute-start.8 = (bf16[127,1024]{1,0:T(8,128)(2,1)S(1)}, bf16[127,1024]{1,0:T(8,128)(2,1)}, u32[]{:S(2)}, u32[]{:S(2)}) collective-permute-start(bf16[127,1024]{1,0:T(8,128)(2,1)S(1)} %slice.65), channel_id=1, source_target_pairs={{4,0},{8,4},{12,8},{16,12},{20,16},{24,20},{28,24},{5,1},{9,5},{13... | collective-permute-start | bytes 780296 | tf_op jit(solution)/shard_map/ppermute | solution.py:30
  136.1 7.0 %copy-start.7 = (bf16[128,1024]{1,0:T(8,128)(2,1)S(1)}, bf16[128,1024]{1,0:T(8,128)(2,1)}, u32[]{:S(2)}) copy-start(bf16[128,1024]{1,0:T(8,128)(2,1)} %param.17) | copy-start | bytes 786436
  145.7 2.4 %collective-permute-start.10 = (bf16[136,1024]{1,0:T(8,128)(2,1)S(1)}, bf16[136,1024]{1,0:T(8,128)(2,1)S(1)}, u32[]{:S(2)}, u32[]{:S(2)}) collective-permute-start(bf16[136,1024]{1,0:T(8,128)(2,1)S(1)} %pad_maximum_fusion.1), channel_id=1, source_target_pairs={{0,4},{4,0},{8,12},{12,8},{16,20},{20,16},{24,28},{28,24},{1,5},{5... | collective-permute-start | bytes 835592 | tf_op jit(solution)/shard_map/ppermute | solution.py:62
  148.2 9.7 %collective-permute-start.11 = (bf16[136,1024]{1,0:T(8,128)(2,1)S(1)}, bf16[136,1024]{1,0:T(8,128)(2,1)S(1)}, u32[]{:S(2)}, u32[]{:S(2)}) collective-permute-start(bf16[136,1024]{1,0:T(8,128)(2,1)S(1)} %add_convert_fusion.1), channel_id=1, source_target_pairs={{0,8},{4,12},{8,0},{12,4},{16,24},{20,28},{24,16},{28,20},{1,9},{5... | collective-permute-start | bytes 835592 | tf_op jit(solution)/shard_map/ppermute | solution.py:62
  148.9 3.1 %collective-permute-start.9 = (bf16[6,1024]{1,0:T(8,128)(2,1)S(1)}, bf16[6,1024]{1,0:T(8,128)(2,1)S(1)}, u32[]{:S(2)}, u32[]{:S(2)}) collective-permute-start(bf16[6,1024]{1,0:T(8,128)(2,1)S(1)} %slice.67), channel_id=1, source_target_pairs={{4,0},{8,4},{12,8},{16,12},{20,16},{24,20},{28,24},{5,1},{9,5},{13... | collective-permute-start | bytes 36872 | tf_op jit(solution)/shard_map/ppermute | solution.py:30
  152.0 6.3 %copy-start.15 = (f32[7,1024]{1,0:T(8,128)S(1)}, f32[7,1024]{1,0:T(8,128)}, u32[]{:S(2)}) copy-start(f32[7,1024]{1,0:T(8,128)} %param.15) | copy-start | bytes 86020
  152.0 6.3 %copy-start.17 = (pred[8,17]{0,1:T(8,128)(4,1)S(1)}, pred[8,17]{0,1:T(8,128)(4,1)}, u32[]{:S(2)}) copy-start(pred[8,17]{0,1:T(8,128)(4,1)} %constant.100) | copy-start | bytes 412
  158.0 8.9 %collective-permute-start.12 = (bf16[136,1024]{1,0:T(8,128)(2,1)S(1)}, bf16[136,1024]{1,0:T(8,128)(2,1)S(1)}, u32[]{:S(2)}, u32[]{:S(2)}) collective-permute-start(bf16[136,1024]{1,0:T(8,128)(2,1)S(1)} %add_convert_fusion), channel_id=1, source_target_pairs={{0,16},{4,20},{8,24},{12,28},{16,0},{20,4},{24,8},{28,12},{1,17},{... | collective-permute-start | bytes 835592 | tf_op jit(solution)/shard_map/ppermute | solution.py:62
  (9 other events, 13.3 us)
Sparse Core Ops, SparseCore 0:
  9.9 31.8 all-gather.1
  122.7 38.5 reduce-scatter.1

commit v19 on v12

--- a/solution.py
+++ b/solution.py
@@ -94,28 +94,28 @@
     return (raised * (1.0 / jnp.sum(raised, axis=1, keepdims=True))).astype(jnp.bfloat16)
 
 
-def value_block(scale_factor, q_ref, k_ref, cot_ref, vis_ref, dv_ref, w_ref):
+def value_block(scale_factor, q_ref, k_ref, cot_ref, vis_ref, dv_ref):
     contract_first = (((0,), (0,)), ((), ()))
     visible = vis_ref[...] > 0.5
-    for head in range(w_ref.shape[0]):
+    for head in range(q_ref.shape[1] // HD):
         columns = slice(head * HD, (head + 1) * HD)
         weights = head_weights(scale_factor, q_ref[:, columns], k_ref[:, columns], visible)
-        w_ref[head] = weights
         dv_ref[:, columns] = lax.dot_general(
             weights, cot_ref[:, columns], contract_first, preferred_element_type=jnp.float32
         ).astype(jnp.bfloat16)
 
 
-def attention_block(scale_factor, q_ref, k_ref, v_ref, cot_ref, w_ref, dk_ref, att_ref, dq_ref):
+def attention_block(scale_factor, q_ref, k_ref, v_ref, cot_ref, vis_ref, dk_ref, att_ref, dq_ref):
     contract_last = (((1,), (1,)), ((), ()))
     contract_first = (((0,), (0,)), ((), ()))
-    for head in range(w_ref.shape[0]):
+    visible = vis_ref[...] > 0.5
+    for head in range(q_ref.shape[1] // HD):
         columns = slice(head * HD, (head + 1) * HD)
         query_head = q_ref[:, columns]
         key_head = k_ref[:, columns]
         value_head = v_ref[:, columns]
         cotangent_head = cot_ref[:, columns]
-        weights = w_ref[head]
+        weights = head_weights(scale_factor, query_head, key_head, visible)
         attended = jnp.dot(weights, value_head, preferred_element_type=jnp.float32)
         weight_grad = lax.dot_general(
             cotangent_head, value_head, contract_last, preferred_element_type=jnp.float32
@@ -150,29 +150,27 @@
         functools.partial(value_block, scale_factor),
         grid=(steps,),
         in_specs=[local_spec, whole_spec, local_spec, mask_spec],
-        out_specs=[whole_spec, weight_spec],
-        out_shape=[
-            jax.ShapeDtypeStruct((total_rows, width_local), jnp.bfloat16),
-            jax.ShapeDtypeStruct((width_local // HD, local_rows, total_rows), jnp.bfloat16),
-        ],
+        out_specs=whole_spec,
+        out_shape=jax.ShapeDtypeStruct((total_rows, width_local), jnp.bfloat16),
     )(queries, keys_whole, cotangent, visible)
 
 
-def head_attention(queries, keys_whole, values_whole, cotangent, weights, scale_factor):
+def head_attention(queries, keys_whole, values_whole, cotangent, visible, scale_factor):
     local_rows, width_local = queries.shape
     total_rows = keys_whole.shape[0]
     local_spec, whole_spec, weight_spec, steps = head_specs(local_rows, total_rows, width_local)
+    mask_spec = pl.BlockSpec((local_rows, total_rows), lambda h: (0, 0))
     return pl.pallas_call(
         functools.partial(attention_block, scale_factor),
         grid=(steps,),
-        in_specs=[local_spec, whole_spec, whole_spec, local_spec, weight_spec],
+        in_specs=[local_spec, whole_spec, whole_spec, local_spec, mask_spec],
         out_specs=[whole_spec, local_spec, local_spec],
         out_shape=[
             jax.ShapeDtypeStruct((total_rows, width_local), jnp.bfloat16),
             jax.ShapeDtypeStruct((local_rows, width_local), jnp.float32),
             jax.ShapeDtypeStruct((local_rows, width_local), jnp.bfloat16),
         ],
-    )(queries, keys_whole, values_whole, cotangent, weights)
+    )(queries, keys_whole, values_whole, cotangent, visible)
 
 
 def shards(
@@ -220,7 +218,7 @@
     query_seg = lax.dynamic_slice_in_dim(segments, position, local_rows, 0)
     visible = (key_pos[None, :] <= query_pos[:, None]) & (segments[None, :] == query_seg[:, None])
     mask = visible.astype(jnp.float32)
-    value_part, weights_all = head_values_grad(queries, keys_whole, cotangent, mask, scale_factor)
+    value_part = head_values_grad(queries, keys_whole, cotangent, mask, scale_factor)
     value_grad = (
         lax.all_to_all(value_part, "ctx", 0, 0, tiled=True)
         .reshape(ctx_count, local_rows, width_local)
@@ -229,7 +227,7 @@
     )
     values_whole = lax.all_gather(normed, "ctx", axis=0, tiled=True)
     key_part, attended_all, queries_grad = head_attention(
-        queries, keys_whole, values_whole, cotangent, weights_all, scale_factor
+        queries, keys_whole, values_whole, cotangent, mask, scale_factor
     )
     result = (second_wide + attended_all).astype(jnp.bfloat16)
     key_part, value_grad = lax.optimization_barrier((key_part, value_grad))

time: 155 us -> 158 us (1.019)
  Pallas kernels: 15 us -> 17.9 us
    pallas_call x1, Pallas kernels: 7.27 us -> 10.2 us  [head_attention(): pl.pallas_call(functools.partial(attention_block, scale_factor), grid=(st...]
  transfers between devices with their start and end apart: 17 -> 17, of which waited for: 12 -> 11; matrix products, arithmetic and copies ran while one was open for 22% -> 22% of each run, Pallas kernels for 10% -> 11%
where the time goes in v19:
time: 158 us; the launch traced here: 157 us
  waiting for transfers between devices  51.4 us (33%)
  starting transfers between devices  35.8 us (23%)
  matrix products  19.7 us (12%)
  Pallas kernels  17.9 us (11%)
  between operations  14.4 us (9%)
  other arithmetic  9.97 us (6%)
  local copies, waits for them, and re-layouts  8.26 us (5%)
    all_gather x1, waiting for transfers between devices, shards(): values_whole = lax.all_gather(normed, 'ctx', axis=0, tiled=True)  27.6 us
    conv_general_dilated x6, matrix products, depthwise(): lax.conv_general_dilated(padded[None], tap_rows[:, None, :], (1,), 'VALID...  19.7 us
    ppermute x3, waiting for transfers between devices, butterfly_total(): lax.ppermute(rounded, axis, pairs).astype(value.dtype)  13.2 us
    ppermute x6, starting transfers between devices, exchange_total(): arrived = lax.ppermute(value, axis, pairs)  10.9 us
    pallas_call x1, Pallas kernels, head_attention(): pl.pallas_call(functools.partial(attention_block, scale_factor), grid=(st...  10.2 us
    ppermute x4, starting transfers between devices, passed_along(): lax.ppermute(value, axis, [(source, source + steps) for source in range(l...  9.57 us
    ppermute x3, starting transfers between devices, butterfly_total(): lax.ppermute(rounded, axis, pairs).astype(value.dtype)  9.39 us
    pallas_call x1, Pallas kernels, head_values_grad(): pl.pallas_call(functools.partial(value_block, scale_factor), grid=(steps,...  7.72 us
  transfers between devices with their start and end apart: 17, of which 11 were waited for; matrix products, arithmetic and copies ran while one was open for 22% of the time, Pallas kernels for 11%

profile of v19, /device:TPU:0, one launch (start us, length us, event | category | flops | bytes accessed | tf_op | source)
XLA Modules:
  0.0 157.4 jit_solution(5548830750355920648)
XLA Ops:
  9.1 2.4 %collective-permute-start = (bf16[6,1024]{1,0:T(8,128)(2,1)S(1)}, bf16[6,1024]{1,0:T(8,128)(2,1)S(1)}, u32[]{:S(2)}, u32[]{:S(2)}) collective-permute-start(bf16[6,1024]{1,0:T(8,128)(2,1)S(1)} %slice.58), channel_id=1, source_target_pairs={{0,4},{4,8},{8,12},{12,16},{16,20},{20,24},{24,28},{1,5},{5,9},{9,... | collective-permute-start | bytes 36872 | tf_op jit(solution)/shard_map/ppermute | solution.py:30
  11.4 2.8 %rev.12 = f32[7,1024]{1,0:T(8,128)S(1)} reverse(f32[7,1024]{1,0:T(8,128)} %param.15), dimensions={0} | reverse | bytes 57344 | tf_op jit(solution)/shard_map/rev | solution.py:200
  15.9 4.7 %collective-permute-start.1 = (bf16[127,1024]{1,0:T(8,128)(2,1)S(1)}, bf16[127,1024]{1,0:T(8,128)(2,1)S(1)}, u32[]{:S(2)}, u32[]{:S(2)}) collective-permute-start(bf16[127,1024]{1,0:T(8,128)(2,1)S(1)} %slice.56), channel_id=1, source_target_pairs={{0,4},{4,8},{8,12},{12,16},{16,20},{20,24},{24,28},{1,5},{5,9},{9,... | collective-permute-start | bytes 780296 | tf_op jit(solution)/shard_map/ppermute | solution.py:30
  21.9 5.8 %fusion.8 = f32[1,128,1024]{2,0,1:T(1,128)S(1)} fusion(f32[1,255,1024]{2,1,0:T(8,128)S(1)} %maximum_bitcast_fusion, f32[128,1,1024]{2,0,1:T(8,128)S(1)} %bitcast.60), kind=kOutput, calls=%fused_computation.36 | convolution fusion | flops 201326592 | bytes 2093056 | tf_op jit(solution)/shard_map/conv_general_dilated | solution.py:34
  28.7 1.6 %collective-permute-start.2 = (f32[128]{0:T(128)S(1)}, f32[128]{0:T(128)S(1)}, u32[]{:S(2)}, u32[]{:S(2)}) collective-permute-start(f32[128]{0:T(128)S(1)} %get-tuple-element.27), channel_id=1, source_target_pairs={{0,1},{1,2},{2,3},{3,0},{4,5},{5,6},{6,7},{7,4},{8,9},{9,10},{10,1... | collective-permute-start | bytes 1544 | tf_op jit(solution)/shard_map/ppermute | solution.py:74
  30.3 2.6 %collective-permute-start.3 = (f32[128]{0:T(128)S(1)}, f32[128]{0:T(128)S(1)}, u32[]{:S(2)}, u32[]{:S(2)}) collective-permute-start(f32[128]{0:T(128)S(1)} %get-tuple-element.27), channel_id=1, source_target_pairs={{0,2},{1,3},{2,0},{3,1},{4,6},{5,7},{6,4},{7,5},{8,10},{9,11},{10,... | collective-permute-start | bytes 1544 | tf_op jit(solution)/shard_map/ppermute | solution.py:74
  34.8 1.7 %collective-permute-done.4 = f32[128]{0:T(128)S(1)} collective-permute-done((f32[128]{0:T(128)S(1)}, f32[128]{0:T(128)S(1)}, u32[]{:S(2)}, u32[]{:S(2)}) %collective-permute-start.4) | collective-permute-done | bytes 544 | tf_op jit(solution)/shard_map/ppermute | solution.py:74
  38.5 3.2 %all-gather.3.cloned.1.call-done.k_ref = bf16[1024,1024]{1,0:T(8,128)(2,1)} async-done(((bf16[128,1024]{1,0:T(8,128)(2,1)}), bf16[1024,1024]{1,0:T(8,128)(2,1)}) %all-gather.3.cloned.1.call-update) | async-done | bytes 2097168 | tf_op jit(solution)/shard_map/all_gather | solution.py:214
  41.7 7.7 %shard_map.204 = bf16[1024,1024]{1,0:T(8,128)(2,1)} custom-call(bf16[128,1024]{1,0:T(8,128)(2,1)} %q_ref.3, bf16[1024,1024]{1,0:T(8,128)(2,1)} %all-gather.3.cloned.1.call-done.k_ref, bf16[128,1024]{1,0:T(8,128)(2,1)} %cot_ref.3, f32[128,1024]{1,0:T(8,128)} %fusion.33.vis_ref), custom_call_target="tpu_custom_call" | custom-call | tf_op jit(solution)/shard_map/pallas_call | solution.py:149
  49.4 5.8 %all-to-all-start = ((bf16[8,128,1024]{2,1,0:T(8,128)(2,1)}), bf16[8,128,1024]{2,1,0:T(8,128)(2,1)S(1)}, u32[]{:S(2)}, u32[]{:S(2)}) async-start(bf16[8,128,1024]{2,1,0:T(8,128)(2,1)} %bitcast.55), calls=%async_computation | async-start | bytes 4194304 | tf_op jit(solution)/shard_map/all_to_all | solution.py:223
  55.3 27.6 %all-gather.5.cloned.1.call-done.v_ref = bf16[1024,1024]{1,0:T(8,128)(2,1)} async-done(((bf16[128,1024]{1,0:T(8,128)(2,1)}), bf16[1024,1024]{1,0:T(8,128)(2,1)}) %all-gather.5.cloned.1.call-update) | async-done | bytes 2097168 | tf_op jit(solution)/shard_map/all_gather | solution.py:228
  82.9 10.2 %shard_map.203 = (bf16[1024,1024]{1,0:T(8,128)(2,1)}, f32[128,1024]{1,0:T(8,128)}, bf16[128,1024]{1,0:T(8,128)(2,1)}) custom-call(bf16[128,1024]{1,0:T(8,128)(2,1)} %q_ref.3, bf16[1024,1024]{1,0:T(8,128)(2,1)} %all-gather.3.cloned.1.call-done.k_ref, bf16[1024,1024]{1,0:T(8,128)(2,1)} %all-gather.5.cloned.1.call-done.v_ref, bf16[128,1024]{1,0:T(8,128)(2,1)} %cot_ref.3, ...), custom_call_target="tpu_custom_call" | custom-call | tf_op jit(solution)/shard_map/pallas_call | solution.py:163
  93.7 1.5 collective-permute-start.5
  95.2 2.4 %collective-permute-start.6 = (f32[128]{0:T(128)S(1)}, f32[128]{0:T(128)S(1)}, u32[]{:S(2)}, u32[]{:S(2)}) collective-permute-start(f32[128]{0:T(128)S(1)} %get-tuple-element.22), channel_id=1, source_target_pairs={{0,2},{1,3},{2,0},{3,1},{4,6},{5,7},{6,4},{7,5},{8,10},{9,11},{10,... | collective-permute-start | bytes 1544 | tf_op jit(solution)/shard_map/ppermute | solution.py:74
  97.6 1.4 collective-permute-start.7
  99.7 1.5 collective-permute-done.7
  104.5 5.8 %fusion.6 = bf16[1,128,1024]{2,0,1:T(2,128)(2,1)S(1)} fusion(f32[1,255,1024]{2,1,0:T(8,128)S(1)} %copy-done.9, f32[128,1,1024]{2,0,1:T(8,128)S(1)} %bitcast.56), kind=kOutput, calls=%fused_computation.34 | convolution fusion | flops 201326592 | bytes 1830912 | tf_op jit(solution)/shard_map/conv_general_dilated | solution.py:34
  111.3 5.8 %fusion = f32[1,128,1024]{2,0,1:T(1,128)S(1)} fusion(f32[1,255,1024]{2,1,0:T(8,128)S(1)} %maximum_bitcast_fusion.1, f32[128,1,1024]{2,0,1:T(8,128)S(1)} %bitcast.59), kind=kOutput, calls=%fused_computation.10 | convolution fusion | flops 201326592 | bytes 2093056 | tf_op jit(solution)/shard_map/conv_general_dilated | solution.py:34
  119.8 5.0 %collective-permute-start.10 = (bf16[136,1024]{1,0:T(8,128)(2,1)S(1)}, bf16[136,1024]{1,0:T(8,128)(2,1)S(1)}, u32[]{:S(2)}, u32[]{:S(2)}) collective-permute-start(bf16[136,1024]{1,0:T(8,128)(2,1)S(1)} %pad_maximum_fusion), channel_id=1, source_target_pairs={{0,4},{4,0},{8,12},{12,8},{16,20},{20,16},{24,28},{28,24},{1,5},{5... | collective-permute-start | bytes 835592 | tf_op jit(solution)/shard_map/ppermute | solution.py:62
  126.1 2.9 %collective-permute-start.11 = (bf16[136,1024]{1,0:T(8,128)(2,1)S(1)}, bf16[136,1024]{1,0:T(8,128)(2,1)S(1)}, u32[]{:S(2)}, u32[]{:S(2)}) collective-permute-start(bf16[136,1024]{1,0:T(8,128)(2,1)S(1)} %add_convert_fusion.1), channel_id=1, source_target_pairs={{0,8},{4,12},{8,0},{12,4},{16,24},{20,28},{24,16},{28,20},{1,9},{5... | collective-permute-start | bytes 835592 | tf_op jit(solution)/shard_map/ppermute | solution.py:62
  130.2 1.8 %collective-permute-done.9 = bf16[6,1024]{1,0:T(8,128)(2,1)S(1)} collective-permute-done((bf16[6,1024]{1,0:T(8,128)(2,1)S(1)}, bf16[6,1024]{1,0:T(8,128)(2,1)S(1)}, u32[]{:S(2)}, u32[]{:S(2)}) %collective-permute-start.9) | collective-permute-done | bytes 12320 | tf_op jit(solution)/shard_map/ppermute | solution.py:30
  132.9 3.4 %collective-permute-done.11 = bf16[136,1024]{1,0:T(8,128)(2,1)S(1)} collective-permute-done((bf16[136,1024]{1,0:T(8,128)(2,1)S(1)}, bf16[136,1024]{1,0:T(8,128)(2,1)S(1)}, u32[]{:S(2)}, u32[]{:S(2)}) %collective-permute-start.11) | collective-permute-done | bytes 278560 | tf_op jit(solution)/shard_map/ppermute | solution.py:62
  136.4 1.5 collective-permute-start.12
  140.1 8.6 %collective-permute-done.12 = bf16[136,1024]{1,0:T(8,128)(2,1)S(1)} collective-permute-done((bf16[136,1024]{1,0:T(8,128)(2,1)S(1)}, bf16[136,1024]{1,0:T(8,128)(2,1)S(1)}, u32[]{:S(2)}, u32[]{:S(2)}) %collective-permute-start.12) | collective-permute-done | bytes 278560 | tf_op jit(solution)/shard_map/ppermute | solution.py:62
  (129 shorter events, 25.4 us)
Async XLA Ops:
  7.2 34.5 %all-gather.3.cloned.1.call-start = ((), (), s32[]{:S(2)}) async-start(), calls=%async_computation.2 | async-start | bytes 2359296 | tf_op jit(solution)/shard_map/all_gather | solution.py:214
  7.9 75.0 %all-gather.5.cloned.1.call-start = ((), (), s32[]{:S(2)}) async-start(), calls=%async_computation.3 | async-start | bytes 2359296 | tf_op jit(solution)/shard_map/all_gather | solution.py:228
  9.1 5.2 %collective-permute-start = (bf16[6,1024]{1,0:T(8,128)(2,1)S(1)}, bf16[6,1024]{1,0:T(8,128)(2,1)S(1)}, u32[]{:S(2)}, u32[]{:S(2)}) collective-permute-start(bf16[6,1024]{1,0:T(8,128)(2,1)S(1)} %slice.58), channel_id=1, source_target_pairs={{0,4},{4,8},{8,12},{12,16},{16,20},{20,24},{24,28},{1,5},{5,9},{9,... | collective-permute-start | bytes 36872 | tf_op jit(solution)/shard_map/ppermute | solution.py:30
  15.9 5.8 %collective-permute-start.1 = (bf16[127,1024]{1,0:T(8,128)(2,1)S(1)}, bf16[127,1024]{1,0:T(8,128)(2,1)S(1)}, u32[]{:S(2)}, u32[]{:S(2)}) collective-permute-start(bf16[127,1024]{1,0:T(8,128)(2,1)S(1)} %slice.56), channel_id=1, source_target_pairs={{0,4},{4,8},{8,12},{12,16},{16,20},{20,24},{24,28},{1,5},{5,9},{9,... | collective-permute-start | bytes 780296 | tf_op jit(solution)/shard_map/ppermute | solution.py:30
  21.9 6.6 %copy-start.6 = (bf16[128,1024]{1,0:T(8,128)(2,1)S(1)}, bf16[128,1024]{1,0:T(8,128)(2,1)}, u32[]{:S(2)}) copy-start(bf16[128,1024]{1,0:T(8,128)(2,1)} %param.16) | copy-start | bytes 786436
  21.9 14.6 %copy-start.20 = (f32[1024]{0:T(1024)S(1)}, f32[1024]{0:T(1024)}, u32[]{:S(2)}) copy-start(f32[1024]{0:T(1024)} %param.19) | copy-start | bytes 12292
  27.7 9.7 %copy-start.22 = (s32[1024]{0:T(1024)S(1)}, s32[1024]{0:T(1024)}, u32[]{:S(2)}) copy-start(s32[1024]{0:T(1024)} %param.22) | copy-start | bytes 12292
  28.7 5.6 %collective-permute-start.2 = (f32[128]{0:T(128)S(1)}, f32[128]{0:T(128)S(1)}, u32[]{:S(2)}, u32[]{:S(2)}) collective-permute-start(f32[128]{0:T(128)S(1)} %get-tuple-element.27), channel_id=1, source_target_pairs={{0,1},{1,2},{2,3},{3,0},{4,5},{5,6},{6,7},{7,4},{8,9},{9,10},{10,1... | collective-permute-start | bytes 1544 | tf_op jit(solution)/shard_map/ppermute | solution.py:74
  30.3 4.4 %collective-permute-start.3 = (f32[128]{0:T(128)S(1)}, f32[128]{0:T(128)S(1)}, u32[]{:S(2)}, u32[]{:S(2)}) collective-permute-start(f32[128]{0:T(128)S(1)} %get-tuple-element.27), channel_id=1, source_target_pairs={{0,2},{1,3},{2,0},{3,1},{4,6},{5,7},{6,4},{7,5},{8,10},{9,11},{10,... | collective-permute-start | bytes 1544 | tf_op jit(solution)/shard_map/ppermute | solution.py:74
  32.9 3.5 %collective-permute-start.4 = (f32[128]{0:T(128)S(1)}, f32[128]{0:T(128)S(1)}, u32[]{:S(2)}, u32[]{:S(2)}) collective-permute-start(f32[128]{0:T(128)S(1)} %get-tuple-element.27), channel_id=1, source_target_pairs={{0,3},{1,0},{2,1},{3,2},{4,7},{5,4},{6,5},{7,6},{8,11},{9,8},{10,9... | collective-permute-start | bytes 1544 | tf_op jit(solution)/shard_map/ppermute | solution.py:74
  49.4 43.7 %all-to-all-start = ((bf16[8,128,1024]{2,1,0:T(8,128)(2,1)}), bf16[8,128,1024]{2,1,0:T(8,128)(2,1)S(1)}, u32[]{:S(2)}, u32[]{:S(2)}) async-start(bf16[8,128,1024]{2,1,0:T(8,128)(2,1)} %bitcast.55), calls=%async_computation | async-start | bytes 4194304 | tf_op jit(solution)/shard_map/all_to_all | solution.py:223
  55.2 95.6 %reduce-scatter.2.cloned.1.call-start = ((), (), s32[]{:S(2)}) async-start(), calls=%async_computation.4 | async-start | bytes 2359296 | tf_op jit(solution)/shard_map/reduce_scatter | solution.py:234
  93.4 7.8 %copy-start = (bf16[128,1024]{1,0:T(8,128)(2,1)S(1)}, bf16[128,1024]{1,0:T(8,128)(2,1)}, u32[]{:S(2)}) copy-start(bf16[128,1024]{1,0:T(8,128)(2,1)} %cot_ref.3) | copy-start | bytes 786436
  93.4 7.8 %copy-start.3 = (f32[1,128,1024]{2,0,1:T(1,128)S(1)}, f32[1,128,1024]{2,0,1:T(1,128)}, u32[]{:S(2)}) copy-start(f32[1,128,1024]{2,0,1:T(1,128)} %copy-done.2) | copy-start | bytes 1572868
  93.5 7.7 %copy-start.19 = (f32[128,1024]{1,0:T(8,128)S(1)}, f32[128,1024]{1,0:T(8,128)}, u32[]{:S(2)}) copy-start(f32[128,1024]{1,0:T(8,128)} %get-tuple-element.16) | copy-start | bytes 1572868
  93.7 5.5 %collective-permute-start.5 = (f32[128]{0:T(128)S(1)}, f32[128]{0:T(128)S(1)}, u32[]{:S(2)}, u32[]{:S(2)}) collective-permute-start(f32[128]{0:T(128)S(1)} %get-tuple-element.22), channel_id=1, source_target_pairs={{0,1},{1,2},{2,3},{3,0},{4,5},{5,6},{6,7},{7,4},{8,9},{9,10},{10,1... | collective-permute-start | bytes 1544 | tf_op jit(solution)/shard_map/ppermute | solution.py:74
  95.2 4.4 %collective-permute-start.6 = (f32[128]{0:T(128)S(1)}, f32[128]{0:T(128)S(1)}, u32[]{:S(2)}, u32[]{:S(2)}) collective-permute-start(f32[128]{0:T(128)S(1)} %get-tuple-element.22), channel_id=1, source_target_pairs={{0,2},{1,3},{2,0},{3,1},{4,6},{5,7},{6,4},{7,5},{8,10},{9,11},{10,... | collective-permute-start | bytes 1544 | tf_op jit(solution)/shard_map/ppermute | solution.py:74
  97.6 3.5 %collective-permute-start.7 = (f32[128]{0:T(128)S(1)}, f32[128]{0:T(128)S(1)}, u32[]{:S(2)}, u32[]{:S(2)}) collective-permute-start(f32[128]{0:T(128)S(1)} %get-tuple-element.22), channel_id=1, source_target_pairs={{0,3},{1,0},{2,1},{3,2},{4,7},{5,4},{6,5},{7,6},{8,11},{9,8},{10,9... | collective-permute-start | bytes 1544 | tf_op jit(solution)/shard_map/ppermute | solution.py:74
  103.2 7.5 %collective-permute-start.8 = (bf16[127,1024]{1,0:T(8,128)(2,1)}, bf16[127,1024]{1,0:T(8,128)(2,1)S(1)}, u32[]{:S(2)}, u32[]{:S(2)}) collective-permute-start(bf16[127,1024]{1,0:T(8,128)(2,1)} %slice.55), channel_id=1, source_target_pairs={{4,0},{8,4},{12,8},{16,12},{20,16},{24,20},{28,24},{5,1},{9,5},{13... | collective-permute-start | bytes 780296 | tf_op jit(solution)/shard_map/ppermute | solution.py:30
  119.8 6.2 %collective-permute-start.10 = (bf16[136,1024]{1,0:T(8,128)(2,1)S(1)}, bf16[136,1024]{1,0:T(8,128)(2,1)S(1)}, u32[]{:S(2)}, u32[]{:S(2)}) collective-permute-start(bf16[136,1024]{1,0:T(8,128)(2,1)S(1)} %pad_maximum_fusion), channel_id=1, source_target_pairs={{0,4},{4,0},{8,12},{12,8},{16,20},{20,16},{24,28},{28,24},{1,5},{5... | collective-permute-start | bytes 835592 | tf_op jit(solution)/shard_map/ppermute | solution.py:62
  126.1 10.3 %collective-permute-start.11 = (bf16[136,1024]{1,0:T(8,128)(2,1)S(1)}, bf16[136,1024]{1,0:T(8,128)(2,1)S(1)}, u32[]{:S(2)}, u32[]{:S(2)}) collective-permute-start(bf16[136,1024]{1,0:T(8,128)(2,1)S(1)} %add_convert_fusion.1), channel_id=1, source_target_pairs={{0,8},{4,12},{8,0},{12,4},{16,24},{20,28},{24,16},{28,20},{1,9},{5... | collective-permute-start | bytes 835592 | tf_op jit(solution)/shard_map/ppermute | solution.py:62
  128.9 3.1 %collective-permute-start.9 = (bf16[6,1024]{1,0:T(8,128)(2,1)S(1)}, bf16[6,1024]{1,0:T(8,128)(2,1)S(1)}, u32[]{:S(2)}, u32[]{:S(2)}) collective-permute-start(bf16[6,1024]{1,0:T(8,128)(2,1)S(1)} %slice.57), channel_id=1, source_target_pairs={{4,0},{8,4},{12,8},{16,12},{20,16},{24,20},{28,24},{5,1},{9,5},{13... | collective-permute-start | bytes 36872 | tf_op jit(solution)/shard_map/ppermute | solution.py:30
  132.0 5.9 %copy-start.21 = (f32[7,1024]{1,0:T(8,128)S(1)}, f32[7,1024]{1,0:T(8,128)}, u32[]{:S(2)}) copy-start(f32[7,1024]{1,0:T(8,128)} %param.15) | copy-start | bytes 86020
  136.4 12.3 %collective-permute-start.12 = (bf16[136,1024]{1,0:T(8,128)(2,1)S(1)}, bf16[136,1024]{1,0:T(8,128)(2,1)S(1)}, u32[]{:S(2)}, u32[]{:S(2)}) collective-permute-start(bf16[136,1024]{1,0:T(8,128)(2,1)S(1)} %add_convert_fusion), channel_id=1, source_target_pairs={{0,16},{4,20},{8,24},{12,28},{16,0},{20,4},{24,8},{28,12},{1,17},{... | collective-permute-start | bytes 835592 | tf_op jit(solution)/shard_map/ppermute | solution.py:62
  (17 other events, 50.1 us)
Sparse Core Ops, SparseCore 0:
  9.9 31.7 all-gather.2
  44.1 38.7 all-gather.4
  99.2 48.1 reduce-scatter.1
